TPU v7x, 32 devices: a whole 2x2x4 slice. The times are simulated.
32 devices in a mesh: blk: 8 (over z, x), col: 4 (over y, core).
Axes of the slice: x: 2, y: 2, z: 4, core: 2. Of those that a mesh axis runs over, the one named last changes fastest.
Arguments:
- node_features: bfloat16 [16384, 128], P(('blk', 'col')), may hold values from -6 to 6
- degree: int32 [16384], P(('blk', 'col')), may hold values from 1 to 8
- adjacency: bfloat16 [11520, 128, 128], P(('blk', 'col')), may hold values from -0.125 to 0.125
- tile_rows: int32 [11520], P(('blk', 'col')), may hold values from 0 to 15
- tile_cols: int32 [11520], P(('blk', 'col')), may hold values from 0 to 3
- counts: int32 [160], P(('blk', 'col')), may hold values from 1 to 72, as said below
- weight: bfloat16 [128, 256], replicated, may hold values from -0.5 to 0.5
- bias_vector: float32 [256], replicated, may hold values from -3 to 3
- cotangent: bfloat16 [16384, 256], P(('blk', 'col')), may hold values from -6 to 6
Outputs:
- activations: bfloat16 [16384, 256], P(('blk', 'col'))
- grad_features: bfloat16 [16384, 128], P(('blk', 'col'))
- grad_weight: float32 [128, 256], replicated
- grad_bias: float32 [256], replicated
Inputs may be any that keep to these rules, and one draw needn't show every extreme that they name: `counts`: every draw has some pair with all 72 slots live.
All inputs are finite; a program needn't handle non-finite values.
Results may differ from a plain program's by a relative error of at most 0.012.
Values may be sent and summed in bfloat16 or wider, within the bound.
No kernel may reach another device: no remote copies, remote signals or barrier semaphores. Data moves between devices by JAX's collectives and lax.ppermute only.
A program may use at most 128 MiB of HBM per device.

v0:
```python
import jax
import jax.numpy as jnp
from jax import lax
from jax.sharding import PartitionSpec as P


def from_behind(value, axis, by):
    length = lax.axis_size(axis)
    return lax.ppermute(value, axis, [(i, (i + by) % length) for i in range(length)])


def shortened(value):

    def short(part):
        return part.astype(jnp.bfloat16) if part.dtype == jnp.float32 else part

    return jax.tree.map(short, value)


def local(
    node_features, degree, adjacency, tile_rows, tile_cols, counts, weight, bias_vector, cotangent
):
    offset_count = counts.shape[0]
    reach_steps = (offset_count - 1) // 2
    tile_size = adjacency.shape[1]
    slot_count = adjacency.shape[0] // offset_count
    own_rows, features = node_features.shape
    own_tiles = own_rows // tile_size
    col_count = lax.axis_size("col")
    block_tiles = col_count * own_tiles
    live_slots = jnp.arange(slot_count)[None, :] < counts[:, None]
    adjacency = adjacency.reshape(offset_count, slot_count, tile_size, tile_size)
    adjacency = jnp.where(live_slots[:, :, None, None], adjacency, jnp.zeros_like(adjacency))
    dest_tiles = tile_rows.reshape(offset_count, slot_count)
    source_tiles = tile_cols.reshape(offset_count, slot_count)
    row_scale = lax.rsqrt(degree.astype(jnp.float32))
    source = (row_scale[:, None] * node_features.astype(jnp.float32)).astype(jnp.bfloat16)
    fetched = [source] * offset_count
    ahead_rows = source
    behind_rows = source
    for distance in range(1, reach_steps + 1):
        ahead_rows = from_behind(ahead_rows, "blk", -1)
        behind_rows = from_behind(behind_rows, "blk", 1)
        fetched[reach_steps + distance] = ahead_rows
        fetched[reach_steps - distance] = behind_rows
    picked = jnp.stack(
        [
            fetched[offset].reshape(own_tiles, tile_size, features)[source_tiles[offset]]
            for offset in range(offset_count)
        ]
    )
    products = jnp.einsum("ksrq,ksqf->ksrf", adjacency, picked, preferred_element_type=jnp.float32)
    block_sums = jax.ops.segment_sum(
        products.reshape(-1, tile_size, features), dest_tiles.reshape(-1), block_tiles
    )
    block_sums = block_sums.reshape(block_tiles * tile_size, features)
    sums = lax.psum_scatter(block_sums, "col", scatter_dimension=0, tiled=True)
    aggregated = (row_scale[:, None] * sums).astype(jnp.bfloat16)
    pre_act = jnp.dot(aggregated, weight, preferred_element_type=jnp.float32) + bias_vector
    gate_value = jax.nn.sigmoid(pre_act)
    activations = (pre_act * gate_value).astype(jnp.bfloat16)
    grad_pre = cotangent.astype(jnp.float32) * gate_value * (1.0 + pre_act * (1.0 - gate_value))
    grad_low = grad_pre.astype(jnp.bfloat16)
    weight_part = lax.dot_general(
        aggregated, grad_low, (((0,), (0,)), ((), ())), preferred_element_type=jnp.float32
    )
    bias_part = jnp.sum(grad_pre, axis=0)
    weight_sum, bias_sum = lax.psum((weight_part, bias_part), ("blk", "col"))
    norm_factor = float(own_rows * lax.axis_size("blk") * col_count) ** (-0.5)
    grad_rows = lax.dot_general(
        grad_low, weight, (((1,), (1,)), ((), ())), preferred_element_type=jnp.float32
    )
    grad_hidden = (row_scale[:, None] * grad_rows).astype(jnp.bfloat16)
    block_grad = lax.all_gather(grad_hidden, "col", axis=0, tiled=True)
    picked_grad = block_grad.reshape(block_tiles, tile_size, features)[dest_tiles]
    back_terms = jnp.einsum(
        "ksrq,ksrf->ksqf", adjacency, picked_grad, preferred_element_type=jnp.float32
    )
    target_ids = jnp.arange(offset_count)[:, None] * own_tiles + source_tiles
    outgoing = jax.ops.segment_sum(
        back_terms.reshape(-1, tile_size, features),
        target_ids.reshape(-1),
        offset_count * own_tiles,
    )
    outgoing = outgoing.reshape(offset_count, own_rows, features)
    total_back = outgoing[reach_steps]
    carry_up = jnp.zeros((own_rows, features), jnp.float32)
    carry_down = jnp.zeros((own_rows, features), jnp.float32)
    for distance in range(reach_steps, 0, -1):
        carry_up = from_behind(shortened(carry_up + outgoing[reach_steps + distance]), "blk", 1)
        carry_down = from_behind(
            shortened(carry_down + outgoing[reach_steps - distance]), "blk", -1
        )
    total_back = total_back + carry_up + carry_down
    grad_features = (row_scale[:, None] * total_back).astype(jnp.bfloat16)
    return (activations, grad_features, weight_sum * norm_factor, bias_sum * norm_factor)


def solution(mesh):
    return jax.shard_map(
        local,
        mesh=mesh,
        in_specs=(
            P(("blk", "col"), None),
            P(("blk", "col")),
            P(("blk", "col"), None, None),
            P(("blk", "col")),
            P(("blk", "col")),
            P(("blk", "col")),
            P(),
            P(),
            P(("blk", "col"), None),
        ),
        out_specs=(P(("blk", "col"), None), P(("blk", "col"), None), P(), P()),
        check_vma=False,
    )
```

profile of v0, /device:TPU:0, one launch (start us, length us, event | category | flops | bytes accessed | tf_op | source)
XLA Modules:
  0.0 366.2 jit_solution(6979004536410822082)
XLA Ops:
  7.2 0.0 copy-start
  7.2 0.0 reduce-scatter.2.cloned.1.call-start
  7.2 0.7 convert_rsqrt_fusion
  7.9 1.0 multiply_convert_fusion.2
  9.0 3.0 collective-permute-start
  12.0 3.1 collective-permute-start.2
  15.1 0.9 compare_select_fusion.1
  16.0 0.7 iota_compare_fusion
  16.8 1.9 collective-permute-done
  18.6 1.4 collective-permute-start.1
  20.0 16.3 %copy.15 = bf16[5,72,128,128]{2,3,1,0:T(8,128)(2,1)} copy(bf16[5,72,128,128]{3,2,1,0:T(8,128)(2,1)} %bitcast.57) | data formatting | bytes 23592960 | tf_op jit(solution)/shard_map/reshape | solution.py:32
  36.3 1.0 gather_fusion.2
  37.3 2.4 gather_fusion.1
  39.8 0.0 collective-permute-done.2
  39.8 2.4 gather_fusion.3
  42.2 3.3 collective-permute-start.3
  45.5 0.0 collective-permute-done.1
  45.5 2.5 gather_fusion
  48.0 2.0 bitcast_dynamic-update-slice_fusion.4
  50.0 2.1 bitcast_dynamic-update-slice_fusion.3
  52.1 0.3 bitcast_dynamic-update-slice_fusion.2
  52.4 0.3 bitcast_dynamic-update-slice_fusion.1
  52.7 0.0 collective-permute-done.3
  52.7 4.3 %copy-done.3 = bf16[5,72,128,128]{3,2,1,0:T(8,128)(2,1)} copy-done((bf16[5,72,128,128]{3,2,1,0:T(8,128)(2,1)}, bf16[5,72,128,128]{3,2,1,0:T(8,128)(2,1)S(1)}, u32[]{:S(2)}) %copy-start.3) | copy-done | bytes 11796504
  57.0 1.0 gather_fusion.4
  58.0 1.6 bitcast_dynamic-update-slice_fusion
  59.7 14.5 %fusion.1 = f32[5,72,128,128]{3,2,1,0:T(8,128)} fusion(bf16[5,72,128,128]{3,2,1,0:T(8,128)(2,1)} %bitcast_dynamic-update-slice_fusion, bf16[5,72,128,128]{2,3,1,0:T(8,128)(2,1)} %copy.15, pred[5,72]{1,0:T(8,128)(4,1)S(1)} %iota_compare_fusion), kind=kOutput, calls=%fused_computation.10 | convolution fusion | flops 1515847680 | bytes 47186280 | tf_op jit(solution)/shard_map/ksrq,ksqf->ksrf/dot_general | solution.py:52
  74.2 0.1 broadcast_in_dim.42
  74.3 0.0 copy-start.6
  74.3 0.0 copy-start.8
  74.4 0.0 copy-start.9
  74.4 47.9 %scatter_fusion = f32[16,128,128]{2,1,0:T(8,128)S(1)} fusion(f32[16,128,128]{2,1,0:T(8,128)S(1)} %broadcast_in_dim.42, s32[360]{0:T(512)S(1)} %copy-done.7, f32[360,128,128]{2,1,0:T(8,128)} %bitcast.50), kind=kCustom, calls=%fused_computation.6 | custom fusion | flops 5898240 | bytes 70780320 | tf_op jit(solution)/shard_map/scatter-add | solution.py:53
  122.3 1.0 copy-done.2
  123.3 0.0 reduce-scatter.2.cloned.1.call-update
  123.3 0.0 all-reduce.2.cloned.1.call-start
  123.4 0.1 reshape.136
  123.5 0.1 reshape.180
  123.5 0.1 add.86
  123.6 0.1 add.87
  123.7 22.6 %reduce-scatter.2.cloned.1.call-done = f32[512,128]{1,0:T(8,128)} async-done(((f32[2048,128]{1,0:T(8,128)}), f32[512,128]{1,0:T(8,128)}) %reduce-scatter.2.cloned.1.call-update) | async-done | bytes 262160 | tf_op jit(solution)/shard_map/reduce_scatter | solution.py:57
  146.3 2.1 fusion.15
  148.4 0.2 fusion.4
  148.7 6.8 %all_gather.3 = bf16[2048,128]{1,0:T(8,128)(2,1)S(1)} all-gather(bf16[512,128]{1,0:T(8,128)(2,1)S(1)} %fusion.4), channel_id=1, replica_groups=mesh['blk'=8,'col'=4] {'col'}, dimensions={0}, use_global_device_ids=true | all-gather | bytes 655360 | tf_op jit(solution)/shard_map/all_gather | solution.py:74
  155.5 11.1 %gather_fusion.5 = bf16[360,128,128]{2,1,0:T(8,128)(2,1)} fusion(bf16[16,128,128]{2,1,0:T(8,128)(2,1)S(1)} %bitcast.48, s32[1024]{0:T(1024)S(1)} %pad_clamp_fusion), kind=kCustom, calls=%fused_computation.5 | custom fusion | bytes 23594400 | tf_op jit(solution)/shard_map/gather | solution.py:75
  166.5 15.2 %fusion = f32[5,72,128,128]{3,2,1,0:T(8,128)} fusion(bf16[5,72,128,128]{3,2,1,0:T(8,128)(2,1)} %bitcast.52, bf16[5,72,128,128]{2,3,1,0:T(8,128)(2,1)} %copy.15, pred[5,72]{1,0:T(8,128)(4,1)S(1)} %iota_compare_fusion), kind=kOutput, calls=%fused_computation.9 | convolution fusion | flops 1515847680 | bytes 47186280 | tf_op jit(solution)/shard_map/ksrq,ksrf->ksqf/dot_general | solution.py:76
  181.8 0.1 broadcast_in_dim.50
  181.9 0.0 copy-start.1
  181.9 47.9 %scatter_fusion.1 = f32[20,128,128]{2,1,0:T(8,128)S(1)} fusion(f32[20,128,128]{2,1,0:T(8,128)S(1)} %broadcast_in_dim.50, s32[360]{0:T(512)S(1)} %add.88, f32[360,128,128]{2,1,0:T(8,128)} %bitcast.49), kind=kCustom, calls=%fused_computation.7 | custom fusion | flops 5898240 | bytes 70780320 | tf_op jit(solution)/shard_map/scatter-add | solution.py:80
  229.8 0.1 fusion.16
  229.9 0.1 convert.4
  230.0 1.0 fusion.10
  231.0 0.0 all-reduce.2.cloned.1.call-update
  231.0 1.5 collective-permute-start.4
  232.5 3.3 collective-permute-start.6
  235.8 38.5 %psum.15 = f32[256]{0:T(256)S(1)} all-reduce(f32[256]{0:T(256)S(1)} %get-tuple-element.4), channel_id=1, replica_groups=mesh['blk'=8,'col'=4] {'blk','col'}, use_global_device_ids=true, to_apply=%region_5.6 | all-reduce | flops 256 | bytes 2048 | tf_op jit(solution)/shard_map/psum | solution.py:68
  274.3 0.6 broadcast_multiply_fusion.1
  274.8 0.0 collective-permute-done.4
  274.9 2.3 collective-permute-start.5
  277.2 0.0 collective-permute-done.6
  277.2 2.5 collective-permute-start.7
  279.7 77.3 %all-reduce.2.cloned.1.call-done = f32[128,256]{1,0:T(8,128)} async-done(((f32[128,256]{1,0:T(8,128)}), f32[128,256]{1,0:T(8,128)}) %all-reduce.2.cloned.1.call-update) | async-done | bytes 131088 | tf_op jit(solution)/shard_map/psum | solution.py:68
  357.0 1.6 broadcast_multiply_fusion
  358.6 0.0 collective-permute-done.5
  358.6 0.8 fusion.9
  (25 shorter events, 0.2 us)
Async XLA Ops:
  7.2 139.1 %copy-start = (bf16[128,256]{1,0:T(8,128)(2,1)S(1)}, bf16[128,256]{1,0:T(8,128)(2,1)}, u32[]{:S(2)}) copy-start(bf16[128,256]{1,0:T(8,128)(2,1)} %param.15) | copy-start | bytes 196612
  7.2 139.1 %reduce-scatter.2.cloned.1.call-start = ((), (), s32[]{:S(2)}) async-start(), calls=%async_computation.1 | async-start | bytes 1310720 | tf_op jit(solution)/shard_map/reduce_scatter | solution.py:57
  9.0 9.7 %collective-permute-start = (bf16[512,128]{1,0:T(8,128)(2,1)S(1)}, bf16[512,128]{1,0:T(8,128)(2,1)S(1)}, u32[]{:S(2)}, u32[]{:S(2)}) collective-permute-start(bf16[512,128]{1,0:T(8,128)(2,1)S(1)} %multiply_convert_fusion.2), channel_id=1, source_target_pairs={{0,4},{4,8},{8,12},{12,16},{16,20},{20,24},{24,28},{28,0},{1,5},{5... | collective-permute-start | bytes 393224 | tf_op jit(solution)/shard_map/ppermute | solution.py:9
  12.0 27.8 %collective-permute-start.2 = (bf16[512,128]{1,0:T(8,128)(2,1)S(1)}, bf16[512,128]{1,0:T(8,128)(2,1)S(1)}, u32[]{:S(2)}, u32[]{:S(2)}) collective-permute-start(bf16[512,128]{1,0:T(8,128)(2,1)S(1)} %multiply_convert_fusion.2), channel_id=1, source_target_pairs={{0,28},{4,0},{8,4},{12,8},{16,12},{20,16},{24,20},{28,24},{1,29},{... | collective-permute-start | bytes 393224 | tf_op jit(solution)/shard_map/ppermute | solution.py:9
  18.6 26.9 %collective-permute-start.1 = (bf16[512,128]{1,0:T(8,128)(2,1)S(1)}, bf16[512,128]{1,0:T(8,128)(2,1)S(1)}, u32[]{:S(2)}, u32[]{:S(2)}) collective-permute-start(bf16[512,128]{1,0:T(8,128)(2,1)S(1)} %collective-permute-done), channel_id=1, source_target_pairs={{0,4},{4,8},{8,12},{12,16},{16,20},{20,24},{24,28},{28,0},{1,5},{5... | collective-permute-start | bytes 393224 | tf_op jit(solution)/shard_map/ppermute | solution.py:9
  42.2 10.5 %collective-permute-start.3 = (bf16[512,128]{1,0:T(8,128)(2,1)S(1)}, bf16[512,128]{1,0:T(8,128)(2,1)S(1)}, u32[]{:S(2)}, u32[]{:S(2)}) collective-permute-start(bf16[512,128]{1,0:T(8,128)(2,1)S(1)} %collective-permute-done.2), channel_id=1, source_target_pairs={{0,28},{4,0},{8,4},{12,8},{16,12},{20,16},{24,20},{28,24},{1,29},{... | collective-permute-start | bytes 393224 | tf_op jit(solution)/shard_map/ppermute | solution.py:9
  48.0 4.4 %copy-start.4 = (bf16[72,128,128]{2,1,0:T(8,128)(2,1)S(1)}, bf16[72,128,128]{2,1,0:T(8,128)(2,1)}, u32[]{:S(2)}) copy-start(bf16[72,128,128]{2,1,0:T(8,128)(2,1)} %gather_fusion.3) | copy-start | bytes 7077892
  52.7 4.3 %copy-start.3 = (bf16[5,72,128,128]{3,2,1,0:T(8,128)(2,1)}, bf16[5,72,128,128]{3,2,1,0:T(8,128)(2,1)S(1)}, u32[]{:S(2)}) copy-start(bf16[5,72,128,128]{3,2,1,0:T(8,128)(2,1)S(1)} %bitcast_dynamic-update-slice_fusion.1) | copy-start | bytes 35389444
  59.7 14.7 %copy-start.7 = (s32[360]{0:T(512)S(1)}, s32[360]{0:T(512)}, u32[]{:S(2)}) copy-start(s32[360]{0:T(512)} %param.12) | copy-start | bytes 4324
  74.3 49.4 %copy-start.6 = (s32[360]{0:T(512)S(1)}, s32[360]{0:T(512)}, u32[]{:S(2)}) copy-start(s32[360]{0:T(512)} %param.13) | copy-start | bytes 4324
  74.3 72.0 %copy-start.8 = (bf16[512,256]{1,0:T(8,128)(2,1)S(1)}, bf16[512,256]{1,0:T(8,128)(2,1)}, u32[]{:S(2)}) copy-start(bf16[512,256]{1,0:T(8,128)(2,1)} %param.17) | copy-start | bytes 786436
  74.4 72.0 %copy-start.9 = (f32[256]{0:T(256)S(1)}, f32[256]{0:T(256)}, u32[]{:S(2)}) copy-start(f32[256]{0:T(256)} %param.16) | copy-start | bytes 3076
  122.3 1.0 copy-start.2
  123.3 233.7 %all-reduce.2.cloned.1.call-start = ((), (), s32[]{:S(2)}) async-start(), calls=%async_computation.2 | async-start | bytes 262144 | tf_op jit(solution)/shard_map/psum | solution.py:68
  181.9 48.1 %copy-start.5 = (f32[512,128]{1,0:T(8,128)S(1)}, f32[512,128]{1,0:T(8,128)}, u32[]{:S(2)}) copy-start(f32[512,128]{1,0:T(8,128)} %reduce-scatter.2.cloned.1.call-done) | copy-start | bytes 786436
  181.9 177.4 %copy-start.1 = (bf16[128,256]{1,0:T(8,128)(2,1)S(1)}, bf16[128,256]{1,0:T(8,128)(2,1)}, u32[]{:S(2)}) copy-start(bf16[128,256]{1,0:T(8,128)(2,1)} %param.15) | copy-start | bytes 196612
  231.0 43.8 %collective-permute-start.4 = (bf16[512,128]{1,0:T(8,128)(2,1)S(1)}, bf16[512,128]{1,0:T(8,128)(2,1)S(1)}, u32[]{:S(2)}, u32[]{:S(2)}) collective-permute-start(bf16[512,128]{1,0:T(8,128)(2,1)S(1)} %bitcast.59), channel_id=1, source_target_pairs={{0,4},{4,8},{8,12},{12,16},{16,20},{20,24},{24,28},{28,0},{1,5},{5... | collective-permute-start | bytes 393224 | tf_op jit(solution)/shard_map/ppermute | solution.py:9
  232.5 44.7 %collective-permute-start.6 = (bf16[512,128]{1,0:T(8,128)(2,1)S(1)}, bf16[512,128]{1,0:T(8,128)(2,1)S(1)}, u32[]{:S(2)}, u32[]{:S(2)}) collective-permute-start(bf16[512,128]{1,0:T(8,128)(2,1)S(1)} %bitcast.58), channel_id=1, source_target_pairs={{0,28},{4,0},{8,4},{12,8},{16,12},{20,16},{24,20},{28,24},{1,29},{... | collective-permute-start | bytes 393224 | tf_op jit(solution)/shard_map/ppermute | solution.py:9
  274.9 83.7 %collective-permute-start.5 = (bf16[512,128]{1,0:T(8,128)(2,1)S(1)}, bf16[512,128]{1,0:T(8,128)(2,1)S(1)}, u32[]{:S(2)}, u32[]{:S(2)}) collective-permute-start(bf16[512,128]{1,0:T(8,128)(2,1)S(1)} %fusion.6), channel_id=1, source_target_pairs={{0,4},{4,8},{8,12},{12,16},{16,20},{20,24},{24,28},{28,0},{1,5},{5... | collective-permute-start | bytes 393224 | tf_op jit(solution)/shard_map/ppermute | solution.py:9
  277.2 81.3 %collective-permute-start.7 = (bf16[512,128]{1,0:T(8,128)(2,1)S(1)}, bf16[512,128]{1,0:T(8,128)(2,1)S(1)}, u32[]{:S(2)}, u32[]{:S(2)}) collective-permute-start(bf16[512,128]{1,0:T(8,128)(2,1)S(1)} %fusion.5), channel_id=1, source_target_pairs={{0,28},{4,0},{8,4},{12,8},{16,12},{20,16},{24,20},{28,24},{1,29},{... | collective-permute-start | bytes 393224 | tf_op jit(solution)/shard_map/ppermute | solution.py:9
Sparse Core Ops, SparseCore 0:
  123.4 22.8 reduce-scatter.1
  231.1 125.8 all-reduce.1
where the time goes:
time: 369 us; the launch traced here: 366 us
  other arithmetic  102 us (28%)
  waiting for transfers between devices  102 us (28%)
  local copies, waits for them, and re-layouts  48.9 us (13%)
  blocking collectives  45.3 us (12%)
  matrix products  33.1 us (9%)
  starting transfers between devices  20.5 us (6%)
  between operations  14.3 us (4%)
    psum x1, waiting for transfers between devices, local(): weight_sum, bias_sum = lax.psum((weight_part, bias_part), ('blk', 'col'))  77.3 us
    scatter-add x1, other arithmetic, local(): jax.ops.segment_sum(products.reshape(-1, tile_size, features), dest_tiles...  47.9 us
    scatter-add x1, other arithmetic, local(): jax.ops.segment_sum(back_terms.reshape(-1, tile_size, features), target_i...  47.9 us
    psum x1, blocking collectives, local(): weight_sum, bias_sum = lax.psum((weight_part, bias_part), ('blk', 'col'))  38.5 us
    reduce_scatter x1, waiting for transfers between devices, local(): sums = lax.psum_scatter(block_sums, 'col', scatter_dimension=0, tiled=True)  22.6 us
    ppermute x8, starting transfers between devices, from_behind(): lax.ppermute(value, axis, [(i, (i + by) % length) for i in range(length)])  20.4 us
    reshape x1, local copies, waits for them, and re-layouts, local(): adjacency.reshape(offset_count, slot_count, tile_size, tile_size)  16.3 us
    dot_general x1, matrix products, local(): jnp.einsum('ksrq,ksrf->ksqf', adjacency, picked_grad, preferred_element_t...  15.2 us
  transfers between devices with their start and end apart: 10, of which 3 were waited for; matrix products, arithmetic and copies ran while one was open for 9% of the time, Pallas kernels for 0%

commit v1 on v0

v1 whole, which is shorter than its diff:
```python
import jax
import jax.numpy as jnp
from jax import lax
from jax.experimental import pallas as pl
from jax.experimental.pallas import tpu as pltpu
from jax.sharding import PartitionSpec as P


def from_behind(value, axis, by):
    length = lax.axis_size(axis)
    return lax.ppermute(value, axis, [(i, (i + by) % length) for i in range(length)])


def slot_chunk(slot_count, limit=24):
    return max(c for c in range(1, limit + 1) if slot_count % c == 0)


def tile_products(rows, cols, counts, adjacency, operand, out_tiles, own_tiles, forward):
    offset_count = counts.shape[0]
    slot_count = adjacency.shape[0] // offset_count
    tile = adjacency.shape[1]
    width = operand.shape[2]
    chunk = slot_chunk(slot_count)
    chunks = slot_count // chunk
    out_width = width if forward else tile

    def kernel(rows_ref, cols_ref, counts_ref, adj_ref, opnd_ref, out_ref):
        k = pl.program_id(0)
        j = pl.program_id(1)

        @pl.when((k == 0) & (j == 0))
        def _():
            out_ref[...] = jnp.zeros_like(out_ref)

        count = counts_ref[k]

        def body(i, carry):
            slot = j * chunk + i

            @pl.when(slot < count)
            def _():
                g = k * slot_count + slot
                d = rows_ref[g]
                c = k * own_tiles + cols_ref[g]
                if forward:
                    out_ref[d] += jnp.dot(
                        adj_ref[i], opnd_ref[c], preferred_element_type=jnp.float32
                    )
                else:
                    out_ref[c] += jnp.dot(
                        opnd_ref[d], adj_ref[i], preferred_element_type=jnp.float32
                    )

            return carry

        lax.fori_loop(0, chunk, body, 0)

    def adj_map(k, j, rows_ref, cols_ref, counts_ref):
        last = jnp.maximum(counts_ref[k] - 1, 0) // chunk
        return (k * chunks + jnp.minimum(j, last), 0, 0)

    def whole_map(k, j, rows_ref, cols_ref, counts_ref):
        return (0, 0, 0)

    flops = 2 * adjacency.shape[0] * tile * tile * width
    bytes_accessed = adjacency.size * 2 + operand.size * 2 + out_tiles * tile * out_width * 4
    return pl.pallas_call(
        kernel,
        grid_spec=pltpu.PrefetchScalarGridSpec(
            num_scalar_prefetch=3,
            grid=(offset_count, chunks),
            in_specs=[
                pl.BlockSpec((chunk, tile, tile), adj_map),
                pl.BlockSpec(operand.shape, whole_map),
            ],
            out_specs=pl.BlockSpec((out_tiles, tile, out_width), whole_map),
        ),
        out_shape=jax.ShapeDtypeStruct((out_tiles, tile, out_width), jnp.float32),
        compiler_params=pltpu.CompilerParams(dimension_semantics=("arbitrary", "arbitrary")),
        cost_estimate=pl.CostEstimate(
            flops=flops, transcendentals=0, bytes_accessed=bytes_accessed
        ),
    )(rows, cols, counts, adjacency, operand)


def all_sum(value, axes):
    size = 1
    for axis in axes:
        size *= lax.axis_size(axis)
    if size & (size - 1):
        return lax.psum(value, axes)
    bit = 1
    while bit < size:
        value = value + lax.ppermute(value, axes, [(i, i ^ bit) for i in range(size)])
        bit *= 2
    return value


def local(
    node_features, degree, adjacency, tile_rows, tile_cols, counts, weight, bias_vector, cotangent
):
    offset_count = counts.shape[0]
    reach_steps = (offset_count - 1) // 2
    tile_size = adjacency.shape[1]
    own_rows, features = node_features.shape
    hidden = weight.shape[1]
    own_tiles = own_rows // tile_size
    col_count = lax.axis_size("col")
    block_tiles = col_count * own_tiles
    row_scale = lax.rsqrt(degree.astype(jnp.float32))
    source = (row_scale[:, None] * node_features.astype(jnp.float32)).astype(jnp.bfloat16)
    fetched = [
        source if k == reach_steps else from_behind(source, "blk", reach_steps - k)
        for k in range(offset_count)
    ]
    source_tiles = jnp.stack(fetched).reshape(offset_count * own_tiles, tile_size, features)
    block_sums = tile_products(
        tile_rows, tile_cols, counts, adjacency, source_tiles, block_tiles, own_tiles, True
    )
    block_sums = block_sums.reshape(block_tiles * tile_size, features)
    sums = lax.psum_scatter(block_sums, "col", scatter_dimension=0, tiled=True)
    aggregated = (row_scale[:, None] * sums).astype(jnp.bfloat16)
    pre_act = jnp.dot(aggregated, weight, preferred_element_type=jnp.float32) + bias_vector
    gate_value = jax.nn.sigmoid(pre_act)
    activations = (pre_act * gate_value).astype(jnp.bfloat16)
    grad_pre = cotangent.astype(jnp.float32) * gate_value * (1.0 + pre_act * (1.0 - gate_value))
    grad_low = grad_pre.astype(jnp.bfloat16)
    weight_part = lax.dot_general(
        aggregated, grad_low, (((0,), (0,)), ((), ())), preferred_element_type=jnp.float32
    )
    bias_part = jnp.sum(grad_pre, axis=0)
    packed = jnp.concatenate(
        [weight_part, bias_part[None, :], jnp.zeros((7, hidden), jnp.float32)], axis=0
    )
    packed = all_sum(packed, ("blk", "col"))
    norm_factor = float(own_rows * lax.axis_size("blk") * col_count) ** (-0.5)
    weight_sum = packed[:features]
    bias_sum = packed[features]
    grad_rows = lax.dot_general(
        grad_low, weight, (((1,), (1,)), ((), ())), preferred_element_type=jnp.float32
    )
    grad_hidden = (row_scale[:, None] * grad_rows).astype(jnp.bfloat16)
    block_grad = lax.all_gather(grad_hidden, "col", axis=0, tiled=True)
    grad_tiles_t = jnp.swapaxes(block_grad.reshape(block_tiles, tile_size, features), 1, 2)
    outgoing_t = tile_products(
        tile_rows, tile_cols, counts, adjacency, grad_tiles_t, offset_count * own_tiles,
        own_tiles, False,
    )
    outgoing = jnp.swapaxes(outgoing_t, 1, 2).reshape(offset_count, own_rows, features)
    total_back = outgoing[reach_steps]
    for k in range(offset_count):
        if k != reach_steps:
            sent = outgoing[k].astype(jnp.bfloat16)
            total_back = total_back + from_behind(sent, "blk", k - reach_steps).astype(jnp.float32)
    grad_features = (row_scale[:, None] * total_back).astype(jnp.bfloat16)
    return (activations, grad_features, weight_sum * norm_factor, bias_sum * norm_factor)


def solution(mesh):
    return jax.shard_map(
        local,
        mesh=mesh,
        in_specs=(
            P(("blk", "col"), None),
            P(("blk", "col")),
            P(("blk", "col"), None, None),
            P(("blk", "col")),
            P(("blk", "col")),
            P(("blk", "col")),
            P(),
            P(),
            P(("blk", "col"), None),
        ),
        out_specs=(P(("blk", "col"), None), P(("blk", "col"), None), P(), P()),
        check_vma=False,
    )
```

time: 369 us -> 185 us (0.50)
  other arithmetic: 102 us -> 6.5 us
  Pallas kernels: 0 us -> 73.6 us
  waiting for transfers between devices: 102 us -> 49.3 us
  local copies, waits for them, and re-layouts: 48.9 us -> 3.72 us
  blocking collectives: 45.3 us -> 7.41 us
  matrix products: 33.1 us -> 2.73 us
  starting transfers between devices: 20.5 us -> 26.8 us
    scatter-add x2 -> x0, other arithmetic: 95.8 us -> none  [the longest x1 47.9 us: local(): jax.ops.segment_sum(products.reshape(-1, tile_size, features), dest_tiles...]
    psum x1 -> x0, waiting for transfers between devices: 77.3 us -> none  [local(): weight_sum, bias_sum = lax.psum((weight_part, bias_part), ('blk', 'col'))]
    pallas_call x0 -> x2, Pallas kernels: none -> 73.6 us  [tile_products(): pl.pallas_call(kernel, grid_spec=pltpu.PrefetchScalarGridSpec(num_scalar_...]
    psum x1 -> x0, blocking collectives: 38.5 us -> none  [local(): weight_sum, bias_sum = lax.psum((weight_part, bias_part), ('blk', 'col'))]
    dot_general x2 -> x0, matrix products: 29.8 us -> none  [the longest x1 15.2 us: local(): jnp.einsum('ksrq,ksrf->ksqf', adjacency, picked_grad, preferred_element_t...]
    gather x6 -> x0, local copies, waits for them, and re-layouts: 20.4 us -> none  [the longest x1 11.1 us: local(): block_grad.reshape(block_tiles, tile_size, features)[dest_tiles]]
    reshape x2 -> x1, local copies, waits for them, and re-layouts: 16.4 us -> 1.02 us  [local(): block_grad.reshape(block_tiles, tile_size, features)]
    ppermute x0 -> x5, starting transfers between devices: none -> 12.8 us  [all_sum(): lax.ppermute(value, axes, [(i, i ^ bit) for i in range(size)])]
  transfers between devices with their start and end apart: 10 -> 14, of which waited for: 3 -> 8; matrix products, arithmetic and copies ran while one was open for 9% -> 3% of each run, Pallas kernels for 0% -> 20%
where the time goes in v1:
time: 185 us; the launch traced here: 184 us
  Pallas kernels  73.6 us (40%)
  waiting for transfers between devices  49.3 us (27%)
  starting transfers between devices  26.8 us (14%)
  between operations  14.2 us (8%)
  blocking collectives  7.41 us (4%)
  other arithmetic  6.5 us (4%)
  local copies, waits for them, and re-layouts  3.72 us (2%)
  matrix products  2.73 us (1%)
    pallas_call x2, Pallas kernels, tile_products(): pl.pallas_call(kernel, grid_spec=pltpu.PrefetchScalarGridSpec(num_scalar_...  73.6 us
    reduce_scatter x1, waiting for transfers between devices, local(): sums = lax.psum_scatter(block_sums, 'col', scatter_dimension=0, tiled=True)  30.5 us
    ppermute x8, waiting for transfers between devices, from_behind(): lax.ppermute(value, axis, [(i, (i + by) % length) for i in range(length)])  14.2 us
    ppermute x8, starting transfers between devices, from_behind(): lax.ppermute(value, axis, [(i, (i + by) % length) for i in range(length)])  14 us
    ppermute x5, starting transfers between devices, all_sum(): lax.ppermute(value, axes, [(i, i ^ bit) for i in range(size)])  12.8 us
    all_gather x1, blocking collectives, local(): block_grad = lax.all_gather(grad_hidden, 'col', axis=0, tiled=True)  7.41 us
    ppermute x5, waiting for transfers between devices, all_sum(): lax.ppermute(value, axes, [(i, i ^ bit) for i in range(size)])  4.63 us
  transfers between devices with their start and end apart: 14, of which 8 were waited for; matrix products, arithmetic and copies ran while one was open for 3% of the time, Pallas kernels for 20%

profile of v1, /device:TPU:0, one launch (start us, length us, event | category | flops | bytes accessed | tf_op | source)
XLA Modules:
  0.0 184.3 jit_solution(18197054801815263777)
XLA Ops:
  7.2 0.0 copy-start
  7.2 0.0 reduce-scatter.2.cloned.1.call-start
  7.2 0.7 convert_rsqrt_fusion
  7.9 1.0 multiply_convert_fusion.2
  9.0 3.1 %collective-permute-start = (bf16[512,128]{1,0:T(8,128)(2,1)S(1)}, bf16[512,128]{1,0:T(8,128)(2,1)S(1)}, u32[]{:S(2)}, u32[]{:S(2)}) collective-permute-start(bf16[512,128]{1,0:T(8,128)(2,1)S(1)} %multiply_convert_fusion.2), channel_id=1, source_target_pairs={{0,8},{4,12},{8,16},{12,20},{16,24},{20,28},{24,0},{28,4},{1,9},{5... | collective-permute-start | bytes 393224 | tf_op jit(solution)/shard_map/ppermute | solution.py:11
  12.1 3.2 %collective-permute-start.2 = (bf16[512,128]{1,0:T(8,128)(2,1)S(1)}, bf16[512,128]{1,0:T(8,128)(2,1)S(1)}, u32[]{:S(2)}, u32[]{:S(2)}) collective-permute-start(bf16[512,128]{1,0:T(8,128)(2,1)S(1)} %multiply_convert_fusion.2), channel_id=1, source_target_pairs={{0,28},{4,0},{8,4},{12,8},{16,12},{20,16},{24,20},{28,24},{1,29},{... | collective-permute-start | bytes 393224 | tf_op jit(solution)/shard_map/ppermute | solution.py:11
  15.2 1.8 collective-permute-start.3
  17.0 0.0 collective-permute-start.1
  17.0 1.0 collective-permute-done
  18.0 6.7 %collective-permute-done.1 = bf16[512,128]{1,0:T(8,128)(2,1)S(1)} collective-permute-done((bf16[512,128]{1,0:T(8,128)(2,1)S(1)}, bf16[512,128]{1,0:T(8,128)(2,1)S(1)}, u32[]{:S(2)}, u32[]{:S(2)}) %collective-permute-start.1) | collective-permute-done | bytes 131104 | tf_op jit(solution)/shard_map/ppermute | solution.py:11
  24.7 1.1 bitcast_dynamic-update-slice_fusion.2
  25.8 0.0 collective-permute-done.2
  25.8 0.0 collective-permute-done.3
  25.9 0.0 copy-start.1
  25.9 0.9 copy-done.1
  26.7 0.0 copy-start.3
  26.8 0.0 copy-start.4
  26.8 37.0 %shard_map.120 = f32[16,128,128]{2,1,0:T(8,128)} custom-call(s32[360]{0:T(512)} %rows_ref.3, s32[360]{0:T(512)} %cols_ref.3, s32[5]{0:T(128)} %counts_ref.3, bf16[360,128,128]{2,1,0:T(8,128)(2,1)} %adj_ref.3, bf16[20,128,128]{2,1,0:T(8,128)(2,1)} %bitcast.42), custom_call_target="tpu_custom_call" | custom-call | flops 1509949440 | bytes 13500416 | tf_op jit(solution)/shard_map/pallas_call | solution.py:67
  63.8 0.0 reduce-scatter.2.cloned.1.call-update
  63.8 0.1 pad.2.clone
  63.9 30.5 %reduce-scatter.2.cloned.1.call-done = f32[512,128]{1,0:T(8,128)} async-done(((f32[2048,128]{1,0:T(8,128)}), f32[512,128]{1,0:T(8,128)}) %reduce-scatter.2.cloned.1.call-update) | async-done | bytes 262160 | tf_op jit(solution)/shard_map/reduce_scatter | solution.py:121
  94.5 0.0 copy-done
  94.5 0.0 copy-done.3
  94.5 0.0 copy-done.4
  94.5 0.0 copy-start.2
  94.5 2.2 %fusion.10 = (f32[256]{0:T(256)S(1)}, bf16[512,256]{1,0:T(8,128)(2,1)S(1)}, bf16[512,256]{1,0:T(8,128)(2,1)}) fusion(bf16[512,256]{1,0:T(8,128)(2,1)S(1)} %copy-done.3, f32[256]{0:T(256)S(1)} %copy-done.4, bf16[128,256]{1,0:T(8,128)(2,1)S(1)} %copy-done, f32[512,128]{1,0:T(8,128)} %reduce-scatter.2.cloned.1.call-done, f32[512]{0:T(512)S(1)} %convert_rsqrt_fusion), kind=kOutput, calls=%fused_computation.28 | convolution fusion | flops 35520256 | bytes 1118208 | tf_op jit(solution)/shard_map/dot_general | solution.py:123
  96.6 0.2 fusion
  96.9 0.0 copy-done.2
  96.9 0.3 fusion.6
  97.2 0.1 maximum_maximum_fusion
  97.3 0.1 collective-permute-start.8
  97.4 7.4 %all_gather.3 = bf16[2048,128]{1,0:T(8,128)(2,1)S(1)} all-gather(bf16[512,128]{1,0:T(8,128)(2,1)S(1)} %fusion), channel_id=1, replica_groups=mesh['blk'=8,'col'=4] {'col'}, dimensions={0}, use_global_device_ids=true | all-gather | bytes 655360 | tf_op jit(solution)/shard_map/all_gather | solution.py:143
  104.8 1.0 copy.13
  105.8 0.0 collective-permute-done.8
  105.8 0.1 fusion.9
  105.9 0.4 collective-permute-start.9
  106.3 36.5 %shard_map.121 = f32[20,128,128]{2,1,0:T(8,128)} custom-call(s32[360]{0:T(512)} %rows_ref.3, s32[360]{0:T(512)} %cols_ref.3, s32[5]{0:T(128)} %counts_ref.3, bf16[360,128,128]{2,1,0:T(8,128)(2,1)} %adj_ref.3, bf16[16,128,128]{2,1,0:T(8,128)(2,1)} %bitcast.40), custom_call_target="tpu_custom_call" | custom-call | flops 1509949440 | bytes 13631488 | tf_op jit(solution)/shard_map/pallas_call | solution.py:67
  142.8 0.0 collective-permute-done.9
  142.9 4.7 %collective-permute-start.10 = (f32[136,256]{1,0:T(8,128)S(1)}, f32[136,256]{1,0:T(8,128)S(1)}, u32[]{:S(2)}, u32[]{:S(2)}) collective-permute-start(f32[136,256]{1,0:T(8,128)S(1)} %add.52), channel_id=1, source_target_pairs={{0,4},{1,5},{2,6},{3,7},{4,0},{5,1},{6,2},{7,3},{8,12},{9,13},{10,... | collective-permute-start | bytes 417800 | tf_op jit(solution)/shard_map/ppermute | solution.py:94
  147.5 1.4 bitcast_convert_fusion
  149.0 2.1 %collective-permute-done.10 = f32[136,256]{1,0:T(8,128)S(1)} collective-permute-done((f32[136,256]{1,0:T(8,128)S(1)}, f32[136,256]{1,0:T(8,128)S(1)}, u32[]{:S(2)}, u32[]{:S(2)}) %collective-permute-start.10) | collective-permute-done | bytes 139296 | tf_op jit(solution)/shard_map/ppermute | solution.py:94
  151.1 7.6 %collective-permute-start.11 = (f32[136,256]{1,0:T(8,128)S(1)}, f32[136,256]{1,0:T(8,128)S(1)}, u32[]{:S(2)}, u32[]{:S(2)}) collective-permute-start(f32[136,256]{1,0:T(8,128)S(1)} %add.53), channel_id=1, source_target_pairs={{0,8},{1,9},{2,10},{3,11},{4,12},{5,13},{6,14},{7,15},{8,0},{9,1},... | collective-permute-start | bytes 417800 | tf_op jit(solution)/shard_map/ppermute | solution.py:94
  158.7 0.1 copy.15
  158.9 0.1 copy.18
  159.0 0.1 copy.17
  159.2 0.1 copy.16
  159.3 0.1 collective-permute-start.5
  159.4 2.0 %collective-permute-start.6 = (bf16[512,128]{1,0:T(8,128)(2,1)S(1)}, bf16[512,128]{1,0:T(8,128)(2,1)S(1)}, u32[]{:S(2)}, u32[]{:S(2)}) collective-permute-start(bf16[512,128]{1,0:T(8,128)(2,1)S(1)} %bitcast.45), channel_id=1, source_target_pairs={{0,4},{4,8},{8,12},{12,16},{16,20},{20,24},{24,28},{28,0},{1,5},{5... | collective-permute-start | bytes 393224 | tf_op jit(solution)/shard_map/ppermute | solution.py:11
  161.4 0.0 collective-permute-start.7
  161.4 3.8 %collective-permute-start.4 = (bf16[512,128]{1,0:T(8,128)(2,1)S(1)}, bf16[512,128]{1,0:T(8,128)(2,1)S(1)}, u32[]{:S(2)}, u32[]{:S(2)}) collective-permute-start(bf16[512,128]{1,0:T(8,128)(2,1)S(1)} %bitcast.43), channel_id=1, source_target_pairs={{0,24},{4,28},{8,0},{12,4},{16,8},{20,12},{24,16},{28,20},{1,25},{... | collective-permute-start | bytes 393224 | tf_op jit(solution)/shard_map/ppermute | solution.py:11
  165.2 1.0 slice.37
  166.2 0.1 copy.14
  166.3 0.0 collective-permute-done.11
  166.3 0.1 collective-permute-start.12
  166.4 0.0 collective-permute-done.5
  166.4 0.9 collective-permute-done.6
  167.3 2.3 %collective-permute-done.7 = bf16[512,128]{1,0:T(8,128)(2,1)S(1)} collective-permute-done((bf16[512,128]{1,0:T(8,128)(2,1)S(1)}, bf16[512,128]{1,0:T(8,128)(2,1)S(1)}, u32[]{:S(2)}, u32[]{:S(2)}) %collective-permute-start.7) | collective-permute-done | bytes 131104 | tf_op jit(solution)/shard_map/ppermute | solution.py:11
  169.6 3.3 %collective-permute-done.4 = bf16[512,128]{1,0:T(8,128)(2,1)S(1)} collective-permute-done((bf16[512,128]{1,0:T(8,128)(2,1)S(1)}, bf16[512,128]{1,0:T(8,128)(2,1)S(1)}, u32[]{:S(2)}, u32[]{:S(2)}) %collective-permute-start.4) | collective-permute-done | bytes 131104 | tf_op jit(solution)/shard_map/ppermute | solution.py:11
  172.9 0.8 fusion.5
  173.7 2.5 %collective-permute-done.12 = f32[136,256]{1,0:T(8,128)S(1)} collective-permute-done((f32[136,256]{1,0:T(8,128)S(1)}, f32[136,256]{1,0:T(8,128)S(1)}, u32[]{:S(2)}, u32[]{:S(2)}) %collective-permute-start.12) | collective-permute-done | bytes 139296 | tf_op jit(solution)/shard_map/ppermute | solution.py:94
  176.3 0.6 slice_multiply_fusion.1
  176.8 0.7 slice_multiply_fusion
  (10 shorter events, 0.2 us)
Async XLA Ops:
  7.2 87.3 %copy-start = (bf16[128,256]{1,0:T(8,128)(2,1)S(1)}, bf16[128,256]{1,0:T(8,128)(2,1)}, u32[]{:S(2)}) copy-start(bf16[128,256]{1,0:T(8,128)(2,1)} %param.15) | copy-start | bytes 196612
  7.2 87.3 %reduce-scatter.2.cloned.1.call-start = ((), (), s32[]{:S(2)}) async-start(), calls=%async_computation.1 | async-start | bytes 1310720 | tf_op jit(solution)/shard_map/reduce_scatter | solution.py:121
  9.0 9.0 %collective-permute-start = (bf16[512,128]{1,0:T(8,128)(2,1)S(1)}, bf16[512,128]{1,0:T(8,128)(2,1)S(1)}, u32[]{:S(2)}, u32[]{:S(2)}) collective-permute-start(bf16[512,128]{1,0:T(8,128)(2,1)S(1)} %multiply_convert_fusion.2), channel_id=1, source_target_pairs={{0,8},{4,12},{8,16},{12,20},{16,24},{20,28},{24,0},{28,4},{1,9},{5... | collective-permute-start | bytes 393224 | tf_op jit(solution)/shard_map/ppermute | solution.py:11
  12.1 13.7 %collective-permute-start.2 = (bf16[512,128]{1,0:T(8,128)(2,1)S(1)}, bf16[512,128]{1,0:T(8,128)(2,1)S(1)}, u32[]{:S(2)}, u32[]{:S(2)}) collective-permute-start(bf16[512,128]{1,0:T(8,128)(2,1)S(1)} %multiply_convert_fusion.2), channel_id=1, source_target_pairs={{0,28},{4,0},{8,4},{12,8},{16,12},{20,16},{24,20},{28,24},{1,29},{... | collective-permute-start | bytes 393224 | tf_op jit(solution)/shard_map/ppermute | solution.py:11
  15.2 10.6 %collective-permute-start.3 = (bf16[512,128]{1,0:T(8,128)(2,1)S(1)}, bf16[512,128]{1,0:T(8,128)(2,1)S(1)}, u32[]{:S(2)}, u32[]{:S(2)}) collective-permute-start(bf16[512,128]{1,0:T(8,128)(2,1)S(1)} %multiply_convert_fusion.2), channel_id=1, source_target_pairs={{0,24},{4,28},{8,0},{12,4},{16,8},{20,12},{24,16},{28,20},{1,25},{... | collective-permute-start | bytes 393224 | tf_op jit(solution)/shard_map/ppermute | solution.py:11
  17.0 7.7 %collective-permute-start.1 = (bf16[512,128]{1,0:T(8,128)(2,1)S(1)}, bf16[512,128]{1,0:T(8,128)(2,1)S(1)}, u32[]{:S(2)}, u32[]{:S(2)}) collective-permute-start(bf16[512,128]{1,0:T(8,128)(2,1)S(1)} %multiply_convert_fusion.2), channel_id=1, source_target_pairs={{0,4},{4,8},{8,12},{12,16},{16,20},{20,24},{24,28},{28,0},{1,5},{5... | collective-permute-start | bytes 393224 | tf_op jit(solution)/shard_map/ppermute | solution.py:11
  25.9 0.9 copy-start.1
  26.7 67.7 %copy-start.3 = (bf16[512,256]{1,0:T(8,128)(2,1)S(1)}, bf16[512,256]{1,0:T(8,128)(2,1)}, u32[]{:S(2)}) copy-start(bf16[512,256]{1,0:T(8,128)(2,1)} %param.17) | copy-start | bytes 786436
  26.8 67.7 %copy-start.4 = (f32[256]{0:T(256)S(1)}, f32[256]{0:T(256)}, u32[]{:S(2)}) copy-start(f32[256]{0:T(256)} %param.16) | copy-start | bytes 3076
  94.5 2.4 %copy-start.2 = (f32[512,128]{1,0:T(8,128)S(1)}, f32[512,128]{1,0:T(8,128)}, u32[]{:S(2)}) copy-start(f32[512,128]{1,0:T(8,128)} %reduce-scatter.2.cloned.1.call-done) | copy-start | bytes 786436
  97.3 8.5 %collective-permute-start.8 = (f32[136,256]{1,0:T(8,128)S(1)}, f32[136,256]{1,0:T(8,128)S(1)}, u32[]{:S(2)}, u32[]{:S(2)}) collective-permute-start(f32[136,256]{1,0:T(8,128)S(1)} %maximum_maximum_fusion), channel_id=1, source_target_pairs={{0,1},{1,0},{2,3},{3,2},{4,5},{5,4},{6,7},{7,6},{8,9},{9,8},{10,11... | collective-permute-start | bytes 417800 | tf_op jit(solution)/shard_map/ppermute | solution.py:94
  105.9 36.9 %collective-permute-start.9 = (f32[136,256]{1,0:T(8,128)S(1)}, f32[136,256]{1,0:T(8,128)S(1)}, u32[]{:S(2)}, u32[]{:S(2)}) collective-permute-start(f32[136,256]{1,0:T(8,128)S(1)} %fusion.9), channel_id=1, source_target_pairs={{0,2},{1,3},{2,0},{3,1},{4,6},{5,7},{6,4},{7,5},{8,10},{9,11},{10,... | collective-permute-start | bytes 417800 | tf_op jit(solution)/shard_map/ppermute | solution.py:94
  142.9 8.2 %collective-permute-start.10 = (f32[136,256]{1,0:T(8,128)S(1)}, f32[136,256]{1,0:T(8,128)S(1)}, u32[]{:S(2)}, u32[]{:S(2)}) collective-permute-start(f32[136,256]{1,0:T(8,128)S(1)} %add.52), channel_id=1, source_target_pairs={{0,4},{1,5},{2,6},{3,7},{4,0},{5,1},{6,2},{7,3},{8,12},{9,13},{10,... | collective-permute-start | bytes 417800 | tf_op jit(solution)/shard_map/ppermute | solution.py:94
  151.1 15.2 %collective-permute-start.11 = (f32[136,256]{1,0:T(8,128)S(1)}, f32[136,256]{1,0:T(8,128)S(1)}, u32[]{:S(2)}, u32[]{:S(2)}) collective-permute-start(f32[136,256]{1,0:T(8,128)S(1)} %add.53), channel_id=1, source_target_pairs={{0,8},{1,9},{2,10},{3,11},{4,12},{5,13},{6,14},{7,15},{8,0},{9,1},... | collective-permute-start | bytes 417800 | tf_op jit(solution)/shard_map/ppermute | solution.py:94
  159.3 7.1 %collective-permute-start.5 = (bf16[512,128]{1,0:T(8,128)(2,1)S(1)}, bf16[512,128]{1,0:T(8,128)(2,1)S(1)}, u32[]{:S(2)}, u32[]{:S(2)}) collective-permute-start(bf16[512,128]{1,0:T(8,128)(2,1)S(1)} %bitcast.46), channel_id=1, source_target_pairs={{0,28},{4,0},{8,4},{12,8},{16,12},{20,16},{24,20},{28,24},{1,29},{... | collective-permute-start | bytes 393224 | tf_op jit(solution)/shard_map/ppermute | solution.py:11
  159.4 8.0 %collective-permute-start.6 = (bf16[512,128]{1,0:T(8,128)(2,1)S(1)}, bf16[512,128]{1,0:T(8,128)(2,1)S(1)}, u32[]{:S(2)}, u32[]{:S(2)}) collective-permute-start(bf16[512,128]{1,0:T(8,128)(2,1)S(1)} %bitcast.45), channel_id=1, source_target_pairs={{0,4},{4,8},{8,12},{12,16},{16,20},{20,24},{24,28},{28,0},{1,5},{5... | collective-permute-start | bytes 393224 | tf_op jit(solution)/shard_map/ppermute | solution.py:11
  161.4 8.2 %collective-permute-start.7 = (bf16[512,128]{1,0:T(8,128)(2,1)S(1)}, bf16[512,128]{1,0:T(8,128)(2,1)S(1)}, u32[]{:S(2)}, u32[]{:S(2)}) collective-permute-start(bf16[512,128]{1,0:T(8,128)(2,1)S(1)} %bitcast.44), channel_id=1, source_target_pairs={{0,8},{4,12},{8,16},{12,20},{16,24},{20,28},{24,0},{28,4},{1,9},{5... | collective-permute-start | bytes 393224 | tf_op jit(solution)/shard_map/ppermute | solution.py:11
  161.4 11.5 %collective-permute-start.4 = (bf16[512,128]{1,0:T(8,128)(2,1)S(1)}, bf16[512,128]{1,0:T(8,128)(2,1)S(1)}, u32[]{:S(2)}, u32[]{:S(2)}) collective-permute-start(bf16[512,128]{1,0:T(8,128)(2,1)S(1)} %bitcast.43), channel_id=1, source_target_pairs={{0,24},{4,28},{8,0},{12,4},{16,8},{20,12},{24,16},{28,20},{1,25},{... | collective-permute-start | bytes 393224 | tf_op jit(solution)/shard_map/ppermute | solution.py:11
  166.3 9.9 %collective-permute-start.12 = (f32[136,256]{1,0:T(8,128)S(1)}, f32[136,256]{1,0:T(8,128)S(1)}, u32[]{:S(2)}, u32[]{:S(2)}) collective-permute-start(f32[136,256]{1,0:T(8,128)S(1)} %add.54), channel_id=1, source_target_pairs={{0,16},{1,17},{2,18},{3,19},{4,20},{5,21},{6,22},{7,23},{8,24},{9,... | collective-permute-start | bytes 417800 | tf_op jit(solution)/shard_map/ppermute | solution.py:94
Sparse Core Ops, SparseCore 0:
  63.9 30.4 reduce-scatter.1

commit v2 on v1

--- a/solution.py
+++ b/solution.py
@@ -24,7 +24,9 @@
     chunks = slot_count // chunk
     out_width = width if forward else tile
 
-    def kernel(rows_ref, cols_ref, counts_ref, adj_ref, opnd_ref, out_ref):
+    group = slot_chunk(chunk, 8)
+
+    def kernel(rows_ref, cols_ref, counts_ref, adj_ref, opnd_ref, out_ref, prod_ref):
         k = pl.program_id(0)
         j = pl.program_id(1)
 
@@ -32,24 +34,31 @@
         def _():
             out_ref[...] = jnp.zeros_like(out_ref)
 
-        count = counts_ref[k]
+        live = counts_ref[k] - j * chunk
+        first = k * slot_count + j * chunk
+
+        for start in range(0, chunk, group):
+
+            @pl.when(live > start)
+            def _():
+                for i in range(start, start + group):
+                    g = first + i
+                    if forward:
+                        c = k * own_tiles + cols_ref[g]
+                        prod_ref[i] = jnp.dot(
+                            adj_ref[i], opnd_ref[c], preferred_element_type=jnp.float32
+                        )
+                    else:
+                        prod_ref[i] = jnp.dot(
+                            opnd_ref[rows_ref[g]], adj_ref[i], preferred_element_type=jnp.float32
+                        )
 
         def body(i, carry):
-            slot = j * chunk + i
-
-            @pl.when(slot < count)
+            @pl.when(i < live)
             def _():
-                g = k * slot_count + slot
-                d = rows_ref[g]
-                c = k * own_tiles + cols_ref[g]
-                if forward:
-                    out_ref[d] += jnp.dot(
-                        adj_ref[i], opnd_ref[c], preferred_element_type=jnp.float32
-                    )
-                else:
-                    out_ref[c] += jnp.dot(
-                        opnd_ref[d], adj_ref[i], preferred_element_type=jnp.float32
-                    )
+                g = first + i
+                target = rows_ref[g] if forward else k * own_tiles + cols_ref[g]
+                out_ref[target] += prod_ref[i]
 
             return carry
 
@@ -74,6 +83,7 @@
                 pl.BlockSpec(operand.shape, whole_map),
             ],
             out_specs=pl.BlockSpec((out_tiles, tile, out_width), whole_map),
+            scratch_shapes=[pltpu.VMEM((chunk, tile, out_width), jnp.float32)],
         ),
         out_shape=jax.ShapeDtypeStruct((out_tiles, tile, out_width), jnp.float32),
         compiler_params=pltpu.CompilerParams(dimension_semantics=("arbitrary", "arbitrary")),

time: 185 us -> 138 us (0.75)
  the two profiles are of different devices: /device:TPU:0 before, /device:TPU:7 now
where the time goes in v2:
time: 138 us; the launch traced here: 136 us
  waiting for transfers between devices  46.8 us (34%)
  Pallas kernels  35.8 us (26%)
  starting transfers between devices  18.8 us (14%)
  between operations  14.2 us (10%)
  blocking collectives  7.26 us (5%)
  other arithmetic  6.51 us (5%)
  local copies, waits for them, and re-layouts  3.72 us (3%)
  matrix products  2.73 us (2%)
    pallas_call x2, Pallas kernels, tile_products(): pl.pallas_call(kernel, grid_spec=pltpu.PrefetchScalarGridSpec(num_scalar_...  35.8 us
    reduce_scatter x1, waiting for transfers between devices, local(): sums = lax.psum_scatter(block_sums, 'col', scatter_dimension=0, tiled=True)  24.6 us
    ppermute x8, starting transfers between devices, from_behind(): lax.ppermute(value, axis, [(i, (i + by) % length) for i in range(length)])  11.6 us
    ppermute x5, waiting for transfers between devices, all_sum(): lax.ppermute(value, axes, [(i, i ^ bit) for i in range(size)])  11.5 us
    ppermute x8, waiting for transfers between devices, from_behind(): lax.ppermute(value, axis, [(i, (i + by) % length) for i in range(length)])  10.8 us
    all_gather x1, blocking collectives, local(): block_grad = lax.all_gather(grad_hidden, 'col', axis=0, tiled=True)  7.26 us
    ppermute x5, starting transfers between devices, all_sum(): lax.ppermute(value, axes, [(i, i ^ bit) for i in range(size)])  7.17 us
  transfers between devices with their start and end apart: 14, of which 8 were waited for; matrix products, arithmetic and copies ran while one was open for 5% of the time, Pallas kernels for 13%

profile of v2, /device:TPU:7, one launch (start us, length us, event | category | flops | bytes accessed | tf_op | source)
XLA Modules:
  0.0 135.8 jit_solution(7034352738846382726)
XLA Ops:
  7.2 0.0 copy-start
  7.2 0.0 reduce-scatter.2.cloned.1.call-start
  7.2 0.7 convert_rsqrt_fusion
  7.9 1.0 multiply_convert_fusion.2
  9.0 1.3 collective-permute-start
  10.3 0.3 collective-permute-start.2
  10.6 2.1 %collective-permute-start.3 = (bf16[512,128]{1,0:T(8,128)(2,1)S(1)}, bf16[512,128]{1,0:T(8,128)(2,1)S(1)}, u32[]{:S(2)}, u32[]{:S(2)}) collective-permute-start(bf16[512,128]{1,0:T(8,128)(2,1)S(1)} %multiply_convert_fusion.2), channel_id=1, source_target_pairs={{0,24},{4,28},{8,0},{12,4},{16,8},{20,12},{24,16},{28,20},{1,25},{... | collective-permute-start | bytes 393224 | tf_op jit(solution)/shard_map/ppermute | solution.py:11
  12.7 2.1 %collective-permute-start.1 = (bf16[512,128]{1,0:T(8,128)(2,1)S(1)}, bf16[512,128]{1,0:T(8,128)(2,1)S(1)}, u32[]{:S(2)}, u32[]{:S(2)}) collective-permute-start(bf16[512,128]{1,0:T(8,128)(2,1)S(1)} %multiply_convert_fusion.2), channel_id=1, source_target_pairs={{0,4},{4,8},{8,12},{12,16},{16,20},{20,24},{24,28},{28,0},{1,5},{5... | collective-permute-start | bytes 393224 | tf_op jit(solution)/shard_map/ppermute | solution.py:11
  14.8 0.5 collective-permute-done
  15.3 6.0 %collective-permute-done.1 = bf16[512,128]{1,0:T(8,128)(2,1)S(1)} collective-permute-done((bf16[512,128]{1,0:T(8,128)(2,1)S(1)}, bf16[512,128]{1,0:T(8,128)(2,1)S(1)}, u32[]{:S(2)}, u32[]{:S(2)}) %collective-permute-start.1) | collective-permute-done | bytes 131104 | tf_op jit(solution)/shard_map/ppermute | solution.py:11
  21.3 1.1 bitcast_dynamic-update-slice_fusion.2
  22.4 0.0 collective-permute-done.2
  22.5 0.0 collective-permute-done.3
  22.5 0.0 copy-start.1
  22.5 0.9 copy-done.1
  23.4 0.0 copy-start.3
  23.4 0.0 copy-start.4
  23.4 18.0 %shard_map.120 = f32[16,128,128]{2,1,0:T(8,128)} custom-call(s32[360]{0:T(512)} %rows_ref.3, s32[360]{0:T(512)} %cols_ref.3, s32[5]{0:T(128)} %counts_ref.3, bf16[360,128,128]{2,1,0:T(8,128)(2,1)} %adj_ref.3, bf16[20,128,128]{2,1,0:T(8,128)(2,1)} %bitcast.42), custom_call_target="tpu_custom_call" | custom-call | flops 1509949440 | bytes 13500416 | tf_op jit(solution)/shard_map/pallas_call | solution.py:76
  41.3 0.0 reduce-scatter.2.cloned.1.call-update
  41.4 0.1 pad.2.clone
  41.4 24.6 %reduce-scatter.2.cloned.1.call-done = f32[512,128]{1,0:T(8,128)} async-done(((f32[2048,128]{1,0:T(8,128)}), f32[512,128]{1,0:T(8,128)}) %reduce-scatter.2.cloned.1.call-update) | async-done | bytes 262160 | tf_op jit(solution)/shard_map/reduce_scatter | solution.py:131
  66.0 0.0 copy-done
  66.0 0.0 copy-done.3
  66.0 0.0 copy-done.4
  66.0 0.0 copy-start.2
  66.0 2.2 %fusion.10 = (f32[256]{0:T(256)S(1)}, bf16[512,256]{1,0:T(8,128)(2,1)S(1)}, bf16[512,256]{1,0:T(8,128)(2,1)}) fusion(bf16[512,256]{1,0:T(8,128)(2,1)S(1)} %copy-done.3, f32[256]{0:T(256)S(1)} %copy-done.4, bf16[128,256]{1,0:T(8,128)(2,1)S(1)} %copy-done, f32[512,128]{1,0:T(8,128)} %reduce-scatter.2.cloned.1.call-done, f32[512]{0:T(512)S(1)} %convert_rsqrt_fusion), kind=kOutput, calls=%fused_computation.28 | convolution fusion | flops 35520256 | bytes 1118208 | tf_op jit(solution)/shard_map/dot_general | solution.py:133
  68.2 0.2 fusion
  68.4 0.0 copy-done.2
  68.4 0.3 fusion.6
  68.7 0.1 maximum_maximum_fusion
  68.8 0.9 collective-permute-start.8
  69.7 7.3 %all_gather.3 = bf16[2048,128]{1,0:T(8,128)(2,1)S(1)} all-gather(bf16[512,128]{1,0:T(8,128)(2,1)S(1)} %fusion), channel_id=1, replica_groups=mesh['blk'=8,'col'=4] {'col'}, dimensions={0}, use_global_device_ids=true | all-gather | bytes 655360 | tf_op jit(solution)/shard_map/all_gather | solution.py:153
  77.0 1.0 copy.13
  78.0 0.0 collective-permute-done.8
  78.0 0.1 fusion.9
  78.1 1.3 collective-permute-start.9
  79.4 17.8 %shard_map.121 = f32[20,128,128]{2,1,0:T(8,128)} custom-call(s32[360]{0:T(512)} %rows_ref.3, s32[360]{0:T(512)} %cols_ref.3, s32[5]{0:T(128)} %counts_ref.3, bf16[360,128,128]{2,1,0:T(8,128)(2,1)} %adj_ref.3, bf16[16,128,128]{2,1,0:T(8,128)(2,1)} %bitcast.40), custom_call_target="tpu_custom_call" | custom-call | flops 1509949440 | bytes 13631488 | tf_op jit(solution)/shard_map/pallas_call | solution.py:76
  97.2 0.0 collective-permute-done.9
  97.2 0.1 collective-permute-start.10
  97.3 1.4 %bitcast_convert_fusion = bf16[20,128,128]{1,2,0:T(8,128)(2,1)S(1)} fusion(f32[20,128,128]{2,1,0:T(8,128)} %shard_map.121), kind=kLoop, calls=%fused_computation.26 | loop fusion | flops 327680 | bytes 1966080 | tf_op jit(solution)/shard_map/convert.3
  98.7 2.5 %collective-permute-done.10 = f32[136,256]{1,0:T(8,128)S(1)} collective-permute-done((f32[136,256]{1,0:T(8,128)S(1)}, f32[136,256]{1,0:T(8,128)S(1)}, u32[]{:S(2)}, u32[]{:S(2)}) %collective-permute-start.10) | collective-permute-done | bytes 139296 | tf_op jit(solution)/shard_map/ppermute | solution.py:104
  101.2 4.6 %collective-permute-start.11 = (f32[136,256]{1,0:T(8,128)S(1)}, f32[136,256]{1,0:T(8,128)S(1)}, u32[]{:S(2)}, u32[]{:S(2)}) collective-permute-start(f32[136,256]{1,0:T(8,128)S(1)} %add.53), channel_id=1, source_target_pairs={{0,8},{1,9},{2,10},{3,11},{4,12},{5,13},{6,14},{7,15},{8,0},{9,1},... | collective-permute-start | bytes 417800 | tf_op jit(solution)/shard_map/ppermute | solution.py:104
  105.8 0.1 copy.15
  106.0 0.1 copy.18
  106.1 0.1 copy.17
  106.3 0.1 copy.16
  106.4 0.1 collective-permute-start.5
  106.5 2.4 %collective-permute-start.6 = (bf16[512,128]{1,0:T(8,128)(2,1)S(1)}, bf16[512,128]{1,0:T(8,128)(2,1)S(1)}, u32[]{:S(2)}, u32[]{:S(2)}) collective-permute-start(bf16[512,128]{1,0:T(8,128)(2,1)S(1)} %bitcast.45), channel_id=1, source_target_pairs={{0,4},{4,8},{8,12},{12,16},{16,20},{20,24},{24,28},{28,0},{1,5},{5... | collective-permute-start | bytes 393224 | tf_op jit(solution)/shard_map/ppermute | solution.py:11
  108.8 0.0 collective-permute-start.7
  108.8 3.4 %collective-permute-start.4 = (bf16[512,128]{1,0:T(8,128)(2,1)S(1)}, bf16[512,128]{1,0:T(8,128)(2,1)S(1)}, u32[]{:S(2)}, u32[]{:S(2)}) collective-permute-start(bf16[512,128]{1,0:T(8,128)(2,1)S(1)} %bitcast.43), channel_id=1, source_target_pairs={{0,24},{4,28},{8,0},{12,4},{16,8},{20,12},{24,16},{28,20},{1,25},{... | collective-permute-start | bytes 393224 | tf_op jit(solution)/shard_map/ppermute | solution.py:11
  112.2 1.0 slice.37
  113.2 0.1 copy.14
  113.3 0.0 collective-permute-done.11
  113.3 0.3 collective-permute-start.12
  113.7 0.0 collective-permute-done.5
  113.7 1.9 %collective-permute-done.6 = bf16[512,128]{1,0:T(8,128)(2,1)S(1)} collective-permute-done((bf16[512,128]{1,0:T(8,128)(2,1)S(1)}, bf16[512,128]{1,0:T(8,128)(2,1)S(1)}, u32[]{:S(2)}, u32[]{:S(2)}) %collective-permute-start.6) | collective-permute-done | bytes 131104 | tf_op jit(solution)/shard_map/ppermute | solution.py:11
  115.6 1.8 %collective-permute-done.7 = bf16[512,128]{1,0:T(8,128)(2,1)S(1)} collective-permute-done((bf16[512,128]{1,0:T(8,128)(2,1)S(1)}, bf16[512,128]{1,0:T(8,128)(2,1)S(1)}, u32[]{:S(2)}, u32[]{:S(2)}) %collective-permute-start.7) | collective-permute-done | bytes 131104 | tf_op jit(solution)/shard_map/ppermute | solution.py:11
  117.3 0.6 collective-permute-done.4
  117.9 0.8 fusion.5
  118.7 9.0 %collective-permute-done.12 = f32[136,256]{1,0:T(8,128)S(1)} collective-permute-done((f32[136,256]{1,0:T(8,128)S(1)}, f32[136,256]{1,0:T(8,128)S(1)}, u32[]{:S(2)}, u32[]{:S(2)}) %collective-permute-start.12) | collective-permute-done | bytes 139296 | tf_op jit(solution)/shard_map/ppermute | solution.py:104
  127.8 0.6 slice_multiply_fusion.1
  128.3 0.7 slice_multiply_fusion
  (10 shorter events, 0.2 us)
Async XLA Ops:
  7.2 58.8 %copy-start = (bf16[128,256]{1,0:T(8,128)(2,1)S(1)}, bf16[128,256]{1,0:T(8,128)(2,1)}, u32[]{:S(2)}) copy-start(bf16[128,256]{1,0:T(8,128)(2,1)} %param.15) | copy-start | bytes 196612
  7.2 58.8 %reduce-scatter.2.cloned.1.call-start = ((), (), s32[]{:S(2)}) async-start(), calls=%async_computation.1 | async-start | bytes 1310720 | tf_op jit(solution)/shard_map/reduce_scatter | solution.py:131
  9.0 6.4 %collective-permute-start = (bf16[512,128]{1,0:T(8,128)(2,1)S(1)}, bf16[512,128]{1,0:T(8,128)(2,1)S(1)}, u32[]{:S(2)}, u32[]{:S(2)}) collective-permute-start(bf16[512,128]{1,0:T(8,128)(2,1)S(1)} %multiply_convert_fusion.2), channel_id=1, source_target_pairs={{0,8},{4,12},{8,16},{12,20},{16,24},{20,28},{24,0},{28,4},{1,9},{5... | collective-permute-start | bytes 393224 | tf_op jit(solution)/shard_map/ppermute | solution.py:11
  10.3 12.1 %collective-permute-start.2 = (bf16[512,128]{1,0:T(8,128)(2,1)S(1)}, bf16[512,128]{1,0:T(8,128)(2,1)S(1)}, u32[]{:S(2)}, u32[]{:S(2)}) collective-permute-start(bf16[512,128]{1,0:T(8,128)(2,1)S(1)} %multiply_convert_fusion.2), channel_id=1, source_target_pairs={{0,28},{4,0},{8,4},{12,8},{16,12},{20,16},{24,20},{28,24},{1,29},{... | collective-permute-start | bytes 393224 | tf_op jit(solution)/shard_map/ppermute | solution.py:11
  10.6 11.9 %collective-permute-start.3 = (bf16[512,128]{1,0:T(8,128)(2,1)S(1)}, bf16[512,128]{1,0:T(8,128)(2,1)S(1)}, u32[]{:S(2)}, u32[]{:S(2)}) collective-permute-start(bf16[512,128]{1,0:T(8,128)(2,1)S(1)} %multiply_convert_fusion.2), channel_id=1, source_target_pairs={{0,24},{4,28},{8,0},{12,4},{16,8},{20,12},{24,16},{28,20},{1,25},{... | collective-permute-start | bytes 393224 | tf_op jit(solution)/shard_map/ppermute | solution.py:11
  12.7 8.7 %collective-permute-start.1 = (bf16[512,128]{1,0:T(8,128)(2,1)S(1)}, bf16[512,128]{1,0:T(8,128)(2,1)S(1)}, u32[]{:S(2)}, u32[]{:S(2)}) collective-permute-start(bf16[512,128]{1,0:T(8,128)(2,1)S(1)} %multiply_convert_fusion.2), channel_id=1, source_target_pairs={{0,4},{4,8},{8,12},{12,16},{16,20},{20,24},{24,28},{28,0},{1,5},{5... | collective-permute-start | bytes 393224 | tf_op jit(solution)/shard_map/ppermute | solution.py:11
  22.5 0.9 copy-start.1
  23.4 42.6 %copy-start.3 = (bf16[512,256]{1,0:T(8,128)(2,1)S(1)}, bf16[512,256]{1,0:T(8,128)(2,1)}, u32[]{:S(2)}) copy-start(bf16[512,256]{1,0:T(8,128)(2,1)} %param.17) | copy-start | bytes 786436
  23.4 42.6 %copy-start.4 = (f32[256]{0:T(256)S(1)}, f32[256]{0:T(256)}, u32[]{:S(2)}) copy-start(f32[256]{0:T(256)} %param.16) | copy-start | bytes 3076
  66.0 2.4 %copy-start.2 = (f32[512,128]{1,0:T(8,128)S(1)}, f32[512,128]{1,0:T(8,128)}, u32[]{:S(2)}) copy-start(f32[512,128]{1,0:T(8,128)} %reduce-scatter.2.cloned.1.call-done) | copy-start | bytes 786436
  68.8 9.2 %collective-permute-start.8 = (f32[136,256]{1,0:T(8,128)S(1)}, f32[136,256]{1,0:T(8,128)S(1)}, u32[]{:S(2)}, u32[]{:S(2)}) collective-permute-start(f32[136,256]{1,0:T(8,128)S(1)} %maximum_maximum_fusion), channel_id=1, source_target_pairs={{0,1},{1,0},{2,3},{3,2},{4,5},{5,4},{6,7},{7,6},{8,9},{9,8},{10,11... | collective-permute-start | bytes 417800 | tf_op jit(solution)/shard_map/ppermute | solution.py:104
  78.1 19.1 %collective-permute-start.9 = (f32[136,256]{1,0:T(8,128)S(1)}, f32[136,256]{1,0:T(8,128)S(1)}, u32[]{:S(2)}, u32[]{:S(2)}) collective-permute-start(f32[136,256]{1,0:T(8,128)S(1)} %fusion.9), channel_id=1, source_target_pairs={{0,2},{1,3},{2,0},{3,1},{4,6},{5,7},{6,4},{7,5},{8,10},{9,11},{10,... | collective-permute-start | bytes 417800 | tf_op jit(solution)/shard_map/ppermute | solution.py:104
  97.2 4.0 %collective-permute-start.10 = (f32[136,256]{1,0:T(8,128)S(1)}, f32[136,256]{1,0:T(8,128)S(1)}, u32[]{:S(2)}, u32[]{:S(2)}) collective-permute-start(f32[136,256]{1,0:T(8,128)S(1)} %add.52), channel_id=1, source_target_pairs={{0,4},{1,5},{2,6},{3,7},{4,0},{5,1},{6,2},{7,3},{8,12},{9,13},{10,... | collective-permute-start | bytes 417800 | tf_op jit(solution)/shard_map/ppermute | solution.py:104
  101.2 12.1 %collective-permute-start.11 = (f32[136,256]{1,0:T(8,128)S(1)}, f32[136,256]{1,0:T(8,128)S(1)}, u32[]{:S(2)}, u32[]{:S(2)}) collective-permute-start(f32[136,256]{1,0:T(8,128)S(1)} %add.53), channel_id=1, source_target_pairs={{0,8},{1,9},{2,10},{3,11},{4,12},{5,13},{6,14},{7,15},{8,0},{9,1},... | collective-permute-start | bytes 417800 | tf_op jit(solution)/shard_map/ppermute | solution.py:104
  106.4 7.3 %collective-permute-start.5 = (bf16[512,128]{1,0:T(8,128)(2,1)S(1)}, bf16[512,128]{1,0:T(8,128)(2,1)S(1)}, u32[]{:S(2)}, u32[]{:S(2)}) collective-permute-start(bf16[512,128]{1,0:T(8,128)(2,1)S(1)} %bitcast.46), channel_id=1, source_target_pairs={{0,28},{4,0},{8,4},{12,8},{16,12},{20,16},{24,20},{28,24},{1,29},{... | collective-permute-start | bytes 393224 | tf_op jit(solution)/shard_map/ppermute | solution.py:11
  106.5 9.1 %collective-permute-start.6 = (bf16[512,128]{1,0:T(8,128)(2,1)S(1)}, bf16[512,128]{1,0:T(8,128)(2,1)S(1)}, u32[]{:S(2)}, u32[]{:S(2)}) collective-permute-start(bf16[512,128]{1,0:T(8,128)(2,1)S(1)} %bitcast.45), channel_id=1, source_target_pairs={{0,4},{4,8},{8,12},{12,16},{16,20},{20,24},{24,28},{28,0},{1,5},{5... | collective-permute-start | bytes 393224 | tf_op jit(solution)/shard_map/ppermute | solution.py:11
  108.8 8.5 %collective-permute-start.7 = (bf16[512,128]{1,0:T(8,128)(2,1)S(1)}, bf16[512,128]{1,0:T(8,128)(2,1)S(1)}, u32[]{:S(2)}, u32[]{:S(2)}) collective-permute-start(bf16[512,128]{1,0:T(8,128)(2,1)S(1)} %bitcast.44), channel_id=1, source_target_pairs={{0,8},{4,12},{8,16},{12,20},{16,24},{20,28},{24,0},{28,4},{1,9},{5... | collective-permute-start | bytes 393224 | tf_op jit(solution)/shard_map/ppermute | solution.py:11
  108.8 9.1 %collective-permute-start.4 = (bf16[512,128]{1,0:T(8,128)(2,1)S(1)}, bf16[512,128]{1,0:T(8,128)(2,1)S(1)}, u32[]{:S(2)}, u32[]{:S(2)}) collective-permute-start(bf16[512,128]{1,0:T(8,128)(2,1)S(1)} %bitcast.43), channel_id=1, source_target_pairs={{0,24},{4,28},{8,0},{12,4},{16,8},{20,12},{24,16},{28,20},{1,25},{... | collective-permute-start | bytes 393224 | tf_op jit(solution)/shard_map/ppermute | solution.py:11
  113.3 14.4 %collective-permute-start.12 = (f32[136,256]{1,0:T(8,128)S(1)}, f32[136,256]{1,0:T(8,128)S(1)}, u32[]{:S(2)}, u32[]{:S(2)}) collective-permute-start(f32[136,256]{1,0:T(8,128)S(1)} %add.54), channel_id=1, source_target_pairs={{0,16},{1,17},{2,18},{3,19},{4,20},{5,21},{6,22},{7,23},{8,24},{9,... | collective-permute-start | bytes 417800 | tf_op jit(solution)/shard_map/ppermute | solution.py:104
Sparse Core Ops, SparseCore 0:
  41.5 24.4 reduce-scatter.1

commit v3 on v2

--- a/solution.py
+++ b/solution.py
@@ -15,24 +15,28 @@
     return max(c for c in range(1, limit + 1) if slot_count % c == 0)
 
 
-def tile_products(rows, cols, counts, adjacency, operand, out_tiles, own_tiles, forward):
+def tile_products(rows, cols, counts, adjacency, operand, k, out_shape, forward, acc=None):
     offset_count = counts.shape[0]
     slot_count = adjacency.shape[0] // offset_count
     tile = adjacency.shape[1]
-    width = operand.shape[2]
     chunk = slot_chunk(slot_count)
     chunks = slot_count // chunk
-    out_width = width if forward else tile
-
     group = slot_chunk(chunk, 8)
-
-    def kernel(rows_ref, cols_ref, counts_ref, adj_ref, opnd_ref, out_ref, prod_ref):
-        k = pl.program_id(0)
-        j = pl.program_id(1)
-
-        @pl.when((k == 0) & (j == 0))
+    out_width = out_shape[2]
+
+    def kernel(rows_ref, cols_ref, counts_ref, adj_ref, opnd_ref, *rest):
+        if acc is None:
+            out_ref, prod_ref = rest
+        else:
+            acc_ref, out_ref, prod_ref = rest
+        j = pl.program_id(0)
+
+        @pl.when(j == 0)
         def _():
-            out_ref[...] = jnp.zeros_like(out_ref)
+            if acc is None:
+                out_ref[...] = jnp.zeros_like(out_ref)
+            else:
+                out_ref[...] = acc_ref[...]
 
         live = counts_ref[k] - j * chunk
         first = k * slot_count + j * chunk
@@ -44,9 +48,8 @@
                 for i in range(start, start + group):
                     g = first + i
                     if forward:
-                        c = k * own_tiles + cols_ref[g]
                         prod_ref[i] = jnp.dot(
-                            adj_ref[i], opnd_ref[c], preferred_element_type=jnp.float32
+                            adj_ref[i], opnd_ref[cols_ref[g]], preferred_element_type=jnp.float32
                         )
                     else:
                         prod_ref[i] = jnp.dot(
@@ -57,40 +60,48 @@
             @pl.when(i < live)
             def _():
                 g = first + i
-                target = rows_ref[g] if forward else k * own_tiles + cols_ref[g]
+                target = rows_ref[g] if forward else cols_ref[g]
                 out_ref[target] += prod_ref[i]
 
             return carry
 
         lax.fori_loop(0, chunk, body, 0)
 
-    def adj_map(k, j, rows_ref, cols_ref, counts_ref):
+    def adj_map(j, rows_ref, cols_ref, counts_ref):
         last = jnp.maximum(counts_ref[k] - 1, 0) // chunk
         return (k * chunks + jnp.minimum(j, last), 0, 0)
 
-    def whole_map(k, j, rows_ref, cols_ref, counts_ref):
+    def whole_map(j, rows_ref, cols_ref, counts_ref):
         return (0, 0, 0)
 
-    flops = 2 * adjacency.shape[0] * tile * tile * width
-    bytes_accessed = adjacency.size * 2 + operand.size * 2 + out_tiles * tile * out_width * 4
+    in_specs = [
+        pl.BlockSpec((chunk, tile, tile), adj_map),
+        pl.BlockSpec(operand.shape, whole_map),
+    ]
+    args = [rows, cols, counts, adjacency, operand]
+    aliases = {}
+    if acc is not None:
+        in_specs.append(pl.BlockSpec(out_shape, whole_map))
+        args.append(acc)
+        aliases = {5: 0}
+    flops = 2 * slot_count * tile * tile * out_width
+    bytes_accessed = slot_count * tile * tile * 2 + operand.size * 2 + 8 * out_shape[0] * tile * out_width
     return pl.pallas_call(
         kernel,
         grid_spec=pltpu.PrefetchScalarGridSpec(
             num_scalar_prefetch=3,
-            grid=(offset_count, chunks),
-            in_specs=[
-                pl.BlockSpec((chunk, tile, tile), adj_map),
-                pl.BlockSpec(operand.shape, whole_map),
-            ],
-            out_specs=pl.BlockSpec((out_tiles, tile, out_width), whole_map),
+            grid=(chunks,),
+            in_specs=in_specs,
+            out_specs=pl.BlockSpec(out_shape, whole_map),
             scratch_shapes=[pltpu.VMEM((chunk, tile, out_width), jnp.float32)],
         ),
-        out_shape=jax.ShapeDtypeStruct((out_tiles, tile, out_width), jnp.float32),
-        compiler_params=pltpu.CompilerParams(dimension_semantics=("arbitrary", "arbitrary")),
+        out_shape=jax.ShapeDtypeStruct(out_shape, jnp.float32),
+        input_output_aliases=aliases,
+        compiler_params=pltpu.CompilerParams(dimension_semantics=("arbitrary",)),
         cost_estimate=pl.CostEstimate(
             flops=flops, transcendentals=0, bytes_accessed=bytes_accessed
         ),
-    )(rows, cols, counts, adjacency, operand)
+    )(*args)
 
 
 def all_sum(value, axes):
@@ -119,14 +130,17 @@
     block_tiles = col_count * own_tiles
     row_scale = lax.rsqrt(degree.astype(jnp.float32))
     source = (row_scale[:, None] * node_features.astype(jnp.float32)).astype(jnp.bfloat16)
-    fetched = [
-        source if k == reach_steps else from_behind(source, "blk", reach_steps - k)
-        for k in range(offset_count)
-    ]
-    source_tiles = jnp.stack(fetched).reshape(offset_count * own_tiles, tile_size, features)
-    block_sums = tile_products(
-        tile_rows, tile_cols, counts, adjacency, source_tiles, block_tiles, own_tiles, True
-    )
+    source_tiles = source.reshape(own_tiles, tile_size, features)
+    block_sums = None
+    for distance in range(reach_steps + 1):
+        for k in sorted({reach_steps - distance, reach_steps + distance}):
+            fetched = source_tiles
+            if k != reach_steps:
+                fetched = from_behind(source_tiles, "blk", reach_steps - k)
+            block_sums = tile_products(
+                tile_rows, tile_cols, counts, adjacency, fetched, k,
+                (block_tiles, tile_size, features), True, block_sums,
+            )
     block_sums = block_sums.reshape(block_tiles * tile_size, features)
     sums = lax.psum_scatter(block_sums, "col", scatter_dimension=0, tiled=True)
     aggregated = (row_scale[:, None] * sums).astype(jnp.bfloat16)
@@ -152,16 +166,18 @@
     grad_hidden = (row_scale[:, None] * grad_rows).astype(jnp.bfloat16)
     block_grad = lax.all_gather(grad_hidden, "col", axis=0, tiled=True)
     grad_tiles_t = jnp.swapaxes(block_grad.reshape(block_tiles, tile_size, features), 1, 2)
-    outgoing_t = tile_products(
-        tile_rows, tile_cols, counts, adjacency, grad_tiles_t, offset_count * own_tiles,
-        own_tiles, False,
-    )
-    outgoing = jnp.swapaxes(outgoing_t, 1, 2).reshape(offset_count, own_rows, features)
-    total_back = outgoing[reach_steps]
-    for k in range(offset_count):
-        if k != reach_steps:
-            sent = outgoing[k].astype(jnp.bfloat16)
-            total_back = total_back + from_behind(sent, "blk", k - reach_steps).astype(jnp.float32)
+    total_back = None
+    for distance in range(reach_steps, -1, -1):
+        for k in sorted({reach_steps - distance, reach_steps + distance}):
+            outgoing_t = tile_products(
+                tile_rows, tile_cols, counts, adjacency, grad_tiles_t, k,
+                (own_tiles, features, tile_size), False,
+            )
+            outgoing = jnp.swapaxes(outgoing_t, 1, 2).reshape(own_rows, features)
+            if k != reach_steps:
+                sent = outgoing.astype(jnp.bfloat16)
+                outgoing = from_behind(sent, "blk", k - reach_steps).astype(jnp.float32)
+            total_back = outgoing if total_back is None else total_back + outgoing
     grad_features = (row_scale[:, None] * total_back).astype(jnp.bfloat16)
     return (activations, grad_features, weight_sum * norm_factor, bias_sum * norm_factor)
 

time: 138 us -> 147 us (1.065)
  the two profiles are of different devices: /device:TPU:7 before, /device:TPU:0 now
where the time goes in v3:
time: 147 us; the launch traced here: 146 us
  Pallas kernels  52.3 us (36%)
  waiting for transfers between devices  30.7 us (21%)
  starting transfers between devices  24.7 us (17%)
  between operations  14.2 us (10%)
  other arithmetic  7.88 us (5%)
  blocking collectives  7.41 us (5%)
  local copies, waits for them, and re-layouts  5.33 us (4%)
  matrix products  3.61 us (2%)
    pallas_call x10, Pallas kernels, tile_products(): pl.pallas_call(kernel, grid_spec=pltpu.PrefetchScalarGridSpec(num_scalar_...  52.3 us
    reduce_scatter x1, waiting for transfers between devices, local(): sums = lax.psum_scatter(block_sums, 'col', scatter_dimension=0, tiled=True)  24.1 us
    ppermute x8, starting transfers between devices, from_behind(): lax.ppermute(value, axis, [(i, (i + by) % length) for i in range(length)])  16.6 us
    ppermute x5, starting transfers between devices, all_sum(): lax.ppermute(value, axes, [(i, i ^ bit) for i in range(size)])  8.1 us
    all_gather x1, blocking collectives, local(): block_grad = lax.all_gather(grad_hidden, 'col', axis=0, tiled=True)  7.41 us
    ppermute x5, waiting for transfers between devices, all_sum(): lax.ppermute(value, axes, [(i, i ^ bit) for i in range(size)])  6.56 us
    convert_element_type x4, other arithmetic, local(): sent = outgoing.astype(jnp.bfloat16)  3.88 us
  transfers between devices with their start and end apart: 14, of which 2 were waited for; matrix products, arithmetic and copies ran while one was open for 5% of the time, Pallas kernels for 32%

profile of v3, /device:TPU:0, one launch (start us, length us, event | category | flops | bytes accessed | tf_op | source)
XLA Modules:
  0.0 146.2 jit_solution(2160223808184160446)
XLA Ops:
  7.2 0.0 copy-start
  7.2 0.0 reduce-scatter.2.cloned.1.call-start
  7.2 0.7 convert_rsqrt_fusion
  7.9 1.0 multiply_convert_fusion.2
  9.0 0.0 copy-start.1
  9.0 3.0 %collective-permute-start.3 = (bf16[4,128,128]{2,1,0:T(8,128)(2,1)S(1)}, bf16[4,128,128]{2,1,0:T(8,128)(2,1)S(1)}, u32[]{:S(2)}, u32[]{:S(2)}) collective-permute-start(bf16[4,128,128]{2,1,0:T(8,128)(2,1)S(1)} %bitcast.37), channel_id=1, source_target_pairs={{0,4},{4,8},{8,12},{12,16},{16,20},{20,24},{24,28},{28,0},{1,5},{5... | collective-permute-start | bytes 393224 | tf_op jit(solution)/shard_map/ppermute | solution.py:11
  12.0 3.1 %collective-permute-start.2 = (bf16[4,128,128]{2,1,0:T(8,128)(2,1)S(1)}, bf16[4,128,128]{2,1,0:T(8,128)(2,1)S(1)}, u32[]{:S(2)}, u32[]{:S(2)}) collective-permute-start(bf16[4,128,128]{2,1,0:T(8,128)(2,1)S(1)} %bitcast.38), channel_id=1, source_target_pairs={{0,28},{4,0},{8,4},{12,8},{16,12},{20,16},{24,20},{28,24},{1,29},{... | collective-permute-start | bytes 393224 | tf_op jit(solution)/shard_map/ppermute | solution.py:11
  15.1 0.0 collective-permute-start.1
  15.1 3.8 %collective-permute-start = (bf16[4,128,128]{2,1,0:T(8,128)(2,1)S(1)}, bf16[4,128,128]{2,1,0:T(8,128)(2,1)S(1)}, u32[]{:S(2)}, u32[]{:S(2)}) collective-permute-start(bf16[4,128,128]{2,1,0:T(8,128)(2,1)S(1)} %bitcast.40), channel_id=1, source_target_pairs={{0,24},{4,28},{8,0},{12,4},{16,8},{20,12},{24,16},{28,20},{1,25},{... | collective-permute-start | bytes 393224 | tf_op jit(solution)/shard_map/ppermute | solution.py:11
  18.9 4.6 %shard_map.120.rest_0_ = f32[16,128,128]{2,1,0:T(8,128)} custom-call(s32[360]{0:T(512)} %rows_ref.19, s32[360]{0:T(512)} %cols_ref.19, s32[5]{0:T(128)} %counts_ref.19, bf16[360,128,128]{2,1,0:T(8,128)(2,1)} %adj_ref.19, bf16[4,128,128]{2,1,0:T(8,128)(2,1)} %bitcast.41), custom_call_target="tpu_custom_call" | custom-call | flops 301989888 | bytes 4587520 | tf_op jit(solution)/shard_map/pallas_call | solution.py:89
  23.5 0.0 collective-permute-done.3.opnd_ref
  23.5 0.7 copy-done.5
  24.2 4.7 %shard_map.121.rest_0_ = f32[16,128,128]{2,1,0:T(8,128)} custom-call(s32[360]{0:T(512)} %rows_ref.19, s32[360]{0:T(512)} %cols_ref.19, s32[5]{0:T(128)} %counts_ref.19, bf16[360,128,128]{2,1,0:T(8,128)(2,1)} %adj_ref.19, bf16[4,128,128]{2,1,0:T(8,128)(2,1)} %copy-done.5, f32[16,128,128]{2,1,0:T(8,128)} %shard_map.120.rest_0_), custom_call_target="tpu_custom_call", output_to_operand_aliasing={{}: (5, {})} | custom-call | flops 301989888 | bytes 4587520 | tf_op jit(solution)/shard_map/pallas_call | solution.py:89
  28.9 0.0 collective-permute-done.2.opnd_ref
  28.9 0.7 copy-done.4
  29.5 6.6 %shard_map.122.rest_0_ = f32[16,128,128]{2,1,0:T(8,128)} custom-call(s32[360]{0:T(512)} %rows_ref.19, s32[360]{0:T(512)} %cols_ref.19, s32[5]{0:T(128)} %counts_ref.19, bf16[360,128,128]{2,1,0:T(8,128)(2,1)} %adj_ref.19, bf16[4,128,128]{2,1,0:T(8,128)(2,1)} %copy-done.4, f32[16,128,128]{2,1,0:T(8,128)} %shard_map.121.rest_0_), custom_call_target="tpu_custom_call", output_to_operand_aliasing={{}: (5, {})} | custom-call | flops 301989888 | bytes 4587520 | tf_op jit(solution)/shard_map/pallas_call | solution.py:89
  36.1 0.0 collective-permute-done.1.opnd_ref
  36.1 0.0 copy-start.3
  36.2 0.6 copy-done.3
  36.8 6.6 %shard_map.123.rest_0_ = f32[16,128,128]{2,1,0:T(8,128)} custom-call(s32[360]{0:T(512)} %rows_ref.19, s32[360]{0:T(512)} %cols_ref.19, s32[5]{0:T(128)} %counts_ref.19, bf16[360,128,128]{2,1,0:T(8,128)(2,1)} %adj_ref.19, bf16[4,128,128]{2,1,0:T(8,128)(2,1)} %copy-done.3, f32[16,128,128]{2,1,0:T(8,128)} %shard_map.122.rest_0_), custom_call_target="tpu_custom_call", output_to_operand_aliasing={{}: (5, {})} | custom-call | flops 301989888 | bytes 4587520 | tf_op jit(solution)/shard_map/pallas_call | solution.py:89
  43.4 0.0 collective-permute-done.opnd_ref
  43.4 0.7 copy-done.2
  44.0 5.0 %shard_map.124 = f32[16,128,128]{2,1,0:T(8,128)} custom-call(s32[360]{0:T(512)} %rows_ref.19, s32[360]{0:T(512)} %cols_ref.19, s32[5]{0:T(128)} %counts_ref.19, bf16[360,128,128]{2,1,0:T(8,128)(2,1)} %adj_ref.19, bf16[4,128,128]{2,1,0:T(8,128)(2,1)} %copy-done.2, f32[16,128,128]{2,1,0:T(8,128)} %shard_map.123.rest_0_), custom_call_target="tpu_custom_call", output_to_operand_aliasing={{}: (5, {})} | custom-call | flops 301989888 | bytes 4587520 | tf_op jit(solution)/shard_map/pallas_call | solution.py:89
  49.0 0.0 reduce-scatter.2.cloned.1.call-update
  49.0 0.1 pad.2.clone
  49.1 24.1 %reduce-scatter.2.cloned.1.call-done = f32[512,128]{1,0:T(8,128)} async-done(((f32[2048,128]{1,0:T(8,128)}), f32[512,128]{1,0:T(8,128)}) %reduce-scatter.2.cloned.1.call-update) | async-done | bytes 262160 | tf_op jit(solution)/shard_map/reduce_scatter | solution.py:145
  73.2 2.1 %fusion.7 = (f32[256]{0:T(256)S(1)}, bf16[512,256]{1,0:T(8,128)(2,1)S(1)}, bf16[512,256]{1,0:T(8,128)(2,1)}) fusion(bf16[512,256]{1,0:T(8,128)(2,1)S(1)} %copy-done.6, f32[256]{0:T(256)S(1)} %copy-done.7, bf16[128,256]{1,0:T(8,128)(2,1)S(1)} %copy-done, f32[512,128]{1,0:T(8,128)} %reduce-scatter.2.cloned.1.call-done, f32[512]{0:T(512)S(1)} %convert_rsqrt_fusion), kind=kOutput, calls=%fused_computation.23 | convolution fusion | flops 35520256 | bytes 1118208 | tf_op jit(solution)/shard_map/dot_general | solution.py:147
  75.3 0.2 fusion
  75.5 1.3 fusion.3
  76.8 0.1 maximum_maximum_fusion
  76.9 0.1 collective-permute-start.8
  77.0 7.4 %all_gather.3 = bf16[2048,128]{1,0:T(8,128)(2,1)S(1)} all-gather(bf16[512,128]{1,0:T(8,128)(2,1)S(1)} %fusion), channel_id=1, replica_groups=mesh['blk'=8,'col'=4] {'col'}, dimensions={0}, use_global_device_ids=true | all-gather | bytes 655360 | tf_op jit(solution)/shard_map/all_gather | solution.py:167
  84.4 1.0 copy.17
  85.4 6.0 %shard_map.125 = f32[4,128,128]{2,1,0:T(8,128)} custom-call(s32[360]{0:T(512)} %rows_ref.19, s32[360]{0:T(512)} %cols_ref.19, s32[5]{0:T(128)} %counts_ref.19, bf16[360,128,128]{2,1,0:T(8,128)(2,1)} %adj_ref.19, bf16[16,128,128]{2,1,0:T(8,128)(2,1)} %bitcast.30), custom_call_target="tpu_custom_call" | custom-call | flops 301989888 | bytes 3407872 | tf_op jit(solution)/shard_map/pallas_call | solution.py:89
  91.4 1.0 convert_bitcast_fusion.3
  92.4 0.1 copy.18
  92.5 2.9 %collective-permute-start.4 = (bf16[512,128]{1,0:T(8,128)(2,1)S(1)}, bf16[512,128]{1,0:T(8,128)(2,1)S(1)}, u32[]{:S(2)}, u32[]{:S(2)}) collective-permute-start(bf16[512,128]{1,0:T(8,128)(2,1)S(1)} %bitcast.42), channel_id=1, source_target_pairs={{0,24},{4,28},{8,0},{12,4},{16,8},{20,12},{24,16},{28,20},{1,25},{... | collective-permute-start | bytes 393224 | tf_op jit(solution)/shard_map/ppermute | solution.py:11
  95.4 4.4 %shard_map.126 = f32[4,128,128]{2,1,0:T(8,128)} custom-call(s32[360]{0:T(512)} %rows_ref.19, s32[360]{0:T(512)} %cols_ref.19, s32[5]{0:T(128)} %counts_ref.19, bf16[360,128,128]{2,1,0:T(8,128)(2,1)} %adj_ref.19, bf16[16,128,128]{2,1,0:T(8,128)(2,1)} %bitcast.31), custom_call_target="tpu_custom_call" | custom-call | flops 301989888 | bytes 3407872 | tf_op jit(solution)/shard_map/pallas_call | solution.py:89
  99.8 0.0 collective-permute-done.8
  99.8 0.1 fusion.6
  99.9 2.2 %collective-permute-start.9 = (f32[136,256]{1,0:T(8,128)S(1)}, f32[136,256]{1,0:T(8,128)S(1)}, u32[]{:S(2)}, u32[]{:S(2)}) collective-permute-start(f32[136,256]{1,0:T(8,128)S(1)} %fusion.6), channel_id=1, source_target_pairs={{0,2},{1,3},{2,0},{3,1},{4,6},{5,7},{6,4},{7,5},{8,10},{9,11},{10,... | collective-permute-start | bytes 417800 | tf_op jit(solution)/shard_map/ppermute | solution.py:115
  102.1 1.0 convert_bitcast_fusion.2
  103.1 0.1 copy.19
  103.2 0.1 collective-permute-start.5
  103.3 4.1 %shard_map.127 = f32[4,128,128]{2,1,0:T(8,128)} custom-call(s32[360]{0:T(512)} %rows_ref.19, s32[360]{0:T(512)} %cols_ref.19, s32[5]{0:T(128)} %counts_ref.19, bf16[360,128,128]{2,1,0:T(8,128)(2,1)} %adj_ref.19, bf16[16,128,128]{2,1,0:T(8,128)(2,1)} %bitcast.32), custom_call_target="tpu_custom_call" | custom-call | flops 301989888 | bytes 3407872 | tf_op jit(solution)/shard_map/pallas_call | solution.py:89
  107.4 0.0 collective-permute-done.9
  107.4 3.1 %collective-permute-start.10 = (f32[136,256]{1,0:T(8,128)S(1)}, f32[136,256]{1,0:T(8,128)S(1)}, u32[]{:S(2)}, u32[]{:S(2)}) collective-permute-start(f32[136,256]{1,0:T(8,128)S(1)} %add.52), channel_id=1, source_target_pairs={{0,4},{1,5},{2,6},{3,7},{4,0},{5,1},{6,2},{7,3},{8,12},{9,13},{10,... | collective-permute-start | bytes 417800 | tf_op jit(solution)/shard_map/ppermute | solution.py:115
  110.5 1.0 convert_bitcast_fusion.1
  111.5 0.1 copy.20
  111.6 3.6 %collective-permute-start.6 = (bf16[512,128]{1,0:T(8,128)(2,1)S(1)}, bf16[512,128]{1,0:T(8,128)(2,1)S(1)}, u32[]{:S(2)}, u32[]{:S(2)}) collective-permute-start(bf16[512,128]{1,0:T(8,128)(2,1)S(1)} %bitcast.44), channel_id=1, source_target_pairs={{0,28},{4,0},{8,4},{12,8},{16,12},{20,16},{24,20},{28,24},{1,29},{... | collective-permute-start | bytes 393224 | tf_op jit(solution)/shard_map/ppermute | solution.py:11
  115.3 6.0 %shard_map.128 = f32[4,128,128]{2,1,0:T(8,128)} custom-call(s32[360]{0:T(512)} %rows_ref.19, s32[360]{0:T(512)} %cols_ref.19, s32[5]{0:T(128)} %counts_ref.19, bf16[360,128,128]{2,1,0:T(8,128)(2,1)} %adj_ref.19, bf16[16,128,128]{2,1,0:T(8,128)(2,1)} %bitcast.33), custom_call_target="tpu_custom_call" | custom-call | flops 301989888 | bytes 3407872 | tf_op jit(solution)/shard_map/pallas_call | solution.py:89
  121.3 0.1 collective-permute-start.11
  121.4 1.0 convert_bitcast_fusion
  122.3 0.1 copy.21
  122.5 0.1 collective-permute-start.7
  122.5 4.4 %shard_map.129 = f32[4,128,128]{2,1,0:T(8,128)} custom-call(s32[360]{0:T(512)} %rows_ref.19, s32[360]{0:T(512)} %cols_ref.19, s32[5]{0:T(128)} %counts_ref.19, bf16[360,128,128]{2,1,0:T(8,128)(2,1)} %adj_ref.19, bf16[16,128,128]{2,1,0:T(8,128)(2,1)} %bitcast.34), custom_call_target="tpu_custom_call" | custom-call | flops 301989888 | bytes 3407872 | tf_op jit(solution)/shard_map/pallas_call | solution.py:89
  126.9 1.1 copy.22
  128.1 2.6 %collective-permute-start.12 = (f32[136,256]{1,0:T(8,128)S(1)}, f32[136,256]{1,0:T(8,128)S(1)}, u32[]{:S(2)}, u32[]{:S(2)}) collective-permute-start(f32[136,256]{1,0:T(8,128)S(1)} %add.54), channel_id=1, source_target_pairs={{0,16},{1,17},{2,18},{3,19},{4,20},{5,21},{6,22},{7,23},{8,24},{9,... | collective-permute-start | bytes 417800 | tf_op jit(solution)/shard_map/ppermute | solution.py:115
  130.7 0.0 collective-permute-done.4
  130.7 0.0 collective-permute-done.7
  130.7 0.8 fusion.2
  131.5 6.6 %collective-permute-done.12 = f32[136,256]{1,0:T(8,128)S(1)} collective-permute-done((f32[136,256]{1,0:T(8,128)S(1)}, f32[136,256]{1,0:T(8,128)S(1)}, u32[]{:S(2)}, u32[]{:S(2)}) %collective-permute-start.12) | collective-permute-done | bytes 139296 | tf_op jit(solution)/shard_map/ppermute | solution.py:115
  138.1 0.7 slice_multiply_fusion
  138.8 0.6 slice_multiply_fusion.1
  (18 shorter events, 0.1 us)
Async XLA Ops:
  7.2 66.0 %copy-start = (bf16[128,256]{1,0:T(8,128)(2,1)S(1)}, bf16[128,256]{1,0:T(8,128)(2,1)}, u32[]{:S(2)}) copy-start(bf16[128,256]{1,0:T(8,128)(2,1)} %param.15) | copy-start | bytes 196612
  7.2 66.0 %reduce-scatter.2.cloned.1.call-start = ((), (), s32[]{:S(2)}) async-start(), calls=%async_computation.1 | async-start | bytes 1310720 | tf_op jit(solution)/shard_map/reduce_scatter | solution.py:145
  9.0 10.0 %copy-start.1 = (bf16[512,128]{1,0:T(8,128)(2,1)}, bf16[512,128]{1,0:T(8,128)(2,1)S(1)}, u32[]{:S(2)}) copy-start(bf16[512,128]{1,0:T(8,128)(2,1)S(1)} %multiply_convert_fusion.2) | copy-start | bytes 393220
  9.0 14.6 %collective-permute-start.3 = (bf16[4,128,128]{2,1,0:T(8,128)(2,1)S(1)}, bf16[4,128,128]{2,1,0:T(8,128)(2,1)S(1)}, u32[]{:S(2)}, u32[]{:S(2)}) collective-permute-start(bf16[4,128,128]{2,1,0:T(8,128)(2,1)S(1)} %bitcast.37), channel_id=1, source_target_pairs={{0,4},{4,8},{8,12},{12,16},{16,20},{20,24},{24,28},{28,0},{1,5},{5... | collective-permute-start | bytes 393224 | tf_op jit(solution)/shard_map/ppermute | solution.py:11
  12.0 16.9 %collective-permute-start.2 = (bf16[4,128,128]{2,1,0:T(8,128)(2,1)S(1)}, bf16[4,128,128]{2,1,0:T(8,128)(2,1)S(1)}, u32[]{:S(2)}, u32[]{:S(2)}) collective-permute-start(bf16[4,128,128]{2,1,0:T(8,128)(2,1)S(1)} %bitcast.38), channel_id=1, source_target_pairs={{0,28},{4,0},{8,4},{12,8},{16,12},{20,16},{24,20},{28,24},{1,29},{... | collective-permute-start | bytes 393224 | tf_op jit(solution)/shard_map/ppermute | solution.py:11
  15.1 21.1 %collective-permute-start.1 = (bf16[4,128,128]{2,1,0:T(8,128)(2,1)S(1)}, bf16[4,128,128]{2,1,0:T(8,128)(2,1)S(1)}, u32[]{:S(2)}, u32[]{:S(2)}) collective-permute-start(bf16[4,128,128]{2,1,0:T(8,128)(2,1)S(1)} %bitcast.39), channel_id=1, source_target_pairs={{0,8},{4,12},{8,16},{12,20},{16,24},{20,28},{24,0},{28,4},{1,9},{5... | collective-permute-start | bytes 393224 | tf_op jit(solution)/shard_map/ppermute | solution.py:11
  15.1 28.3 %collective-permute-start = (bf16[4,128,128]{2,1,0:T(8,128)(2,1)S(1)}, bf16[4,128,128]{2,1,0:T(8,128)(2,1)S(1)}, u32[]{:S(2)}, u32[]{:S(2)}) collective-permute-start(bf16[4,128,128]{2,1,0:T(8,128)(2,1)S(1)} %bitcast.40), channel_id=1, source_target_pairs={{0,24},{4,28},{8,0},{12,4},{16,8},{20,12},{24,16},{28,20},{1,25},{... | collective-permute-start | bytes 393224 | tf_op jit(solution)/shard_map/ppermute | solution.py:11
  23.5 0.7 copy-start.5
  28.9 0.7 copy-start.4
  36.1 37.1 %copy-start.6 = (bf16[512,256]{1,0:T(8,128)(2,1)S(1)}, bf16[512,256]{1,0:T(8,128)(2,1)}, u32[]{:S(2)}) copy-start(bf16[512,256]{1,0:T(8,128)(2,1)} %param.17) | copy-start | bytes 786436
  36.1 37.1 %copy-start.7 = (f32[256]{0:T(256)S(1)}, f32[256]{0:T(256)}, u32[]{:S(2)}) copy-start(f32[256]{0:T(256)} %param.16) | copy-start | bytes 3076
  36.1 0.7 copy-start.3
  43.4 0.7 copy-start.2
  76.9 22.9 %collective-permute-start.8 = (f32[136,256]{1,0:T(8,128)S(1)}, f32[136,256]{1,0:T(8,128)S(1)}, u32[]{:S(2)}, u32[]{:S(2)}) collective-permute-start(f32[136,256]{1,0:T(8,128)S(1)} %maximum_maximum_fusion), channel_id=1, source_target_pairs={{0,1},{1,0},{2,3},{3,2},{4,5},{5,4},{6,7},{7,6},{8,9},{9,8},{10,11... | collective-permute-start | bytes 417800 | tf_op jit(solution)/shard_map/ppermute | solution.py:115
  92.5 38.2 %collective-permute-start.4 = (bf16[512,128]{1,0:T(8,128)(2,1)S(1)}, bf16[512,128]{1,0:T(8,128)(2,1)S(1)}, u32[]{:S(2)}, u32[]{:S(2)}) collective-permute-start(bf16[512,128]{1,0:T(8,128)(2,1)S(1)} %bitcast.42), channel_id=1, source_target_pairs={{0,24},{4,28},{8,0},{12,4},{16,8},{20,12},{24,16},{28,20},{1,25},{... | collective-permute-start | bytes 393224 | tf_op jit(solution)/shard_map/ppermute | solution.py:11
  99.9 7.5 %collective-permute-start.9 = (f32[136,256]{1,0:T(8,128)S(1)}, f32[136,256]{1,0:T(8,128)S(1)}, u32[]{:S(2)}, u32[]{:S(2)}) collective-permute-start(f32[136,256]{1,0:T(8,128)S(1)} %fusion.6), channel_id=1, source_target_pairs={{0,2},{1,3},{2,0},{3,1},{4,6},{5,7},{6,4},{7,5},{8,10},{9,11},{10,... | collective-permute-start | bytes 417800 | tf_op jit(solution)/shard_map/ppermute | solution.py:115
  103.2 27.5 %collective-permute-start.5 = (bf16[512,128]{1,0:T(8,128)(2,1)S(1)}, bf16[512,128]{1,0:T(8,128)(2,1)S(1)}, u32[]{:S(2)}, u32[]{:S(2)}) collective-permute-start(bf16[512,128]{1,0:T(8,128)(2,1)S(1)} %bitcast.43), channel_id=1, source_target_pairs={{0,8},{4,12},{8,16},{12,20},{16,24},{20,28},{24,0},{28,4},{1,9},{5... | collective-permute-start | bytes 393224 | tf_op jit(solution)/shard_map/ppermute | solution.py:11
  107.4 13.9 %collective-permute-start.10 = (f32[136,256]{1,0:T(8,128)S(1)}, f32[136,256]{1,0:T(8,128)S(1)}, u32[]{:S(2)}, u32[]{:S(2)}) collective-permute-start(f32[136,256]{1,0:T(8,128)S(1)} %add.52), channel_id=1, source_target_pairs={{0,4},{1,5},{2,6},{3,7},{4,0},{5,1},{6,2},{7,3},{8,12},{9,13},{10,... | collective-permute-start | bytes 417800 | tf_op jit(solution)/shard_map/ppermute | solution.py:115
  111.6 19.1 %collective-permute-start.6 = (bf16[512,128]{1,0:T(8,128)(2,1)S(1)}, bf16[512,128]{1,0:T(8,128)(2,1)S(1)}, u32[]{:S(2)}, u32[]{:S(2)}) collective-permute-start(bf16[512,128]{1,0:T(8,128)(2,1)S(1)} %bitcast.44), channel_id=1, source_target_pairs={{0,28},{4,0},{8,4},{12,8},{16,12},{20,16},{24,20},{28,24},{1,29},{... | collective-permute-start | bytes 393224 | tf_op jit(solution)/shard_map/ppermute | solution.py:11
  121.3 6.7 %collective-permute-start.11 = (f32[136,256]{1,0:T(8,128)S(1)}, f32[136,256]{1,0:T(8,128)S(1)}, u32[]{:S(2)}, u32[]{:S(2)}) collective-permute-start(f32[136,256]{1,0:T(8,128)S(1)} %add.53), channel_id=1, source_target_pairs={{0,8},{1,9},{2,10},{3,11},{4,12},{5,13},{6,14},{7,15},{8,0},{9,1},... | collective-permute-start | bytes 417800 | tf_op jit(solution)/shard_map/ppermute | solution.py:115
  122.5 8.2 %collective-permute-start.7 = (bf16[512,128]{1,0:T(8,128)(2,1)S(1)}, bf16[512,128]{1,0:T(8,128)(2,1)S(1)}, u32[]{:S(2)}, u32[]{:S(2)}) collective-permute-start(bf16[512,128]{1,0:T(8,128)(2,1)S(1)} %bitcast.45), channel_id=1, source_target_pairs={{0,4},{4,8},{8,12},{12,16},{16,20},{20,24},{24,28},{28,0},{1,5},{5... | collective-permute-start | bytes 393224 | tf_op jit(solution)/shard_map/ppermute | solution.py:11
  128.1 10.0 %collective-permute-start.12 = (f32[136,256]{1,0:T(8,128)S(1)}, f32[136,256]{1,0:T(8,128)S(1)}, u32[]{:S(2)}, u32[]{:S(2)}) collective-permute-start(f32[136,256]{1,0:T(8,128)S(1)} %add.54), channel_id=1, source_target_pairs={{0,16},{1,17},{2,18},{3,19},{4,20},{5,21},{6,22},{7,23},{8,24},{9,... | collective-permute-start | bytes 417800 | tf_op jit(solution)/shard_map/ppermute | solution.py:115
Sparse Core Ops, SparseCore 0:
  49.2 23.9 reduce-scatter.1

commit v4 on v2

--- a/solution.py
+++ b/solution.py
@@ -124,11 +124,15 @@
         for k in range(offset_count)
     ]
     source_tiles = jnp.stack(fetched).reshape(offset_count * own_tiles, tile_size, features)
+    col_index = lax.axis_index("col")
+    rows_here = (tile_rows - col_index * own_tiles) % block_tiles
     block_sums = tile_products(
-        tile_rows, tile_cols, counts, adjacency, source_tiles, block_tiles, own_tiles, True
+        rows_here, tile_cols, counts, adjacency, source_tiles, block_tiles, own_tiles, True
     )
-    block_sums = block_sums.reshape(block_tiles * tile_size, features)
-    sums = lax.psum_scatter(block_sums, "col", scatter_dimension=0, tiled=True)
+    pieces = block_sums.reshape(col_count, own_rows, features)
+    sums = pieces[0]
+    for shift in range(1, col_count):
+        sums = sums + from_behind(pieces[shift], "col", shift)
     aggregated = (row_scale[:, None] * sums).astype(jnp.bfloat16)
     pre_act = jnp.dot(aggregated, weight, preferred_element_type=jnp.float32) + bias_vector
     gate_value = jax.nn.sigmoid(pre_act)

time: 138 us -> 113 us (0.82)
  the two profiles are of different devices: /device:TPU:7 before, /device:TPU:3 now
where the time goes in v4:
time: 113 us; the launch traced here: 112 us
  Pallas kernels  38.9 us (34%)
  waiting for transfers between devices  29.6 us (26%)
  starting transfers between devices  21.4 us (19%)
  other arithmetic  7.92 us (7%)
  blocking collectives  7.26 us (6%)
  local copies, waits for them, and re-layouts  5.01 us (4%)
  matrix products  1.57 us (1%)
    pallas_call x2, Pallas kernels, tile_products(): pl.pallas_call(kernel, grid_spec=pltpu.PrefetchScalarGridSpec(num_scalar_...  38.9 us
    ppermute x11, waiting for transfers between devices, from_behind(): lax.ppermute(value, axis, [(i, (i + by) % length) for i in range(length)])  18.5 us
    ppermute x11, starting transfers between devices, from_behind(): lax.ppermute(value, axis, [(i, (i + by) % length) for i in range(length)])  14.4 us
    ppermute x5, waiting for transfers between devices, all_sum(): lax.ppermute(value, axes, [(i, i ^ bit) for i in range(size)])  11 us
    all_gather x1, blocking collectives, local(): block_grad = lax.all_gather(grad_hidden, 'col', axis=0, tiled=True)  7.26 us
    ppermute x5, starting transfers between devices, all_sum(): lax.ppermute(value, axes, [(i, i ^ bit) for i in range(size)])  7.02 us
  transfers between devices with their start and end apart: 16, of which 7 were waited for; matrix products, arithmetic and copies ran while one was open for 7% of the time, Pallas kernels for 17%

profile of v4, /device:TPU:3, one launch (start us, length us, event | category | flops | bytes accessed | tf_op | source)
XLA Modules:
  0.0 112.5 jit_solution(14323255222315629655)
XLA Ops:
  0.6 0.0 copy-start
  0.6 0.7 convert_rsqrt_fusion
  1.4 1.0 multiply_convert_fusion.1
  2.4 0.1 collective-permute-start.2
  2.5 3.6 %collective-permute-start.3 = (bf16[512,128]{1,0:T(8,128)(2,1)S(1)}, bf16[512,128]{1,0:T(8,128)(2,1)S(1)}, u32[]{:S(2)}, u32[]{:S(2)}) collective-permute-start(bf16[512,128]{1,0:T(8,128)(2,1)S(1)} %multiply_convert_fusion.1), channel_id=1, source_target_pairs={{0,24},{4,28},{8,0},{12,4},{16,8},{20,12},{24,16},{28,20},{1,25},{... | collective-permute-start | bytes 393224 | tf_op jit(solution)/shard_map/ppermute | solution.py:11
  6.0 2.1 %collective-permute-start.1 = (bf16[512,128]{1,0:T(8,128)(2,1)S(1)}, bf16[512,128]{1,0:T(8,128)(2,1)S(1)}, u32[]{:S(2)}, u32[]{:S(2)}) collective-permute-start(bf16[512,128]{1,0:T(8,128)(2,1)S(1)} %multiply_convert_fusion.1), channel_id=1, source_target_pairs={{0,4},{4,8},{8,12},{12,16},{16,20},{20,24},{24,28},{28,0},{1,5},{5... | collective-permute-start | bytes 393224 | tf_op jit(solution)/shard_map/ppermute | solution.py:11
  8.1 0.0 collective-permute-start
  8.2 1.3 %add_select_fusion.rows_ref = s32[360]{0:T(512)} fusion(s32[360]{0:T(512)} %rows_ref.1, s32[]{:T(128)S(6)} %mul.57), kind=kLoop, calls=%fused_computation.28 | loop fusion | flops 4320 | bytes 2884 | tf_op jit(solution)/shard_map/jit(remainder)/select_n | solution.py:128
  9.4 5.6 %collective-permute-done = bf16[512,128]{1,0:T(8,128)(2,1)S(1)} collective-permute-done((bf16[512,128]{1,0:T(8,128)(2,1)S(1)}, bf16[512,128]{1,0:T(8,128)(2,1)S(1)}, u32[]{:S(2)}, u32[]{:S(2)}) %collective-permute-start) | collective-permute-done | bytes 131104 | tf_op jit(solution)/shard_map/ppermute | solution.py:11
  15.0 0.0 collective-permute-done.1
  15.0 1.1 bitcast_dynamic-update-slice_fusion.2
  16.1 0.0 collective-permute-done.2
  16.1 0.0 collective-permute-done.3
  16.2 0.0 copy-start.1
  16.2 0.8 copy-done.1
  17.0 19.5 %shard_map.120 = f32[16,128,128]{2,1,0:T(8,128)} custom-call(s32[360]{0:T(512)} %add_select_fusion.rows_ref, s32[360]{0:T(512)} %cols_ref.3, s32[5]{0:T(128)} %counts_ref.3, bf16[360,128,128]{2,1,0:T(8,128)(2,1)} %adj_ref.3, bf16[20,128,128]{2,1,0:T(8,128)(2,1)} %bitcast.55), custom_call_target="tpu_custom_call" | custom-call | flops 1509949440 | bytes 13500416 | tf_op jit(solution)/shard_map/pallas_call | solution.py:76
  36.5 1.3 %fusion.16 = (f32[4,128,128]{2,1,0:T(8,128)S(1)}, f32[4,128,128]{2,1,0:T(8,128)S(1)}, f32[4,128,128]{2,1,0:T(8,128)S(1)}, f32[4,128,128]{2,1,0:T(8,128)S(1)}) fusion(f32[16,128,128]{2,1,0:T(8,128)} %shard_map.120), kind=kLoop, calls=%fused_computation.37 | loop fusion | bytes 2097152 | tf_op jit(solution)/shard_map/slice | solution.py:133
  37.8 0.1 collective-permute-start.6
  37.9 1.8 %collective-permute-start.5 = (f32[512,128]{1,0:T(8,128)S(1)}, f32[512,128]{1,0:T(8,128)S(1)}, u32[]{:S(2)}, u32[]{:S(2)}) collective-permute-start(f32[512,128]{1,0:T(8,128)S(1)} %bitcast.57), channel_id=1, source_target_pairs={{0,2},{1,3},{2,0},{3,1},{4,6},{5,7},{6,4},{7,5},{8,10},{9,11},{10,... | collective-permute-start | bytes 786440 | tf_op jit(solution)/shard_map/ppermute | solution.py:11
  39.7 0.0 collective-permute-start.4
  39.8 0.1 pad.2.clone
  39.9 6.9 %collective-permute-done.6 = f32[512,128]{1,0:T(8,128)S(1)} collective-permute-done((f32[512,128]{1,0:T(8,128)S(1)}, f32[512,128]{1,0:T(8,128)S(1)}, u32[]{:S(2)}, u32[]{:S(2)}) %collective-permute-start.6) | collective-permute-done | bytes 262176 | tf_op jit(solution)/shard_map/ppermute | solution.py:11
  46.8 0.0 collective-permute-done.5
  46.8 2.8 %collective-permute-done.4 = f32[512,128]{1,0:T(8,128)S(1)} collective-permute-done((f32[512,128]{1,0:T(8,128)S(1)}, f32[512,128]{1,0:T(8,128)S(1)}, u32[]{:S(2)}, u32[]{:S(2)}) %collective-permute-start.4) | collective-permute-done | bytes 262176 | tf_op jit(solution)/shard_map/ppermute | solution.py:11
  49.6 0.1 fusion.9
  49.7 0.0 copy-done
  49.7 0.0 copy-done.2
  49.7 0.0 copy-done.3
  49.7 1.1 fusion.15
  50.9 0.2 fusion.10
  51.1 0.2 fusion
  51.3 0.1 maximum_maximum_fusion
  51.4 3.1 %collective-permute-start.11 = (f32[136,256]{1,0:T(8,128)S(1)}, f32[136,256]{1,0:T(8,128)S(1)}, u32[]{:S(2)}, u32[]{:S(2)}) collective-permute-start(f32[136,256]{1,0:T(8,128)S(1)} %maximum_maximum_fusion), channel_id=1, source_target_pairs={{0,1},{1,0},{2,3},{3,2},{4,5},{5,4},{6,7},{7,6},{8,9},{9,8},{10,11... | collective-permute-start | bytes 417800 | tf_op jit(solution)/shard_map/ppermute | solution.py:104
  54.5 7.3 %all_gather.3 = bf16[2048,128]{1,0:T(8,128)(2,1)S(1)} all-gather(bf16[512,128]{1,0:T(8,128)(2,1)S(1)} %fusion), channel_id=1, replica_groups=mesh['blk'=8,'col'=4] {'col'}, dimensions={0}, use_global_device_ids=true | all-gather | bytes 655360 | tf_op jit(solution)/shard_map/all_gather | solution.py:157
  61.8 1.0 copy.13
  62.8 0.0 collective-permute-done.11
  62.8 0.1 fusion.14
  62.9 0.1 collective-permute-start.12
  63.0 19.5 %shard_map.121 = f32[20,128,128]{2,1,0:T(8,128)} custom-call(s32[360]{0:T(512)} %rows_ref.1, s32[360]{0:T(512)} %cols_ref.3, s32[5]{0:T(128)} %counts_ref.3, bf16[360,128,128]{2,1,0:T(8,128)(2,1)} %adj_ref.3, bf16[16,128,128]{2,1,0:T(8,128)(2,1)} %bitcast.53), custom_call_target="tpu_custom_call" | custom-call | flops 1509949440 | bytes 13631488 | tf_op jit(solution)/shard_map/pallas_call | solution.py:76
  82.5 0.0 collective-permute-done.12
  82.5 2.3 %collective-permute-start.13 = (f32[136,256]{1,0:T(8,128)S(1)}, f32[136,256]{1,0:T(8,128)S(1)}, u32[]{:S(2)}, u32[]{:S(2)}) collective-permute-start(f32[136,256]{1,0:T(8,128)S(1)} %add.69), channel_id=1, source_target_pairs={{0,4},{1,5},{2,6},{3,7},{4,0},{5,1},{6,2},{7,3},{8,12},{9,13},{10,... | collective-permute-start | bytes 417800 | tf_op jit(solution)/shard_map/ppermute | solution.py:104
  84.8 1.4 %bitcast_convert_fusion = bf16[20,128,128]{1,2,0:T(8,128)(2,1)S(1)} fusion(f32[20,128,128]{2,1,0:T(8,128)} %shard_map.121), kind=kLoop, calls=%fused_computation.34 | loop fusion | flops 327680 | bytes 1966080 | tf_op jit(solution)/shard_map/convert.3
  86.2 1.0 collective-permute-done.13
  87.2 1.2 %collective-permute-start.14 = (f32[136,256]{1,0:T(8,128)S(1)}, f32[136,256]{1,0:T(8,128)S(1)}, u32[]{:S(2)}, u32[]{:S(2)}) collective-permute-start(f32[136,256]{1,0:T(8,128)S(1)} %add.70), channel_id=1, source_target_pairs={{0,8},{1,9},{2,10},{3,11},{4,12},{5,13},{6,14},{7,15},{8,0},{9,1},... | collective-permute-start | bytes 417800 | tf_op jit(solution)/shard_map/ppermute | solution.py:104
  88.5 0.1 copy.15
  88.6 0.1 copy.18
  88.7 0.1 copy.17
  88.9 0.1 copy.16
  89.0 2.3 %collective-permute-start.8 = (bf16[512,128]{1,0:T(8,128)(2,1)S(1)}, bf16[512,128]{1,0:T(8,128)(2,1)S(1)}, u32[]{:S(2)}, u32[]{:S(2)}) collective-permute-start(bf16[512,128]{1,0:T(8,128)(2,1)S(1)} %bitcast.62), channel_id=1, source_target_pairs={{0,28},{4,0},{8,4},{12,8},{16,12},{20,16},{24,20},{28,24},{1,29},{... | collective-permute-start | bytes 393224 | tf_op jit(solution)/shard_map/ppermute | solution.py:11
  91.3 0.2 collective-permute-start.9
  91.4 0.4 collective-permute-start.10
  91.8 3.9 %collective-permute-start.7 = (bf16[512,128]{1,0:T(8,128)(2,1)S(1)}, bf16[512,128]{1,0:T(8,128)(2,1)S(1)}, u32[]{:S(2)}, u32[]{:S(2)}) collective-permute-start(bf16[512,128]{1,0:T(8,128)(2,1)S(1)} %bitcast.59), channel_id=1, source_target_pairs={{0,24},{4,28},{8,0},{12,4},{16,8},{20,12},{24,16},{28,20},{1,25},{... | collective-permute-start | bytes 393224 | tf_op jit(solution)/shard_map/ppermute | solution.py:11
  95.7 1.0 slice.61
  96.7 0.1 copy.14
  96.8 0.0 collective-permute-done.14
  96.8 0.3 collective-permute-start.15
  97.2 0.0 collective-permute-done.8
  97.2 0.9 collective-permute-done.9
  98.1 2.3 %collective-permute-done.10 = bf16[512,128]{1,0:T(8,128)(2,1)S(1)} collective-permute-done((bf16[512,128]{1,0:T(8,128)(2,1)S(1)}, bf16[512,128]{1,0:T(8,128)(2,1)S(1)}, u32[]{:S(2)}, u32[]{:S(2)}) %collective-permute-start.10) | collective-permute-done | bytes 131104 | tf_op jit(solution)/shard_map/ppermute | solution.py:11
  100.4 0.0 collective-permute-done.7
  100.4 0.8 fusion.5
  101.2 10.0 %collective-permute-done.15 = f32[136,256]{1,0:T(8,128)S(1)} collective-permute-done((f32[136,256]{1,0:T(8,128)S(1)}, f32[136,256]{1,0:T(8,128)S(1)}, u32[]{:S(2)}, u32[]{:S(2)}) %collective-permute-start.15) | collective-permute-done | bytes 139296 | tf_op jit(solution)/shard_map/ppermute | solution.py:104
  111.3 0.6 slice_multiply_fusion.1
  111.8 0.7 slice_multiply_fusion
  (12 shorter events, 0.2 us)
Async XLA Ops:
  0.6 49.1 %copy-start = (bf16[128,256]{1,0:T(8,128)(2,1)S(1)}, bf16[128,256]{1,0:T(8,128)(2,1)}, u32[]{:S(2)}) copy-start(bf16[128,256]{1,0:T(8,128)(2,1)} %param.15) | copy-start | bytes 196612
  2.4 13.7 %collective-permute-start.2 = (bf16[512,128]{1,0:T(8,128)(2,1)S(1)}, bf16[512,128]{1,0:T(8,128)(2,1)S(1)}, u32[]{:S(2)}, u32[]{:S(2)}) collective-permute-start(bf16[512,128]{1,0:T(8,128)(2,1)S(1)} %multiply_convert_fusion.1), channel_id=1, source_target_pairs={{0,28},{4,0},{8,4},{12,8},{16,12},{20,16},{24,20},{28,24},{1,29},{... | collective-permute-start | bytes 393224 | tf_op jit(solution)/shard_map/ppermute | solution.py:11
  2.5 13.7 %collective-permute-start.3 = (bf16[512,128]{1,0:T(8,128)(2,1)S(1)}, bf16[512,128]{1,0:T(8,128)(2,1)S(1)}, u32[]{:S(2)}, u32[]{:S(2)}) collective-permute-start(bf16[512,128]{1,0:T(8,128)(2,1)S(1)} %multiply_convert_fusion.1), channel_id=1, source_target_pairs={{0,24},{4,28},{8,0},{12,4},{16,8},{20,12},{24,16},{28,20},{1,25},{... | collective-permute-start | bytes 393224 | tf_op jit(solution)/shard_map/ppermute | solution.py:11
  6.0 9.0 %collective-permute-start.1 = (bf16[512,128]{1,0:T(8,128)(2,1)S(1)}, bf16[512,128]{1,0:T(8,128)(2,1)S(1)}, u32[]{:S(2)}, u32[]{:S(2)}) collective-permute-start(bf16[512,128]{1,0:T(8,128)(2,1)S(1)} %multiply_convert_fusion.1), channel_id=1, source_target_pairs={{0,4},{4,8},{8,12},{12,16},{16,20},{20,24},{24,28},{28,0},{1,5},{5... | collective-permute-start | bytes 393224 | tf_op jit(solution)/shard_map/ppermute | solution.py:11
  8.1 6.8 %collective-permute-start = (bf16[512,128]{1,0:T(8,128)(2,1)S(1)}, bf16[512,128]{1,0:T(8,128)(2,1)S(1)}, u32[]{:S(2)}, u32[]{:S(2)}) collective-permute-start(bf16[512,128]{1,0:T(8,128)(2,1)S(1)} %multiply_convert_fusion.1), channel_id=1, source_target_pairs={{0,8},{4,12},{8,16},{12,20},{16,24},{20,28},{24,0},{28,4},{1,9},{5... | collective-permute-start | bytes 393224 | tf_op jit(solution)/shard_map/ppermute | solution.py:11
  16.2 0.9 copy-start.1
  36.5 13.2 %copy-start.2 = (bf16[512,256]{1,0:T(8,128)(2,1)S(1)}, bf16[512,256]{1,0:T(8,128)(2,1)}, u32[]{:S(2)}) copy-start(bf16[512,256]{1,0:T(8,128)(2,1)} %param.17) | copy-start | bytes 786436
  36.5 13.2 %copy-start.3 = (f32[256]{0:T(256)S(1)}, f32[256]{0:T(256)}, u32[]{:S(2)}) copy-start(f32[256]{0:T(256)} %param.16) | copy-start | bytes 3076
  37.8 9.0 %collective-permute-start.6 = (f32[512,128]{1,0:T(8,128)S(1)}, f32[512,128]{1,0:T(8,128)S(1)}, u32[]{:S(2)}, u32[]{:S(2)}) collective-permute-start(f32[512,128]{1,0:T(8,128)S(1)} %bitcast.58), channel_id=1, source_target_pairs={{0,3},{1,0},{2,1},{3,2},{4,7},{5,4},{6,5},{7,6},{8,11},{9,8},{10,9... | collective-permute-start | bytes 786440 | tf_op jit(solution)/shard_map/ppermute | solution.py:11
  37.9 8.9 %collective-permute-start.5 = (f32[512,128]{1,0:T(8,128)S(1)}, f32[512,128]{1,0:T(8,128)S(1)}, u32[]{:S(2)}, u32[]{:S(2)}) collective-permute-start(f32[512,128]{1,0:T(8,128)S(1)} %bitcast.57), channel_id=1, source_target_pairs={{0,2},{1,3},{2,0},{3,1},{4,6},{5,7},{6,4},{7,5},{8,10},{9,11},{10,... | collective-permute-start | bytes 786440 | tf_op jit(solution)/shard_map/ppermute | solution.py:11
  39.7 9.8 %collective-permute-start.4 = (f32[512,128]{1,0:T(8,128)S(1)}, f32[512,128]{1,0:T(8,128)S(1)}, u32[]{:S(2)}, u32[]{:S(2)}) collective-permute-start(f32[512,128]{1,0:T(8,128)S(1)} %bitcast.56), channel_id=1, source_target_pairs={{0,1},{1,2},{2,3},{3,0},{4,5},{5,6},{6,7},{7,4},{8,9},{9,10},{10,1... | collective-permute-start | bytes 786440 | tf_op jit(solution)/shard_map/ppermute | solution.py:11
  51.4 11.4 %collective-permute-start.11 = (f32[136,256]{1,0:T(8,128)S(1)}, f32[136,256]{1,0:T(8,128)S(1)}, u32[]{:S(2)}, u32[]{:S(2)}) collective-permute-start(f32[136,256]{1,0:T(8,128)S(1)} %maximum_maximum_fusion), channel_id=1, source_target_pairs={{0,1},{1,0},{2,3},{3,2},{4,5},{5,4},{6,7},{7,6},{8,9},{9,8},{10,11... | collective-permute-start | bytes 417800 | tf_op jit(solution)/shard_map/ppermute | solution.py:104
  62.9 19.5 %collective-permute-start.12 = (f32[136,256]{1,0:T(8,128)S(1)}, f32[136,256]{1,0:T(8,128)S(1)}, u32[]{:S(2)}, u32[]{:S(2)}) collective-permute-start(f32[136,256]{1,0:T(8,128)S(1)} %fusion.14), channel_id=1, source_target_pairs={{0,2},{1,3},{2,0},{3,1},{4,6},{5,7},{6,4},{7,5},{8,10},{9,11},{10,... | collective-permute-start | bytes 417800 | tf_op jit(solution)/shard_map/ppermute | solution.py:104
  82.5 4.7 %collective-permute-start.13 = (f32[136,256]{1,0:T(8,128)S(1)}, f32[136,256]{1,0:T(8,128)S(1)}, u32[]{:S(2)}, u32[]{:S(2)}) collective-permute-start(f32[136,256]{1,0:T(8,128)S(1)} %add.69), channel_id=1, source_target_pairs={{0,4},{1,5},{2,6},{3,7},{4,0},{5,1},{6,2},{7,3},{8,12},{9,13},{10,... | collective-permute-start | bytes 417800 | tf_op jit(solution)/shard_map/ppermute | solution.py:104
  87.2 9.6 %collective-permute-start.14 = (f32[136,256]{1,0:T(8,128)S(1)}, f32[136,256]{1,0:T(8,128)S(1)}, u32[]{:S(2)}, u32[]{:S(2)}) collective-permute-start(f32[136,256]{1,0:T(8,128)S(1)} %add.70), channel_id=1, source_target_pairs={{0,8},{1,9},{2,10},{3,11},{4,12},{5,13},{6,14},{7,15},{8,0},{9,1},... | collective-permute-start | bytes 417800 | tf_op jit(solution)/shard_map/ppermute | solution.py:104
  89.0 8.2 %collective-permute-start.8 = (bf16[512,128]{1,0:T(8,128)(2,1)S(1)}, bf16[512,128]{1,0:T(8,128)(2,1)S(1)}, u32[]{:S(2)}, u32[]{:S(2)}) collective-permute-start(bf16[512,128]{1,0:T(8,128)(2,1)S(1)} %bitcast.62), channel_id=1, source_target_pairs={{0,28},{4,0},{8,4},{12,8},{16,12},{20,16},{24,20},{28,24},{1,29},{... | collective-permute-start | bytes 393224 | tf_op jit(solution)/shard_map/ppermute | solution.py:11
  91.3 6.9 %collective-permute-start.9 = (bf16[512,128]{1,0:T(8,128)(2,1)S(1)}, bf16[512,128]{1,0:T(8,128)(2,1)S(1)}, u32[]{:S(2)}, u32[]{:S(2)}) collective-permute-start(bf16[512,128]{1,0:T(8,128)(2,1)S(1)} %bitcast.61), channel_id=1, source_target_pairs={{0,4},{4,8},{8,12},{12,16},{16,20},{20,24},{24,28},{28,0},{1,5},{5... | collective-permute-start | bytes 393224 | tf_op jit(solution)/shard_map/ppermute | solution.py:11
  91.4 9.0 %collective-permute-start.10 = (bf16[512,128]{1,0:T(8,128)(2,1)S(1)}, bf16[512,128]{1,0:T(8,128)(2,1)S(1)}, u32[]{:S(2)}, u32[]{:S(2)}) collective-permute-start(bf16[512,128]{1,0:T(8,128)(2,1)S(1)} %bitcast.60), channel_id=1, source_target_pairs={{0,8},{4,12},{8,16},{12,20},{16,24},{20,28},{24,0},{28,4},{1,9},{5... | collective-permute-start | bytes 393224 | tf_op jit(solution)/shard_map/ppermute | solution.py:11
  91.8 8.6 %collective-permute-start.7 = (bf16[512,128]{1,0:T(8,128)(2,1)S(1)}, bf16[512,128]{1,0:T(8,128)(2,1)S(1)}, u32[]{:S(2)}, u32[]{:S(2)}) collective-permute-start(bf16[512,128]{1,0:T(8,128)(2,1)S(1)} %bitcast.59), channel_id=1, source_target_pairs={{0,24},{4,28},{8,0},{12,4},{16,8},{20,12},{24,16},{28,20},{1,25},{... | collective-permute-start | bytes 393224 | tf_op jit(solution)/shard_map/ppermute | solution.py:11
  96.8 14.4 %collective-permute-start.15 = (f32[136,256]{1,0:T(8,128)S(1)}, f32[136,256]{1,0:T(8,128)S(1)}, u32[]{:S(2)}, u32[]{:S(2)}) collective-permute-start(f32[136,256]{1,0:T(8,128)S(1)} %add.71), channel_id=1, source_target_pairs={{0,16},{1,17},{2,18},{3,19},{4,20},{5,21},{6,22},{7,23},{8,24},{9,... | collective-permute-start | bytes 417800 | tf_op jit(solution)/shard_map/ppermute | solution.py:104

commit v5 on v4

--- a/solution.py
+++ b/solution.py
@@ -93,16 +93,38 @@
     )(rows, cols, counts, adjacency, operand)
 
 
+def radix_split(size, limit=8):
+    radices = []
+    while size > 1:
+        radix = max(r for r in range(2, limit + 1) if size % r == 0)
+        radices.append(radix)
+        size //= radix
+    return radices
+
+
 def all_sum(value, axes):
+    sizes = [lax.axis_size(axis) for axis in axes]
     size = 1
-    for axis in axes:
-        size *= lax.axis_size(axis)
-    if size & (size - 1):
-        return lax.psum(value, axes)
-    bit = 1
-    while bit < size:
-        value = value + lax.ppermute(value, axes, [(i, i ^ bit) for i in range(size)])
-        bit *= 2
+    index = 0
+    for axis, axis_size in zip(axes, sizes):
+        size *= axis_size
+        index = index * axis_size + lax.axis_index(axis)
+    stride = 1
+    for radix in radix_split(size)[::-1]:
+        digit = (index // stride) % radix
+        parts = [value]
+        for shift in range(1, radix):
+            pairs = []
+            for i in range(size):
+                d = (i // stride) % radix
+                pairs.append((i, i + (((d + shift) % radix) - d) * stride))
+            parts.append(lax.ppermute(value, axes, pairs))
+        stacked = jnp.stack(parts)
+        ordered = jnp.take(stacked, (digit - jnp.arange(radix)) % radix, axis=0)
+        value = ordered[0]
+        for j in range(1, radix):
+            value = value + ordered[j]
+        stride *= radix
     return value
 
 

time: 113 us -> 132 us (1.17)
  the two profiles are of different devices: /device:TPU:3 before, /device:TPU:14 now
where the time goes in v5:
time: 132 us; the launch traced here: 131 us
  waiting for transfers between devices  39.6 us (30%)
  Pallas kernels  36.3 us (27%)
  starting transfers between devices  26.9 us (20%)
  blocking collectives  10.9 us (8%)
  other arithmetic  8.23 us (6%)
  local copies, waits for them, and re-layouts  6.86 us (5%)
  matrix products  1.57 us (1%)
    pallas_call x2, Pallas kernels, tile_products(): pl.pallas_call(kernel, grid_spec=pltpu.PrefetchScalarGridSpec(num_scalar_...  36.3 us
    ppermute x11, waiting for transfers between devices, from_behind(): lax.ppermute(value, axis, [(i, (i + by) % length) for i in range(length)])  21.7 us
    ppermute x10, waiting for transfers between devices, all_sum(): parts.append(lax.ppermute(value, axes, pairs))  17.9 us
    ppermute x10, starting transfers between devices, all_sum(): parts.append(lax.ppermute(value, axes, pairs))  16.1 us
    all_gather x1, blocking collectives, local(): block_grad = lax.all_gather(grad_hidden, 'col', axis=0, tiled=True)  10.9 us
    ppermute x11, starting transfers between devices, from_behind(): lax.ppermute(value, axis, [(i, (i + by) % length) for i in range(length)])  10.9 us
  transfers between devices with their start and end apart: 21, of which 13 were waited for; matrix products, arithmetic and copies ran while one was open for 7% of the time, Pallas kernels for 14%

profile of v5, /device:TPU:14, one launch (start us, length us, event | category | flops | bytes accessed | tf_op | source)
XLA Modules:
  0.0 131.4 jit_solution(17153183470187013483)
XLA Ops:
  0.6 0.7 convert_rsqrt_fusion
  1.4 1.0 multiply_convert_fusion.1
  2.4 1.6 %collective-permute-start = (bf16[512,128]{1,0:T(8,128)(2,1)S(1)}, bf16[512,128]{1,0:T(8,128)(2,1)S(1)}, u32[]{:S(2)}, u32[]{:S(2)}) collective-permute-start(bf16[512,128]{1,0:T(8,128)(2,1)S(1)} %multiply_convert_fusion.1), channel_id=1, source_target_pairs={{0,8},{4,12},{8,16},{12,20},{16,24},{20,28},{24,0},{28,4},{1,9},{5... | collective-permute-start | bytes 393224 | tf_op jit(solution)/shard_map/ppermute | solution.py:11
  4.0 1.5 %collective-permute-start.1 = (bf16[512,128]{1,0:T(8,128)(2,1)S(1)}, bf16[512,128]{1,0:T(8,128)(2,1)S(1)}, u32[]{:S(2)}, u32[]{:S(2)}) collective-permute-start(bf16[512,128]{1,0:T(8,128)(2,1)S(1)} %multiply_convert_fusion.1), channel_id=1, source_target_pairs={{0,4},{4,8},{8,12},{12,16},{16,20},{20,24},{24,28},{28,0},{1,5},{5... | collective-permute-start | bytes 393224 | tf_op jit(solution)/shard_map/ppermute | solution.py:11
  5.6 0.5 collective-permute-start.2
  6.1 0.4 collective-permute-start.3
  6.5 1.3 add_select_fusion.rows_ref
  7.9 1.0 collective-permute-done
  8.8 1.9 %collective-permute-done.1 = bf16[512,128]{1,0:T(8,128)(2,1)S(1)} collective-permute-done((bf16[512,128]{1,0:T(8,128)(2,1)S(1)}, bf16[512,128]{1,0:T(8,128)(2,1)S(1)}, u32[]{:S(2)}, u32[]{:S(2)}) %collective-permute-start.1) | collective-permute-done | bytes 131104 | tf_op jit(solution)/shard_map/ppermute | solution.py:11
  10.8 1.1 bitcast_dynamic-update-slice_fusion.9
  11.9 1.0 collective-permute-done.2
  12.9 1.3 collective-permute-done.3
  14.2 0.8 copy-done.1
  15.0 18.2 %shard_map.120 = f32[16,128,128]{2,1,0:T(8,128)} custom-call(s32[360]{0:T(512)} %add_select_fusion.rows_ref, s32[360]{0:T(512)} %cols_ref.3, s32[5]{0:T(128)} %counts_ref.3, bf16[360,128,128]{2,1,0:T(8,128)(2,1)} %adj_ref.3, bf16[20,128,128]{2,1,0:T(8,128)(2,1)} %bitcast.81), custom_call_target="tpu_custom_call" | custom-call | flops 1509949440 | bytes 13500416 | tf_op jit(solution)/shard_map/pallas_call | solution.py:76
  33.2 1.3 fusion.23
  34.5 0.1 collective-permute-start.6
  34.6 0.6 collective-permute-start.5
  35.1 0.2 collective-permute-start.4
  35.3 0.1 pad.6.clone
  35.4 5.8 %collective-permute-done.6 = f32[512,128]{1,0:T(8,128)S(1)} collective-permute-done((f32[512,128]{1,0:T(8,128)S(1)}, f32[512,128]{1,0:T(8,128)S(1)}, u32[]{:S(2)}, u32[]{:S(2)}) %collective-permute-start.6) | collective-permute-done | bytes 262176 | tf_op jit(solution)/shard_map/ppermute | solution.py:11
  41.2 5.6 %collective-permute-done.5 = f32[512,128]{1,0:T(8,128)S(1)} collective-permute-done((f32[512,128]{1,0:T(8,128)S(1)}, f32[512,128]{1,0:T(8,128)S(1)}, u32[]{:S(2)}, u32[]{:S(2)}) %collective-permute-start.5) | collective-permute-done | bytes 262176 | tf_op jit(solution)/shard_map/ppermute | solution.py:11
  46.8 1.0 collective-permute-done.4
  47.8 0.1 fusion.9
  48.0 1.1 fusion.22
  49.1 0.2 fusion
  49.4 0.2 fusion.11
  49.6 0.1 fusion.21
  49.7 0.1 collective-permute-start.13
  49.7 1.6 %collective-permute-start.12 = (f32[136,256]{1,0:T(8,128)S(1)}, f32[136,256]{1,0:T(8,128)S(1)}, u32[]{:S(2)}, u32[]{:S(2)}) collective-permute-start(f32[136,256]{1,0:T(8,128)S(1)} %get-tuple-element.18), channel_id=1, source_target_pairs={{0,2},{1,3},{2,0},{3,1},{4,6},{5,7},{6,4},{7,5},{8,10},{9,11},{10,... | collective-permute-start | bytes 417800 | tf_op jit(solution)/shard_map/ppermute | solution.py:121
  51.3 0.2 collective-permute-start.11
  51.5 10.9 %all_gather.3 = bf16[2048,128]{1,0:T(8,128)(2,1)S(1)} all-gather(bf16[512,128]{1,0:T(8,128)(2,1)S(1)} %fusion), channel_id=1, replica_groups=mesh['blk'=8,'col'=4] {'col'}, dimensions={0}, use_global_device_ids=true | all-gather | bytes 655360 | tf_op jit(solution)/shard_map/all_gather | solution.py:179
  62.4 1.0 copy.13
  63.4 18.1 %shard_map.121 = f32[20,128,128]{2,1,0:T(8,128)} custom-call(s32[360]{0:T(512)} %rows_ref.1, s32[360]{0:T(512)} %cols_ref.3, s32[5]{0:T(128)} %counts_ref.3, bf16[360,128,128]{2,1,0:T(8,128)(2,1)} %adj_ref.3, bf16[16,128,128]{2,1,0:T(8,128)(2,1)} %bitcast.79), custom_call_target="tpu_custom_call" | custom-call | flops 1509949440 | bytes 13631488 | tf_op jit(solution)/shard_map/pallas_call | solution.py:76
  81.5 1.4 %bitcast_convert_fusion = bf16[20,128,128]{1,2,0:T(8,128)(2,1)S(1)} fusion(f32[20,128,128]{2,1,0:T(8,128)} %shard_map.121), kind=kLoop, calls=%fused_computation.84 | loop fusion | flops 327680 | bytes 1966080 | tf_op jit(solution)/shard_map/convert.3
  83.0 1.0 slice.115
  83.9 0.1 copy.14
  84.1 0.1 copy.18
  84.2 2.3 %collective-permute-start.10 = (bf16[512,128]{1,0:T(8,128)(2,1)S(1)}, bf16[512,128]{1,0:T(8,128)(2,1)S(1)}, u32[]{:S(2)}, u32[]{:S(2)}) collective-permute-start(bf16[512,128]{1,0:T(8,128)(2,1)S(1)} %bitcast.95), channel_id=1, source_target_pairs={{0,8},{4,12},{8,16},{12,20},{16,24},{20,28},{24,0},{28,4},{1,9},{5... | collective-permute-start | bytes 393224 | tf_op jit(solution)/shard_map/ppermute | solution.py:11
  86.5 0.1 copy.17
  86.7 3.5 %collective-permute-start.9 = (bf16[512,128]{1,0:T(8,128)(2,1)S(1)}, bf16[512,128]{1,0:T(8,128)(2,1)S(1)}, u32[]{:S(2)}, u32[]{:S(2)}) collective-permute-start(bf16[512,128]{1,0:T(8,128)(2,1)S(1)} %bitcast.96), channel_id=1, source_target_pairs={{0,4},{4,8},{8,12},{12,16},{16,20},{20,24},{24,28},{28,0},{1,5},{5... | collective-permute-start | bytes 393224 | tf_op jit(solution)/shard_map/ppermute | solution.py:11
  90.2 0.8 copy.16
  90.9 0.1 copy.15
  91.2 0.1 collective-permute-start.7
  91.3 0.6 gather_fusion
  91.9 0.1 broadcast_select_fusion.1
  92.1 2.8 %collective-permute-start.14 = (f32[136,256]{1,0:T(8,128)S(1)}, f32[136,256]{1,0:T(8,128)S(1)}, u32[]{:S(2)}, u32[]{:S(2)}) collective-permute-start(f32[136,256]{1,0:T(8,128)S(1)} %bitcast.85), channel_id=1, source_target_pairs={{0,4},{1,5},{2,6},{3,7},{4,8},{5,9},{6,10},{7,11},{8,12},{9,13},{1... | collective-permute-start | bytes 417800 | tf_op jit(solution)/shard_map/ppermute | solution.py:121
  94.9 3.7 %collective-permute-done.8 = bf16[512,128]{1,0:T(8,128)(2,1)S(1)} collective-permute-done((bf16[512,128]{1,0:T(8,128)(2,1)}, bf16[512,128]{1,0:T(8,128)(2,1)S(1)}, u32[]{:S(2)}, u32[]{:S(2)}) %collective-permute-start.8) | collective-permute-done | bytes 131104 | tf_op jit(solution)/shard_map/ppermute | solution.py:11
  98.6 0.4 collective-permute-done.7
  99.0 0.8 fusion.5
  99.8 2.0 %collective-permute-start.15 = (f32[136,256]{1,0:T(8,128)S(1)}, f32[136,256]{1,0:T(8,128)S(1)}, u32[]{:S(2)}, u32[]{:S(2)}) collective-permute-start(f32[136,256]{1,0:T(8,128)S(1)} %bitcast.86), channel_id=1, source_target_pairs={{0,8},{1,9},{2,10},{3,11},{4,12},{5,13},{6,14},{7,15},{8,16},{9,17... | collective-permute-start | bytes 417800 | tf_op jit(solution)/shard_map/ppermute | solution.py:121
  101.9 3.4 %collective-permute-start.16 = (f32[136,256]{1,0:T(8,128)S(1)}, f32[136,256]{1,0:T(8,128)S(1)}, u32[]{:S(2)}, u32[]{:S(2)}) collective-permute-start(f32[136,256]{1,0:T(8,128)S(1)} %bitcast.87), channel_id=1, source_target_pairs={{0,12},{1,13},{2,14},{3,15},{4,16},{5,17},{6,18},{7,19},{8,20},{9,... | collective-permute-start | bytes 417800 | tf_op jit(solution)/shard_map/ppermute | solution.py:121
  105.3 0.9 collective-permute-start.17
  106.2 0.6 collective-permute-start.18
  106.8 2.2 %collective-permute-start.19 = (f32[136,256]{1,0:T(8,128)S(1)}, f32[136,256]{1,0:T(8,128)S(1)}, u32[]{:S(2)}, u32[]{:S(2)}) collective-permute-start(f32[136,256]{1,0:T(8,128)S(1)} %bitcast.90), channel_id=1, source_target_pairs={{0,24},{1,25},{2,26},{3,27},{4,28},{5,29},{6,30},{7,31},{8,0},{9,1... | collective-permute-start | bytes 417800 | tf_op jit(solution)/shard_map/ppermute | solution.py:121
  109.0 2.3 %collective-permute-start.20 = (f32[136,256]{1,0:T(8,128)S(1)}, f32[136,256]{1,0:T(8,128)S(1)}, u32[]{:S(2)}, u32[]{:S(2)}) collective-permute-start(f32[136,256]{1,0:T(8,128)S(1)} %bitcast.91), channel_id=1, source_target_pairs={{0,28},{1,29},{2,30},{3,31},{4,0},{5,1},{6,2},{7,3},{8,4},{9,5},{1... | collective-permute-start | bytes 417800 | tf_op jit(solution)/shard_map/ppermute | solution.py:121
  111.3 8.7 %collective-permute-done.16 = f32[136,256]{1,0:T(8,128)S(1)} collective-permute-done((f32[136,256]{1,0:T(8,128)S(1)}, f32[136,256]{1,0:T(8,128)S(1)}, u32[]{:S(2)}, u32[]{:S(2)}) %collective-permute-start.16) | collective-permute-done | bytes 139296 | tf_op jit(solution)/shard_map/ppermute | solution.py:121
  120.0 2.7 %collective-permute-done.17 = f32[136,256]{1,0:T(8,128)S(1)} collective-permute-done((f32[136,256]{1,0:T(8,128)S(1)}, f32[136,256]{1,0:T(8,128)S(1)}, u32[]{:S(2)}, u32[]{:S(2)}) %collective-permute-start.17) | collective-permute-done | bytes 139296 | tf_op jit(solution)/shard_map/ppermute | solution.py:121
  122.8 2.4 %collective-permute-done.19 = f32[136,256]{1,0:T(8,128)S(1)} collective-permute-done((f32[136,256]{1,0:T(8,128)S(1)}, f32[136,256]{1,0:T(8,128)S(1)}, u32[]{:S(2)}, u32[]{:S(2)}) %collective-permute-start.19) | collective-permute-done | bytes 139296 | tf_op jit(solution)/shard_map/ppermute | solution.py:121
  125.2 4.1 %collective-permute-done.20 = f32[136,256]{1,0:T(8,128)S(1)} collective-permute-done((f32[136,256]{1,0:T(8,128)S(1)}, f32[136,256]{1,0:T(8,128)S(1)}, u32[]{:S(2)}, u32[]{:S(2)}) %collective-permute-start.20) | collective-permute-done | bytes 139296 | tf_op jit(solution)/shard_map/ppermute | solution.py:121
  129.3 0.6 gather_fusion.1
  129.9 0.2 broadcast_select_fusion
  130.1 0.1 slice_add_fusion
  130.1 0.7 fusion.10
  130.8 0.6 slice_multiply_fusion.1
  (37 shorter events, 0.4 us)
Async XLA Ops:
  0.6 47.4 %copy-start = (bf16[128,256]{1,0:T(8,128)(2,1)S(1)}, bf16[128,256]{1,0:T(8,128)(2,1)}, u32[]{:S(2)}) copy-start(bf16[128,256]{1,0:T(8,128)(2,1)} %param.15) | copy-start | bytes 196612
  2.4 6.4 %collective-permute-start = (bf16[512,128]{1,0:T(8,128)(2,1)S(1)}, bf16[512,128]{1,0:T(8,128)(2,1)S(1)}, u32[]{:S(2)}, u32[]{:S(2)}) collective-permute-start(bf16[512,128]{1,0:T(8,128)(2,1)S(1)} %multiply_convert_fusion.1), channel_id=1, source_target_pairs={{0,8},{4,12},{8,16},{12,20},{16,24},{20,28},{24,0},{28,4},{1,9},{5... | collective-permute-start | bytes 393224 | tf_op jit(solution)/shard_map/ppermute | solution.py:11
  4.0 6.7 %collective-permute-start.1 = (bf16[512,128]{1,0:T(8,128)(2,1)S(1)}, bf16[512,128]{1,0:T(8,128)(2,1)S(1)}, u32[]{:S(2)}, u32[]{:S(2)}) collective-permute-start(bf16[512,128]{1,0:T(8,128)(2,1)S(1)} %multiply_convert_fusion.1), channel_id=1, source_target_pairs={{0,4},{4,8},{8,12},{12,16},{16,20},{20,24},{24,28},{28,0},{1,5},{5... | collective-permute-start | bytes 393224 | tf_op jit(solution)/shard_map/ppermute | solution.py:11
  5.6 7.3 %collective-permute-start.2 = (bf16[512,128]{1,0:T(8,128)(2,1)S(1)}, bf16[512,128]{1,0:T(8,128)(2,1)S(1)}, u32[]{:S(2)}, u32[]{:S(2)}) collective-permute-start(bf16[512,128]{1,0:T(8,128)(2,1)S(1)} %multiply_convert_fusion.1), channel_id=1, source_target_pairs={{0,28},{4,0},{8,4},{12,8},{16,12},{20,16},{24,20},{28,24},{1,29},{... | collective-permute-start | bytes 393224 | tf_op jit(solution)/shard_map/ppermute | solution.py:11
  6.1 8.1 %collective-permute-start.3 = (bf16[512,128]{1,0:T(8,128)(2,1)S(1)}, bf16[512,128]{1,0:T(8,128)(2,1)S(1)}, u32[]{:S(2)}, u32[]{:S(2)}) collective-permute-start(bf16[512,128]{1,0:T(8,128)(2,1)S(1)} %multiply_convert_fusion.1), channel_id=1, source_target_pairs={{0,24},{4,28},{8,0},{12,4},{16,8},{20,12},{24,16},{28,20},{1,25},{... | collective-permute-start | bytes 393224 | tf_op jit(solution)/shard_map/ppermute | solution.py:11
  14.2 0.8 copy-start.1
  34.5 13.5 %copy-start.2 = (bf16[512,256]{1,0:T(8,128)(2,1)S(1)}, bf16[512,256]{1,0:T(8,128)(2,1)}, u32[]{:S(2)}) copy-start(bf16[512,256]{1,0:T(8,128)(2,1)} %param.17) | copy-start | bytes 786436
  34.5 13.5 %copy-start.3 = (f32[256]{0:T(256)S(1)}, f32[256]{0:T(256)}, u32[]{:S(2)}) copy-start(f32[256]{0:T(256)} %param.16) | copy-start | bytes 3076
  34.5 6.7 %collective-permute-start.6 = (f32[512,128]{1,0:T(8,128)S(1)}, f32[512,128]{1,0:T(8,128)S(1)}, u32[]{:S(2)}, u32[]{:S(2)}) collective-permute-start(f32[512,128]{1,0:T(8,128)S(1)} %bitcast.84), channel_id=1, source_target_pairs={{0,3},{1,0},{2,1},{3,2},{4,7},{5,4},{6,5},{7,6},{8,11},{9,8},{10,9... | collective-permute-start | bytes 786440 | tf_op jit(solution)/shard_map/ppermute | solution.py:11
  34.6 12.3 %collective-permute-start.5 = (f32[512,128]{1,0:T(8,128)S(1)}, f32[512,128]{1,0:T(8,128)S(1)}, u32[]{:S(2)}, u32[]{:S(2)}) collective-permute-start(f32[512,128]{1,0:T(8,128)S(1)} %bitcast.83), channel_id=1, source_target_pairs={{0,2},{1,3},{2,0},{3,1},{4,6},{5,7},{6,4},{7,5},{8,10},{9,11},{10,... | collective-permute-start | bytes 786440 | tf_op jit(solution)/shard_map/ppermute | solution.py:11
  35.1 12.7 %collective-permute-start.4 = (f32[512,128]{1,0:T(8,128)S(1)}, f32[512,128]{1,0:T(8,128)S(1)}, u32[]{:S(2)}, u32[]{:S(2)}) collective-permute-start(f32[512,128]{1,0:T(8,128)S(1)} %bitcast.82), channel_id=1, source_target_pairs={{0,1},{1,2},{2,3},{3,0},{4,5},{5,6},{6,7},{7,4},{8,9},{9,10},{10,1... | collective-permute-start | bytes 786440 | tf_op jit(solution)/shard_map/ppermute | solution.py:11
  49.7 41.4 %collective-permute-start.13 = (f32[136,256]{1,0:T(8,128)S(1)}, f32[136,256]{1,0:T(8,128)S(1)}, u32[]{:S(2)}, u32[]{:S(2)}) collective-permute-start(f32[136,256]{1,0:T(8,128)S(1)} %get-tuple-element.18), channel_id=1, source_target_pairs={{0,3},{1,0},{2,1},{3,2},{4,7},{5,4},{6,5},{7,6},{8,11},{9,8},{10,9... | collective-permute-start | bytes 417800 | tf_op jit(solution)/shard_map/ppermute | solution.py:121
  49.7 41.4 %collective-permute-start.12 = (f32[136,256]{1,0:T(8,128)S(1)}, f32[136,256]{1,0:T(8,128)S(1)}, u32[]{:S(2)}, u32[]{:S(2)}) collective-permute-start(f32[136,256]{1,0:T(8,128)S(1)} %get-tuple-element.18), channel_id=1, source_target_pairs={{0,2},{1,3},{2,0},{3,1},{4,6},{5,7},{6,4},{7,5},{8,10},{9,11},{10,... | collective-permute-start | bytes 417800 | tf_op jit(solution)/shard_map/ppermute | solution.py:121
  51.3 40.0 %collective-permute-start.11 = (f32[136,256]{1,0:T(8,128)S(1)}, f32[136,256]{1,0:T(8,128)S(1)}, u32[]{:S(2)}, u32[]{:S(2)}) collective-permute-start(f32[136,256]{1,0:T(8,128)S(1)} %get-tuple-element.18), channel_id=1, source_target_pairs={{0,1},{1,2},{2,3},{3,0},{4,5},{5,6},{6,7},{7,4},{8,9},{9,10},{10,1... | collective-permute-start | bytes 417800 | tf_op jit(solution)/shard_map/ppermute | solution.py:121
  84.2 10.7 %collective-permute-start.10 = (bf16[512,128]{1,0:T(8,128)(2,1)S(1)}, bf16[512,128]{1,0:T(8,128)(2,1)S(1)}, u32[]{:S(2)}, u32[]{:S(2)}) collective-permute-start(bf16[512,128]{1,0:T(8,128)(2,1)S(1)} %bitcast.95), channel_id=1, source_target_pairs={{0,8},{4,12},{8,16},{12,20},{16,24},{20,28},{24,0},{28,4},{1,9},{5... | collective-permute-start | bytes 393224 | tf_op jit(solution)/shard_map/ppermute | solution.py:11
  86.7 8.3 %collective-permute-start.9 = (bf16[512,128]{1,0:T(8,128)(2,1)S(1)}, bf16[512,128]{1,0:T(8,128)(2,1)S(1)}, u32[]{:S(2)}, u32[]{:S(2)}) collective-permute-start(bf16[512,128]{1,0:T(8,128)(2,1)S(1)} %bitcast.96), channel_id=1, source_target_pairs={{0,4},{4,8},{8,12},{12,16},{16,20},{20,24},{24,28},{28,0},{1,5},{5... | collective-permute-start | bytes 393224 | tf_op jit(solution)/shard_map/ppermute | solution.py:11
  91.1 7.5 %collective-permute-start.8 = (bf16[512,128]{1,0:T(8,128)(2,1)}, bf16[512,128]{1,0:T(8,128)(2,1)S(1)}, u32[]{:S(2)}, u32[]{:S(2)}) collective-permute-start(bf16[512,128]{1,0:T(8,128)(2,1)} %bitcast.15), channel_id=1, source_target_pairs={{0,28},{4,0},{8,4},{12,8},{16,12},{20,16},{24,20},{28,24},{1,29},{... | collective-permute-start | bytes 393224 | tf_op jit(solution)/shard_map/ppermute | solution.py:11
  91.2 7.9 %collective-permute-start.7 = (bf16[512,128]{1,0:T(8,128)(2,1)S(1)}, bf16[512,128]{1,0:T(8,128)(2,1)S(1)}, u32[]{:S(2)}, u32[]{:S(2)}) collective-permute-start(bf16[512,128]{1,0:T(8,128)(2,1)S(1)} %bitcast.97), channel_id=1, source_target_pairs={{0,24},{4,28},{8,0},{12,4},{16,8},{20,12},{24,16},{28,20},{1,25},{... | collective-permute-start | bytes 393224 | tf_op jit(solution)/shard_map/ppermute | solution.py:11
  92.1 14.8 %collective-permute-start.14 = (f32[136,256]{1,0:T(8,128)S(1)}, f32[136,256]{1,0:T(8,128)S(1)}, u32[]{:S(2)}, u32[]{:S(2)}) collective-permute-start(f32[136,256]{1,0:T(8,128)S(1)} %bitcast.85), channel_id=1, source_target_pairs={{0,4},{1,5},{2,6},{3,7},{4,8},{5,9},{6,10},{7,11},{8,12},{9,13},{1... | collective-permute-start | bytes 417800 | tf_op jit(solution)/shard_map/ppermute | solution.py:121
  99.8 9.2 %collective-permute-start.15 = (f32[136,256]{1,0:T(8,128)S(1)}, f32[136,256]{1,0:T(8,128)S(1)}, u32[]{:S(2)}, u32[]{:S(2)}) collective-permute-start(f32[136,256]{1,0:T(8,128)S(1)} %bitcast.86), channel_id=1, source_target_pairs={{0,8},{1,9},{2,10},{3,11},{4,12},{5,13},{6,14},{7,15},{8,16},{9,17... | collective-permute-start | bytes 417800 | tf_op jit(solution)/shard_map/ppermute | solution.py:121
  101.9 18.2 %collective-permute-start.16 = (f32[136,256]{1,0:T(8,128)S(1)}, f32[136,256]{1,0:T(8,128)S(1)}, u32[]{:S(2)}, u32[]{:S(2)}) collective-permute-start(f32[136,256]{1,0:T(8,128)S(1)} %bitcast.87), channel_id=1, source_target_pairs={{0,12},{1,13},{2,14},{3,15},{4,16},{5,17},{6,18},{7,19},{8,20},{9,... | collective-permute-start | bytes 417800 | tf_op jit(solution)/shard_map/ppermute | solution.py:121
  105.3 17.5 %collective-permute-start.17 = (f32[136,256]{1,0:T(8,128)S(1)}, f32[136,256]{1,0:T(8,128)S(1)}, u32[]{:S(2)}, u32[]{:S(2)}) collective-permute-start(f32[136,256]{1,0:T(8,128)S(1)} %bitcast.88), channel_id=1, source_target_pairs={{0,16},{1,17},{2,18},{3,19},{4,20},{5,21},{6,22},{7,23},{8,24},{9,... | collective-permute-start | bytes 417800 | tf_op jit(solution)/shard_map/ppermute | solution.py:121
  106.2 16.6 %collective-permute-start.18 = (f32[136,256]{1,0:T(8,128)S(1)}, f32[136,256]{1,0:T(8,128)S(1)}, u32[]{:S(2)}, u32[]{:S(2)}) collective-permute-start(f32[136,256]{1,0:T(8,128)S(1)} %bitcast.89), channel_id=1, source_target_pairs={{0,20},{1,21},{2,22},{3,23},{4,24},{5,25},{6,26},{7,27},{8,28},{9,... | collective-permute-start | bytes 417800 | tf_op jit(solution)/shard_map/ppermute | solution.py:121
  106.8 18.3 %collective-permute-start.19 = (f32[136,256]{1,0:T(8,128)S(1)}, f32[136,256]{1,0:T(8,128)S(1)}, u32[]{:S(2)}, u32[]{:S(2)}) collective-permute-start(f32[136,256]{1,0:T(8,128)S(1)} %bitcast.90), channel_id=1, source_target_pairs={{0,24},{1,25},{2,26},{3,27},{4,28},{5,29},{6,30},{7,31},{8,0},{9,1... | collective-permute-start | bytes 417800 | tf_op jit(solution)/shard_map/ppermute | solution.py:121
  109.0 20.2 %collective-permute-start.20 = (f32[136,256]{1,0:T(8,128)S(1)}, f32[136,256]{1,0:T(8,128)S(1)}, u32[]{:S(2)}, u32[]{:S(2)}) collective-permute-start(f32[136,256]{1,0:T(8,128)S(1)} %bitcast.91), channel_id=1, source_target_pairs={{0,28},{1,29},{2,30},{3,31},{4,0},{5,1},{6,2},{7,3},{8,4},{9,5},{1... | collective-permute-start | bytes 417800 | tf_op jit(solution)/shard_map/ppermute | solution.py:121

commit v6 on v4

--- a/solution.py
+++ b/solution.py
@@ -20,11 +20,11 @@
     slot_count = adjacency.shape[0] // offset_count
     tile = adjacency.shape[1]
     width = operand.shape[2]
-    chunk = slot_chunk(slot_count)
+    chunk = slot_chunk(slot_count, 72)
     chunks = slot_count // chunk
     out_width = width if forward else tile
 
-    group = slot_chunk(chunk, 8)
+    group = slot_chunk(chunk, 24)
 
     def kernel(rows_ref, cols_ref, counts_ref, adj_ref, opnd_ref, out_ref, prod_ref):
         k = pl.program_id(0)
@@ -53,16 +53,13 @@
                             opnd_ref[rows_ref[g]], adj_ref[i], preferred_element_type=jnp.float32
                         )
 
-        def body(i, carry):
+        for i in range(chunk):
+
             @pl.when(i < live)
             def _():
                 g = first + i
                 target = rows_ref[g] if forward else k * own_tiles + cols_ref[g]
                 out_ref[target] += prod_ref[i]
-
-            return carry
-
-        lax.fori_loop(0, chunk, body, 0)
 
     def adj_map(k, j, rows_ref, cols_ref, counts_ref):
         last = jnp.maximum(counts_ref[k] - 1, 0) // chunk

time: 113 us -> 100 us (0.88)
  the two profiles are of different devices: /device:TPU:3 before, /device:TPU:0 now
where the time goes in v6:
time: 100 us; the launch traced here: 98.5 us
  waiting for transfers between devices  29.9 us (30%)
  starting transfers between devices  23.7 us (24%)
  Pallas kernels  22.1 us (22%)
  other arithmetic  7.92 us (8%)
  blocking collectives  7.41 us (7%)
  local copies, waits for them, and re-layouts  5.01 us (5%)
  matrix products  1.57 us (2%)
    ppermute x11, waiting for transfers between devices, from_behind(): lax.ppermute(value, axis, [(i, (i + by) % length) for i in range(length)])  23.1 us
    pallas_call x2, Pallas kernels, tile_products(): pl.pallas_call(kernel, grid_spec=pltpu.PrefetchScalarGridSpec(num_scalar_...  22.1 us
    ppermute x11, starting transfers between devices, from_behind(): lax.ppermute(value, axis, [(i, (i + by) % length) for i in range(length)])  17.9 us
    all_gather x1, blocking collectives, local(): block_grad = lax.all_gather(grad_hidden, 'col', axis=0, tiled=True)  7.41 us
    ppermute x5, waiting for transfers between devices, all_sum(): lax.ppermute(value, axes, [(i, i ^ bit) for i in range(size)])  6.72 us
    ppermute x5, starting transfers between devices, all_sum(): lax.ppermute(value, axes, [(i, i ^ bit) for i in range(size)])  5.85 us
  transfers between devices with their start and end apart: 16, of which 7 were waited for; matrix products, arithmetic and copies ran while one was open for 7% of the time, Pallas kernels for 11%

profile of v6, /device:TPU:0, one launch (start us, length us, event | category | flops | bytes accessed | tf_op | source)
XLA Modules:
  0.0 98.5 jit_solution(7280226717507888554)
XLA Ops:
  0.6 0.0 copy-start
  0.6 0.7 convert_rsqrt_fusion
  1.4 1.0 %multiply_convert_fusion.1 = bf16[512,128]{1,0:T(8,128)(2,1)S(1)} fusion(bf16[512,128]{1,0:T(8,128)(2,1)} %param.9, f32[512]{0:T(512)S(1)} %convert_rsqrt_fusion), kind=kLoop, calls=%fused_computation.17 | loop fusion | flops 196608 | bytes 264192 | tf_op jit(solution)/shard_map/convert_element_type | solution.py:118
  2.4 6.1 %collective-permute-start.2 = (bf16[512,128]{1,0:T(8,128)(2,1)S(1)}, bf16[512,128]{1,0:T(8,128)(2,1)S(1)}, u32[]{:S(2)}, u32[]{:S(2)}) collective-permute-start(bf16[512,128]{1,0:T(8,128)(2,1)S(1)} %multiply_convert_fusion.1), channel_id=1, source_target_pairs={{0,28},{4,0},{8,4},{12,8},{16,12},{20,16},{24,20},{28,24},{1,29},{... | collective-permute-start | bytes 393224 | tf_op jit(solution)/shard_map/ppermute | solution.py:11
  8.5 0.4 collective-permute-start.3
  8.9 0.6 collective-permute-start.1
  9.6 0.9 collective-permute-start
  10.5 1.3 %add_select_fusion.rows_ref = s32[360]{0:T(512)} fusion(s32[360]{0:T(512)} %rows_ref.1, s32[]{:T(128)S(6)} %mul.57), kind=kLoop, calls=%fused_computation.28 | loop fusion | flops 4320 | bytes 2884 | tf_op jit(solution)/shard_map/jit(remainder)/select_n | solution.py:125
  11.8 6.0 %collective-permute-done = bf16[512,128]{1,0:T(8,128)(2,1)S(1)} collective-permute-done((bf16[512,128]{1,0:T(8,128)(2,1)S(1)}, bf16[512,128]{1,0:T(8,128)(2,1)S(1)}, u32[]{:S(2)}, u32[]{:S(2)}) %collective-permute-start) | collective-permute-done | bytes 131104 | tf_op jit(solution)/shard_map/ppermute | solution.py:11
  17.8 0.0 collective-permute-done.1
  17.8 1.1 %bitcast_dynamic-update-slice_fusion.2 = bf16[5,512,128]{2,1,0:T(8,128)(2,1)S(1)} fusion(bf16[5,512,128]{2,1,0:T(8,128)(2,1)S(1)} %bitcast_dynamic-update-slice_fusion.3, bf16[512,128]{1,0:T(8,128)(2,1)} %param.9, f32[512]{0:T(512)S(1)} %convert_rsqrt_fusion), kind=kLoop, calls=%fused_computation.22 | loop fusion | flops 196608 | bytes 264192
  18.9 0.0 collective-permute-done.2
  19.0 0.0 collective-permute-done.3
  19.0 0.0 copy-start.1
  19.0 0.8 copy-done.1
  19.8 11.0 %shard_map.120 = f32[16,128,128]{2,1,0:T(8,128)} custom-call(s32[360]{0:T(512)} %add_select_fusion.rows_ref, s32[360]{0:T(512)} %cols_ref.3, s32[5]{0:T(128)} %counts_ref.3, bf16[360,128,128]{2,1,0:T(8,128)(2,1)} %adj_ref.3, bf16[20,128,128]{2,1,0:T(8,128)(2,1)} %bitcast.55), custom_call_target="tpu_custom_call" | custom-call | flops 1509949440 | bytes 13500416 | tf_op jit(solution)/shard_map/pallas_call | solution.py:73
  30.9 1.3 %fusion.16 = (f32[4,128,128]{2,1,0:T(8,128)S(1)}, f32[4,128,128]{2,1,0:T(8,128)S(1)}, f32[4,128,128]{2,1,0:T(8,128)S(1)}, f32[4,128,128]{2,1,0:T(8,128)S(1)}) fusion(f32[16,128,128]{2,1,0:T(8,128)} %shard_map.120), kind=kLoop, calls=%fused_computation.37 | loop fusion | bytes 2097152 | tf_op jit(solution)/shard_map/slice | solution.py:130
  32.2 1.2 %collective-permute-start.6 = (f32[512,128]{1,0:T(8,128)S(1)}, f32[512,128]{1,0:T(8,128)S(1)}, u32[]{:S(2)}, u32[]{:S(2)}) collective-permute-start(f32[512,128]{1,0:T(8,128)S(1)} %bitcast.58), channel_id=1, source_target_pairs={{0,3},{1,0},{2,1},{3,2},{4,7},{5,4},{6,5},{7,6},{8,11},{9,8},{10,9... | collective-permute-start | bytes 786440 | tf_op jit(solution)/shard_map/ppermute | solution.py:11
  33.4 1.2 %collective-permute-start.5 = (f32[512,128]{1,0:T(8,128)S(1)}, f32[512,128]{1,0:T(8,128)S(1)}, u32[]{:S(2)}, u32[]{:S(2)}) collective-permute-start(f32[512,128]{1,0:T(8,128)S(1)} %bitcast.57), channel_id=1, source_target_pairs={{0,2},{1,3},{2,0},{3,1},{4,6},{5,7},{6,4},{7,5},{8,10},{9,11},{10,... | collective-permute-start | bytes 786440 | tf_op jit(solution)/shard_map/ppermute | solution.py:11
  34.7 0.0 collective-permute-start.4
  34.7 0.1 pad.2.clone
  34.7 5.4 %collective-permute-done.6 = f32[512,128]{1,0:T(8,128)S(1)} collective-permute-done((f32[512,128]{1,0:T(8,128)S(1)}, f32[512,128]{1,0:T(8,128)S(1)}, u32[]{:S(2)}, u32[]{:S(2)}) %collective-permute-start.6) | collective-permute-done | bytes 262176 | tf_op jit(solution)/shard_map/ppermute | solution.py:11
  40.1 6.8 %collective-permute-done.5 = f32[512,128]{1,0:T(8,128)S(1)} collective-permute-done((f32[512,128]{1,0:T(8,128)S(1)}, f32[512,128]{1,0:T(8,128)S(1)}, u32[]{:S(2)}, u32[]{:S(2)}) %collective-permute-start.5) | collective-permute-done | bytes 262176 | tf_op jit(solution)/shard_map/ppermute | solution.py:11
  46.9 0.0 collective-permute-done.4
  46.9 0.1 fusion.9
  47.1 0.0 copy-done
  47.1 0.0 copy-done.2
  47.1 0.0 copy-done.3
  47.1 1.1 %fusion.15 = (f32[256]{0:T(256)S(1)}, bf16[512,256]{1,0:T(8,128)(2,1)S(1)}, bf16[512,256]{1,0:T(8,128)(2,1)}) fusion(bf16[512,256]{1,0:T(8,128)(2,1)S(1)} %copy-done.2, f32[256]{0:T(256)S(1)} %copy-done.3, bf16[512,128]{1,0:T(8,128)(2,1)S(1)} %fusion.9, bf16[128,256]{1,0:T(8,128)(2,1)S(1)} %copy-done), kind=kOutput, calls=%fused_computation.36 | convolution fusion | flops 35389184 | bytes 985088 | tf_op jit(solution)/shard_map/dot_general | solution.py:134
  48.2 0.2 fusion.10
  48.5 0.2 fusion
  48.7 0.1 maximum_maximum_fusion
  48.8 0.1 collective-permute-start.11
  48.9 7.4 %all_gather.3 = bf16[2048,128]{1,0:T(8,128)(2,1)S(1)} all-gather(bf16[512,128]{1,0:T(8,128)(2,1)S(1)} %fusion), channel_id=1, replica_groups=mesh['blk'=8,'col'=4] {'col'}, dimensions={0}, use_global_device_ids=true | all-gather | bytes 655360 | tf_op jit(solution)/shard_map/all_gather | solution.py:154
  56.3 1.0 %copy.13 = bf16[16,128,128]{1,2,0:T(8,128)(2,1)} copy(bf16[16,128,128]{2,1,0:T(8,128)(2,1)S(1)} %bitcast.54) | data formatting | bytes 1048576 | tf_op jit(solution)/shard_map/reshape | solution.py:155
  57.3 0.0 collective-permute-done.11
  57.3 0.1 fusion.14
  57.4 1.1 %collective-permute-start.12 = (f32[136,256]{1,0:T(8,128)S(1)}, f32[136,256]{1,0:T(8,128)S(1)}, u32[]{:S(2)}, u32[]{:S(2)}) collective-permute-start(f32[136,256]{1,0:T(8,128)S(1)} %fusion.14), channel_id=1, source_target_pairs={{0,2},{1,3},{2,0},{3,1},{4,6},{5,7},{6,4},{7,5},{8,10},{9,11},{10,... | collective-permute-start | bytes 417800 | tf_op jit(solution)/shard_map/ppermute | solution.py:101
  58.4 11.1 %shard_map.121 = f32[20,128,128]{2,1,0:T(8,128)} custom-call(s32[360]{0:T(512)} %rows_ref.1, s32[360]{0:T(512)} %cols_ref.3, s32[5]{0:T(128)} %counts_ref.3, bf16[360,128,128]{2,1,0:T(8,128)(2,1)} %adj_ref.3, bf16[16,128,128]{2,1,0:T(8,128)(2,1)} %bitcast.53), custom_call_target="tpu_custom_call" | custom-call | flops 1509949440 | bytes 13631488 | tf_op jit(solution)/shard_map/pallas_call | solution.py:73
  69.6 0.0 collective-permute-done.12
  69.6 4.2 %collective-permute-start.13 = (f32[136,256]{1,0:T(8,128)S(1)}, f32[136,256]{1,0:T(8,128)S(1)}, u32[]{:S(2)}, u32[]{:S(2)}) collective-permute-start(f32[136,256]{1,0:T(8,128)S(1)} %add.69), channel_id=1, source_target_pairs={{0,4},{1,5},{2,6},{3,7},{4,0},{5,1},{6,2},{7,3},{8,12},{9,13},{10,... | collective-permute-start | bytes 417800 | tf_op jit(solution)/shard_map/ppermute | solution.py:101
  73.8 1.4 %bitcast_convert_fusion = bf16[20,128,128]{1,2,0:T(8,128)(2,1)S(1)} fusion(f32[20,128,128]{2,1,0:T(8,128)} %shard_map.121), kind=kLoop, calls=%fused_computation.34 | loop fusion | flops 327680 | bytes 1966080 | tf_op jit(solution)/shard_map/convert.3
  75.3 2.6 %collective-permute-done.13 = f32[136,256]{1,0:T(8,128)S(1)} collective-permute-done((f32[136,256]{1,0:T(8,128)S(1)}, f32[136,256]{1,0:T(8,128)S(1)}, u32[]{:S(2)}, u32[]{:S(2)}) %collective-permute-start.13) | collective-permute-done | bytes 139296 | tf_op jit(solution)/shard_map/ppermute | solution.py:101
  77.9 0.4 collective-permute-start.14
  78.3 0.1 copy.15
  78.4 0.1 copy.18
  78.6 0.1 copy.17
  78.7 0.1 copy.16
  78.9 3.5 %collective-permute-start.8 = (bf16[512,128]{1,0:T(8,128)(2,1)S(1)}, bf16[512,128]{1,0:T(8,128)(2,1)S(1)}, u32[]{:S(2)}, u32[]{:S(2)}) collective-permute-start(bf16[512,128]{1,0:T(8,128)(2,1)S(1)} %bitcast.62), channel_id=1, source_target_pairs={{0,28},{4,0},{8,4},{12,8},{16,12},{20,16},{24,20},{28,24},{1,29},{... | collective-permute-start | bytes 393224 | tf_op jit(solution)/shard_map/ppermute | solution.py:11
  82.4 0.0 collective-permute-start.9
  82.4 0.2 collective-permute-start.10
  82.6 3.6 %collective-permute-start.7 = (bf16[512,128]{1,0:T(8,128)(2,1)S(1)}, bf16[512,128]{1,0:T(8,128)(2,1)S(1)}, u32[]{:S(2)}, u32[]{:S(2)}) collective-permute-start(bf16[512,128]{1,0:T(8,128)(2,1)S(1)} %bitcast.59), channel_id=1, source_target_pairs={{0,24},{4,28},{8,0},{12,4},{16,8},{20,12},{24,16},{28,20},{1,25},{... | collective-permute-start | bytes 393224 | tf_op jit(solution)/shard_map/ppermute | solution.py:11
  86.2 1.0 slice.61
  87.2 0.1 copy.14
  87.3 0.0 collective-permute-done.14
  87.4 0.1 collective-permute-start.15
  87.4 0.0 collective-permute-done.8
  87.4 4.0 %collective-permute-done.9 = bf16[512,128]{1,0:T(8,128)(2,1)S(1)} collective-permute-done((bf16[512,128]{1,0:T(8,128)(2,1)S(1)}, bf16[512,128]{1,0:T(8,128)(2,1)S(1)}, u32[]{:S(2)}, u32[]{:S(2)}) %collective-permute-start.9) | collective-permute-done | bytes 131104 | tf_op jit(solution)/shard_map/ppermute | solution.py:11
  91.5 0.9 collective-permute-done.10
  92.4 0.0 collective-permute-done.7
  92.4 0.8 fusion.5
  93.1 4.1 %collective-permute-done.15 = f32[136,256]{1,0:T(8,128)S(1)} collective-permute-done((f32[136,256]{1,0:T(8,128)S(1)}, f32[136,256]{1,0:T(8,128)S(1)}, u32[]{:S(2)}, u32[]{:S(2)}) %collective-permute-start.15) | collective-permute-done | bytes 139296 | tf_op jit(solution)/shard_map/ppermute | solution.py:101
  97.3 0.6 slice_multiply_fusion.1
  97.9 0.7 slice_multiply_fusion
  (12 shorter events, 0.2 us)
Async XLA Ops:
  0.6 46.5 %copy-start = (bf16[128,256]{1,0:T(8,128)(2,1)S(1)}, bf16[128,256]{1,0:T(8,128)(2,1)}, u32[]{:S(2)}) copy-start(bf16[128,256]{1,0:T(8,128)(2,1)} %param.15) | copy-start | bytes 196612
  2.4 16.5 %collective-permute-start.2 = (bf16[512,128]{1,0:T(8,128)(2,1)S(1)}, bf16[512,128]{1,0:T(8,128)(2,1)S(1)}, u32[]{:S(2)}, u32[]{:S(2)}) collective-permute-start(bf16[512,128]{1,0:T(8,128)(2,1)S(1)} %multiply_convert_fusion.1), channel_id=1, source_target_pairs={{0,28},{4,0},{8,4},{12,8},{16,12},{20,16},{24,20},{28,24},{1,29},{... | collective-permute-start | bytes 393224 | tf_op jit(solution)/shard_map/ppermute | solution.py:11
  8.5 10.5 %collective-permute-start.3 = (bf16[512,128]{1,0:T(8,128)(2,1)S(1)}, bf16[512,128]{1,0:T(8,128)(2,1)S(1)}, u32[]{:S(2)}, u32[]{:S(2)}) collective-permute-start(bf16[512,128]{1,0:T(8,128)(2,1)S(1)} %multiply_convert_fusion.1), channel_id=1, source_target_pairs={{0,24},{4,28},{8,0},{12,4},{16,8},{20,12},{24,16},{28,20},{1,25},{... | collective-permute-start | bytes 393224 | tf_op jit(solution)/shard_map/ppermute | solution.py:11
  8.9 8.9 %collective-permute-start.1 = (bf16[512,128]{1,0:T(8,128)(2,1)S(1)}, bf16[512,128]{1,0:T(8,128)(2,1)S(1)}, u32[]{:S(2)}, u32[]{:S(2)}) collective-permute-start(bf16[512,128]{1,0:T(8,128)(2,1)S(1)} %multiply_convert_fusion.1), channel_id=1, source_target_pairs={{0,4},{4,8},{8,12},{12,16},{16,20},{20,24},{24,28},{28,0},{1,5},{5... | collective-permute-start | bytes 393224 | tf_op jit(solution)/shard_map/ppermute | solution.py:11
  9.6 8.2 %collective-permute-start = (bf16[512,128]{1,0:T(8,128)(2,1)S(1)}, bf16[512,128]{1,0:T(8,128)(2,1)S(1)}, u32[]{:S(2)}, u32[]{:S(2)}) collective-permute-start(bf16[512,128]{1,0:T(8,128)(2,1)S(1)} %multiply_convert_fusion.1), channel_id=1, source_target_pairs={{0,8},{4,12},{8,16},{12,20},{16,24},{20,28},{24,0},{28,4},{1,9},{5... | collective-permute-start | bytes 393224 | tf_op jit(solution)/shard_map/ppermute | solution.py:11
  19.0 0.9 copy-start.1
  30.9 16.2 %copy-start.2 = (bf16[512,256]{1,0:T(8,128)(2,1)S(1)}, bf16[512,256]{1,0:T(8,128)(2,1)}, u32[]{:S(2)}) copy-start(bf16[512,256]{1,0:T(8,128)(2,1)} %param.17) | copy-start | bytes 786436
  30.9 16.2 %copy-start.3 = (f32[256]{0:T(256)S(1)}, f32[256]{0:T(256)}, u32[]{:S(2)}) copy-start(f32[256]{0:T(256)} %param.16) | copy-start | bytes 3076
  32.2 7.9 %collective-permute-start.6 = (f32[512,128]{1,0:T(8,128)S(1)}, f32[512,128]{1,0:T(8,128)S(1)}, u32[]{:S(2)}, u32[]{:S(2)}) collective-permute-start(f32[512,128]{1,0:T(8,128)S(1)} %bitcast.58), channel_id=1, source_target_pairs={{0,3},{1,0},{2,1},{3,2},{4,7},{5,4},{6,5},{7,6},{8,11},{9,8},{10,9... | collective-permute-start | bytes 786440 | tf_op jit(solution)/shard_map/ppermute | solution.py:11
  33.4 13.5 %collective-permute-start.5 = (f32[512,128]{1,0:T(8,128)S(1)}, f32[512,128]{1,0:T(8,128)S(1)}, u32[]{:S(2)}, u32[]{:S(2)}) collective-permute-start(f32[512,128]{1,0:T(8,128)S(1)} %bitcast.57), channel_id=1, source_target_pairs={{0,2},{1,3},{2,0},{3,1},{4,6},{5,7},{6,4},{7,5},{8,10},{9,11},{10,... | collective-permute-start | bytes 786440 | tf_op jit(solution)/shard_map/ppermute | solution.py:11
  34.7 12.3 %collective-permute-start.4 = (f32[512,128]{1,0:T(8,128)S(1)}, f32[512,128]{1,0:T(8,128)S(1)}, u32[]{:S(2)}, u32[]{:S(2)}) collective-permute-start(f32[512,128]{1,0:T(8,128)S(1)} %bitcast.56), channel_id=1, source_target_pairs={{0,1},{1,2},{2,3},{3,0},{4,5},{5,6},{6,7},{7,4},{8,9},{9,10},{10,1... | collective-permute-start | bytes 786440 | tf_op jit(solution)/shard_map/ppermute | solution.py:11
  48.8 8.5 %collective-permute-start.11 = (f32[136,256]{1,0:T(8,128)S(1)}, f32[136,256]{1,0:T(8,128)S(1)}, u32[]{:S(2)}, u32[]{:S(2)}) collective-permute-start(f32[136,256]{1,0:T(8,128)S(1)} %maximum_maximum_fusion), channel_id=1, source_target_pairs={{0,1},{1,0},{2,3},{3,2},{4,5},{5,4},{6,7},{7,6},{8,9},{9,8},{10,11... | collective-permute-start | bytes 417800 | tf_op jit(solution)/shard_map/ppermute | solution.py:101
  57.4 12.2 %collective-permute-start.12 = (f32[136,256]{1,0:T(8,128)S(1)}, f32[136,256]{1,0:T(8,128)S(1)}, u32[]{:S(2)}, u32[]{:S(2)}) collective-permute-start(f32[136,256]{1,0:T(8,128)S(1)} %fusion.14), channel_id=1, source_target_pairs={{0,2},{1,3},{2,0},{3,1},{4,6},{5,7},{6,4},{7,5},{8,10},{9,11},{10,... | collective-permute-start | bytes 417800 | tf_op jit(solution)/shard_map/ppermute | solution.py:101
  69.6 8.2 %collective-permute-start.13 = (f32[136,256]{1,0:T(8,128)S(1)}, f32[136,256]{1,0:T(8,128)S(1)}, u32[]{:S(2)}, u32[]{:S(2)}) collective-permute-start(f32[136,256]{1,0:T(8,128)S(1)} %add.69), channel_id=1, source_target_pairs={{0,4},{1,5},{2,6},{3,7},{4,0},{5,1},{6,2},{7,3},{8,12},{9,13},{10,... | collective-permute-start | bytes 417800 | tf_op jit(solution)/shard_map/ppermute | solution.py:101
  77.9 9.5 %collective-permute-start.14 = (f32[136,256]{1,0:T(8,128)S(1)}, f32[136,256]{1,0:T(8,128)S(1)}, u32[]{:S(2)}, u32[]{:S(2)}) collective-permute-start(f32[136,256]{1,0:T(8,128)S(1)} %add.70), channel_id=1, source_target_pairs={{0,8},{1,9},{2,10},{3,11},{4,12},{5,13},{6,14},{7,15},{8,0},{9,1},... | collective-permute-start | bytes 417800 | tf_op jit(solution)/shard_map/ppermute | solution.py:101
  78.9 8.6 %collective-permute-start.8 = (bf16[512,128]{1,0:T(8,128)(2,1)S(1)}, bf16[512,128]{1,0:T(8,128)(2,1)S(1)}, u32[]{:S(2)}, u32[]{:S(2)}) collective-permute-start(bf16[512,128]{1,0:T(8,128)(2,1)S(1)} %bitcast.62), channel_id=1, source_target_pairs={{0,28},{4,0},{8,4},{12,8},{16,12},{20,16},{24,20},{28,24},{1,29},{... | collective-permute-start | bytes 393224 | tf_op jit(solution)/shard_map/ppermute | solution.py:11
  82.4 9.1 %collective-permute-start.9 = (bf16[512,128]{1,0:T(8,128)(2,1)S(1)}, bf16[512,128]{1,0:T(8,128)(2,1)S(1)}, u32[]{:S(2)}, u32[]{:S(2)}) collective-permute-start(bf16[512,128]{1,0:T(8,128)(2,1)S(1)} %bitcast.61), channel_id=1, source_target_pairs={{0,4},{4,8},{8,12},{12,16},{16,20},{20,24},{24,28},{28,0},{1,5},{5... | collective-permute-start | bytes 393224 | tf_op jit(solution)/shard_map/ppermute | solution.py:11
  82.4 10.0 %collective-permute-start.10 = (bf16[512,128]{1,0:T(8,128)(2,1)S(1)}, bf16[512,128]{1,0:T(8,128)(2,1)S(1)}, u32[]{:S(2)}, u32[]{:S(2)}) collective-permute-start(bf16[512,128]{1,0:T(8,128)(2,1)S(1)} %bitcast.60), channel_id=1, source_target_pairs={{0,8},{4,12},{8,16},{12,20},{16,24},{20,28},{24,0},{28,4},{1,9},{5... | collective-permute-start | bytes 393224 | tf_op jit(solution)/shard_map/ppermute | solution.py:11
  82.6 9.7 %collective-permute-start.7 = (bf16[512,128]{1,0:T(8,128)(2,1)S(1)}, bf16[512,128]{1,0:T(8,128)(2,1)S(1)}, u32[]{:S(2)}, u32[]{:S(2)}) collective-permute-start(bf16[512,128]{1,0:T(8,128)(2,1)S(1)} %bitcast.59), channel_id=1, source_target_pairs={{0,24},{4,28},{8,0},{12,4},{16,8},{20,12},{24,16},{28,20},{1,25},{... | collective-permute-start | bytes 393224 | tf_op jit(solution)/shard_map/ppermute | solution.py:11
  87.4 9.9 %collective-permute-start.15 = (f32[136,256]{1,0:T(8,128)S(1)}, f32[136,256]{1,0:T(8,128)S(1)}, u32[]{:S(2)}, u32[]{:S(2)}) collective-permute-start(f32[136,256]{1,0:T(8,128)S(1)} %add.71), channel_id=1, source_target_pairs={{0,16},{1,17},{2,18},{3,19},{4,20},{5,21},{6,22},{7,23},{8,24},{9,... | collective-permute-start | bytes 417800 | tf_op jit(solution)/shard_map/ppermute | solution.py:101

commit v7 on v6

--- a/solution.py
+++ b/solution.py
@@ -143,7 +143,11 @@
     packed = jnp.concatenate(
         [weight_part, bias_part[None, :], jnp.zeros((7, hidden), jnp.float32)], axis=0
     )
-    packed = all_sum(packed, ("blk", "col"))
+    packed = all_sum(packed, ("col",))
+    gathered = lax.all_gather(packed, "blk")
+    packed = gathered[0]
+    for b in range(1, gathered.shape[0]):
+        packed = packed + gathered[b]
     norm_factor = float(own_rows * lax.axis_size("blk") * col_count) ** (-0.5)
     weight_sum = packed[:features]
     bias_sum = packed[features]

time: 100 us -> 118 us (1.18); the launches traced: 98.5 us -> 118 us
  between operations: 0.88 us -> 14.2 us
  waiting for transfers between devices: 29.9 us -> 38.8 us
  starting transfers between devices: 23.7 us -> 16.5 us
  Pallas kernels: 22.1 us -> 25.2 us
  other arithmetic: 7.92 us -> 9.86 us
    ppermute x11, waiting for transfers between devices: 23.1 us -> 31.7 us  [from_behind(): lax.ppermute(value, axis, [(i, (i + by) % length) for i in range(length)])]
    ppermute x5 -> x2, starting transfers between devices: 5.85 us -> 0.61 us  [all_sum(): lax.ppermute(value, axes, [(i, i ^ bit) for i in range(size)])]
    pallas_call x2, Pallas kernels: 22.1 us -> 25.2 us  [tile_products(): pl.pallas_call(kernel, grid_spec=pltpu.PrefetchScalarGridSpec(num_scalar_...]
    ppermute x11, starting transfers between devices: 17.9 us -> 15.9 us  [from_behind(): lax.ppermute(value, axis, [(i, (i + by) % length) for i in range(length)])]
    add x0 -> x1, other arithmetic: none -> 1.38 us  [local(): packed = packed + gathered[b]]
    ppermute x5 -> x2, waiting for transfers between devices: 6.72 us -> 6.59 us  [all_sum(): lax.ppermute(value, axes, [(i, i ^ bit) for i in range(size)])]
  transfers between devices with their start and end apart: 16 -> 14, of which waited for: 7 -> 11; matrix products, arithmetic and copies ran while one was open for 7% -> 6% of each run, Pallas kernels for 11% -> 11%
where the time goes in v7:
time: 118 us
  waiting for transfers between devices  38.8 us (33%)
  Pallas kernels  25.2 us (21%)
  starting transfers between devices  16.5 us (14%)
  between operations  14.2 us (12%)
  other arithmetic  9.86 us (8%)
  blocking collectives  6.5 us (6%)
  local copies, waits for them, and re-layouts  5.03 us (4%)
  matrix products  1.57 us (1%)
    ppermute x11, waiting for transfers between devices, from_behind(): lax.ppermute(value, axis, [(i, (i + by) % length) for i in range(length)])  31.7 us
    pallas_call x2, Pallas kernels, tile_products(): pl.pallas_call(kernel, grid_spec=pltpu.PrefetchScalarGridSpec(num_scalar_...  25.2 us
    ppermute x11, starting transfers between devices, from_behind(): lax.ppermute(value, axis, [(i, (i + by) % length) for i in range(length)])  15.9 us
    ppermute x2, waiting for transfers between devices, all_sum(): lax.ppermute(value, axes, [(i, i ^ bit) for i in range(size)])  6.59 us
    all_gather x1, blocking collectives, local(): block_grad = lax.all_gather(grad_hidden, 'col', axis=0, tiled=True)  6.5 us
  transfers between devices with their start and end apart: 14, of which 11 were waited for; matrix products, arithmetic and copies ran while one was open for 6% of the time, Pallas kernels for 11%

profile of v7, /device:TPU:0, one launch (start us, length us, event | category | flops | bytes accessed | tf_op | source)
XLA Modules:
  0.0 117.7 jit_solution(313543465550837244)
XLA Ops:
  7.2 0.0 copy-start
  7.2 0.0 all-gather.3.cloned.1.call-start
  7.2 0.7 convert_rsqrt_fusion
  7.9 1.0 multiply_convert_fusion.1
  9.0 6.1 %collective-permute-start.2 = (bf16[512,128]{1,0:T(8,128)(2,1)S(1)}, bf16[512,128]{1,0:T(8,128)(2,1)S(1)}, u32[]{:S(2)}, u32[]{:S(2)}) collective-permute-start(bf16[512,128]{1,0:T(8,128)(2,1)S(1)} %multiply_convert_fusion.1), channel_id=1, source_target_pairs={{0,28},{4,0},{8,4},{12,8},{16,12},{20,16},{24,20},{28,24},{1,29},{... | collective-permute-start | bytes 393224 | tf_op jit(solution)/shard_map/ppermute | solution.py:11
  15.0 0.4 collective-permute-start.3
  15.5 0.6 collective-permute-start.1
  16.1 0.9 collective-permute-start
  17.0 1.3 %add_select_fusion.rows_ref = s32[360]{0:T(512)} fusion(s32[360]{0:T(512)} %rows_ref.1, s32[]{:T(128)S(6)} %mul.57), kind=kLoop, calls=%fused_computation.37 | loop fusion | flops 4320 | bytes 2884 | tf_op jit(solution)/shard_map/jit(remainder)/select_n | solution.py:125
  18.3 6.0 %collective-permute-done = bf16[512,128]{1,0:T(8,128)(2,1)S(1)} collective-permute-done((bf16[512,128]{1,0:T(8,128)(2,1)S(1)}, bf16[512,128]{1,0:T(8,128)(2,1)S(1)}, u32[]{:S(2)}, u32[]{:S(2)}) %collective-permute-start) | collective-permute-done | bytes 131104 | tf_op jit(solution)/shard_map/ppermute | solution.py:11
  24.4 0.0 collective-permute-done.1
  24.4 1.1 bitcast_dynamic-update-slice_fusion.2
  25.5 0.0 collective-permute-done.2
  25.5 0.0 collective-permute-done.3
  25.5 0.0 copy-start.1
  25.5 0.8 copy-done.1
  26.4 12.5 %shard_map.120 = f32[16,128,128]{2,1,0:T(8,128)} custom-call(s32[360]{0:T(512)} %add_select_fusion.rows_ref, s32[360]{0:T(512)} %cols_ref.3, s32[5]{0:T(128)} %counts_ref.3, bf16[360,128,128]{2,1,0:T(8,128)(2,1)} %adj_ref.3, bf16[20,128,128]{2,1,0:T(8,128)(2,1)} %bitcast.59), custom_call_target="tpu_custom_call" | custom-call | flops 1509949440 | bytes 13500416 | tf_op jit(solution)/shard_map/pallas_call | solution.py:73
  38.9 0.0 copy-start.2
  38.9 1.3 %fusion.18 = (f32[4,128,128]{2,1,0:T(8,128)S(1)}, f32[4,128,128]{2,1,0:T(8,128)S(1)}, f32[4,128,128]{2,1,0:T(8,128)S(1)}, f32[4,128,128]{2,1,0:T(8,128)S(1)}) fusion(f32[16,128,128]{2,1,0:T(8,128)} %shard_map.120), kind=kLoop, calls=%fused_computation.46 | loop fusion | bytes 2097152 | tf_op jit(solution)/shard_map/slice | solution.py:130
  40.3 0.1 collective-permute-start.6
  40.3 1.4 %collective-permute-start.5 = (f32[512,128]{1,0:T(8,128)S(1)}, f32[512,128]{1,0:T(8,128)S(1)}, u32[]{:S(2)}, u32[]{:S(2)}) collective-permute-start(f32[512,128]{1,0:T(8,128)S(1)} %bitcast.61), channel_id=1, source_target_pairs={{0,2},{1,3},{2,0},{3,1},{4,6},{5,7},{6,4},{7,5},{8,10},{9,11},{10,... | collective-permute-start | bytes 786440 | tf_op jit(solution)/shard_map/ppermute | solution.py:11
  41.7 0.0 collective-permute-start.4
  41.7 0.1 pad.2.clone
  41.8 5.2 %collective-permute-done.6 = f32[512,128]{1,0:T(8,128)S(1)} collective-permute-done((f32[512,128]{1,0:T(8,128)S(1)}, f32[512,128]{1,0:T(8,128)S(1)}, u32[]{:S(2)}, u32[]{:S(2)}) %collective-permute-start.6) | collective-permute-done | bytes 262176 | tf_op jit(solution)/shard_map/ppermute | solution.py:11
  47.0 7.2 %collective-permute-done.5 = f32[512,128]{1,0:T(8,128)S(1)} collective-permute-done((f32[512,128]{1,0:T(8,128)S(1)}, f32[512,128]{1,0:T(8,128)S(1)}, u32[]{:S(2)}, u32[]{:S(2)}) %collective-permute-start.5) | collective-permute-done | bytes 262176 | tf_op jit(solution)/shard_map/ppermute | solution.py:11
  54.3 0.2 collective-permute-done.4
  54.5 0.1 fusion.9
  54.6 0.0 copy-done
  54.6 0.0 copy-done.2
  54.6 0.0 copy-done.3
  54.6 1.1 fusion.17
  55.7 0.2 fusion.12
  56.0 0.1 maximum_maximum_fusion
  56.1 0.1 collective-permute-start.11
  56.1 1.3 %collective-permute-done.11 = f32[136,256]{1,0:T(8,128)S(1)} collective-permute-done((f32[136,256]{1,0:T(8,128)S(1)}, f32[136,256]{1,0:T(8,128)S(1)}, u32[]{:S(2)}, u32[]{:S(2)}) %collective-permute-start.11) | collective-permute-done | bytes 139296 | tf_op jit(solution)/shard_map/ppermute | solution.py:101
  57.5 0.1 fusion.16
  57.6 0.5 collective-permute-start.12
  58.1 5.2 %collective-permute-done.12 = f32[136,256]{1,0:T(8,128)S(1)} collective-permute-done((f32[136,256]{1,0:T(8,128)S(1)}, f32[136,256]{1,0:T(8,128)S(1)}, u32[]{:S(2)}, u32[]{:S(2)}) %collective-permute-start.12) | collective-permute-done | bytes 139296 | tf_op jit(solution)/shard_map/ppermute | solution.py:101
  63.4 0.7 add.87
  64.1 0.0 all-gather.3.cloned.1.call-update
  64.1 0.2 fusion
  64.3 6.5 %all_gather.9 = bf16[2048,128]{1,0:T(8,128)(2,1)S(1)} all-gather(bf16[512,128]{1,0:T(8,128)(2,1)S(1)} %fusion), channel_id=1, replica_groups=mesh['blk'=8,'col'=4] {'col'}, dimensions={0}, use_global_device_ids=true | all-gather | bytes 655360 | tf_op jit(solution)/shard_map/all_gather | solution.py:158
  70.8 1.0 copy.13
  71.8 12.7 %shard_map.121 = f32[20,128,128]{2,1,0:T(8,128)} custom-call(s32[360]{0:T(512)} %rows_ref.1, s32[360]{0:T(512)} %cols_ref.3, s32[5]{0:T(128)} %counts_ref.3, bf16[360,128,128]{2,1,0:T(8,128)(2,1)} %adj_ref.3, bf16[16,128,128]{2,1,0:T(8,128)(2,1)} %bitcast.57), custom_call_target="tpu_custom_call" | custom-call | flops 1509949440 | bytes 13631488 | tf_op jit(solution)/shard_map/pallas_call | solution.py:73
  84.5 1.4 %bitcast_convert_fusion = bf16[20,128,128]{1,2,0:T(8,128)(2,1)S(1)} fusion(f32[20,128,128]{2,1,0:T(8,128)} %shard_map.121), kind=kLoop, calls=%fused_computation.43 | loop fusion | flops 327680 | bytes 1966080 | tf_op jit(solution)/shard_map/convert.3
  86.0 0.1 copy.15
  86.1 0.1 copy.18
  86.2 0.1 copy.17
  86.4 0.1 copy.16
  86.5 2.5 %collective-permute-start.8 = (bf16[512,128]{1,0:T(8,128)(2,1)S(1)}, bf16[512,128]{1,0:T(8,128)(2,1)S(1)}, u32[]{:S(2)}, u32[]{:S(2)}) collective-permute-start(bf16[512,128]{1,0:T(8,128)(2,1)S(1)} %bitcast.66), channel_id=1, source_target_pairs={{0,28},{4,0},{8,4},{12,8},{16,12},{20,16},{24,20},{28,24},{1,29},{... | collective-permute-start | bytes 393224 | tf_op jit(solution)/shard_map/ppermute | solution.py:11
  89.0 0.0 collective-permute-start.9
  89.0 1.3 %collective-permute-start.10 = (bf16[512,128]{1,0:T(8,128)(2,1)S(1)}, bf16[512,128]{1,0:T(8,128)(2,1)S(1)}, u32[]{:S(2)}, u32[]{:S(2)}) collective-permute-start(bf16[512,128]{1,0:T(8,128)(2,1)S(1)} %bitcast.64), channel_id=1, source_target_pairs={{0,8},{4,12},{8,16},{12,20},{16,24},{20,28},{24,0},{28,4},{1,9},{5... | collective-permute-start | bytes 393224 | tf_op jit(solution)/shard_map/ppermute | solution.py:11
  90.4 2.5 %collective-permute-start.7 = (bf16[512,128]{1,0:T(8,128)(2,1)S(1)}, bf16[512,128]{1,0:T(8,128)(2,1)S(1)}, u32[]{:S(2)}, u32[]{:S(2)}) collective-permute-start(bf16[512,128]{1,0:T(8,128)(2,1)S(1)} %bitcast.63), channel_id=1, source_target_pairs={{0,24},{4,28},{8,0},{12,4},{16,8},{20,12},{24,16},{28,20},{1,25},{... | collective-permute-start | bytes 393224 | tf_op jit(solution)/shard_map/ppermute | solution.py:11
  92.9 1.0 slice.103
  93.8 0.1 copy.14
  94.0 2.4 %collective-permute-done.8 = bf16[512,128]{1,0:T(8,128)(2,1)S(1)} collective-permute-done((bf16[512,128]{1,0:T(8,128)(2,1)S(1)}, bf16[512,128]{1,0:T(8,128)(2,1)S(1)}, u32[]{:S(2)}, u32[]{:S(2)}) %collective-permute-start.8) | collective-permute-done | bytes 131104 | tf_op jit(solution)/shard_map/ppermute | solution.py:11
  96.4 3.8 %collective-permute-done.9 = bf16[512,128]{1,0:T(8,128)(2,1)S(1)} collective-permute-done((bf16[512,128]{1,0:T(8,128)(2,1)S(1)}, bf16[512,128]{1,0:T(8,128)(2,1)S(1)}, u32[]{:S(2)}, u32[]{:S(2)}) %collective-permute-start.9) | collective-permute-done | bytes 131104 | tf_op jit(solution)/shard_map/ppermute | solution.py:11
  100.1 1.3 %collective-permute-done.10 = bf16[512,128]{1,0:T(8,128)(2,1)S(1)} collective-permute-done((bf16[512,128]{1,0:T(8,128)(2,1)S(1)}, bf16[512,128]{1,0:T(8,128)(2,1)S(1)}, u32[]{:S(2)}, u32[]{:S(2)}) %collective-permute-start.10) | collective-permute-done | bytes 131104 | tf_op jit(solution)/shard_map/ppermute | solution.py:11
  101.4 5.5 %collective-permute-done.7 = bf16[512,128]{1,0:T(8,128)(2,1)S(1)} collective-permute-done((bf16[512,128]{1,0:T(8,128)(2,1)S(1)}, bf16[512,128]{1,0:T(8,128)(2,1)S(1)}, u32[]{:S(2)}, u32[]{:S(2)}) %collective-permute-start.7) | collective-permute-done | bytes 131104 | tf_op jit(solution)/shard_map/ppermute | solution.py:11
  106.9 0.8 fusion.5
  107.7 0.6 all-gather.3.cloned.1.call-done
  108.3 1.4 %fusion.10 = f32[1,136,256]{2,1,0:T(8,128)S(1)} fusion(f32[1088,256]{1,0:T(8,128)} %all-gather.3.cloned.1.call-done), kind=kLoop, calls=%fused_computation.19 | loop fusion | flops 243712 | bytes 1253376 | tf_op jit(solution)/shard_map/add | solution.py:150
  109.7 0.6 slice_multiply_fusion.1
  110.2 0.7 fusion.11
  (7 shorter events, 0.1 us)
Async XLA Ops:
  7.2 47.4 %copy-start = (bf16[128,256]{1,0:T(8,128)(2,1)S(1)}, bf16[128,256]{1,0:T(8,128)(2,1)}, u32[]{:S(2)}) copy-start(bf16[128,256]{1,0:T(8,128)(2,1)} %param.15) | copy-start | bytes 196612
  7.2 101.1 %all-gather.3.cloned.1.call-start = ((), (), s32[]{:S(2)}) async-start(), calls=%async_computation | async-start | bytes 1253376 | tf_op jit(solution)/shard_map/all_gather | solution.py:147
  9.0 16.5 %collective-permute-start.2 = (bf16[512,128]{1,0:T(8,128)(2,1)S(1)}, bf16[512,128]{1,0:T(8,128)(2,1)S(1)}, u32[]{:S(2)}, u32[]{:S(2)}) collective-permute-start(bf16[512,128]{1,0:T(8,128)(2,1)S(1)} %multiply_convert_fusion.1), channel_id=1, source_target_pairs={{0,28},{4,0},{8,4},{12,8},{16,12},{20,16},{24,20},{28,24},{1,29},{... | collective-permute-start | bytes 393224 | tf_op jit(solution)/shard_map/ppermute | solution.py:11
  15.0 10.5 %collective-permute-start.3 = (bf16[512,128]{1,0:T(8,128)(2,1)S(1)}, bf16[512,128]{1,0:T(8,128)(2,1)S(1)}, u32[]{:S(2)}, u32[]{:S(2)}) collective-permute-start(bf16[512,128]{1,0:T(8,128)(2,1)S(1)} %multiply_convert_fusion.1), channel_id=1, source_target_pairs={{0,24},{4,28},{8,0},{12,4},{16,8},{20,12},{24,16},{28,20},{1,25},{... | collective-permute-start | bytes 393224 | tf_op jit(solution)/shard_map/ppermute | solution.py:11
  15.5 8.9 %collective-permute-start.1 = (bf16[512,128]{1,0:T(8,128)(2,1)S(1)}, bf16[512,128]{1,0:T(8,128)(2,1)S(1)}, u32[]{:S(2)}, u32[]{:S(2)}) collective-permute-start(bf16[512,128]{1,0:T(8,128)(2,1)S(1)} %multiply_convert_fusion.1), channel_id=1, source_target_pairs={{0,4},{4,8},{8,12},{12,16},{16,20},{20,24},{24,28},{28,0},{1,5},{5... | collective-permute-start | bytes 393224 | tf_op jit(solution)/shard_map/ppermute | solution.py:11
  16.1 8.2 %collective-permute-start = (bf16[512,128]{1,0:T(8,128)(2,1)S(1)}, bf16[512,128]{1,0:T(8,128)(2,1)S(1)}, u32[]{:S(2)}, u32[]{:S(2)}) collective-permute-start(bf16[512,128]{1,0:T(8,128)(2,1)S(1)} %multiply_convert_fusion.1), channel_id=1, source_target_pairs={{0,8},{4,12},{8,16},{12,20},{16,24},{20,28},{24,0},{28,4},{1,9},{5... | collective-permute-start | bytes 393224 | tf_op jit(solution)/shard_map/ppermute | solution.py:11
  25.5 0.9 copy-start.1
  38.9 15.7 %copy-start.2 = (bf16[512,256]{1,0:T(8,128)(2,1)S(1)}, bf16[512,256]{1,0:T(8,128)(2,1)}, u32[]{:S(2)}) copy-start(bf16[512,256]{1,0:T(8,128)(2,1)} %param.17) | copy-start | bytes 786436
  38.9 15.7 %copy-start.3 = (f32[256]{0:T(256)S(1)}, f32[256]{0:T(256)}, u32[]{:S(2)}) copy-start(f32[256]{0:T(256)} %param.16) | copy-start | bytes 3076
  40.3 6.8 %collective-permute-start.6 = (f32[512,128]{1,0:T(8,128)S(1)}, f32[512,128]{1,0:T(8,128)S(1)}, u32[]{:S(2)}, u32[]{:S(2)}) collective-permute-start(f32[512,128]{1,0:T(8,128)S(1)} %bitcast.62), channel_id=1, source_target_pairs={{0,3},{1,0},{2,1},{3,2},{4,7},{5,4},{6,5},{7,6},{8,11},{9,8},{10,9... | collective-permute-start | bytes 786440 | tf_op jit(solution)/shard_map/ppermute | solution.py:11
  40.3 13.9 %collective-permute-start.5 = (f32[512,128]{1,0:T(8,128)S(1)}, f32[512,128]{1,0:T(8,128)S(1)}, u32[]{:S(2)}, u32[]{:S(2)}) collective-permute-start(f32[512,128]{1,0:T(8,128)S(1)} %bitcast.61), channel_id=1, source_target_pairs={{0,2},{1,3},{2,0},{3,1},{4,6},{5,7},{6,4},{7,5},{8,10},{9,11},{10,... | collective-permute-start | bytes 786440 | tf_op jit(solution)/shard_map/ppermute | solution.py:11
  41.7 12.8 %collective-permute-start.4 = (f32[512,128]{1,0:T(8,128)S(1)}, f32[512,128]{1,0:T(8,128)S(1)}, u32[]{:S(2)}, u32[]{:S(2)}) collective-permute-start(f32[512,128]{1,0:T(8,128)S(1)} %bitcast.60), channel_id=1, source_target_pairs={{0,1},{1,2},{2,3},{3,0},{4,5},{5,6},{6,7},{7,4},{8,9},{9,10},{10,1... | collective-permute-start | bytes 786440 | tf_op jit(solution)/shard_map/ppermute | solution.py:11
  56.1 1.4 %collective-permute-start.11 = (f32[136,256]{1,0:T(8,128)S(1)}, f32[136,256]{1,0:T(8,128)S(1)}, u32[]{:S(2)}, u32[]{:S(2)}) collective-permute-start(f32[136,256]{1,0:T(8,128)S(1)} %maximum_maximum_fusion), channel_id=1, source_target_pairs={{0,1},{1,0},{2,3},{3,2},{4,5},{5,4},{6,7},{7,6},{8,9},{9,8},{10,11... | collective-permute-start | bytes 417800 | tf_op jit(solution)/shard_map/ppermute | solution.py:101
  57.6 5.8 %collective-permute-start.12 = (f32[136,256]{1,0:T(8,128)S(1)}, f32[136,256]{1,0:T(8,128)S(1)}, u32[]{:S(2)}, u32[]{:S(2)}) collective-permute-start(f32[136,256]{1,0:T(8,128)S(1)} %fusion.16), channel_id=1, source_target_pairs={{0,2},{1,3},{2,0},{3,1},{4,6},{5,7},{6,4},{7,5},{8,10},{9,11},{10,... | collective-permute-start | bytes 417800 | tf_op jit(solution)/shard_map/ppermute | solution.py:101
  86.5 9.8 %collective-permute-start.8 = (bf16[512,128]{1,0:T(8,128)(2,1)S(1)}, bf16[512,128]{1,0:T(8,128)(2,1)S(1)}, u32[]{:S(2)}, u32[]{:S(2)}) collective-permute-start(bf16[512,128]{1,0:T(8,128)(2,1)S(1)} %bitcast.66), channel_id=1, source_target_pairs={{0,28},{4,0},{8,4},{12,8},{16,12},{20,16},{24,20},{28,24},{1,29},{... | collective-permute-start | bytes 393224 | tf_op jit(solution)/shard_map/ppermute | solution.py:11
  89.0 11.1 %collective-permute-start.9 = (bf16[512,128]{1,0:T(8,128)(2,1)S(1)}, bf16[512,128]{1,0:T(8,128)(2,1)S(1)}, u32[]{:S(2)}, u32[]{:S(2)}) collective-permute-start(bf16[512,128]{1,0:T(8,128)(2,1)S(1)} %bitcast.65), channel_id=1, source_target_pairs={{0,4},{4,8},{8,12},{12,16},{16,20},{20,24},{24,28},{28,0},{1,5},{5... | collective-permute-start | bytes 393224 | tf_op jit(solution)/shard_map/ppermute | solution.py:11
  89.0 12.4 %collective-permute-start.10 = (bf16[512,128]{1,0:T(8,128)(2,1)S(1)}, bf16[512,128]{1,0:T(8,128)(2,1)S(1)}, u32[]{:S(2)}, u32[]{:S(2)}) collective-permute-start(bf16[512,128]{1,0:T(8,128)(2,1)S(1)} %bitcast.64), channel_id=1, source_target_pairs={{0,8},{4,12},{8,16},{12,20},{16,24},{20,28},{24,0},{28,4},{1,9},{5... | collective-permute-start | bytes 393224 | tf_op jit(solution)/shard_map/ppermute | solution.py:11
  90.4 16.5 %collective-permute-start.7 = (bf16[512,128]{1,0:T(8,128)(2,1)S(1)}, bf16[512,128]{1,0:T(8,128)(2,1)S(1)}, u32[]{:S(2)}, u32[]{:S(2)}) collective-permute-start(bf16[512,128]{1,0:T(8,128)(2,1)S(1)} %bitcast.63), channel_id=1, source_target_pairs={{0,24},{4,28},{8,0},{12,4},{16,8},{20,12},{24,16},{28,20},{1,25},{... | collective-permute-start | bytes 393224 | tf_op jit(solution)/shard_map/ppermute | solution.py:11
Sparse Core Ops, SparseCore 0:
  64.2 44.0 all-gather.2

commit v8 on v6

--- a/solution.py
+++ b/solution.py
@@ -96,10 +96,10 @@
         size *= lax.axis_size(axis)
     if size & (size - 1):
         return lax.psum(value, axes)
-    bit = 1
-    while bit < size:
+    bit = size // 2
+    while bit >= 1:
         value = value + lax.ppermute(value, axes, [(i, i ^ bit) for i in range(size)])
-        bit *= 2
+        bit //= 2
     return value
 
 

time: 100 us -> 95.1 us (0.951)
  waiting for transfers between devices: 29.9 us -> 25.5 us
  Pallas kernels: 22.1 us -> 26.3 us
  starting transfers between devices: 23.7 us -> 19.6 us
    pallas_call x2, Pallas kernels: 22.1 us -> 26.3 us  [tile_products(): pl.pallas_call(kernel, grid_spec=pltpu.PrefetchScalarGridSpec(num_scalar_...]
    ppermute x5, waiting for transfers between devices: 6.72 us -> 3.62 us  [all_sum(): lax.ppermute(value, axes, [(i, i ^ bit) for i in range(size)])]
    ppermute x11, starting transfers between devices: 17.9 us -> 15.2 us  [from_behind(): lax.ppermute(value, axis, [(i, (i + by) % length) for i in range(length)])]
    ppermute x5, starting transfers between devices: 5.85 us -> 4.36 us  [all_sum(): lax.ppermute(value, axes, [(i, i ^ bit) for i in range(size)])]
    ppermute x11, waiting for transfers between devices: 23.1 us -> 21.9 us  [from_behind(): lax.ppermute(value, axis, [(i, (i + by) % length) for i in range(length)])]
  transfers between devices with their start and end apart: 16 -> 16, of which waited for: 7 -> 6; matrix products, arithmetic and copies ran while one was open for 7% -> 8% of each run, Pallas kernels for 11% -> 14%
where the time goes in v8:
time: 95.1 us; the launch traced here: 94.2 us
  Pallas kernels  26.3 us (28%)
  waiting for transfers between devices  25.5 us (27%)
  starting transfers between devices  19.6 us (21%)
  other arithmetic  7.92 us (8%)
  blocking collectives  7.36 us (8%)
  local copies, waits for them, and re-layouts  5.01 us (5%)
  matrix products  1.57 us (2%)
    pallas_call x2, Pallas kernels, tile_products(): pl.pallas_call(kernel, grid_spec=pltpu.PrefetchScalarGridSpec(num_scalar_...  26.3 us
    ppermute x11, waiting for transfers between devices, from_behind(): lax.ppermute(value, axis, [(i, (i + by) % length) for i in range(length)])  21.9 us
    ppermute x11, starting transfers between devices, from_behind(): lax.ppermute(value, axis, [(i, (i + by) % length) for i in range(length)])  15.2 us
    all_gather x1, blocking collectives, local(): block_grad = lax.all_gather(grad_hidden, 'col', axis=0, tiled=True)  7.36 us
    ppermute x5, starting transfers between devices, all_sum(): lax.ppermute(value, axes, [(i, i ^ bit) for i in range(size)])  4.36 us
    ppermute x5, waiting for transfers between devices, all_sum(): lax.ppermute(value, axes, [(i, i ^ bit) for i in range(size)])  3.62 us
  transfers between devices with their start and end apart: 16, of which 6 were waited for; matrix products, arithmetic and copies ran while one was open for 8% of the time, Pallas kernels for 14%

profile of v8, /device:TPU:0, one launch (start us, length us, event | category | flops | bytes accessed | tf_op | source)
XLA Modules:
  0.0 94.2 jit_solution(5842224011023067936)
XLA Ops:
  0.6 0.0 copy-start
  0.6 0.7 convert_rsqrt_fusion
  1.4 1.0 %multiply_convert_fusion.1 = bf16[512,128]{1,0:T(8,128)(2,1)S(1)} fusion(bf16[512,128]{1,0:T(8,128)(2,1)} %param.9, f32[512]{0:T(512)S(1)} %convert_rsqrt_fusion), kind=kLoop, calls=%fused_computation.17 | loop fusion | flops 196608 | bytes 264192 | tf_op jit(solution)/shard_map/convert_element_type | solution.py:118
  2.4 6.1 %collective-permute-start.2 = (bf16[512,128]{1,0:T(8,128)(2,1)S(1)}, bf16[512,128]{1,0:T(8,128)(2,1)S(1)}, u32[]{:S(2)}, u32[]{:S(2)}) collective-permute-start(bf16[512,128]{1,0:T(8,128)(2,1)S(1)} %multiply_convert_fusion.1), channel_id=1, source_target_pairs={{0,28},{4,0},{8,4},{12,8},{16,12},{20,16},{24,20},{28,24},{1,29},{... | collective-permute-start | bytes 393224 | tf_op jit(solution)/shard_map/ppermute | solution.py:11
  8.5 0.4 collective-permute-start.3
  8.9 0.6 collective-permute-start.1
  9.6 0.9 collective-permute-start
  10.5 1.3 %add_select_fusion.rows_ref = s32[360]{0:T(512)} fusion(s32[360]{0:T(512)} %rows_ref.1, s32[]{:T(128)S(6)} %mul.57), kind=kLoop, calls=%fused_computation.28 | loop fusion | flops 4320 | bytes 2884 | tf_op jit(solution)/shard_map/jit(remainder)/select_n | solution.py:125
  11.8 6.0 %collective-permute-done = bf16[512,128]{1,0:T(8,128)(2,1)S(1)} collective-permute-done((bf16[512,128]{1,0:T(8,128)(2,1)S(1)}, bf16[512,128]{1,0:T(8,128)(2,1)S(1)}, u32[]{:S(2)}, u32[]{:S(2)}) %collective-permute-start) | collective-permute-done | bytes 131104 | tf_op jit(solution)/shard_map/ppermute | solution.py:11
  17.8 0.0 collective-permute-done.1
  17.8 1.1 %bitcast_dynamic-update-slice_fusion.2 = bf16[5,512,128]{2,1,0:T(8,128)(2,1)S(1)} fusion(bf16[5,512,128]{2,1,0:T(8,128)(2,1)S(1)} %bitcast_dynamic-update-slice_fusion.3, bf16[512,128]{1,0:T(8,128)(2,1)} %param.9, f32[512]{0:T(512)S(1)} %convert_rsqrt_fusion), kind=kLoop, calls=%fused_computation.22 | loop fusion | flops 196608 | bytes 264192
  18.9 0.0 collective-permute-done.2
  19.0 0.0 collective-permute-done.3
  19.0 0.0 copy-start.1
  19.0 0.8 copy-done.1
  19.8 13.1 %shard_map.120 = f32[16,128,128]{2,1,0:T(8,128)} custom-call(s32[360]{0:T(512)} %add_select_fusion.rows_ref, s32[360]{0:T(512)} %cols_ref.3, s32[5]{0:T(128)} %counts_ref.3, bf16[360,128,128]{2,1,0:T(8,128)(2,1)} %adj_ref.3, bf16[20,128,128]{2,1,0:T(8,128)(2,1)} %bitcast.55), custom_call_target="tpu_custom_call" | custom-call | flops 1509949440 | bytes 13500416 | tf_op jit(solution)/shard_map/pallas_call | solution.py:73
  32.9 1.3 %fusion.16 = (f32[4,128,128]{2,1,0:T(8,128)S(1)}, f32[4,128,128]{2,1,0:T(8,128)S(1)}, f32[4,128,128]{2,1,0:T(8,128)S(1)}, f32[4,128,128]{2,1,0:T(8,128)S(1)}) fusion(f32[16,128,128]{2,1,0:T(8,128)} %shard_map.120), kind=kLoop, calls=%fused_computation.37 | loop fusion | bytes 2097152 | tf_op jit(solution)/shard_map/slice | solution.py:130
  34.2 0.1 collective-permute-start.6
  34.3 0.1 collective-permute-start.5
  34.4 0.4 collective-permute-start.4
  34.8 0.1 pad.2.clone
  34.9 6.1 %collective-permute-done.6 = f32[512,128]{1,0:T(8,128)S(1)} collective-permute-done((f32[512,128]{1,0:T(8,128)S(1)}, f32[512,128]{1,0:T(8,128)S(1)}, u32[]{:S(2)}, u32[]{:S(2)}) %collective-permute-start.6) | collective-permute-done | bytes 262176 | tf_op jit(solution)/shard_map/ppermute | solution.py:11
  41.0 5.4 %collective-permute-done.5 = f32[512,128]{1,0:T(8,128)S(1)} collective-permute-done((f32[512,128]{1,0:T(8,128)S(1)}, f32[512,128]{1,0:T(8,128)S(1)}, u32[]{:S(2)}, u32[]{:S(2)}) %collective-permute-start.5) | collective-permute-done | bytes 262176 | tf_op jit(solution)/shard_map/ppermute | solution.py:11
  46.4 0.3 collective-permute-done.4
  46.7 0.1 fusion.9
  46.9 0.0 copy-done
  46.9 0.0 copy-done.2
  46.9 0.0 copy-done.3
  46.9 1.1 %fusion.15 = (f32[256]{0:T(256)S(1)}, bf16[512,256]{1,0:T(8,128)(2,1)S(1)}, bf16[512,256]{1,0:T(8,128)(2,1)}) fusion(bf16[512,256]{1,0:T(8,128)(2,1)S(1)} %copy-done.2, f32[256]{0:T(256)S(1)} %copy-done.3, bf16[512,128]{1,0:T(8,128)(2,1)S(1)} %fusion.9, bf16[128,256]{1,0:T(8,128)(2,1)S(1)} %copy-done), kind=kOutput, calls=%fused_computation.36 | convolution fusion | flops 35389184 | bytes 985088 | tf_op jit(solution)/shard_map/dot_general | solution.py:134
  48.0 0.2 fusion.10
  48.3 0.2 fusion
  48.5 0.1 maximum_maximum_fusion
  48.6 3.5 %collective-permute-start.11 = (f32[136,256]{1,0:T(8,128)S(1)}, f32[136,256]{1,0:T(8,128)S(1)}, u32[]{:S(2)}, u32[]{:S(2)}) collective-permute-start(f32[136,256]{1,0:T(8,128)S(1)} %maximum_maximum_fusion), channel_id=1, source_target_pairs={{0,16},{1,17},{2,18},{3,19},{4,20},{5,21},{6,22},{7,23},{8,24},{9,... | collective-permute-start | bytes 417800 | tf_op jit(solution)/shard_map/ppermute | solution.py:101
  52.1 7.4 %all_gather.3 = bf16[2048,128]{1,0:T(8,128)(2,1)S(1)} all-gather(bf16[512,128]{1,0:T(8,128)(2,1)S(1)} %fusion), channel_id=1, replica_groups=mesh['blk'=8,'col'=4] {'col'}, dimensions={0}, use_global_device_ids=true | all-gather | bytes 655360 | tf_op jit(solution)/shard_map/all_gather | solution.py:154
  59.5 1.0 %copy.13 = bf16[16,128,128]{1,2,0:T(8,128)(2,1)} copy(bf16[16,128,128]{2,1,0:T(8,128)(2,1)S(1)} %bitcast.54) | data formatting | bytes 1048576 | tf_op jit(solution)/shard_map/reshape | solution.py:155
  60.5 0.0 collective-permute-done.11
  60.5 0.1 fusion.14
  60.6 0.1 collective-permute-start.12
  60.7 13.2 %shard_map.121 = f32[20,128,128]{2,1,0:T(8,128)} custom-call(s32[360]{0:T(512)} %rows_ref.1, s32[360]{0:T(512)} %cols_ref.3, s32[5]{0:T(128)} %counts_ref.3, bf16[360,128,128]{2,1,0:T(8,128)(2,1)} %adj_ref.3, bf16[16,128,128]{2,1,0:T(8,128)(2,1)} %bitcast.53), custom_call_target="tpu_custom_call" | custom-call | flops 1509949440 | bytes 13631488 | tf_op jit(solution)/shard_map/pallas_call | solution.py:73
  73.9 0.0 collective-permute-done.12
  73.9 0.1 collective-permute-start.13
  74.0 1.4 %bitcast_convert_fusion = bf16[20,128,128]{1,2,0:T(8,128)(2,1)S(1)} fusion(f32[20,128,128]{2,1,0:T(8,128)} %shard_map.121), kind=kLoop, calls=%fused_computation.34 | loop fusion | flops 327680 | bytes 1966080 | tf_op jit(solution)/shard_map/convert.3
  75.4 3.6 %collective-permute-done.13 = f32[136,256]{1,0:T(8,128)S(1)} collective-permute-done((f32[136,256]{1,0:T(8,128)S(1)}, f32[136,256]{1,0:T(8,128)S(1)}, u32[]{:S(2)}, u32[]{:S(2)}) %collective-permute-start.13) | collective-permute-done | bytes 139296 | tf_op jit(solution)/shard_map/ppermute | solution.py:101
  79.1 0.6 collective-permute-start.14
  79.7 0.1 copy.15
  79.8 0.1 copy.18
  80.0 0.1 copy.17
  80.1 0.1 copy.16
  80.3 2.8 %collective-permute-start.8 = (bf16[512,128]{1,0:T(8,128)(2,1)S(1)}, bf16[512,128]{1,0:T(8,128)(2,1)S(1)}, u32[]{:S(2)}, u32[]{:S(2)}) collective-permute-start(bf16[512,128]{1,0:T(8,128)(2,1)S(1)} %bitcast.62), channel_id=1, source_target_pairs={{0,28},{4,0},{8,4},{12,8},{16,12},{20,16},{24,20},{28,24},{1,29},{... | collective-permute-start | bytes 393224 | tf_op jit(solution)/shard_map/ppermute | solution.py:11
  83.0 0.0 collective-permute-start.9
  83.0 1.4 %collective-permute-start.10 = (bf16[512,128]{1,0:T(8,128)(2,1)S(1)}, bf16[512,128]{1,0:T(8,128)(2,1)S(1)}, u32[]{:S(2)}, u32[]{:S(2)}) collective-permute-start(bf16[512,128]{1,0:T(8,128)(2,1)S(1)} %bitcast.60), channel_id=1, source_target_pairs={{0,8},{4,12},{8,16},{12,20},{16,24},{20,28},{24,0},{28,4},{1,9},{5... | collective-permute-start | bytes 393224 | tf_op jit(solution)/shard_map/ppermute | solution.py:11
  84.5 2.4 %collective-permute-start.7 = (bf16[512,128]{1,0:T(8,128)(2,1)S(1)}, bf16[512,128]{1,0:T(8,128)(2,1)S(1)}, u32[]{:S(2)}, u32[]{:S(2)}) collective-permute-start(bf16[512,128]{1,0:T(8,128)(2,1)S(1)} %bitcast.59), channel_id=1, source_target_pairs={{0,24},{4,28},{8,0},{12,4},{16,8},{20,12},{24,16},{28,20},{1,25},{... | collective-permute-start | bytes 393224 | tf_op jit(solution)/shard_map/ppermute | solution.py:11
  86.9 1.0 %slice.61 = f32[4,128,128]{1,2,0:T(8,128)S(1)} slice(f32[20,128,128]{1,2,0:T(8,128)} %bitcast.52), slice={[8:12], [0:128], [0:128]} | slice | bytes 524288 | tf_op jit(solution)/shard_map/slice | solution.py:161
  87.8 0.1 copy.14
  88.0 0.0 collective-permute-done.14
  88.0 0.1 collective-permute-start.15
  88.1 0.0 collective-permute-done.8
  88.1 4.0 %collective-permute-done.9 = bf16[512,128]{1,0:T(8,128)(2,1)S(1)} collective-permute-done((bf16[512,128]{1,0:T(8,128)(2,1)S(1)}, bf16[512,128]{1,0:T(8,128)(2,1)S(1)}, u32[]{:S(2)}, u32[]{:S(2)}) %collective-permute-start.9) | collective-permute-done | bytes 131104 | tf_op jit(solution)/shard_map/ppermute | solution.py:11
  92.1 0.0 collective-permute-done.10
  92.1 0.0 collective-permute-done.7
  92.1 0.8 fusion.5
  92.9 0.0 collective-permute-done.15
  92.9 0.6 slice_multiply_fusion.1
  93.5 0.7 slice_multiply_fusion
  (12 shorter events, 0.2 us)
Async XLA Ops:
  0.6 46.2 %copy-start = (bf16[128,256]{1,0:T(8,128)(2,1)S(1)}, bf16[128,256]{1,0:T(8,128)(2,1)}, u32[]{:S(2)}) copy-start(bf16[128,256]{1,0:T(8,128)(2,1)} %param.15) | copy-start | bytes 196612
  2.4 16.5 %collective-permute-start.2 = (bf16[512,128]{1,0:T(8,128)(2,1)S(1)}, bf16[512,128]{1,0:T(8,128)(2,1)S(1)}, u32[]{:S(2)}, u32[]{:S(2)}) collective-permute-start(bf16[512,128]{1,0:T(8,128)(2,1)S(1)} %multiply_convert_fusion.1), channel_id=1, source_target_pairs={{0,28},{4,0},{8,4},{12,8},{16,12},{20,16},{24,20},{28,24},{1,29},{... | collective-permute-start | bytes 393224 | tf_op jit(solution)/shard_map/ppermute | solution.py:11
  8.5 10.5 %collective-permute-start.3 = (bf16[512,128]{1,0:T(8,128)(2,1)S(1)}, bf16[512,128]{1,0:T(8,128)(2,1)S(1)}, u32[]{:S(2)}, u32[]{:S(2)}) collective-permute-start(bf16[512,128]{1,0:T(8,128)(2,1)S(1)} %multiply_convert_fusion.1), channel_id=1, source_target_pairs={{0,24},{4,28},{8,0},{12,4},{16,8},{20,12},{24,16},{28,20},{1,25},{... | collective-permute-start | bytes 393224 | tf_op jit(solution)/shard_map/ppermute | solution.py:11
  8.9 8.9 %collective-permute-start.1 = (bf16[512,128]{1,0:T(8,128)(2,1)S(1)}, bf16[512,128]{1,0:T(8,128)(2,1)S(1)}, u32[]{:S(2)}, u32[]{:S(2)}) collective-permute-start(bf16[512,128]{1,0:T(8,128)(2,1)S(1)} %multiply_convert_fusion.1), channel_id=1, source_target_pairs={{0,4},{4,8},{8,12},{12,16},{16,20},{20,24},{24,28},{28,0},{1,5},{5... | collective-permute-start | bytes 393224 | tf_op jit(solution)/shard_map/ppermute | solution.py:11
  9.6 8.2 %collective-permute-start = (bf16[512,128]{1,0:T(8,128)(2,1)S(1)}, bf16[512,128]{1,0:T(8,128)(2,1)S(1)}, u32[]{:S(2)}, u32[]{:S(2)}) collective-permute-start(bf16[512,128]{1,0:T(8,128)(2,1)S(1)} %multiply_convert_fusion.1), channel_id=1, source_target_pairs={{0,8},{4,12},{8,16},{12,20},{16,24},{20,28},{24,0},{28,4},{1,9},{5... | collective-permute-start | bytes 393224 | tf_op jit(solution)/shard_map/ppermute | solution.py:11
  19.0 0.9 copy-start.1
  32.9 14.0 %copy-start.2 = (bf16[512,256]{1,0:T(8,128)(2,1)S(1)}, bf16[512,256]{1,0:T(8,128)(2,1)}, u32[]{:S(2)}) copy-start(bf16[512,256]{1,0:T(8,128)(2,1)} %param.17) | copy-start | bytes 786436
  32.9 14.0 %copy-start.3 = (f32[256]{0:T(256)S(1)}, f32[256]{0:T(256)}, u32[]{:S(2)}) copy-start(f32[256]{0:T(256)} %param.16) | copy-start | bytes 3076
  34.2 6.8 %collective-permute-start.6 = (f32[512,128]{1,0:T(8,128)S(1)}, f32[512,128]{1,0:T(8,128)S(1)}, u32[]{:S(2)}, u32[]{:S(2)}) collective-permute-start(f32[512,128]{1,0:T(8,128)S(1)} %bitcast.58), channel_id=1, source_target_pairs={{0,3},{1,0},{2,1},{3,2},{4,7},{5,4},{6,5},{7,6},{8,11},{9,8},{10,9... | collective-permute-start | bytes 786440 | tf_op jit(solution)/shard_map/ppermute | solution.py:11
  34.3 12.1 %collective-permute-start.5 = (f32[512,128]{1,0:T(8,128)S(1)}, f32[512,128]{1,0:T(8,128)S(1)}, u32[]{:S(2)}, u32[]{:S(2)}) collective-permute-start(f32[512,128]{1,0:T(8,128)S(1)} %bitcast.57), channel_id=1, source_target_pairs={{0,2},{1,3},{2,0},{3,1},{4,6},{5,7},{6,4},{7,5},{8,10},{9,11},{10,... | collective-permute-start | bytes 786440 | tf_op jit(solution)/shard_map/ppermute | solution.py:11
  34.4 12.3 %collective-permute-start.4 = (f32[512,128]{1,0:T(8,128)S(1)}, f32[512,128]{1,0:T(8,128)S(1)}, u32[]{:S(2)}, u32[]{:S(2)}) collective-permute-start(f32[512,128]{1,0:T(8,128)S(1)} %bitcast.56), channel_id=1, source_target_pairs={{0,1},{1,2},{2,3},{3,0},{4,5},{5,6},{6,7},{7,4},{8,9},{9,10},{10,1... | collective-permute-start | bytes 786440 | tf_op jit(solution)/shard_map/ppermute | solution.py:11
  48.6 11.9 %collective-permute-start.11 = (f32[136,256]{1,0:T(8,128)S(1)}, f32[136,256]{1,0:T(8,128)S(1)}, u32[]{:S(2)}, u32[]{:S(2)}) collective-permute-start(f32[136,256]{1,0:T(8,128)S(1)} %maximum_maximum_fusion), channel_id=1, source_target_pairs={{0,16},{1,17},{2,18},{3,19},{4,20},{5,21},{6,22},{7,23},{8,24},{9,... | collective-permute-start | bytes 417800 | tf_op jit(solution)/shard_map/ppermute | solution.py:101
  60.6 13.3 %collective-permute-start.12 = (f32[136,256]{1,0:T(8,128)S(1)}, f32[136,256]{1,0:T(8,128)S(1)}, u32[]{:S(2)}, u32[]{:S(2)}) collective-permute-start(f32[136,256]{1,0:T(8,128)S(1)} %fusion.14), channel_id=1, source_target_pairs={{0,8},{1,9},{2,10},{3,11},{4,12},{5,13},{6,14},{7,15},{8,0},{9,1},... | collective-permute-start | bytes 417800 | tf_op jit(solution)/shard_map/ppermute | solution.py:101
  73.9 5.1 %collective-permute-start.13 = (f32[136,256]{1,0:T(8,128)S(1)}, f32[136,256]{1,0:T(8,128)S(1)}, u32[]{:S(2)}, u32[]{:S(2)}) collective-permute-start(f32[136,256]{1,0:T(8,128)S(1)} %add.69), channel_id=1, source_target_pairs={{0,4},{1,5},{2,6},{3,7},{4,0},{5,1},{6,2},{7,3},{8,12},{9,13},{10,... | collective-permute-start | bytes 417800 | tf_op jit(solution)/shard_map/ppermute | solution.py:101
  79.1 8.9 %collective-permute-start.14 = (f32[136,256]{1,0:T(8,128)S(1)}, f32[136,256]{1,0:T(8,128)S(1)}, u32[]{:S(2)}, u32[]{:S(2)}) collective-permute-start(f32[136,256]{1,0:T(8,128)S(1)} %add.70), channel_id=1, source_target_pairs={{0,2},{1,3},{2,0},{3,1},{4,6},{5,7},{6,4},{7,5},{8,10},{9,11},{10,... | collective-permute-start | bytes 417800 | tf_op jit(solution)/shard_map/ppermute | solution.py:101
  80.3 7.8 %collective-permute-start.8 = (bf16[512,128]{1,0:T(8,128)(2,1)S(1)}, bf16[512,128]{1,0:T(8,128)(2,1)S(1)}, u32[]{:S(2)}, u32[]{:S(2)}) collective-permute-start(bf16[512,128]{1,0:T(8,128)(2,1)S(1)} %bitcast.62), channel_id=1, source_target_pairs={{0,28},{4,0},{8,4},{12,8},{16,12},{20,16},{24,20},{28,24},{1,29},{... | collective-permute-start | bytes 393224 | tf_op jit(solution)/shard_map/ppermute | solution.py:11
  83.0 9.1 %collective-permute-start.9 = (bf16[512,128]{1,0:T(8,128)(2,1)S(1)}, bf16[512,128]{1,0:T(8,128)(2,1)S(1)}, u32[]{:S(2)}, u32[]{:S(2)}) collective-permute-start(bf16[512,128]{1,0:T(8,128)(2,1)S(1)} %bitcast.61), channel_id=1, source_target_pairs={{0,4},{4,8},{8,12},{12,16},{16,20},{20,24},{24,28},{28,0},{1,5},{5... | collective-permute-start | bytes 393224 | tf_op jit(solution)/shard_map/ppermute | solution.py:11
  83.0 9.1 %collective-permute-start.10 = (bf16[512,128]{1,0:T(8,128)(2,1)S(1)}, bf16[512,128]{1,0:T(8,128)(2,1)S(1)}, u32[]{:S(2)}, u32[]{:S(2)}) collective-permute-start(bf16[512,128]{1,0:T(8,128)(2,1)S(1)} %bitcast.60), channel_id=1, source_target_pairs={{0,8},{4,12},{8,16},{12,20},{16,24},{20,28},{24,0},{28,4},{1,9},{5... | collective-permute-start | bytes 393224 | tf_op jit(solution)/shard_map/ppermute | solution.py:11
  84.5 7.6 %collective-permute-start.7 = (bf16[512,128]{1,0:T(8,128)(2,1)S(1)}, bf16[512,128]{1,0:T(8,128)(2,1)S(1)}, u32[]{:S(2)}, u32[]{:S(2)}) collective-permute-start(bf16[512,128]{1,0:T(8,128)(2,1)S(1)} %bitcast.59), channel_id=1, source_target_pairs={{0,24},{4,28},{8,0},{12,4},{16,8},{20,12},{24,16},{28,20},{1,25},{... | collective-permute-start | bytes 393224 | tf_op jit(solution)/shard_map/ppermute | solution.py:11
  88.0 4.9 %collective-permute-start.15 = (f32[136,256]{1,0:T(8,128)S(1)}, f32[136,256]{1,0:T(8,128)S(1)}, u32[]{:S(2)}, u32[]{:S(2)}) collective-permute-start(f32[136,256]{1,0:T(8,128)S(1)} %add.71), channel_id=1, source_target_pairs={{0,1},{1,0},{2,3},{3,2},{4,5},{5,4},{6,7},{7,6},{8,9},{9,8},{10,11... | collective-permute-start | bytes 417800 | tf_op jit(solution)/shard_map/ppermute | solution.py:101

commit v9 on v8

--- a/solution.py
+++ b/solution.py
@@ -129,7 +129,8 @@
     pieces = block_sums.reshape(col_count, own_rows, features)
     sums = pieces[0]
     for shift in range(1, col_count):
-        sums = sums + from_behind(pieces[shift], "col", shift)
+        sent = pieces[shift].astype(jnp.bfloat16)
+        sums = sums + from_behind(sent, "col", shift).astype(jnp.float32)
     aggregated = (row_scale[:, None] * sums).astype(jnp.bfloat16)
     pre_act = jnp.dot(aggregated, weight, preferred_element_type=jnp.float32) + bias_vector
     gate_value = jax.nn.sigmoid(pre_act)

time: 95.1 us -> 89.2 us (0.938)
  waiting for transfers between devices: 25.5 us -> 18.7 us
  starting transfers between devices: 19.6 us -> 24.6 us
  Pallas kernels: 26.3 us -> 22.7 us
  other arithmetic: 7.92 us -> 9.3 us
  local copies, waits for them, and re-layouts: 5.01 us -> 3.76 us
    ppermute x11, waiting for transfers between devices: 21.9 us -> 15.8 us  [from_behind(): lax.ppermute(value, axis, [(i, (i + by) % length) for i in range(length)])]
    ppermute x11, starting transfers between devices: 15.2 us -> 19.2 us  [from_behind(): lax.ppermute(value, axis, [(i, (i + by) % length) for i in range(length)])]
    pallas_call x2, Pallas kernels: 26.3 us -> 22.7 us  [tile_products(): pl.pallas_call(kernel, grid_spec=pltpu.PrefetchScalarGridSpec(num_scalar_...]
    another operation x1 -> x2, other arithmetic: 1.42 us -> 2.8 us
    slice x1 -> x2, local copies, waits for them, and re-layouts: 1.32 us -> 0.01 us  [local(): sums = pieces[0]]
    ppermute x5, starting transfers between devices: 4.36 us -> 5.39 us  [all_sum(): lax.ppermute(value, axes, [(i, i ^ bit) for i in range(size)])]
  transfers between devices with their start and end apart: 16 -> 16, of which waited for: 6 -> 7; matrix products, arithmetic and copies ran while one was open for 8% -> 8% of each run, Pallas kernels for 14% -> 13%
where the time goes in v9:
time: 89.2 us; the launch traced here: 88.5 us
  starting transfers between devices  24.6 us (28%)
  Pallas kernels  22.7 us (25%)
  waiting for transfers between devices  18.7 us (21%)
  other arithmetic  9.3 us (10%)
  blocking collectives  6.99 us (8%)
  local copies, waits for them, and re-layouts  3.76 us (4%)
  matrix products  1.57 us (2%)
  between operations  0.9 us (1%)
    pallas_call x2, Pallas kernels, tile_products(): pl.pallas_call(kernel, grid_spec=pltpu.PrefetchScalarGridSpec(num_scalar_...  22.7 us
    ppermute x11, starting transfers between devices, from_behind(): lax.ppermute(value, axis, [(i, (i + by) % length) for i in range(length)])  19.2 us
    ppermute x11, waiting for transfers between devices, from_behind(): lax.ppermute(value, axis, [(i, (i + by) % length) for i in range(length)])  15.8 us
    all_gather x1, blocking collectives, local(): block_grad = lax.all_gather(grad_hidden, 'col', axis=0, tiled=True)  6.99 us
    ppermute x5, starting transfers between devices, all_sum(): lax.ppermute(value, axes, [(i, i ^ bit) for i in range(size)])  5.39 us
    ppermute x5, waiting for transfers between devices, all_sum(): lax.ppermute(value, axes, [(i, i ^ bit) for i in range(size)])  2.86 us
    another operation x2, other arithmetic  2.8 us
  transfers between devices with their start and end apart: 16, of which 7 were waited for; matrix products, arithmetic and copies ran while one was open for 8% of the time, Pallas kernels for 13%

profile of v9, /device:TPU:0, one launch (start us, length us, event | category | flops | bytes accessed | tf_op | source)
XLA Modules:
  0.0 88.5 jit_solution(223704127207133169)
XLA Ops:
  0.6 0.0 copy-start
  0.6 0.7 convert_rsqrt_fusion
  1.4 1.0 %multiply_convert_fusion.1 = bf16[512,128]{1,0:T(8,128)(2,1)S(1)} fusion(bf16[512,128]{1,0:T(8,128)(2,1)} %param.9, f32[512]{0:T(512)S(1)} %convert_rsqrt_fusion), kind=kLoop, calls=%fused_computation.17 | loop fusion | flops 196608 | bytes 264192 | tf_op jit(solution)/shard_map/convert_element_type | solution.py:118
  2.4 6.1 %collective-permute-start.2 = (bf16[512,128]{1,0:T(8,128)(2,1)S(1)}, bf16[512,128]{1,0:T(8,128)(2,1)S(1)}, u32[]{:S(2)}, u32[]{:S(2)}) collective-permute-start(bf16[512,128]{1,0:T(8,128)(2,1)S(1)} %multiply_convert_fusion.1), channel_id=1, source_target_pairs={{0,28},{4,0},{8,4},{12,8},{16,12},{20,16},{24,20},{28,24},{1,29},{... | collective-permute-start | bytes 393224 | tf_op jit(solution)/shard_map/ppermute | solution.py:11
  8.5 0.4 collective-permute-start.3
  8.9 0.6 collective-permute-start.1
  9.6 0.9 %collective-permute-start = (bf16[512,128]{1,0:T(8,128)(2,1)S(1)}, bf16[512,128]{1,0:T(8,128)(2,1)S(1)}, u32[]{:S(2)}, u32[]{:S(2)}) collective-permute-start(bf16[512,128]{1,0:T(8,128)(2,1)S(1)} %multiply_convert_fusion.1), channel_id=1, source_target_pairs={{0,8},{4,12},{8,16},{12,20},{16,24},{20,28},{24,0},{28,4},{1,9},{5... | collective-permute-start | bytes 393224 | tf_op jit(solution)/shard_map/ppermute | solution.py:11
  10.5 1.3 %add_select_fusion.rows_ref = s32[360]{0:T(512)} fusion(s32[360]{0:T(512)} %rows_ref.1, s32[]{:T(128)S(6)} %mul.57), kind=kLoop, calls=%fused_computation.28 | loop fusion | flops 4320 | bytes 2884 | tf_op jit(solution)/shard_map/jit(remainder)/select_n | solution.py:125
  11.8 6.0 %collective-permute-done = bf16[512,128]{1,0:T(8,128)(2,1)S(1)} collective-permute-done((bf16[512,128]{1,0:T(8,128)(2,1)S(1)}, bf16[512,128]{1,0:T(8,128)(2,1)S(1)}, u32[]{:S(2)}, u32[]{:S(2)}) %collective-permute-start) | collective-permute-done | bytes 131104 | tf_op jit(solution)/shard_map/ppermute | solution.py:11
  17.8 0.0 collective-permute-done.1
  17.8 1.1 %bitcast_dynamic-update-slice_fusion.2 = bf16[5,512,128]{2,1,0:T(8,128)(2,1)S(1)} fusion(bf16[5,512,128]{2,1,0:T(8,128)(2,1)S(1)} %bitcast_dynamic-update-slice_fusion.3, bf16[512,128]{1,0:T(8,128)(2,1)} %param.9, f32[512]{0:T(512)S(1)} %convert_rsqrt_fusion), kind=kLoop, calls=%fused_computation.22 | loop fusion | flops 196608 | bytes 264192
  18.9 0.0 collective-permute-done.2
  19.0 0.0 collective-permute-done.3
  19.0 0.9 copy-done.1
  19.9 11.3 %shard_map.120 = f32[16,128,128]{2,1,0:T(8,128)} custom-call(s32[360]{0:T(512)} %add_select_fusion.rows_ref, s32[360]{0:T(512)} %cols_ref.3, s32[5]{0:T(128)} %counts_ref.3, bf16[360,128,128]{2,1,0:T(8,128)(2,1)} %adj_ref.3, bf16[20,128,128]{2,1,0:T(8,128)(2,1)} %bitcast.55), custom_call_target="tpu_custom_call" | custom-call | flops 1509949440 | bytes 13500416 | tf_op jit(solution)/shard_map/pallas_call | solution.py:73
  31.2 1.4 %convert.11 = bf16[16,128,128]{2,1,0:T(8,128)(2,1)S(1)} convert(f32[16,128,128]{2,1,0:T(8,128)} %shard_map.120) | non-fusion elementwise | flops 262144 | bytes 1572864 | tf_op jit(solution)/shard_map/convert.6
  32.6 0.0 copy-start.2
  32.6 0.0 copy-start.3
  32.6 1.3 %collective-permute-start.6 = (bf16[512,128]{1,0:T(8,128)(2,1)S(1)}, bf16[512,128]{1,0:T(8,128)(2,1)S(1)}, u32[]{:S(2)}, u32[]{:S(2)}) collective-permute-start(bf16[512,128]{1,0:T(8,128)(2,1)S(1)} %bitcast.62), channel_id=1, source_target_pairs={{0,3},{1,0},{2,1},{3,2},{4,7},{5,4},{6,5},{7,6},{8,11},{9,8},{10,9... | collective-permute-start | bytes 393224 | tf_op jit(solution)/shard_map/ppermute | solution.py:11
  33.9 0.0 collective-permute-start.4
  33.9 2.3 %collective-permute-start.5 = (bf16[512,128]{1,0:T(8,128)(2,1)S(1)}, bf16[512,128]{1,0:T(8,128)(2,1)S(1)}, u32[]{:S(2)}, u32[]{:S(2)}) collective-permute-start(bf16[512,128]{1,0:T(8,128)(2,1)S(1)} %bitcast.60), channel_id=1, source_target_pairs={{0,2},{1,3},{2,0},{3,1},{4,6},{5,7},{6,4},{7,5},{8,10},{9,11},{10,... | collective-permute-start | bytes 393224 | tf_op jit(solution)/shard_map/ppermute | solution.py:11
  36.2 0.1 pad.2.clone
  36.3 0.2 collective-permute-done.6
  36.5 3.2 %collective-permute-done.4 = bf16[512,128]{1,0:T(8,128)(2,1)S(1)} collective-permute-done((bf16[512,128]{1,0:T(8,128)(2,1)S(1)}, bf16[512,128]{1,0:T(8,128)(2,1)S(1)}, u32[]{:S(2)}, u32[]{:S(2)}) %collective-permute-start.4) | collective-permute-done | bytes 131104 | tf_op jit(solution)/shard_map/ppermute | solution.py:11
  39.6 3.0 %collective-permute-done.5 = bf16[512,128]{1,0:T(8,128)(2,1)S(1)} collective-permute-done((bf16[512,128]{1,0:T(8,128)(2,1)S(1)}, bf16[512,128]{1,0:T(8,128)(2,1)S(1)}, u32[]{:S(2)}, u32[]{:S(2)}) %collective-permute-start.5) | collective-permute-done | bytes 131104 | tf_op jit(solution)/shard_map/ppermute | solution.py:11
  42.6 0.1 fusion.9
  42.8 0.0 copy-done
  42.8 0.0 copy-done.2
  42.8 1.1 %fusion.15 = (f32[256]{0:T(256)S(1)}, bf16[512,256]{1,0:T(8,128)(2,1)S(1)}, bf16[512,256]{1,0:T(8,128)(2,1)}) fusion(bf16[512,256]{1,0:T(8,128)(2,1)S(1)} %copy-done.2, f32[256]{0:T(256)S(1)} %copy-done.3, bf16[512,128]{1,0:T(8,128)(2,1)S(1)} %fusion.9, bf16[128,256]{1,0:T(8,128)(2,1)S(1)} %copy-done), kind=kOutput, calls=%fused_computation.36 | convolution fusion | flops 35389184 | bytes 985088 | tf_op jit(solution)/shard_map/dot_general | solution.py:135
  43.9 0.2 fusion.10
  44.2 0.2 fusion
  44.4 0.1 maximum_maximum_fusion
  44.5 1.2 %collective-permute-start.11 = (f32[136,256]{1,0:T(8,128)S(1)}, f32[136,256]{1,0:T(8,128)S(1)}, u32[]{:S(2)}, u32[]{:S(2)}) collective-permute-start(f32[136,256]{1,0:T(8,128)S(1)} %maximum_maximum_fusion), channel_id=1, source_target_pairs={{0,16},{1,17},{2,18},{3,19},{4,20},{5,21},{6,22},{7,23},{8,24},{9,... | collective-permute-start | bytes 417800 | tf_op jit(solution)/shard_map/ppermute | solution.py:101
  45.7 7.0 %all_gather.3 = bf16[2048,128]{1,0:T(8,128)(2,1)S(1)} all-gather(bf16[512,128]{1,0:T(8,128)(2,1)S(1)} %fusion), channel_id=1, replica_groups=mesh['blk'=8,'col'=4] {'col'}, dimensions={0}, use_global_device_ids=true | all-gather | bytes 655360 | tf_op jit(solution)/shard_map/all_gather | solution.py:155
  52.7 1.0 %copy.13 = bf16[16,128,128]{1,2,0:T(8,128)(2,1)} copy(bf16[16,128,128]{2,1,0:T(8,128)(2,1)S(1)} %bitcast.54) | data formatting | bytes 1048576 | tf_op jit(solution)/shard_map/reshape | solution.py:156
  53.7 0.2 collective-permute-done.11
  53.9 0.1 fusion.14
  54.0 0.3 collective-permute-start.12
  54.4 11.4 %shard_map.121 = f32[20,128,128]{2,1,0:T(8,128)} custom-call(s32[360]{0:T(512)} %rows_ref.1, s32[360]{0:T(512)} %cols_ref.3, s32[5]{0:T(128)} %counts_ref.3, bf16[360,128,128]{2,1,0:T(8,128)(2,1)} %adj_ref.3, bf16[16,128,128]{2,1,0:T(8,128)(2,1)} %bitcast.53), custom_call_target="tpu_custom_call" | custom-call | flops 1509949440 | bytes 13631488 | tf_op jit(solution)/shard_map/pallas_call | solution.py:73
  65.8 0.0 collective-permute-done.12
  65.8 1.9 %collective-permute-start.13 = (f32[136,256]{1,0:T(8,128)S(1)}, f32[136,256]{1,0:T(8,128)S(1)}, u32[]{:S(2)}, u32[]{:S(2)}) collective-permute-start(f32[136,256]{1,0:T(8,128)S(1)} %add.69), channel_id=1, source_target_pairs={{0,4},{1,5},{2,6},{3,7},{4,0},{5,1},{6,2},{7,3},{8,12},{9,13},{10,... | collective-permute-start | bytes 417800 | tf_op jit(solution)/shard_map/ppermute | solution.py:101
  67.7 1.4 %bitcast_convert_fusion = bf16[20,128,128]{1,2,0:T(8,128)(2,1)S(1)} fusion(f32[20,128,128]{2,1,0:T(8,128)} %shard_map.121), kind=kLoop, calls=%fused_computation.34 | loop fusion | flops 327680 | bytes 1966080 | tf_op jit(solution)/shard_map/convert.3
  69.2 2.6 %collective-permute-done.13 = f32[136,256]{1,0:T(8,128)S(1)} collective-permute-done((f32[136,256]{1,0:T(8,128)S(1)}, f32[136,256]{1,0:T(8,128)S(1)}, u32[]{:S(2)}, u32[]{:S(2)}) %collective-permute-start.13) | collective-permute-done | bytes 139296 | tf_op jit(solution)/shard_map/ppermute | solution.py:101
  71.8 1.8 %collective-permute-start.14 = (f32[136,256]{1,0:T(8,128)S(1)}, f32[136,256]{1,0:T(8,128)S(1)}, u32[]{:S(2)}, u32[]{:S(2)}) collective-permute-start(f32[136,256]{1,0:T(8,128)S(1)} %add.70), channel_id=1, source_target_pairs={{0,2},{1,3},{2,0},{3,1},{4,6},{5,7},{6,4},{7,5},{8,10},{9,11},{10,... | collective-permute-start | bytes 417800 | tf_op jit(solution)/shard_map/ppermute | solution.py:101
  73.7 0.1 copy.15
  73.8 0.1 copy.18
  73.9 0.1 copy.17
  74.1 0.1 copy.16
  74.2 3.7 %collective-permute-start.8 = (bf16[512,128]{1,0:T(8,128)(2,1)S(1)}, bf16[512,128]{1,0:T(8,128)(2,1)S(1)}, u32[]{:S(2)}, u32[]{:S(2)}) collective-permute-start(bf16[512,128]{1,0:T(8,128)(2,1)S(1)} %bitcast.59), channel_id=1, source_target_pairs={{0,28},{4,0},{8,4},{12,8},{16,12},{20,16},{24,20},{28,24},{1,29},{... | collective-permute-start | bytes 393224 | tf_op jit(solution)/shard_map/ppermute | solution.py:11
  77.9 0.0 collective-permute-start.9
  77.9 0.1 collective-permute-start.10
  78.1 3.7 %collective-permute-start.7 = (bf16[512,128]{1,0:T(8,128)(2,1)S(1)}, bf16[512,128]{1,0:T(8,128)(2,1)S(1)}, u32[]{:S(2)}, u32[]{:S(2)}) collective-permute-start(bf16[512,128]{1,0:T(8,128)(2,1)S(1)} %bitcast.56), channel_id=1, source_target_pairs={{0,24},{4,28},{8,0},{12,4},{16,8},{20,12},{24,16},{28,20},{1,25},{... | collective-permute-start | bytes 393224 | tf_op jit(solution)/shard_map/ppermute | solution.py:11
  81.8 1.0 %slice.64 = f32[4,128,128]{1,2,0:T(8,128)S(1)} slice(f32[20,128,128]{1,2,0:T(8,128)} %bitcast.52), slice={[8:12], [0:128], [0:128]} | slice | bytes 524288 | tf_op jit(solution)/shard_map/slice | solution.py:162
  82.7 0.1 copy.14
  82.9 0.0 collective-permute-done.14
  82.9 0.1 collective-permute-start.15
  83.0 0.0 collective-permute-done.8
  83.0 3.4 %collective-permute-done.9 = bf16[512,128]{1,0:T(8,128)(2,1)S(1)} collective-permute-done((bf16[512,128]{1,0:T(8,128)(2,1)S(1)}, bf16[512,128]{1,0:T(8,128)(2,1)S(1)}, u32[]{:S(2)}, u32[]{:S(2)}) %collective-permute-start.9) | collective-permute-done | bytes 131104 | tf_op jit(solution)/shard_map/ppermute | solution.py:11
  86.4 0.0 collective-permute-done.10
  86.4 0.0 collective-permute-done.7
  86.4 0.8 fusion.5
  87.2 0.0 collective-permute-done.15
  87.2 0.6 slice_multiply_fusion.1
  87.8 0.7 slice_multiply_fusion
  (15 shorter events, 0.2 us)
Async XLA Ops:
  0.6 42.2 %copy-start = (bf16[128,256]{1,0:T(8,128)(2,1)S(1)}, bf16[128,256]{1,0:T(8,128)(2,1)}, u32[]{:S(2)}) copy-start(bf16[128,256]{1,0:T(8,128)(2,1)} %param.15) | copy-start | bytes 196612
  2.4 16.5 %collective-permute-start.2 = (bf16[512,128]{1,0:T(8,128)(2,1)S(1)}, bf16[512,128]{1,0:T(8,128)(2,1)S(1)}, u32[]{:S(2)}, u32[]{:S(2)}) collective-permute-start(bf16[512,128]{1,0:T(8,128)(2,1)S(1)} %multiply_convert_fusion.1), channel_id=1, source_target_pairs={{0,28},{4,0},{8,4},{12,8},{16,12},{20,16},{24,20},{28,24},{1,29},{... | collective-permute-start | bytes 393224 | tf_op jit(solution)/shard_map/ppermute | solution.py:11
  8.5 10.5 %collective-permute-start.3 = (bf16[512,128]{1,0:T(8,128)(2,1)S(1)}, bf16[512,128]{1,0:T(8,128)(2,1)S(1)}, u32[]{:S(2)}, u32[]{:S(2)}) collective-permute-start(bf16[512,128]{1,0:T(8,128)(2,1)S(1)} %multiply_convert_fusion.1), channel_id=1, source_target_pairs={{0,24},{4,28},{8,0},{12,4},{16,8},{20,12},{24,16},{28,20},{1,25},{... | collective-permute-start | bytes 393224 | tf_op jit(solution)/shard_map/ppermute | solution.py:11
  8.9 8.9 %collective-permute-start.1 = (bf16[512,128]{1,0:T(8,128)(2,1)S(1)}, bf16[512,128]{1,0:T(8,128)(2,1)S(1)}, u32[]{:S(2)}, u32[]{:S(2)}) collective-permute-start(bf16[512,128]{1,0:T(8,128)(2,1)S(1)} %multiply_convert_fusion.1), channel_id=1, source_target_pairs={{0,4},{4,8},{8,12},{12,16},{16,20},{20,24},{24,28},{28,0},{1,5},{5... | collective-permute-start | bytes 393224 | tf_op jit(solution)/shard_map/ppermute | solution.py:11
  9.6 8.2 %collective-permute-start = (bf16[512,128]{1,0:T(8,128)(2,1)S(1)}, bf16[512,128]{1,0:T(8,128)(2,1)S(1)}, u32[]{:S(2)}, u32[]{:S(2)}) collective-permute-start(bf16[512,128]{1,0:T(8,128)(2,1)S(1)} %multiply_convert_fusion.1), channel_id=1, source_target_pairs={{0,8},{4,12},{8,16},{12,20},{16,24},{20,28},{24,0},{28,4},{1,9},{5... | collective-permute-start | bytes 393224 | tf_op jit(solution)/shard_map/ppermute | solution.py:11
  19.0 0.9 copy-start.1
  31.2 11.5 %slice-start = ((f32[16,128,128]{2,1,0:T(8,128)}), f32[4,128,128]{2,1,0:T(8,128)S(1)}, s32[]{:S(2)}) async-start(f32[16,128,128]{2,1,0:T(8,128)} %shard_map.120), calls=%async_computation | async-start | bytes 524288 | tf_op jit(solution)/shard_map/slice | solution.py:130
  32.6 10.2 %copy-start.2 = (bf16[512,256]{1,0:T(8,128)(2,1)S(1)}, bf16[512,256]{1,0:T(8,128)(2,1)}, u32[]{:S(2)}) copy-start(bf16[512,256]{1,0:T(8,128)(2,1)} %param.17) | copy-start | bytes 786436
  32.6 10.2 %copy-start.3 = (f32[256]{0:T(256)S(1)}, f32[256]{0:T(256)}, u32[]{:S(2)}) copy-start(f32[256]{0:T(256)} %param.16) | copy-start | bytes 3076
  32.6 3.9 %collective-permute-start.6 = (bf16[512,128]{1,0:T(8,128)(2,1)S(1)}, bf16[512,128]{1,0:T(8,128)(2,1)S(1)}, u32[]{:S(2)}, u32[]{:S(2)}) collective-permute-start(bf16[512,128]{1,0:T(8,128)(2,1)S(1)} %bitcast.62), channel_id=1, source_target_pairs={{0,3},{1,0},{2,1},{3,2},{4,7},{5,4},{6,5},{7,6},{8,11},{9,8},{10,9... | collective-permute-start | bytes 393224 | tf_op jit(solution)/shard_map/ppermute | solution.py:11
  33.9 5.8 %collective-permute-start.4 = (bf16[512,128]{1,0:T(8,128)(2,1)S(1)}, bf16[512,128]{1,0:T(8,128)(2,1)S(1)}, u32[]{:S(2)}, u32[]{:S(2)}) collective-permute-start(bf16[512,128]{1,0:T(8,128)(2,1)S(1)} %bitcast.61), channel_id=1, source_target_pairs={{0,1},{1,2},{2,3},{3,0},{4,5},{5,6},{6,7},{7,4},{8,9},{9,10},{10,1... | collective-permute-start | bytes 393224 | tf_op jit(solution)/shard_map/ppermute | solution.py:11
  33.9 8.8 %collective-permute-start.5 = (bf16[512,128]{1,0:T(8,128)(2,1)S(1)}, bf16[512,128]{1,0:T(8,128)(2,1)S(1)}, u32[]{:S(2)}, u32[]{:S(2)}) collective-permute-start(bf16[512,128]{1,0:T(8,128)(2,1)S(1)} %bitcast.60), channel_id=1, source_target_pairs={{0,2},{1,3},{2,0},{3,1},{4,6},{5,7},{6,4},{7,5},{8,10},{9,11},{10,... | collective-permute-start | bytes 393224 | tf_op jit(solution)/shard_map/ppermute | solution.py:11
  44.5 9.5 %collective-permute-start.11 = (f32[136,256]{1,0:T(8,128)S(1)}, f32[136,256]{1,0:T(8,128)S(1)}, u32[]{:S(2)}, u32[]{:S(2)}) collective-permute-start(f32[136,256]{1,0:T(8,128)S(1)} %maximum_maximum_fusion), channel_id=1, source_target_pairs={{0,16},{1,17},{2,18},{3,19},{4,20},{5,21},{6,22},{7,23},{8,24},{9,... | collective-permute-start | bytes 417800 | tf_op jit(solution)/shard_map/ppermute | solution.py:101
  54.0 11.7 %collective-permute-start.12 = (f32[136,256]{1,0:T(8,128)S(1)}, f32[136,256]{1,0:T(8,128)S(1)}, u32[]{:S(2)}, u32[]{:S(2)}) collective-permute-start(f32[136,256]{1,0:T(8,128)S(1)} %fusion.14), channel_id=1, source_target_pairs={{0,8},{1,9},{2,10},{3,11},{4,12},{5,13},{6,14},{7,15},{8,0},{9,1},... | collective-permute-start | bytes 417800 | tf_op jit(solution)/shard_map/ppermute | solution.py:101
  65.8 6.0 %collective-permute-start.13 = (f32[136,256]{1,0:T(8,128)S(1)}, f32[136,256]{1,0:T(8,128)S(1)}, u32[]{:S(2)}, u32[]{:S(2)}) collective-permute-start(f32[136,256]{1,0:T(8,128)S(1)} %add.69), channel_id=1, source_target_pairs={{0,4},{1,5},{2,6},{3,7},{4,0},{5,1},{6,2},{7,3},{8,12},{9,13},{10,... | collective-permute-start | bytes 417800 | tf_op jit(solution)/shard_map/ppermute | solution.py:101
  71.8 11.1 %collective-permute-start.14 = (f32[136,256]{1,0:T(8,128)S(1)}, f32[136,256]{1,0:T(8,128)S(1)}, u32[]{:S(2)}, u32[]{:S(2)}) collective-permute-start(f32[136,256]{1,0:T(8,128)S(1)} %add.70), channel_id=1, source_target_pairs={{0,2},{1,3},{2,0},{3,1},{4,6},{5,7},{6,4},{7,5},{8,10},{9,11},{10,... | collective-permute-start | bytes 417800 | tf_op jit(solution)/shard_map/ppermute | solution.py:101
  74.2 8.8 %collective-permute-start.8 = (bf16[512,128]{1,0:T(8,128)(2,1)S(1)}, bf16[512,128]{1,0:T(8,128)(2,1)S(1)}, u32[]{:S(2)}, u32[]{:S(2)}) collective-permute-start(bf16[512,128]{1,0:T(8,128)(2,1)S(1)} %bitcast.59), channel_id=1, source_target_pairs={{0,28},{4,0},{8,4},{12,8},{16,12},{20,16},{24,20},{28,24},{1,29},{... | collective-permute-start | bytes 393224 | tf_op jit(solution)/shard_map/ppermute | solution.py:11
  77.9 8.5 %collective-permute-start.9 = (bf16[512,128]{1,0:T(8,128)(2,1)S(1)}, bf16[512,128]{1,0:T(8,128)(2,1)S(1)}, u32[]{:S(2)}, u32[]{:S(2)}) collective-permute-start(bf16[512,128]{1,0:T(8,128)(2,1)S(1)} %bitcast.58), channel_id=1, source_target_pairs={{0,4},{4,8},{8,12},{12,16},{16,20},{20,24},{24,28},{28,0},{1,5},{5... | collective-permute-start | bytes 393224 | tf_op jit(solution)/shard_map/ppermute | solution.py:11
  77.9 8.5 %collective-permute-start.10 = (bf16[512,128]{1,0:T(8,128)(2,1)S(1)}, bf16[512,128]{1,0:T(8,128)(2,1)S(1)}, u32[]{:S(2)}, u32[]{:S(2)}) collective-permute-start(bf16[512,128]{1,0:T(8,128)(2,1)S(1)} %bitcast.57), channel_id=1, source_target_pairs={{0,8},{4,12},{8,16},{12,20},{16,24},{20,28},{24,0},{28,4},{1,9},{5... | collective-permute-start | bytes 393224 | tf_op jit(solution)/shard_map/ppermute | solution.py:11
  78.1 8.3 %collective-permute-start.7 = (bf16[512,128]{1,0:T(8,128)(2,1)S(1)}, bf16[512,128]{1,0:T(8,128)(2,1)S(1)}, u32[]{:S(2)}, u32[]{:S(2)}) collective-permute-start(bf16[512,128]{1,0:T(8,128)(2,1)S(1)} %bitcast.56), channel_id=1, source_target_pairs={{0,24},{4,28},{8,0},{12,4},{16,8},{20,12},{24,16},{28,20},{1,25},{... | collective-permute-start | bytes 393224 | tf_op jit(solution)/shard_map/ppermute | solution.py:11
  82.9 4.3 %collective-permute-start.15 = (f32[136,256]{1,0:T(8,128)S(1)}, f32[136,256]{1,0:T(8,128)S(1)}, u32[]{:S(2)}, u32[]{:S(2)}) collective-permute-start(f32[136,256]{1,0:T(8,128)S(1)} %add.71), channel_id=1, source_target_pairs={{0,1},{1,0},{2,3},{3,2},{4,5},{5,4},{6,7},{7,6},{8,9},{9,8},{10,11... | collective-permute-start | bytes 417800 | tf_op jit(solution)/shard_map/ppermute | solution.py:101

commit v10 on v8

--- a/solution.py
+++ b/solution.py
@@ -15,7 +15,7 @@
     return max(c for c in range(1, limit + 1) if slot_count % c == 0)
 
 
-def tile_products(rows, cols, counts, adjacency, operand, out_tiles, own_tiles, forward):
+def tile_products(rows, cols, counts, adjacency, operand, out_tiles, own_tiles, forward, keep):
     offset_count = counts.shape[0]
     slot_count = adjacency.shape[0] // offset_count
     tile = adjacency.shape[1]
@@ -26,7 +26,10 @@
 
     group = slot_chunk(chunk, 24)
 
-    def kernel(rows_ref, cols_ref, counts_ref, adj_ref, opnd_ref, out_ref, prod_ref):
+    kept = list(range(keep * own_tiles, (keep + 1) * own_tiles))
+    sent = [t for t in range(out_tiles) if t not in kept]
+
+    def kernel(rows_ref, cols_ref, counts_ref, adj_ref, opnd_ref, kept_ref, sent_ref, out_ref, prod_ref):
         k = pl.program_id(0)
         j = pl.program_id(1)
 
@@ -61,6 +64,14 @@
                 target = rows_ref[g] if forward else k * own_tiles + cols_ref[g]
                 out_ref[target] += prod_ref[i]
 
+        @pl.when((k == offset_count - 1) & (j == chunks - 1))
+        def _():
+            for place, t in enumerate(kept):
+                kept_ref[place] = out_ref[t] if forward else out_ref[t].T
+            for place, t in enumerate(sent):
+                value = out_ref[t] if forward else out_ref[t].T
+                sent_ref[place] = value.astype(sent_ref.dtype)
+
     def adj_map(k, j, rows_ref, cols_ref, counts_ref):
         last = jnp.maximum(counts_ref[k] - 1, 0) // chunk
         return (k * chunks + jnp.minimum(j, last), 0, 0)
@@ -79,10 +90,19 @@
                 pl.BlockSpec((chunk, tile, tile), adj_map),
                 pl.BlockSpec(operand.shape, whole_map),
             ],
-            out_specs=pl.BlockSpec((out_tiles, tile, out_width), whole_map),
-            scratch_shapes=[pltpu.VMEM((chunk, tile, out_width), jnp.float32)],
+            out_specs=[
+                pl.BlockSpec((len(kept), tile, out_width), whole_map),
+                pl.BlockSpec((len(sent), tile, out_width), whole_map),
+            ],
+            scratch_shapes=[
+                pltpu.VMEM((out_tiles, tile, out_width), jnp.float32),
+                pltpu.VMEM((chunk, tile, out_width), jnp.float32),
+            ],
         ),
-        out_shape=jax.ShapeDtypeStruct((out_tiles, tile, out_width), jnp.float32),
+        out_shape=[
+            jax.ShapeDtypeStruct((len(kept), tile, out_width), jnp.float32),
+            jax.ShapeDtypeStruct((len(sent), tile, out_width), jnp.bfloat16),
+        ],
         compiler_params=pltpu.CompilerParams(dimension_semantics=("arbitrary", "arbitrary")),
         cost_estimate=pl.CostEstimate(
             flops=flops, transcendentals=0, bytes_accessed=bytes_accessed
@@ -123,13 +143,13 @@
     source_tiles = jnp.stack(fetched).reshape(offset_count * own_tiles, tile_size, features)
     col_index = lax.axis_index("col")
     rows_here = (tile_rows - col_index * own_tiles) % block_tiles
-    block_sums = tile_products(
-        rows_here, tile_cols, counts, adjacency, source_tiles, block_tiles, own_tiles, True
-    )
-    pieces = block_sums.reshape(col_count, own_rows, features)
-    sums = pieces[0]
+    own_sums, sent_sums = tile_products(
+        rows_here, tile_cols, counts, adjacency, source_tiles, block_tiles, own_tiles, True, 0
+    )
+    sums = own_sums.reshape(own_rows, features)
+    sent_sums = sent_sums.reshape(col_count - 1, own_rows, features)
     for shift in range(1, col_count):
-        sums = sums + from_behind(pieces[shift], "col", shift)
+        sums = sums + from_behind(sent_sums[shift - 1], "col", shift).astype(jnp.float32)
     aggregated = (row_scale[:, None] * sums).astype(jnp.bfloat16)
     pre_act = jnp.dot(aggregated, weight, preferred_element_type=jnp.float32) + bias_vector
     gate_value = jax.nn.sigmoid(pre_act)
@@ -153,16 +173,18 @@
     grad_hidden = (row_scale[:, None] * grad_rows).astype(jnp.bfloat16)
     block_grad = lax.all_gather(grad_hidden, "col", axis=0, tiled=True)
     grad_tiles_t = jnp.swapaxes(block_grad.reshape(block_tiles, tile_size, features), 1, 2)
-    outgoing_t = tile_products(
+    own_back, sent_back = tile_products(
         tile_rows, tile_cols, counts, adjacency, grad_tiles_t, offset_count * own_tiles,
-        own_tiles, False,
-    )
-    outgoing = jnp.swapaxes(outgoing_t, 1, 2).reshape(offset_count, own_rows, features)
-    total_back = outgoing[reach_steps]
+        own_tiles, False, reach_steps,
+    )
+    total_back = own_back.reshape(own_rows, features)
+    sent_back = sent_back.reshape(offset_count - 1, own_rows, features)
+    place = 0
     for k in range(offset_count):
         if k != reach_steps:
-            sent = outgoing[k].astype(jnp.bfloat16)
-            total_back = total_back + from_behind(sent, "blk", k - reach_steps).astype(jnp.float32)
+            received = from_behind(sent_back[place], "blk", k - reach_steps)
+            total_back = total_back + received.astype(jnp.float32)
+            place += 1
     grad_features = (row_scale[:, None] * total_back).astype(jnp.bfloat16)
     return (activations, grad_features, weight_sum * norm_factor, bias_sum * norm_factor)
 

time: 95.1 us -> 92.2 us (0.970)
  starting transfers between devices: 19.6 us -> 24.8 us
  Pallas kernels: 26.3 us -> 22.7 us
  waiting for transfers between devices: 25.5 us -> 22.5 us
    ppermute x11, waiting for transfers between devices: 21.9 us -> 15 us  [from_behind(): lax.ppermute(value, axis, [(i, (i + by) % length) for i in range(length)])]
    ppermute x5, waiting for transfers between devices: 3.62 us -> 7.5 us  [all_sum(): lax.ppermute(value, axes, [(i, i ^ bit) for i in range(size)])]
    pallas_call x2, Pallas kernels: 26.3 us -> 22.7 us  [tile_products(): pl.pallas_call(kernel, grid_spec=pltpu.PrefetchScalarGridSpec(num_scalar_...]
    ppermute x11, starting transfers between devices: 15.2 us -> 18.6 us  [from_behind(): lax.ppermute(value, axis, [(i, (i + by) % length) for i in range(length)])]
    ppermute x5, starting transfers between devices: 4.36 us -> 6.23 us  [all_sum(): lax.ppermute(value, axes, [(i, i ^ bit) for i in range(size)])]
    another operation x1 -> x0, other arithmetic: 1.42 us -> none
    convert_element_type x1, other arithmetic: 0.79 us -> 1.75 us  [local(): grad_features = (row_scale[:, None] * total_back).astype(jnp.bfloat16)]
    slice x8 -> x2, local copies, waits for them, and re-layouts: 2.99 us -> 2.18 us  [the longest x1 1.13 us: local(): received = from_behind(sent_back[place], 'blk', k - reach_steps)]
  transfers between devices with their start and end apart: 16 -> 16, of which waited for: 6 -> 8; matrix products, arithmetic and copies ran while one was open for 8% -> 7% of each run, Pallas kernels for 14% -> 13%
where the time goes in v10:
time: 92.2 us; the launch traced here: 91.6 us
  starting transfers between devices  24.8 us (27%)
  Pallas kernels  22.7 us (25%)
  waiting for transfers between devices  22.5 us (24%)
  other arithmetic  8.43 us (9%)
  blocking collectives  6.56 us (7%)
  local copies, waits for them, and re-layouts  4.23 us (5%)
  matrix products  1.57 us (2%)
    pallas_call x2, Pallas kernels, tile_products(): pl.pallas_call(kernel, grid_spec=pltpu.PrefetchScalarGridSpec(num_scalar_...  22.7 us
    ppermute x11, starting transfers between devices, from_behind(): lax.ppermute(value, axis, [(i, (i + by) % length) for i in range(length)])  18.6 us
    ppermute x11, waiting for transfers between devices, from_behind(): lax.ppermute(value, axis, [(i, (i + by) % length) for i in range(length)])  15 us
    ppermute x5, waiting for transfers between devices, all_sum(): lax.ppermute(value, axes, [(i, i ^ bit) for i in range(size)])  7.5 us
    all_gather x1, blocking collectives, local(): block_grad = lax.all_gather(grad_hidden, 'col', axis=0, tiled=True)  6.56 us
    ppermute x5, starting transfers between devices, all_sum(): lax.ppermute(value, axes, [(i, i ^ bit) for i in range(size)])  6.23 us
  transfers between devices with their start and end apart: 16, of which 8 were waited for; matrix products, arithmetic and copies ran while one was open for 7% of the time, Pallas kernels for 13%

profile of v10, /device:TPU:0, one launch (start us, length us, event | category | flops | bytes accessed | tf_op | source)
XLA Modules:
  0.0 91.6 jit_solution(15423183434205155198)
XLA Ops:
  0.6 0.0 copy-start
  0.6 0.0 copy-start.3
  0.7 0.0 copy-start.2
  0.7 0.7 convert_rsqrt_fusion
  1.4 1.0 %multiply_convert_fusion.1 = bf16[512,128]{1,0:T(8,128)(2,1)S(1)} fusion(bf16[512,128]{1,0:T(8,128)(2,1)} %param.9, f32[512]{0:T(512)S(1)} %convert_rsqrt_fusion), kind=kLoop, calls=%fused_computation.17 | loop fusion | flops 196608 | bytes 264192 | tf_op jit(solution)/shard_map/convert_element_type | solution.py:138
  2.4 3.1 %collective-permute-start = (bf16[512,128]{1,0:T(8,128)(2,1)S(1)}, bf16[512,128]{1,0:T(8,128)(2,1)S(1)}, u32[]{:S(2)}, u32[]{:S(2)}) collective-permute-start(bf16[512,128]{1,0:T(8,128)(2,1)S(1)} %multiply_convert_fusion.1), channel_id=1, source_target_pairs={{0,8},{4,12},{8,16},{12,20},{16,24},{20,28},{24,0},{28,4},{1,9},{5... | collective-permute-start | bytes 393224 | tf_op jit(solution)/shard_map/ppermute | solution.py:11
  5.5 1.5 %collective-permute-start.1 = (bf16[512,128]{1,0:T(8,128)(2,1)S(1)}, bf16[512,128]{1,0:T(8,128)(2,1)S(1)}, u32[]{:S(2)}, u32[]{:S(2)}) collective-permute-start(bf16[512,128]{1,0:T(8,128)(2,1)S(1)} %multiply_convert_fusion.1), channel_id=1, source_target_pairs={{0,4},{4,8},{8,12},{12,16},{16,20},{20,24},{24,28},{28,0},{1,5},{5... | collective-permute-start | bytes 393224 | tf_op jit(solution)/shard_map/ppermute | solution.py:11
  7.0 3.2 %collective-permute-start.2 = (bf16[512,128]{1,0:T(8,128)(2,1)S(1)}, bf16[512,128]{1,0:T(8,128)(2,1)S(1)}, u32[]{:S(2)}, u32[]{:S(2)}) collective-permute-start(bf16[512,128]{1,0:T(8,128)(2,1)S(1)} %multiply_convert_fusion.1), channel_id=1, source_target_pairs={{0,28},{4,0},{8,4},{12,8},{16,12},{20,16},{24,20},{28,24},{1,29},{... | collective-permute-start | bytes 393224 | tf_op jit(solution)/shard_map/ppermute | solution.py:11
  10.3 0.3 collective-permute-start.3
  10.6 1.3 %add_select_fusion.rows_ref = s32[360]{0:T(512)} fusion(s32[360]{0:T(512)} %rows_ref.1, s32[]{:T(128)S(6)} %mul.57), kind=kLoop, calls=%fused_computation.28 | loop fusion | flops 4320 | bytes 2884 | tf_op jit(solution)/shard_map/jit(remainder)/select_n | solution.py:145
  11.8 0.0 collective-permute-done
  11.8 4.1 %collective-permute-done.1 = bf16[512,128]{1,0:T(8,128)(2,1)S(1)} collective-permute-done((bf16[512,128]{1,0:T(8,128)(2,1)S(1)}, bf16[512,128]{1,0:T(8,128)(2,1)S(1)}, u32[]{:S(2)}, u32[]{:S(2)}) %collective-permute-start.1) | collective-permute-done | bytes 131104 | tf_op jit(solution)/shard_map/ppermute | solution.py:11
  15.9 1.1 %bitcast_dynamic-update-slice_fusion.2 = bf16[5,512,128]{2,1,0:T(8,128)(2,1)S(1)} fusion(bf16[5,512,128]{2,1,0:T(8,128)(2,1)S(1)} %bitcast_dynamic-update-slice_fusion.3, bf16[512,128]{1,0:T(8,128)(2,1)} %param.9, f32[512]{0:T(512)S(1)} %convert_rsqrt_fusion), kind=kLoop, calls=%fused_computation.22 | loop fusion | flops 196608 | bytes 264192
  17.0 0.0 collective-permute-done.2
  17.0 0.0 collective-permute-done.3
  17.1 0.0 copy-start.1
  17.1 0.9 copy-done.1
  18.0 11.2 %shard_map.120 = (f32[4,128,128]{2,1,0:T(8,128)}, bf16[12,128,128]{2,1,0:T(8,128)(2,1)}) custom-call(s32[360]{0:T(512)} %add_select_fusion.rows_ref, s32[360]{0:T(512)} %cols_ref.3, s32[5]{0:T(128)} %counts_ref.3, bf16[360,128,128]{2,1,0:T(8,128)(2,1)} %adj_ref.3, bf16[20,128,128]{2,1,0:T(8,128)(2,1)} %bitcast.52), custom_call_target="tpu_custom_call" | custom-call | flops 1509949440 | bytes 13500416 | tf_op jit(solution)/shard_map/pallas_call | solution.py:84
  29.2 1.1 %fusion.17 = (bf16[4,128,128]{2,1,0:T(8,128)(2,1)S(1)}, bf16[4,128,128]{2,1,0:T(8,128)(2,1)S(1)}, bf16[4,128,128]{2,1,0:T(8,128)(2,1)S(1)}) fusion(bf16[12,128,128]{2,1,0:T(8,128)(2,1)} %get-tuple-element.9), kind=kLoop, calls=%fused_computation.37 | loop fusion | bytes 786432 | tf_op jit(solution)/shard_map/slice | solution.py:152
  30.2 0.6 collective-permute-start.4
  30.8 2.5 %collective-permute-start.5 = (bf16[512,128]{1,0:T(8,128)(2,1)S(1)}, bf16[512,128]{1,0:T(8,128)(2,1)S(1)}, u32[]{:S(2)}, u32[]{:S(2)}) collective-permute-start(bf16[512,128]{1,0:T(8,128)(2,1)S(1)} %bitcast.54), channel_id=1, source_target_pairs={{0,2},{1,3},{2,0},{3,1},{4,6},{5,7},{6,4},{7,5},{8,10},{9,11},{10,... | collective-permute-start | bytes 393224 | tf_op jit(solution)/shard_map/ppermute | solution.py:11
  33.4 1.4 %collective-permute-start.6 = (bf16[512,128]{1,0:T(8,128)(2,1)S(1)}, bf16[512,128]{1,0:T(8,128)(2,1)S(1)}, u32[]{:S(2)}, u32[]{:S(2)}) collective-permute-start(bf16[512,128]{1,0:T(8,128)(2,1)S(1)} %bitcast.53), channel_id=1, source_target_pairs={{0,3},{1,0},{2,1},{3,2},{4,7},{5,4},{6,5},{7,6},{8,11},{9,8},{10,9... | collective-permute-start | bytes 393224 | tf_op jit(solution)/shard_map/ppermute | solution.py:11
  34.7 0.1 pad.2.clone
  34.8 0.0 collective-permute-done.4
  34.8 2.4 %collective-permute-done.5 = bf16[512,128]{1,0:T(8,128)(2,1)S(1)} collective-permute-done((bf16[512,128]{1,0:T(8,128)(2,1)S(1)}, bf16[512,128]{1,0:T(8,128)(2,1)S(1)}, u32[]{:S(2)}, u32[]{:S(2)}) %collective-permute-start.5) | collective-permute-done | bytes 131104 | tf_op jit(solution)/shard_map/ppermute | solution.py:11
  37.2 2.2 %collective-permute-done.6 = bf16[512,128]{1,0:T(8,128)(2,1)S(1)} collective-permute-done((bf16[512,128]{1,0:T(8,128)(2,1)S(1)}, bf16[512,128]{1,0:T(8,128)(2,1)S(1)}, u32[]{:S(2)}, u32[]{:S(2)}) %collective-permute-start.6) | collective-permute-done | bytes 131104 | tf_op jit(solution)/shard_map/ppermute | solution.py:11
  39.4 1.1 %fusion.9 = bf16[512,128]{1,0:T(8,128)(2,1)S(1)} fusion(f32[4,128,128]{2,1,0:T(8,128)} %get-tuple-element.8, bf16[512,128]{1,0:T(8,128)(2,1)S(1)} %collective-permute-done.6, bf16[512,128]{1,0:T(8,128)(2,1)S(1)} %collective-permute-done.5, bf16[512,128]{1,0:T(8,128)(2,1)S(1)} %collective-permute-done.4, f32[512]{0:T(512)S(1)} %convert_rsqrt_fusion), kind=kLoop, calls=%fused_computation.16 | loop fusion | flops 524288 | bytes 788480 | tf_op jit(solution)/shard_map/convert_element_type | solution.py:153
  40.5 0.0 copy-done
  40.5 0.0 copy-done.3
  40.5 0.0 copy-done.2
  40.5 1.1 %fusion.15 = (f32[256]{0:T(256)S(1)}, bf16[512,256]{1,0:T(8,128)(2,1)S(1)}, bf16[512,256]{1,0:T(8,128)(2,1)}) fusion(bf16[512,256]{1,0:T(8,128)(2,1)S(1)} %copy-done.2, f32[256]{0:T(256)S(1)} %copy-done.3, bf16[512,128]{1,0:T(8,128)(2,1)S(1)} %fusion.9, bf16[128,256]{1,0:T(8,128)(2,1)S(1)} %copy-done), kind=kOutput, calls=%fused_computation.35 | convolution fusion | flops 35389184 | bytes 985088 | tf_op jit(solution)/shard_map/dot_general | solution.py:154
  41.6 0.2 fusion.10
  41.9 0.1 maximum_maximum_fusion
  42.0 1.9 %collective-permute-start.11 = (f32[136,256]{1,0:T(8,128)S(1)}, f32[136,256]{1,0:T(8,128)S(1)}, u32[]{:S(2)}, u32[]{:S(2)}) collective-permute-start(f32[136,256]{1,0:T(8,128)S(1)} %maximum_maximum_fusion), channel_id=1, source_target_pairs={{0,16},{1,17},{2,18},{3,19},{4,20},{5,21},{6,22},{7,23},{8,24},{9,... | collective-permute-start | bytes 417800 | tf_op jit(solution)/shard_map/ppermute | solution.py:121
  43.9 0.2 fusion
  44.1 7.5 %collective-permute-done.11 = f32[136,256]{1,0:T(8,128)S(1)} collective-permute-done((f32[136,256]{1,0:T(8,128)S(1)}, f32[136,256]{1,0:T(8,128)S(1)}, u32[]{:S(2)}, u32[]{:S(2)}) %collective-permute-start.11) | collective-permute-done | bytes 139296 | tf_op jit(solution)/shard_map/ppermute | solution.py:121
  51.6 0.1 fusion.14
  51.7 0.3 collective-permute-start.12
  52.0 6.6 %all_gather.3 = bf16[2048,128]{1,0:T(8,128)(2,1)S(1)} all-gather(bf16[512,128]{1,0:T(8,128)(2,1)S(1)} %fusion), channel_id=1, replica_groups=mesh['blk'=8,'col'=4] {'col'}, dimensions={0}, use_global_device_ids=true | all-gather | bytes 655360 | tf_op jit(solution)/shard_map/all_gather | solution.py:174
  58.6 1.0 %copy.13 = bf16[16,128,128]{1,2,0:T(8,128)(2,1)} copy(bf16[16,128,128]{2,1,0:T(8,128)(2,1)S(1)} %bitcast.51) | data formatting | bytes 1048576 | tf_op jit(solution)/shard_map/reshape | solution.py:175
  59.6 0.0 collective-permute-done.12
  59.6 1.7 %collective-permute-start.13 = (f32[136,256]{1,0:T(8,128)S(1)}, f32[136,256]{1,0:T(8,128)S(1)}, u32[]{:S(2)}, u32[]{:S(2)}) collective-permute-start(f32[136,256]{1,0:T(8,128)S(1)} %add.69), channel_id=1, source_target_pairs={{0,4},{1,5},{2,6},{3,7},{4,0},{5,1},{6,2},{7,3},{8,12},{9,13},{10,... | collective-permute-start | bytes 417800 | tf_op jit(solution)/shard_map/ppermute | solution.py:121
  61.3 11.5 %shard_map.121 = (f32[4,128,128]{2,1,0:T(8,128)}, bf16[16,128,128]{2,1,0:T(8,128)(2,1)}) custom-call(s32[360]{0:T(512)} %rows_ref.1, s32[360]{0:T(512)} %cols_ref.3, s32[5]{0:T(128)} %counts_ref.3, bf16[360,128,128]{2,1,0:T(8,128)(2,1)} %adj_ref.3, bf16[16,128,128]{2,1,0:T(8,128)(2,1)} %bitcast.50), custom_call_target="tpu_custom_call" | custom-call | flops 1509949440 | bytes 13631488 | tf_op jit(solution)/shard_map/pallas_call | solution.py:84
  72.7 0.0 collective-permute-done.13
  72.8 2.3 %collective-permute-start.14 = (f32[136,256]{1,0:T(8,128)S(1)}, f32[136,256]{1,0:T(8,128)S(1)}, u32[]{:S(2)}, u32[]{:S(2)}) collective-permute-start(f32[136,256]{1,0:T(8,128)S(1)} %add.70), channel_id=1, source_target_pairs={{0,2},{1,3},{2,0},{3,1},{4,6},{5,7},{6,4},{7,5},{8,10},{9,11},{10,... | collective-permute-start | bytes 417800 | tf_op jit(solution)/shard_map/ppermute | solution.py:121
  75.1 1.1 %fusion.16 = (bf16[4,128,128]{2,1,0:T(8,128)(2,1)S(1)}, bf16[4,128,128]{2,1,0:T(8,128)(2,1)S(1)}, bf16[4,128,128]{2,1,0:T(8,128)(2,1)S(1)}, bf16[4,128,128]{2,1,0:T(8,128)(2,1)S(1)}) fusion(bf16[16,128,128]{2,1,0:T(8,128)(2,1)} %get-tuple-element.11), kind=kLoop, calls=%fused_computation.36 | loop fusion | bytes 1048576 | tf_op jit(solution)/shard_map/slice | solution.py:185
  76.2 1.7 %collective-permute-start.10 = (bf16[512,128]{1,0:T(8,128)(2,1)S(1)}, bf16[512,128]{1,0:T(8,128)(2,1)S(1)}, u32[]{:S(2)}, u32[]{:S(2)}) collective-permute-start(bf16[512,128]{1,0:T(8,128)(2,1)S(1)} %bitcast.59), channel_id=1, source_target_pairs={{0,8},{4,12},{8,16},{12,20},{16,24},{20,28},{24,0},{28,4},{1,9},{5... | collective-permute-start | bytes 393224 | tf_op jit(solution)/shard_map/ppermute | solution.py:11
  77.9 2.1 %collective-permute-start.7 = (bf16[512,128]{1,0:T(8,128)(2,1)S(1)}, bf16[512,128]{1,0:T(8,128)(2,1)S(1)}, u32[]{:S(2)}, u32[]{:S(2)}) collective-permute-start(bf16[512,128]{1,0:T(8,128)(2,1)S(1)} %bitcast.58), channel_id=1, source_target_pairs={{0,24},{4,28},{8,0},{12,4},{16,8},{20,12},{24,16},{28,20},{1,25},{... | collective-permute-start | bytes 393224 | tf_op jit(solution)/shard_map/ppermute | solution.py:11
  80.1 0.8 collective-permute-start.8
  80.9 1.2 %collective-permute-start.9 = (bf16[512,128]{1,0:T(8,128)(2,1)S(1)}, bf16[512,128]{1,0:T(8,128)(2,1)S(1)}, u32[]{:S(2)}, u32[]{:S(2)}) collective-permute-start(bf16[512,128]{1,0:T(8,128)(2,1)S(1)} %bitcast.56), channel_id=1, source_target_pairs={{0,4},{4,8},{8,12},{12,16},{16,20},{20,24},{24,28},{28,0},{1,5},{5... | collective-permute-start | bytes 393224 | tf_op jit(solution)/shard_map/ppermute | solution.py:11
  82.1 0.0 collective-permute-done.14
  82.1 0.1 collective-permute-start.15
  82.2 2.2 %collective-permute-done.10 = bf16[512,128]{1,0:T(8,128)(2,1)S(1)} collective-permute-done((bf16[512,128]{1,0:T(8,128)(2,1)S(1)}, bf16[512,128]{1,0:T(8,128)(2,1)S(1)}, u32[]{:S(2)}, u32[]{:S(2)}) %collective-permute-start.10) | collective-permute-done | bytes 131104 | tf_op jit(solution)/shard_map/ppermute | solution.py:11
  84.4 1.3 %collective-permute-done.7 = bf16[512,128]{1,0:T(8,128)(2,1)S(1)} collective-permute-done((bf16[512,128]{1,0:T(8,128)(2,1)S(1)}, bf16[512,128]{1,0:T(8,128)(2,1)S(1)}, u32[]{:S(2)}, u32[]{:S(2)}) %collective-permute-start.7) | collective-permute-done | bytes 131104 | tf_op jit(solution)/shard_map/ppermute | solution.py:11
  85.7 0.3 collective-permute-done.8
  86.0 2.5 %collective-permute-done.9 = bf16[512,128]{1,0:T(8,128)(2,1)S(1)} collective-permute-done((bf16[512,128]{1,0:T(8,128)(2,1)S(1)}, bf16[512,128]{1,0:T(8,128)(2,1)S(1)}, u32[]{:S(2)}, u32[]{:S(2)}) %collective-permute-start.9) | collective-permute-done | bytes 131104 | tf_op jit(solution)/shard_map/ppermute | solution.py:11
  88.6 1.8 %fusion.5 = bf16[512,128]{1,0:T(8,128)(2,1)} fusion(f32[4,128,128]{2,1,0:T(8,128)} %get-tuple-element.10, bf16[512,128]{1,0:T(8,128)(2,1)S(1)} %collective-permute-done.10, bf16[512,128]{1,0:T(8,128)(2,1)S(1)} %collective-permute-done.9, bf16[512,128]{1,0:T(8,128)(2,1)S(1)} %collective-permute-done.8, bf16[512,128]{1,0:T(8,128)(2,1)S(1)} %collective-permute-done.7, ...), kind=kLoop, calls=%fused_computation.11 | loop fusion | flops 655360 | bytes 919552 | tf_op jit(solution)/shard_map/convert_element_type | solution.py:188
  90.3 0.0 collective-permute-done.15
  90.4 0.7 slice_multiply_fusion
  91.0 0.6 slice_multiply_fusion.1
  (9 shorter events, 0.2 us)
Async XLA Ops:
  0.6 39.9 %copy-start = (bf16[128,256]{1,0:T(8,128)(2,1)S(1)}, bf16[128,256]{1,0:T(8,128)(2,1)}, u32[]{:S(2)}) copy-start(bf16[128,256]{1,0:T(8,128)(2,1)} %param.15) | copy-start | bytes 196612
  0.6 39.9 %copy-start.3 = (f32[256]{0:T(256)S(1)}, f32[256]{0:T(256)}, u32[]{:S(2)}) copy-start(f32[256]{0:T(256)} %param.16) | copy-start | bytes 3076
  0.7 39.9 %copy-start.2 = (bf16[512,256]{1,0:T(8,128)(2,1)S(1)}, bf16[512,256]{1,0:T(8,128)(2,1)}, u32[]{:S(2)}) copy-start(bf16[512,256]{1,0:T(8,128)(2,1)} %param.17) | copy-start | bytes 786436
  2.4 9.4 %collective-permute-start = (bf16[512,128]{1,0:T(8,128)(2,1)S(1)}, bf16[512,128]{1,0:T(8,128)(2,1)S(1)}, u32[]{:S(2)}, u32[]{:S(2)}) collective-permute-start(bf16[512,128]{1,0:T(8,128)(2,1)S(1)} %multiply_convert_fusion.1), channel_id=1, source_target_pairs={{0,8},{4,12},{8,16},{12,20},{16,24},{20,28},{24,0},{28,4},{1,9},{5... | collective-permute-start | bytes 393224 | tf_op jit(solution)/shard_map/ppermute | solution.py:11
  5.5 10.4 %collective-permute-start.1 = (bf16[512,128]{1,0:T(8,128)(2,1)S(1)}, bf16[512,128]{1,0:T(8,128)(2,1)S(1)}, u32[]{:S(2)}, u32[]{:S(2)}) collective-permute-start(bf16[512,128]{1,0:T(8,128)(2,1)S(1)} %multiply_convert_fusion.1), channel_id=1, source_target_pairs={{0,4},{4,8},{8,12},{12,16},{16,20},{20,24},{24,28},{28,0},{1,5},{5... | collective-permute-start | bytes 393224 | tf_op jit(solution)/shard_map/ppermute | solution.py:11
  7.0 10.0 %collective-permute-start.2 = (bf16[512,128]{1,0:T(8,128)(2,1)S(1)}, bf16[512,128]{1,0:T(8,128)(2,1)S(1)}, u32[]{:S(2)}, u32[]{:S(2)}) collective-permute-start(bf16[512,128]{1,0:T(8,128)(2,1)S(1)} %multiply_convert_fusion.1), channel_id=1, source_target_pairs={{0,28},{4,0},{8,4},{12,8},{16,12},{20,16},{24,20},{28,24},{1,29},{... | collective-permute-start | bytes 393224 | tf_op jit(solution)/shard_map/ppermute | solution.py:11
  10.3 6.8 %collective-permute-start.3 = (bf16[512,128]{1,0:T(8,128)(2,1)S(1)}, bf16[512,128]{1,0:T(8,128)(2,1)S(1)}, u32[]{:S(2)}, u32[]{:S(2)}) collective-permute-start(bf16[512,128]{1,0:T(8,128)(2,1)S(1)} %multiply_convert_fusion.1), channel_id=1, source_target_pairs={{0,24},{4,28},{8,0},{12,4},{16,8},{20,12},{24,16},{28,20},{1,25},{... | collective-permute-start | bytes 393224 | tf_op jit(solution)/shard_map/ppermute | solution.py:11
  17.1 0.9 copy-start.1
  30.2 4.6 %collective-permute-start.4 = (bf16[512,128]{1,0:T(8,128)(2,1)S(1)}, bf16[512,128]{1,0:T(8,128)(2,1)S(1)}, u32[]{:S(2)}, u32[]{:S(2)}) collective-permute-start(bf16[512,128]{1,0:T(8,128)(2,1)S(1)} %bitcast.55), channel_id=1, source_target_pairs={{0,1},{1,2},{2,3},{3,0},{4,5},{5,6},{6,7},{7,4},{8,9},{9,10},{10,1... | collective-permute-start | bytes 393224 | tf_op jit(solution)/shard_map/ppermute | solution.py:11
  30.8 6.4 %collective-permute-start.5 = (bf16[512,128]{1,0:T(8,128)(2,1)S(1)}, bf16[512,128]{1,0:T(8,128)(2,1)S(1)}, u32[]{:S(2)}, u32[]{:S(2)}) collective-permute-start(bf16[512,128]{1,0:T(8,128)(2,1)S(1)} %bitcast.54), channel_id=1, source_target_pairs={{0,2},{1,3},{2,0},{3,1},{4,6},{5,7},{6,4},{7,5},{8,10},{9,11},{10,... | collective-permute-start | bytes 393224 | tf_op jit(solution)/shard_map/ppermute | solution.py:11
  33.4 6.0 %collective-permute-start.6 = (bf16[512,128]{1,0:T(8,128)(2,1)S(1)}, bf16[512,128]{1,0:T(8,128)(2,1)S(1)}, u32[]{:S(2)}, u32[]{:S(2)}) collective-permute-start(bf16[512,128]{1,0:T(8,128)(2,1)S(1)} %bitcast.53), channel_id=1, source_target_pairs={{0,3},{1,0},{2,1},{3,2},{4,7},{5,4},{6,5},{7,6},{8,11},{9,8},{10,9... | collective-permute-start | bytes 393224 | tf_op jit(solution)/shard_map/ppermute | solution.py:11
  42.0 9.6 %collective-permute-start.11 = (f32[136,256]{1,0:T(8,128)S(1)}, f32[136,256]{1,0:T(8,128)S(1)}, u32[]{:S(2)}, u32[]{:S(2)}) collective-permute-start(f32[136,256]{1,0:T(8,128)S(1)} %maximum_maximum_fusion), channel_id=1, source_target_pairs={{0,16},{1,17},{2,18},{3,19},{4,20},{5,21},{6,22},{7,23},{8,24},{9,... | collective-permute-start | bytes 417800 | tf_op jit(solution)/shard_map/ppermute | solution.py:121
  51.7 7.9 %collective-permute-start.12 = (f32[136,256]{1,0:T(8,128)S(1)}, f32[136,256]{1,0:T(8,128)S(1)}, u32[]{:S(2)}, u32[]{:S(2)}) collective-permute-start(f32[136,256]{1,0:T(8,128)S(1)} %fusion.14), channel_id=1, source_target_pairs={{0,8},{1,9},{2,10},{3,11},{4,12},{5,13},{6,14},{7,15},{8,0},{9,1},... | collective-permute-start | bytes 417800 | tf_op jit(solution)/shard_map/ppermute | solution.py:121
  59.6 13.1 %collective-permute-start.13 = (f32[136,256]{1,0:T(8,128)S(1)}, f32[136,256]{1,0:T(8,128)S(1)}, u32[]{:S(2)}, u32[]{:S(2)}) collective-permute-start(f32[136,256]{1,0:T(8,128)S(1)} %add.69), channel_id=1, source_target_pairs={{0,4},{1,5},{2,6},{3,7},{4,0},{5,1},{6,2},{7,3},{8,12},{9,13},{10,... | collective-permute-start | bytes 417800 | tf_op jit(solution)/shard_map/ppermute | solution.py:121
  72.8 9.3 %collective-permute-start.14 = (f32[136,256]{1,0:T(8,128)S(1)}, f32[136,256]{1,0:T(8,128)S(1)}, u32[]{:S(2)}, u32[]{:S(2)}) collective-permute-start(f32[136,256]{1,0:T(8,128)S(1)} %add.70), channel_id=1, source_target_pairs={{0,2},{1,3},{2,0},{3,1},{4,6},{5,7},{6,4},{7,5},{8,10},{9,11},{10,... | collective-permute-start | bytes 417800 | tf_op jit(solution)/shard_map/ppermute | solution.py:121
  76.2 8.2 %collective-permute-start.10 = (bf16[512,128]{1,0:T(8,128)(2,1)S(1)}, bf16[512,128]{1,0:T(8,128)(2,1)S(1)}, u32[]{:S(2)}, u32[]{:S(2)}) collective-permute-start(bf16[512,128]{1,0:T(8,128)(2,1)S(1)} %bitcast.59), channel_id=1, source_target_pairs={{0,8},{4,12},{8,16},{12,20},{16,24},{20,28},{24,0},{28,4},{1,9},{5... | collective-permute-start | bytes 393224 | tf_op jit(solution)/shard_map/ppermute | solution.py:11
  77.9 7.8 %collective-permute-start.7 = (bf16[512,128]{1,0:T(8,128)(2,1)S(1)}, bf16[512,128]{1,0:T(8,128)(2,1)S(1)}, u32[]{:S(2)}, u32[]{:S(2)}) collective-permute-start(bf16[512,128]{1,0:T(8,128)(2,1)S(1)} %bitcast.58), channel_id=1, source_target_pairs={{0,24},{4,28},{8,0},{12,4},{16,8},{20,12},{24,16},{28,20},{1,25},{... | collective-permute-start | bytes 393224 | tf_op jit(solution)/shard_map/ppermute | solution.py:11
  80.1 6.0 %collective-permute-start.8 = (bf16[512,128]{1,0:T(8,128)(2,1)S(1)}, bf16[512,128]{1,0:T(8,128)(2,1)S(1)}, u32[]{:S(2)}, u32[]{:S(2)}) collective-permute-start(bf16[512,128]{1,0:T(8,128)(2,1)S(1)} %bitcast.57), channel_id=1, source_target_pairs={{0,28},{4,0},{8,4},{12,8},{16,12},{20,16},{24,20},{28,24},{1,29},{... | collective-permute-start | bytes 393224 | tf_op jit(solution)/shard_map/ppermute | solution.py:11
  80.9 7.7 %collective-permute-start.9 = (bf16[512,128]{1,0:T(8,128)(2,1)S(1)}, bf16[512,128]{1,0:T(8,128)(2,1)S(1)}, u32[]{:S(2)}, u32[]{:S(2)}) collective-permute-start(bf16[512,128]{1,0:T(8,128)(2,1)S(1)} %bitcast.56), channel_id=1, source_target_pairs={{0,4},{4,8},{8,12},{12,16},{16,20},{20,24},{24,28},{28,0},{1,5},{5... | collective-permute-start | bytes 393224 | tf_op jit(solution)/shard_map/ppermute | solution.py:11
  82.1 8.2 %collective-permute-start.15 = (f32[136,256]{1,0:T(8,128)S(1)}, f32[136,256]{1,0:T(8,128)S(1)}, u32[]{:S(2)}, u32[]{:S(2)}) collective-permute-start(f32[136,256]{1,0:T(8,128)S(1)} %add.71), channel_id=1, source_target_pairs={{0,1},{1,0},{2,3},{3,2},{4,5},{5,4},{6,7},{7,6},{8,9},{9,8},{10,11... | collective-permute-start | bytes 417800 | tf_op jit(solution)/shard_map/ppermute | solution.py:121

commit v11 on v10

--- a/solution.py
+++ b/solution.py
@@ -171,10 +171,12 @@
         grad_low, weight, (((1,), (1,)), ((), ())), preferred_element_type=jnp.float32
     )
     grad_hidden = (row_scale[:, None] * grad_rows).astype(jnp.bfloat16)
-    block_grad = lax.all_gather(grad_hidden, "col", axis=0, tiled=True)
+    block_grad = jnp.concatenate(
+        [grad_hidden] + [from_behind(grad_hidden, "col", -shift) for shift in range(1, col_count)]
+    )
     grad_tiles_t = jnp.swapaxes(block_grad.reshape(block_tiles, tile_size, features), 1, 2)
     own_back, sent_back = tile_products(
-        tile_rows, tile_cols, counts, adjacency, grad_tiles_t, offset_count * own_tiles,
+        rows_here, tile_cols, counts, adjacency, grad_tiles_t, offset_count * own_tiles,
         own_tiles, False, reach_steps,
     )
     total_back = own_back.reshape(own_rows, features)

time: 92.2 us -> 91.2 us (0.989)
  blocking collectives: 6.56 us -> 0 us
  starting transfers between devices: 24.8 us -> 27.2 us
  waiting for transfers between devices: 22.5 us -> 24.6 us
  Pallas kernels: 22.7 us -> 24 us
    all_gather x1 -> x0, blocking collectives: 6.56 us -> none  [local(): block_grad = lax.all_gather(grad_hidden, 'col', axis=0, tiled=True)]
    ppermute x11 -> x14, starting transfers between devices: 18.6 us -> 23.1 us  [from_behind(): lax.ppermute(value, axis, [(i, (i + by) % length) for i in range(length)])]
    ppermute x11 -> x14, waiting for transfers between devices: 15 us -> 17.4 us  [from_behind(): lax.ppermute(value, axis, [(i, (i + by) % length) for i in range(length)])]
    ppermute x5, starting transfers between devices: 6.23 us -> 4.03 us  [all_sum(): lax.ppermute(value, axes, [(i, i ^ bit) for i in range(size)])]
    pallas_call x2, Pallas kernels: 22.7 us -> 24 us  [tile_products(): pl.pallas_call(kernel, grid_spec=pltpu.PrefetchScalarGridSpec(num_scalar_...]
  transfers between devices with their start and end apart: 16 -> 19, of which waited for: 8 -> 7; matrix products, arithmetic and copies ran while one was open for 7% -> 7% of each run, Pallas kernels for 13% -> 13%
where the time goes in v11:
time: 91.2 us; the launch traced here: 90.9 us
  starting transfers between devices  27.2 us (30%)
  waiting for transfers between devices  24.6 us (27%)
  Pallas kernels  24 us (26%)
  other arithmetic  8.47 us (9%)
  local copies, waits for them, and re-layouts  4.22 us (5%)
  matrix products  1.57 us (2%)
    pallas_call x2, Pallas kernels, tile_products(): pl.pallas_call(kernel, grid_spec=pltpu.PrefetchScalarGridSpec(num_scalar_...  24 us
    ppermute x14, starting transfers between devices, from_behind(): lax.ppermute(value, axis, [(i, (i + by) % length) for i in range(length)])  23.1 us
    ppermute x14, waiting for transfers between devices, from_behind(): lax.ppermute(value, axis, [(i, (i + by) % length) for i in range(length)])  17.4 us
    ppermute x5, waiting for transfers between devices, all_sum(): lax.ppermute(value, axes, [(i, i ^ bit) for i in range(size)])  7.18 us
    ppermute x5, starting transfers between devices, all_sum(): lax.ppermute(value, axes, [(i, i ^ bit) for i in range(size)])  4.03 us
  transfers between devices with their start and end apart: 19, of which 7 were waited for; matrix products, arithmetic and copies ran while one was open for 7% of the time, Pallas kernels for 13%

profile of v11, /device:TPU:0, one launch (start us, length us, event | category | flops | bytes accessed | tf_op | source)
XLA Modules:
  0.0 90.9 jit_solution(9874527682233869944)
XLA Ops:
  0.6 0.0 copy-start
  0.6 0.0 copy-start.2
  0.7 0.0 copy-start.3
  0.7 0.7 convert_rsqrt_fusion
  1.4 1.0 %multiply_convert_fusion.1 = bf16[512,128]{1,0:T(8,128)(2,1)S(1)} fusion(bf16[512,128]{1,0:T(8,128)(2,1)} %param.9, f32[512]{0:T(512)S(1)} %convert_rsqrt_fusion), kind=kLoop, calls=%fused_computation.18 | loop fusion | flops 196608 | bytes 264192 | tf_op jit(solution)/shard_map/convert_element_type | solution.py:138
  2.4 6.1 %collective-permute-start.2 = (bf16[512,128]{1,0:T(8,128)(2,1)S(1)}, bf16[512,128]{1,0:T(8,128)(2,1)S(1)}, u32[]{:S(2)}, u32[]{:S(2)}) collective-permute-start(bf16[512,128]{1,0:T(8,128)(2,1)S(1)} %multiply_convert_fusion.1), channel_id=1, source_target_pairs={{0,28},{4,0},{8,4},{12,8},{16,12},{20,16},{24,20},{28,24},{1,29},{... | collective-permute-start | bytes 393224 | tf_op jit(solution)/shard_map/ppermute | solution.py:11
  8.5 0.4 collective-permute-start.3
  8.9 0.6 collective-permute-start.1
  9.6 0.9 %collective-permute-start = (bf16[512,128]{1,0:T(8,128)(2,1)S(1)}, bf16[512,128]{1,0:T(8,128)(2,1)S(1)}, u32[]{:S(2)}, u32[]{:S(2)}) collective-permute-start(bf16[512,128]{1,0:T(8,128)(2,1)S(1)} %multiply_convert_fusion.1), channel_id=1, source_target_pairs={{0,8},{4,12},{8,16},{12,20},{16,24},{20,28},{24,0},{28,4},{1,9},{5... | collective-permute-start | bytes 393224 | tf_op jit(solution)/shard_map/ppermute | solution.py:11
  10.5 1.3 %add_select_fusion.rows_ref = s32[360]{0:T(512)} fusion(s32[360]{0:T(512)} %param.12, s32[]{:T(128)S(6)} %mul.57), kind=kLoop, calls=%fused_computation.29 | loop fusion | flops 4320 | bytes 2884 | tf_op jit(solution)/shard_map/jit(remainder)/select_n | solution.py:145
  11.8 6.0 %collective-permute-done = bf16[512,128]{1,0:T(8,128)(2,1)S(1)} collective-permute-done((bf16[512,128]{1,0:T(8,128)(2,1)S(1)}, bf16[512,128]{1,0:T(8,128)(2,1)S(1)}, u32[]{:S(2)}, u32[]{:S(2)}) %collective-permute-start) | collective-permute-done | bytes 131104 | tf_op jit(solution)/shard_map/ppermute | solution.py:11
  17.8 0.0 collective-permute-done.1
  17.9 1.1 %bitcast_dynamic-update-slice_fusion.2 = bf16[5,512,128]{2,1,0:T(8,128)(2,1)S(1)} fusion(bf16[5,512,128]{2,1,0:T(8,128)(2,1)S(1)} %bitcast_dynamic-update-slice_fusion.3, bf16[512,128]{1,0:T(8,128)(2,1)} %param.9, f32[512]{0:T(512)S(1)} %convert_rsqrt_fusion), kind=kLoop, calls=%fused_computation.23 | loop fusion | flops 196608 | bytes 264192
  18.9 0.0 collective-permute-done.2
  19.0 0.0 collective-permute-done.3
  19.0 0.0 copy-start.1
  19.0 0.8 copy-done.1
  19.9 11.9 %shard_map.120 = (f32[4,128,128]{2,1,0:T(8,128)}, bf16[12,128,128]{2,1,0:T(8,128)(2,1)}) custom-call(s32[360]{0:T(512)} %add_select_fusion.rows_ref, s32[360]{0:T(512)} %cols_ref.3, s32[5]{0:T(128)} %counts_ref.3, bf16[360,128,128]{2,1,0:T(8,128)(2,1)} %adj_ref.3, bf16[20,128,128]{2,1,0:T(8,128)(2,1)} %bitcast.52), custom_call_target="tpu_custom_call" | custom-call | flops 1509949440 | bytes 13500416 | tf_op jit(solution)/shard_map/pallas_call | solution.py:84
  31.8 1.1 %fusion.17 = (bf16[4,128,128]{2,1,0:T(8,128)(2,1)S(1)}, bf16[4,128,128]{2,1,0:T(8,128)(2,1)S(1)}, bf16[4,128,128]{2,1,0:T(8,128)(2,1)S(1)}) fusion(bf16[12,128,128]{2,1,0:T(8,128)(2,1)} %get-tuple-element.9), kind=kLoop, calls=%fused_computation.38 | loop fusion | bytes 786432 | tf_op jit(solution)/shard_map/slice | solution.py:152
  32.8 0.1 collective-permute-start.6
  32.9 0.4 collective-permute-start.4
  33.4 2.1 %collective-permute-start.5 = (bf16[512,128]{1,0:T(8,128)(2,1)S(1)}, bf16[512,128]{1,0:T(8,128)(2,1)S(1)}, u32[]{:S(2)}, u32[]{:S(2)}) collective-permute-start(bf16[512,128]{1,0:T(8,128)(2,1)S(1)} %bitcast.53), channel_id=1, source_target_pairs={{0,2},{1,3},{2,0},{3,1},{4,6},{5,7},{6,4},{7,5},{8,10},{9,11},{10,... | collective-permute-start | bytes 393224 | tf_op jit(solution)/shard_map/ppermute | solution.py:11
  35.5 0.1 pad.2.clone
  35.5 0.0 collective-permute-done.6
  35.5 3.4 %collective-permute-done.4 = bf16[512,128]{1,0:T(8,128)(2,1)S(1)} collective-permute-done((bf16[512,128]{1,0:T(8,128)(2,1)S(1)}, bf16[512,128]{1,0:T(8,128)(2,1)S(1)}, u32[]{:S(2)}, u32[]{:S(2)}) %collective-permute-start.4) | collective-permute-done | bytes 131104 | tf_op jit(solution)/shard_map/ppermute | solution.py:11
  38.9 3.0 %collective-permute-done.5 = bf16[512,128]{1,0:T(8,128)(2,1)S(1)} collective-permute-done((bf16[512,128]{1,0:T(8,128)(2,1)S(1)}, bf16[512,128]{1,0:T(8,128)(2,1)S(1)}, u32[]{:S(2)}, u32[]{:S(2)}) %collective-permute-start.5) | collective-permute-done | bytes 131104 | tf_op jit(solution)/shard_map/ppermute | solution.py:11
  41.9 1.1 %fusion.9 = bf16[512,128]{1,0:T(8,128)(2,1)S(1)} fusion(f32[4,128,128]{2,1,0:T(8,128)} %get-tuple-element.8, bf16[512,128]{1,0:T(8,128)(2,1)S(1)} %collective-permute-done.6, bf16[512,128]{1,0:T(8,128)(2,1)S(1)} %collective-permute-done.5, bf16[512,128]{1,0:T(8,128)(2,1)S(1)} %collective-permute-done.4, f32[512]{0:T(512)S(1)} %convert_rsqrt_fusion), kind=kLoop, calls=%fused_computation.17 | loop fusion | flops 524288 | bytes 788480 | tf_op jit(solution)/shard_map/convert_element_type | solution.py:153
  43.0 0.0 copy-done
  43.0 0.0 copy-done.2
  43.0 1.1 %fusion.15 = (f32[256]{0:T(256)S(1)}, bf16[512,256]{1,0:T(8,128)(2,1)S(1)}, bf16[512,256]{1,0:T(8,128)(2,1)}) fusion(bf16[512,256]{1,0:T(8,128)(2,1)S(1)} %copy-done.2, f32[256]{0:T(256)S(1)} %copy-done.3, bf16[512,128]{1,0:T(8,128)(2,1)S(1)} %fusion.9, bf16[128,256]{1,0:T(8,128)(2,1)S(1)} %copy-done), kind=kOutput, calls=%fused_computation.36 | convolution fusion | flops 35389184 | bytes 985088 | tf_op jit(solution)/shard_map/dot_general | solution.py:154
  44.2 0.2 fusion.10
  44.4 0.1 maximum_maximum_fusion
  44.5 1.8 %collective-permute-start.14 = (f32[136,256]{1,0:T(8,128)S(1)}, f32[136,256]{1,0:T(8,128)S(1)}, u32[]{:S(2)}, u32[]{:S(2)}) collective-permute-start(f32[136,256]{1,0:T(8,128)S(1)} %maximum_maximum_fusion), channel_id=1, source_target_pairs={{0,16},{1,17},{2,18},{3,19},{4,20},{5,21},{6,22},{7,23},{8,24},{9,... | collective-permute-start | bytes 417800 | tf_op jit(solution)/shard_map/ppermute | solution.py:121
  46.3 0.2 fusion
  46.5 0.4 collective-permute-start.9
  47.0 2.0 %collective-permute-start.8 = (bf16[512,128]{1,0:T(8,128)(2,1)S(1)}, bf16[512,128]{1,0:T(8,128)(2,1)S(1)}, u32[]{:S(2)}, u32[]{:S(2)}) collective-permute-start(bf16[512,128]{1,0:T(8,128)(2,1)S(1)} %fusion), channel_id=1, source_target_pairs={{0,2},{1,3},{2,0},{3,1},{4,6},{5,7},{6,4},{7,5},{8,10},{9,11},{10,... | collective-permute-start | bytes 393224 | tf_op jit(solution)/shard_map/ppermute | solution.py:11
  49.0 1.4 %collective-permute-start.7 = (bf16[512,128]{1,0:T(8,128)(2,1)S(1)}, bf16[512,128]{1,0:T(8,128)(2,1)S(1)}, u32[]{:S(2)}, u32[]{:S(2)}) collective-permute-start(bf16[512,128]{1,0:T(8,128)(2,1)S(1)} %fusion), channel_id=1, source_target_pairs={{0,3},{1,0},{2,1},{3,2},{4,7},{5,4},{6,5},{7,6},{8,11},{9,8},{10,9... | collective-permute-start | bytes 393224 | tf_op jit(solution)/shard_map/ppermute | solution.py:11
  50.3 3.6 %collective-permute-done.14 = f32[136,256]{1,0:T(8,128)S(1)} collective-permute-done((f32[136,256]{1,0:T(8,128)S(1)}, f32[136,256]{1,0:T(8,128)S(1)}, u32[]{:S(2)}, u32[]{:S(2)}) %collective-permute-start.14) | collective-permute-done | bytes 139296 | tf_op jit(solution)/shard_map/ppermute | solution.py:121
  53.9 0.1 fusion.14
  54.0 0.1 collective-permute-start.15
  54.1 0.0 collective-permute-done.9
  54.1 0.0 collective-permute-done.8
  54.1 0.9 collective-permute-done.7
  55.0 1.0 %copy.13 = bf16[16,128,128]{1,2,0:T(8,128)(2,1)} copy(bf16[16,128,128]{2,1,0:T(8,128)(2,1)S(1)} %bitcast.51) | data formatting | bytes 1048576 | tf_op jit(solution)/shard_map/reshape | solution.py:177
  56.1 3.6 %collective-permute-done.15 = f32[136,256]{1,0:T(8,128)S(1)} collective-permute-done((f32[136,256]{1,0:T(8,128)S(1)}, f32[136,256]{1,0:T(8,128)S(1)}, u32[]{:S(2)}, u32[]{:S(2)}) %collective-permute-start.15) | collective-permute-done | bytes 139296 | tf_op jit(solution)/shard_map/ppermute | solution.py:121
  59.7 0.9 collective-permute-start.16
  60.6 12.2 %shard_map.121 = (f32[4,128,128]{2,1,0:T(8,128)}, bf16[16,128,128]{2,1,0:T(8,128)(2,1)}) custom-call(s32[360]{0:T(512)} %add_select_fusion.rows_ref, s32[360]{0:T(512)} %cols_ref.3, s32[5]{0:T(128)} %counts_ref.3, bf16[360,128,128]{2,1,0:T(8,128)(2,1)} %adj_ref.3, bf16[16,128,128]{2,1,0:T(8,128)(2,1)} %bitcast.50), custom_call_target="tpu_custom_call" | custom-call | flops 1509949440 | bytes 13631488 | tf_op jit(solution)/shard_map/pallas_call | solution.py:84
  72.7 0.0 collective-permute-done.16
  72.7 1.2 %collective-permute-start.17 = (f32[136,256]{1,0:T(8,128)S(1)}, f32[136,256]{1,0:T(8,128)S(1)}, u32[]{:S(2)}, u32[]{:S(2)}) collective-permute-start(f32[136,256]{1,0:T(8,128)S(1)} %add.70), channel_id=1, source_target_pairs={{0,2},{1,3},{2,0},{3,1},{4,6},{5,7},{6,4},{7,5},{8,10},{9,11},{10,... | collective-permute-start | bytes 417800 | tf_op jit(solution)/shard_map/ppermute | solution.py:121
  73.9 1.1 %fusion.16 = (bf16[4,128,128]{2,1,0:T(8,128)(2,1)S(1)}, bf16[4,128,128]{2,1,0:T(8,128)(2,1)S(1)}, bf16[4,128,128]{2,1,0:T(8,128)(2,1)S(1)}, bf16[4,128,128]{2,1,0:T(8,128)(2,1)S(1)}) fusion(bf16[16,128,128]{2,1,0:T(8,128)(2,1)} %get-tuple-element.11), kind=kLoop, calls=%fused_computation.37 | loop fusion | bytes 1048576 | tf_op jit(solution)/shard_map/slice | solution.py:187
  75.1 0.1 collective-permute-start.13
  75.1 3.8 %collective-permute-start.10 = (bf16[512,128]{1,0:T(8,128)(2,1)S(1)}, bf16[512,128]{1,0:T(8,128)(2,1)S(1)}, u32[]{:S(2)}, u32[]{:S(2)}) collective-permute-start(bf16[512,128]{1,0:T(8,128)(2,1)S(1)} %bitcast.58), channel_id=1, source_target_pairs={{0,24},{4,28},{8,0},{12,4},{16,8},{20,12},{24,16},{28,20},{1,25},{... | collective-permute-start | bytes 393224 | tf_op jit(solution)/shard_map/ppermute | solution.py:11
  78.9 1.1 %collective-permute-start.12 = (bf16[512,128]{1,0:T(8,128)(2,1)S(1)}, bf16[512,128]{1,0:T(8,128)(2,1)S(1)}, u32[]{:S(2)}, u32[]{:S(2)}) collective-permute-start(bf16[512,128]{1,0:T(8,128)(2,1)S(1)} %bitcast.57), channel_id=1, source_target_pairs={{0,4},{4,8},{8,12},{12,16},{16,20},{20,24},{24,28},{28,0},{1,5},{5... | collective-permute-start | bytes 393224 | tf_op jit(solution)/shard_map/ppermute | solution.py:11
  80.1 3.6 %collective-permute-start.11 = (bf16[512,128]{1,0:T(8,128)(2,1)S(1)}, bf16[512,128]{1,0:T(8,128)(2,1)S(1)}, u32[]{:S(2)}, u32[]{:S(2)}) collective-permute-start(bf16[512,128]{1,0:T(8,128)(2,1)S(1)} %bitcast.56), channel_id=1, source_target_pairs={{0,28},{4,0},{8,4},{12,8},{16,12},{20,16},{24,20},{28,24},{1,29},{... | collective-permute-start | bytes 393224 | tf_op jit(solution)/shard_map/ppermute | solution.py:11
  83.7 0.0 collective-permute-done.17
  83.7 0.1 collective-permute-start.18
  83.8 0.0 collective-permute-done.13
  83.8 0.0 collective-permute-done.10
  83.8 4.1 %collective-permute-done.12 = bf16[512,128]{1,0:T(8,128)(2,1)S(1)} collective-permute-done((bf16[512,128]{1,0:T(8,128)(2,1)S(1)}, bf16[512,128]{1,0:T(8,128)(2,1)S(1)}, u32[]{:S(2)}, u32[]{:S(2)}) %collective-permute-start.12) | collective-permute-done | bytes 131104 | tf_op jit(solution)/shard_map/ppermute | solution.py:11
  87.9 0.0 collective-permute-done.11
  87.9 1.8 %fusion.5 = bf16[512,128]{1,0:T(8,128)(2,1)} fusion(f32[4,128,128]{2,1,0:T(8,128)} %get-tuple-element.10, bf16[512,128]{1,0:T(8,128)(2,1)S(1)} %collective-permute-done.13, bf16[512,128]{1,0:T(8,128)(2,1)S(1)} %collective-permute-done.12, bf16[512,128]{1,0:T(8,128)(2,1)S(1)} %collective-permute-done.11, bf16[512,128]{1,0:T(8,128)(2,1)S(1)} %collective-permute-done.10, ...), kind=kLoop, calls=%fused_computation.12 | loop fusion | flops 655360 | bytes 919552 | tf_op jit(solution)/shard_map/convert_element_type | solution.py:190
  89.7 0.0 collective-permute-done.18
  89.7 0.6 slice_multiply_fusion.1
  90.3 0.7 slice_multiply_fusion
  (11 shorter events, 0.2 us)
Async XLA Ops:
  0.6 42.4 %copy-start = (bf16[128,256]{1,0:T(8,128)(2,1)S(1)}, bf16[128,256]{1,0:T(8,128)(2,1)}, u32[]{:S(2)}) copy-start(bf16[128,256]{1,0:T(8,128)(2,1)} %param.15) | copy-start | bytes 196612
  0.6 42.4 %copy-start.2 = (bf16[512,256]{1,0:T(8,128)(2,1)S(1)}, bf16[512,256]{1,0:T(8,128)(2,1)}, u32[]{:S(2)}) copy-start(bf16[512,256]{1,0:T(8,128)(2,1)} %param.17) | copy-start | bytes 786436
  0.7 42.4 %copy-start.3 = (f32[256]{0:T(256)S(1)}, f32[256]{0:T(256)}, u32[]{:S(2)}) copy-start(f32[256]{0:T(256)} %param.16) | copy-start | bytes 3076
  2.4 16.5 %collective-permute-start.2 = (bf16[512,128]{1,0:T(8,128)(2,1)S(1)}, bf16[512,128]{1,0:T(8,128)(2,1)S(1)}, u32[]{:S(2)}, u32[]{:S(2)}) collective-permute-start(bf16[512,128]{1,0:T(8,128)(2,1)S(1)} %multiply_convert_fusion.1), channel_id=1, source_target_pairs={{0,28},{4,0},{8,4},{12,8},{16,12},{20,16},{24,20},{28,24},{1,29},{... | collective-permute-start | bytes 393224 | tf_op jit(solution)/shard_map/ppermute | solution.py:11
  8.5 10.5 %collective-permute-start.3 = (bf16[512,128]{1,0:T(8,128)(2,1)S(1)}, bf16[512,128]{1,0:T(8,128)(2,1)S(1)}, u32[]{:S(2)}, u32[]{:S(2)}) collective-permute-start(bf16[512,128]{1,0:T(8,128)(2,1)S(1)} %multiply_convert_fusion.1), channel_id=1, source_target_pairs={{0,24},{4,28},{8,0},{12,4},{16,8},{20,12},{24,16},{28,20},{1,25},{... | collective-permute-start | bytes 393224 | tf_op jit(solution)/shard_map/ppermute | solution.py:11
  8.9 8.9 %collective-permute-start.1 = (bf16[512,128]{1,0:T(8,128)(2,1)S(1)}, bf16[512,128]{1,0:T(8,128)(2,1)S(1)}, u32[]{:S(2)}, u32[]{:S(2)}) collective-permute-start(bf16[512,128]{1,0:T(8,128)(2,1)S(1)} %multiply_convert_fusion.1), channel_id=1, source_target_pairs={{0,4},{4,8},{8,12},{12,16},{16,20},{20,24},{24,28},{28,0},{1,5},{5... | collective-permute-start | bytes 393224 | tf_op jit(solution)/shard_map/ppermute | solution.py:11
  9.6 8.2 %collective-permute-start = (bf16[512,128]{1,0:T(8,128)(2,1)S(1)}, bf16[512,128]{1,0:T(8,128)(2,1)S(1)}, u32[]{:S(2)}, u32[]{:S(2)}) collective-permute-start(bf16[512,128]{1,0:T(8,128)(2,1)S(1)} %multiply_convert_fusion.1), channel_id=1, source_target_pairs={{0,8},{4,12},{8,16},{12,20},{16,24},{20,28},{24,0},{28,4},{1,9},{5... | collective-permute-start | bytes 393224 | tf_op jit(solution)/shard_map/ppermute | solution.py:11
  19.0 0.9 copy-start.1
  32.8 2.7 %collective-permute-start.6 = (bf16[512,128]{1,0:T(8,128)(2,1)S(1)}, bf16[512,128]{1,0:T(8,128)(2,1)S(1)}, u32[]{:S(2)}, u32[]{:S(2)}) collective-permute-start(bf16[512,128]{1,0:T(8,128)(2,1)S(1)} %bitcast.55), channel_id=1, source_target_pairs={{0,3},{1,0},{2,1},{3,2},{4,7},{5,4},{6,5},{7,6},{8,11},{9,8},{10,9... | collective-permute-start | bytes 393224 | tf_op jit(solution)/shard_map/ppermute | solution.py:11
  32.9 6.0 %collective-permute-start.4 = (bf16[512,128]{1,0:T(8,128)(2,1)S(1)}, bf16[512,128]{1,0:T(8,128)(2,1)S(1)}, u32[]{:S(2)}, u32[]{:S(2)}) collective-permute-start(bf16[512,128]{1,0:T(8,128)(2,1)S(1)} %bitcast.54), channel_id=1, source_target_pairs={{0,1},{1,2},{2,3},{3,0},{4,5},{5,6},{6,7},{7,4},{8,9},{9,10},{10,1... | collective-permute-start | bytes 393224 | tf_op jit(solution)/shard_map/ppermute | solution.py:11
  33.4 8.6 %collective-permute-start.5 = (bf16[512,128]{1,0:T(8,128)(2,1)S(1)}, bf16[512,128]{1,0:T(8,128)(2,1)S(1)}, u32[]{:S(2)}, u32[]{:S(2)}) collective-permute-start(bf16[512,128]{1,0:T(8,128)(2,1)S(1)} %bitcast.53), channel_id=1, source_target_pairs={{0,2},{1,3},{2,0},{3,1},{4,6},{5,7},{6,4},{7,5},{8,10},{9,11},{10,... | collective-permute-start | bytes 393224 | tf_op jit(solution)/shard_map/ppermute | solution.py:11
  44.5 9.5 %collective-permute-start.14 = (f32[136,256]{1,0:T(8,128)S(1)}, f32[136,256]{1,0:T(8,128)S(1)}, u32[]{:S(2)}, u32[]{:S(2)}) collective-permute-start(f32[136,256]{1,0:T(8,128)S(1)} %maximum_maximum_fusion), channel_id=1, source_target_pairs={{0,16},{1,17},{2,18},{3,19},{4,20},{5,21},{6,22},{7,23},{8,24},{9,... | collective-permute-start | bytes 417800 | tf_op jit(solution)/shard_map/ppermute | solution.py:121
  46.5 7.6 %collective-permute-start.9 = (bf16[512,128]{1,0:T(8,128)(2,1)S(1)}, bf16[512,128]{1,0:T(8,128)(2,1)S(1)}, u32[]{:S(2)}, u32[]{:S(2)}) collective-permute-start(bf16[512,128]{1,0:T(8,128)(2,1)S(1)} %fusion), channel_id=1, source_target_pairs={{0,1},{1,2},{2,3},{3,0},{4,5},{5,6},{6,7},{7,4},{8,9},{9,10},{10,1... | collective-permute-start | bytes 393224 | tf_op jit(solution)/shard_map/ppermute | solution.py:11
  47.0 7.1 %collective-permute-start.8 = (bf16[512,128]{1,0:T(8,128)(2,1)S(1)}, bf16[512,128]{1,0:T(8,128)(2,1)S(1)}, u32[]{:S(2)}, u32[]{:S(2)}) collective-permute-start(bf16[512,128]{1,0:T(8,128)(2,1)S(1)} %fusion), channel_id=1, source_target_pairs={{0,2},{1,3},{2,0},{3,1},{4,6},{5,7},{6,4},{7,5},{8,10},{9,11},{10,... | collective-permute-start | bytes 393224 | tf_op jit(solution)/shard_map/ppermute | solution.py:11
  49.0 6.0 %collective-permute-start.7 = (bf16[512,128]{1,0:T(8,128)(2,1)S(1)}, bf16[512,128]{1,0:T(8,128)(2,1)S(1)}, u32[]{:S(2)}, u32[]{:S(2)}) collective-permute-start(bf16[512,128]{1,0:T(8,128)(2,1)S(1)} %fusion), channel_id=1, source_target_pairs={{0,3},{1,0},{2,1},{3,2},{4,7},{5,4},{6,5},{7,6},{8,11},{9,8},{10,9... | collective-permute-start | bytes 393224 | tf_op jit(solution)/shard_map/ppermute | solution.py:11
  54.0 5.6 %collective-permute-start.15 = (f32[136,256]{1,0:T(8,128)S(1)}, f32[136,256]{1,0:T(8,128)S(1)}, u32[]{:S(2)}, u32[]{:S(2)}) collective-permute-start(f32[136,256]{1,0:T(8,128)S(1)} %fusion.14), channel_id=1, source_target_pairs={{0,8},{1,9},{2,10},{3,11},{4,12},{5,13},{6,14},{7,15},{8,0},{9,1},... | collective-permute-start | bytes 417800 | tf_op jit(solution)/shard_map/ppermute | solution.py:121
  59.7 13.1 %collective-permute-start.16 = (f32[136,256]{1,0:T(8,128)S(1)}, f32[136,256]{1,0:T(8,128)S(1)}, u32[]{:S(2)}, u32[]{:S(2)}) collective-permute-start(f32[136,256]{1,0:T(8,128)S(1)} %add.69), channel_id=1, source_target_pairs={{0,4},{1,5},{2,6},{3,7},{4,0},{5,1},{6,2},{7,3},{8,12},{9,13},{10,... | collective-permute-start | bytes 417800 | tf_op jit(solution)/shard_map/ppermute | solution.py:121
  72.7 10.9 %collective-permute-start.17 = (f32[136,256]{1,0:T(8,128)S(1)}, f32[136,256]{1,0:T(8,128)S(1)}, u32[]{:S(2)}, u32[]{:S(2)}) collective-permute-start(f32[136,256]{1,0:T(8,128)S(1)} %add.70), channel_id=1, source_target_pairs={{0,2},{1,3},{2,0},{3,1},{4,6},{5,7},{6,4},{7,5},{8,10},{9,11},{10,... | collective-permute-start | bytes 417800 | tf_op jit(solution)/shard_map/ppermute | solution.py:121
  75.1 8.7 %collective-permute-start.13 = (bf16[512,128]{1,0:T(8,128)(2,1)S(1)}, bf16[512,128]{1,0:T(8,128)(2,1)S(1)}, u32[]{:S(2)}, u32[]{:S(2)}) collective-permute-start(bf16[512,128]{1,0:T(8,128)(2,1)S(1)} %bitcast.59), channel_id=1, source_target_pairs={{0,8},{4,12},{8,16},{12,20},{16,24},{20,28},{24,0},{28,4},{1,9},{5... | collective-permute-start | bytes 393224 | tf_op jit(solution)/shard_map/ppermute | solution.py:11
  75.1 8.7 %collective-permute-start.10 = (bf16[512,128]{1,0:T(8,128)(2,1)S(1)}, bf16[512,128]{1,0:T(8,128)(2,1)S(1)}, u32[]{:S(2)}, u32[]{:S(2)}) collective-permute-start(bf16[512,128]{1,0:T(8,128)(2,1)S(1)} %bitcast.58), channel_id=1, source_target_pairs={{0,24},{4,28},{8,0},{12,4},{16,8},{20,12},{24,16},{28,20},{1,25},{... | collective-permute-start | bytes 393224 | tf_op jit(solution)/shard_map/ppermute | solution.py:11
  78.9 9.0 %collective-permute-start.12 = (bf16[512,128]{1,0:T(8,128)(2,1)S(1)}, bf16[512,128]{1,0:T(8,128)(2,1)S(1)}, u32[]{:S(2)}, u32[]{:S(2)}) collective-permute-start(bf16[512,128]{1,0:T(8,128)(2,1)S(1)} %bitcast.57), channel_id=1, source_target_pairs={{0,4},{4,8},{8,12},{12,16},{16,20},{20,24},{24,28},{28,0},{1,5},{5... | collective-permute-start | bytes 393224 | tf_op jit(solution)/shard_map/ppermute | solution.py:11
  80.1 7.9 %collective-permute-start.11 = (bf16[512,128]{1,0:T(8,128)(2,1)S(1)}, bf16[512,128]{1,0:T(8,128)(2,1)S(1)}, u32[]{:S(2)}, u32[]{:S(2)}) collective-permute-start(bf16[512,128]{1,0:T(8,128)(2,1)S(1)} %bitcast.56), channel_id=1, source_target_pairs={{0,28},{4,0},{8,4},{12,8},{16,12},{20,16},{24,20},{28,24},{1,29},{... | collective-permute-start | bytes 393224 | tf_op jit(solution)/shard_map/ppermute | solution.py:11
  83.7 6.0 %collective-permute-start.18 = (f32[136,256]{1,0:T(8,128)S(1)}, f32[136,256]{1,0:T(8,128)S(1)}, u32[]{:S(2)}, u32[]{:S(2)}) collective-permute-start(f32[136,256]{1,0:T(8,128)S(1)} %add.71), channel_id=1, source_target_pairs={{0,1},{1,0},{2,3},{3,2},{4,5},{5,4},{6,7},{7,6},{8,9},{9,8},{10,11... | collective-permute-start | bytes 417800 | tf_op jit(solution)/shard_map/ppermute | solution.py:121

commit v12 on v11

--- a/solution.py
+++ b/solution.py
@@ -118,7 +118,9 @@
         return lax.psum(value, axes)
     bit = size // 2
     while bit >= 1:
-        value = value + lax.ppermute(value, axes, [(i, i ^ bit) for i in range(size)])
+        sent = value.astype(jnp.bfloat16)
+        received = lax.ppermute(sent, axes, [(i, i ^ bit) for i in range(size)])
+        value = sent.astype(jnp.float32) + received.astype(jnp.float32)
         bit //= 2
     return value
 

time: 91.2 us -> 88.4 us (0.969)
  waiting for transfers between devices: 24.6 us -> 21.2 us
    ppermute x5, waiting for transfers between devices: 7.18 us -> 0.86 us  [all_sum(): received = lax.ppermute(sent, axes, [(i, i ^ bit) for i in range(size)])]
    ppermute x14, waiting for transfers between devices: 17.4 us -> 20.3 us  [from_behind(): lax.ppermute(value, axis, [(i, (i + by) % length) for i in range(length)])]
    ppermute x5, starting transfers between devices: 4.03 us -> 5.71 us  [all_sum(): received = lax.ppermute(sent, axes, [(i, i ^ bit) for i in range(size)])]
  transfers between devices with their start and end apart: 19 -> 19, of which waited for: 7 -> 10; matrix products, arithmetic and copies ran while one was open for 7% -> 8% of each run, Pallas kernels for 13% -> 14%
where the time goes in v12:
time: 88.4 us; the launch traced here: 88.1 us
  starting transfers between devices  28 us (32%)
  Pallas kernels  23.8 us (27%)
  waiting for transfers between devices  21.2 us (24%)
  other arithmetic  8.45 us (10%)
  local copies, waits for them, and re-layouts  4.23 us (5%)
  matrix products  1.57 us (2%)
    pallas_call x2, Pallas kernels, tile_products(): pl.pallas_call(kernel, grid_spec=pltpu.PrefetchScalarGridSpec(num_scalar_...  23.8 us
    ppermute x14, starting transfers between devices, from_behind(): lax.ppermute(value, axis, [(i, (i + by) % length) for i in range(length)])  22.3 us
    ppermute x14, waiting for transfers between devices, from_behind(): lax.ppermute(value, axis, [(i, (i + by) % length) for i in range(length)])  20.3 us
    ppermute x5, starting transfers between devices, all_sum(): received = lax.ppermute(sent, axes, [(i, i ^ bit) for i in range(size)])  5.71 us
  transfers between devices with their start and end apart: 19, of which 10 were waited for; matrix products, arithmetic and copies ran while one was open for 8% of the time, Pallas kernels for 14%

profile of v12, /device:TPU:0, one launch (start us, length us, event | category | flops | bytes accessed | tf_op | source)
XLA Modules:
  0.0 88.1 jit_solution(4731482568368646955)
XLA Ops:
  0.6 0.0 copy-start
  0.6 0.0 copy-start.2
  0.7 0.0 copy-start.3
  0.7 0.7 convert_rsqrt_fusion
  1.4 1.0 %multiply_convert_fusion.1 = bf16[512,128]{1,0:T(8,128)(2,1)S(1)} fusion(bf16[512,128]{1,0:T(8,128)(2,1)} %param.9, f32[512]{0:T(512)S(1)} %convert_rsqrt_fusion), kind=kLoop, calls=%fused_computation.19 | loop fusion | flops 196608 | bytes 264192 | tf_op jit(solution)/shard_map/convert_element_type | solution.py:140
  2.4 6.1 %collective-permute-start.2 = (bf16[512,128]{1,0:T(8,128)(2,1)S(1)}, bf16[512,128]{1,0:T(8,128)(2,1)S(1)}, u32[]{:S(2)}, u32[]{:S(2)}) collective-permute-start(bf16[512,128]{1,0:T(8,128)(2,1)S(1)} %multiply_convert_fusion.1), channel_id=1, source_target_pairs={{0,28},{4,0},{8,4},{12,8},{16,12},{20,16},{24,20},{28,24},{1,29},{... | collective-permute-start | bytes 393224 | tf_op jit(solution)/shard_map/ppermute | solution.py:11
  8.5 0.4 collective-permute-start.3
  8.9 0.6 collective-permute-start.1
  9.6 0.9 %collective-permute-start = (bf16[512,128]{1,0:T(8,128)(2,1)S(1)}, bf16[512,128]{1,0:T(8,128)(2,1)S(1)}, u32[]{:S(2)}, u32[]{:S(2)}) collective-permute-start(bf16[512,128]{1,0:T(8,128)(2,1)S(1)} %multiply_convert_fusion.1), channel_id=1, source_target_pairs={{0,8},{4,12},{8,16},{12,20},{16,24},{20,28},{24,0},{28,4},{1,9},{5... | collective-permute-start | bytes 393224 | tf_op jit(solution)/shard_map/ppermute | solution.py:11
  10.5 1.3 %add_select_fusion.rows_ref = s32[360]{0:T(512)} fusion(s32[360]{0:T(512)} %param.12, s32[]{:T(128)S(6)} %mul.57), kind=kLoop, calls=%fused_computation.34 | loop fusion | flops 4320 | bytes 2884 | tf_op jit(solution)/shard_map/jit(remainder)/select_n | solution.py:147
  11.8 6.0 %collective-permute-done = bf16[512,128]{1,0:T(8,128)(2,1)S(1)} collective-permute-done((bf16[512,128]{1,0:T(8,128)(2,1)S(1)}, bf16[512,128]{1,0:T(8,128)(2,1)S(1)}, u32[]{:S(2)}, u32[]{:S(2)}) %collective-permute-start) | collective-permute-done | bytes 131104 | tf_op jit(solution)/shard_map/ppermute | solution.py:11
  17.8 0.0 collective-permute-done.1
  17.9 1.1 %bitcast_dynamic-update-slice_fusion.2 = bf16[5,512,128]{2,1,0:T(8,128)(2,1)S(1)} fusion(bf16[5,512,128]{2,1,0:T(8,128)(2,1)S(1)} %bitcast_dynamic-update-slice_fusion.3, bf16[512,128]{1,0:T(8,128)(2,1)} %param.9, f32[512]{0:T(512)S(1)} %convert_rsqrt_fusion), kind=kLoop, calls=%fused_computation.28 | loop fusion | flops 196608 | bytes 264192
  18.9 0.0 collective-permute-done.2
  19.0 0.0 collective-permute-done.3
  19.0 0.0 copy-start.1
  19.0 0.8 copy-done.1
  19.9 11.8 %shard_map.120 = (f32[4,128,128]{2,1,0:T(8,128)}, bf16[12,128,128]{2,1,0:T(8,128)(2,1)}) custom-call(s32[360]{0:T(512)} %add_select_fusion.rows_ref, s32[360]{0:T(512)} %cols_ref.3, s32[5]{0:T(128)} %counts_ref.3, bf16[360,128,128]{2,1,0:T(8,128)(2,1)} %adj_ref.3, bf16[20,128,128]{2,1,0:T(8,128)(2,1)} %bitcast.51), custom_call_target="tpu_custom_call" | custom-call | flops 1509949440 | bytes 13500416 | tf_op jit(solution)/shard_map/pallas_call | solution.py:84
  31.6 1.1 %fusion.15 = (bf16[4,128,128]{2,1,0:T(8,128)(2,1)S(1)}, bf16[4,128,128]{2,1,0:T(8,128)(2,1)S(1)}, bf16[4,128,128]{2,1,0:T(8,128)(2,1)S(1)}) fusion(bf16[12,128,128]{2,1,0:T(8,128)(2,1)} %get-tuple-element.9), kind=kLoop, calls=%fused_computation.42 | loop fusion | bytes 786432 | tf_op jit(solution)/shard_map/slice | solution.py:154
  32.7 1.2 %collective-permute-start.6 = (bf16[512,128]{1,0:T(8,128)(2,1)S(1)}, bf16[512,128]{1,0:T(8,128)(2,1)S(1)}, u32[]{:S(2)}, u32[]{:S(2)}) collective-permute-start(bf16[512,128]{1,0:T(8,128)(2,1)S(1)} %bitcast.54), channel_id=1, source_target_pairs={{0,3},{1,0},{2,1},{3,2},{4,7},{5,4},{6,5},{7,6},{8,11},{9,8},{10,9... | collective-permute-start | bytes 393224 | tf_op jit(solution)/shard_map/ppermute | solution.py:11
  33.9 0.0 collective-permute-start.4
  33.9 2.0 %collective-permute-start.5 = (bf16[512,128]{1,0:T(8,128)(2,1)S(1)}, bf16[512,128]{1,0:T(8,128)(2,1)S(1)}, u32[]{:S(2)}, u32[]{:S(2)}) collective-permute-start(bf16[512,128]{1,0:T(8,128)(2,1)S(1)} %bitcast.52), channel_id=1, source_target_pairs={{0,2},{1,3},{2,0},{3,1},{4,6},{5,7},{6,4},{7,5},{8,10},{9,11},{10,... | collective-permute-start | bytes 393224 | tf_op jit(solution)/shard_map/ppermute | solution.py:11
  35.9 0.1 pad.2.clone
  35.9 0.9 collective-permute-done.6
  36.8 2.8 %collective-permute-done.4 = bf16[512,128]{1,0:T(8,128)(2,1)S(1)} collective-permute-done((bf16[512,128]{1,0:T(8,128)(2,1)S(1)}, bf16[512,128]{1,0:T(8,128)(2,1)S(1)}, u32[]{:S(2)}, u32[]{:S(2)}) %collective-permute-start.4) | collective-permute-done | bytes 131104 | tf_op jit(solution)/shard_map/ppermute | solution.py:11
  39.6 2.8 %collective-permute-done.5 = bf16[512,128]{1,0:T(8,128)(2,1)S(1)} collective-permute-done((bf16[512,128]{1,0:T(8,128)(2,1)S(1)}, bf16[512,128]{1,0:T(8,128)(2,1)S(1)}, u32[]{:S(2)}, u32[]{:S(2)}) %collective-permute-start.5) | collective-permute-done | bytes 131104 | tf_op jit(solution)/shard_map/ppermute | solution.py:11
  42.5 1.1 %fusion.9 = bf16[512,128]{1,0:T(8,128)(2,1)S(1)} fusion(f32[4,128,128]{2,1,0:T(8,128)} %get-tuple-element.8, bf16[512,128]{1,0:T(8,128)(2,1)S(1)} %collective-permute-done.6, bf16[512,128]{1,0:T(8,128)(2,1)S(1)} %collective-permute-done.5, bf16[512,128]{1,0:T(8,128)(2,1)S(1)} %collective-permute-done.4, f32[512]{0:T(512)S(1)} %convert_rsqrt_fusion), kind=kLoop, calls=%fused_computation.18 | loop fusion | flops 524288 | bytes 788480 | tf_op jit(solution)/shard_map/convert_element_type | solution.py:155
  43.6 0.0 copy-done
  43.6 0.0 copy-done.2
  43.6 1.1 %fusion.13 = (bf16[256]{0:T(256)(128)(2,1)S(1)}, bf16[512,256]{1,0:T(8,128)(2,1)S(1)}, bf16[512,256]{1,0:T(8,128)(2,1)}) fusion(bf16[512,256]{1,0:T(8,128)(2,1)S(1)} %copy-done.2, f32[256]{0:T(256)S(1)} %copy-done.3, bf16[512,128]{1,0:T(8,128)(2,1)S(1)} %fusion.9, bf16[128,256]{1,0:T(8,128)(2,1)S(1)} %copy-done), kind=kOutput, calls=%fused_computation.40 | convolution fusion | flops 35389184 | bytes 984576 | tf_op jit(solution)/shard_map/dot_general | solution.py:156
  44.7 0.2 convolution_convert_fusion
  45.0 0.1 maximum_maximum_fusion
  45.0 2.3 %collective-permute-start.14 = (bf16[136,256]{1,0:T(8,128)(2,1)S(1)}, bf16[136,256]{1,0:T(8,128)(2,1)S(1)}, u32[]{:S(2)}, u32[]{:S(2)}) collective-permute-start(bf16[136,256]{1,0:T(8,128)(2,1)S(1)} %maximum_maximum_fusion), channel_id=1, source_target_pairs={{0,16},{1,17},{2,18},{3,19},{4,20},{5,21},{6,22},{7,23},{8,24},{9,... | collective-permute-start | bytes 208904 | tf_op jit(solution)/shard_map/ppermute | solution.py:122
  47.3 0.2 fusion
  47.6 0.1 collective-permute-start.9
  47.6 1.0 %collective-permute-start.8 = (bf16[512,128]{1,0:T(8,128)(2,1)S(1)}, bf16[512,128]{1,0:T(8,128)(2,1)S(1)}, u32[]{:S(2)}, u32[]{:S(2)}) collective-permute-start(bf16[512,128]{1,0:T(8,128)(2,1)S(1)} %fusion), channel_id=1, source_target_pairs={{0,2},{1,3},{2,0},{3,1},{4,6},{5,7},{6,4},{7,5},{8,10},{9,11},{10,... | collective-permute-start | bytes 393224 | tf_op jit(solution)/shard_map/ppermute | solution.py:11
  48.6 1.4 %collective-permute-start.7 = (bf16[512,128]{1,0:T(8,128)(2,1)S(1)}, bf16[512,128]{1,0:T(8,128)(2,1)S(1)}, u32[]{:S(2)}, u32[]{:S(2)}) collective-permute-start(bf16[512,128]{1,0:T(8,128)(2,1)S(1)} %fusion), channel_id=1, source_target_pairs={{0,3},{1,0},{2,1},{3,2},{4,7},{5,4},{6,5},{7,6},{8,11},{9,8},{10,9... | collective-permute-start | bytes 393224 | tf_op jit(solution)/shard_map/ppermute | solution.py:11
  50.0 0.8 collective-permute-done.14
  50.9 0.1 add_convert_fusion.3
  51.0 0.1 collective-permute-start.15
  51.0 1.7 %collective-permute-done.9 = bf16[512,128]{1,0:T(8,128)(2,1)S(1)} collective-permute-done((bf16[512,128]{1,0:T(8,128)(2,1)S(1)}, bf16[512,128]{1,0:T(8,128)(2,1)S(1)}, u32[]{:S(2)}, u32[]{:S(2)}) %collective-permute-start.9) | collective-permute-done | bytes 131104 | tf_op jit(solution)/shard_map/ppermute | solution.py:11
  52.8 1.3 %collective-permute-done.8 = bf16[512,128]{1,0:T(8,128)(2,1)S(1)} collective-permute-done((bf16[512,128]{1,0:T(8,128)(2,1)S(1)}, bf16[512,128]{1,0:T(8,128)(2,1)S(1)}, u32[]{:S(2)}, u32[]{:S(2)}) %collective-permute-start.8) | collective-permute-done | bytes 131104 | tf_op jit(solution)/shard_map/ppermute | solution.py:11
  54.1 0.6 collective-permute-done.7
  54.7 1.0 %copy.13 = bf16[16,128,128]{1,2,0:T(8,128)(2,1)} copy(bf16[16,128,128]{2,1,0:T(8,128)(2,1)S(1)} %bitcast.50) | data formatting | bytes 1048576 | tf_op jit(solution)/shard_map/reshape | solution.py:179
  55.7 0.0 collective-permute-done.15
  55.8 1.9 %collective-permute-start.16 = (bf16[136,256]{1,0:T(8,128)(2,1)S(1)}, bf16[136,256]{1,0:T(8,128)(2,1)S(1)}, u32[]{:S(2)}, u32[]{:S(2)}) collective-permute-start(bf16[136,256]{1,0:T(8,128)(2,1)S(1)} %add_convert_fusion.2), channel_id=1, source_target_pairs={{0,4},{1,5},{2,6},{3,7},{4,0},{5,1},{6,2},{7,3},{8,12},{9,13},{10,... | collective-permute-start | bytes 208904 | tf_op jit(solution)/shard_map/ppermute | solution.py:122
  57.7 12.0 %shard_map.121 = (f32[4,128,128]{2,1,0:T(8,128)}, bf16[16,128,128]{2,1,0:T(8,128)(2,1)}) custom-call(s32[360]{0:T(512)} %add_select_fusion.rows_ref, s32[360]{0:T(512)} %cols_ref.3, s32[5]{0:T(128)} %counts_ref.3, bf16[360,128,128]{2,1,0:T(8,128)(2,1)} %adj_ref.3, bf16[16,128,128]{2,1,0:T(8,128)(2,1)} %bitcast.49), custom_call_target="tpu_custom_call" | custom-call | flops 1509949440 | bytes 13631488 | tf_op jit(solution)/shard_map/pallas_call | solution.py:84
  69.7 0.0 collective-permute-done.16
  69.7 1.4 %collective-permute-start.17 = (bf16[136,256]{1,0:T(8,128)(2,1)S(1)}, bf16[136,256]{1,0:T(8,128)(2,1)S(1)}, u32[]{:S(2)}, u32[]{:S(2)}) collective-permute-start(bf16[136,256]{1,0:T(8,128)(2,1)S(1)} %add_convert_fusion.1), channel_id=1, source_target_pairs={{0,2},{1,3},{2,0},{3,1},{4,6},{5,7},{6,4},{7,5},{8,10},{9,11},{10,... | collective-permute-start | bytes 208904 | tf_op jit(solution)/shard_map/ppermute | solution.py:122
  71.1 1.1 %fusion.14 = (bf16[4,128,128]{2,1,0:T(8,128)(2,1)S(1)}, bf16[4,128,128]{2,1,0:T(8,128)(2,1)S(1)}, bf16[4,128,128]{2,1,0:T(8,128)(2,1)S(1)}, bf16[4,128,128]{2,1,0:T(8,128)(2,1)S(1)}) fusion(bf16[16,128,128]{2,1,0:T(8,128)(2,1)} %get-tuple-element.11), kind=kLoop, calls=%fused_computation.41 | loop fusion | bytes 1048576 | tf_op jit(solution)/shard_map/slice | solution.py:189
  72.2 0.1 collective-permute-start.13
  72.3 3.8 %collective-permute-start.10 = (bf16[512,128]{1,0:T(8,128)(2,1)S(1)}, bf16[512,128]{1,0:T(8,128)(2,1)S(1)}, u32[]{:S(2)}, u32[]{:S(2)}) collective-permute-start(bf16[512,128]{1,0:T(8,128)(2,1)S(1)} %bitcast.57), channel_id=1, source_target_pairs={{0,24},{4,28},{8,0},{12,4},{16,8},{20,12},{24,16},{28,20},{1,25},{... | collective-permute-start | bytes 393224 | tf_op jit(solution)/shard_map/ppermute | solution.py:11
  76.1 1.0 %collective-permute-start.12 = (bf16[512,128]{1,0:T(8,128)(2,1)S(1)}, bf16[512,128]{1,0:T(8,128)(2,1)S(1)}, u32[]{:S(2)}, u32[]{:S(2)}) collective-permute-start(bf16[512,128]{1,0:T(8,128)(2,1)S(1)} %bitcast.56), channel_id=1, source_target_pairs={{0,4},{4,8},{8,12},{12,16},{16,20},{20,24},{24,28},{28,0},{1,5},{5... | collective-permute-start | bytes 393224 | tf_op jit(solution)/shard_map/ppermute | solution.py:11
  77.1 3.7 %collective-permute-start.11 = (bf16[512,128]{1,0:T(8,128)(2,1)S(1)}, bf16[512,128]{1,0:T(8,128)(2,1)S(1)}, u32[]{:S(2)}, u32[]{:S(2)}) collective-permute-start(bf16[512,128]{1,0:T(8,128)(2,1)S(1)} %bitcast.55), channel_id=1, source_target_pairs={{0,28},{4,0},{8,4},{12,8},{16,12},{20,16},{24,20},{28,24},{1,29},{... | collective-permute-start | bytes 393224 | tf_op jit(solution)/shard_map/ppermute | solution.py:11
  80.8 0.0 collective-permute-done.17
  80.9 0.1 collective-permute-start.18
  80.9 0.0 collective-permute-done.13
  81.0 0.5 collective-permute-done.10
  81.5 3.6 %collective-permute-done.12 = bf16[512,128]{1,0:T(8,128)(2,1)S(1)} collective-permute-done((bf16[512,128]{1,0:T(8,128)(2,1)S(1)}, bf16[512,128]{1,0:T(8,128)(2,1)S(1)}, u32[]{:S(2)}, u32[]{:S(2)}) %collective-permute-start.12) | collective-permute-done | bytes 131104 | tf_op jit(solution)/shard_map/ppermute | solution.py:11
  85.1 0.0 collective-permute-done.11
  85.1 1.8 %fusion.5 = bf16[512,128]{1,0:T(8,128)(2,1)} fusion(f32[4,128,128]{2,1,0:T(8,128)} %get-tuple-element.10, bf16[512,128]{1,0:T(8,128)(2,1)S(1)} %collective-permute-done.13, bf16[512,128]{1,0:T(8,128)(2,1)S(1)} %collective-permute-done.12, bf16[512,128]{1,0:T(8,128)(2,1)S(1)} %collective-permute-done.11, bf16[512,128]{1,0:T(8,128)(2,1)S(1)} %collective-permute-done.10, ...), kind=kLoop, calls=%fused_computation.13 | loop fusion | flops 655360 | bytes 919552 | tf_op jit(solution)/shard_map/convert_element_type | solution.py:192
  86.8 0.0 collective-permute-done.18
  86.9 0.6 slice_multiply_fusion.1
  87.4 0.7 slice_multiply_fusion
  (12 shorter events, 0.2 us)
Async XLA Ops:
  0.6 42.9 %copy-start = (bf16[128,256]{1,0:T(8,128)(2,1)S(1)}, bf16[128,256]{1,0:T(8,128)(2,1)}, u32[]{:S(2)}) copy-start(bf16[128,256]{1,0:T(8,128)(2,1)} %param.15) | copy-start | bytes 196612
  0.6 42.9 %copy-start.2 = (bf16[512,256]{1,0:T(8,128)(2,1)S(1)}, bf16[512,256]{1,0:T(8,128)(2,1)}, u32[]{:S(2)}) copy-start(bf16[512,256]{1,0:T(8,128)(2,1)} %param.17) | copy-start | bytes 786436
  0.7 42.9 %copy-start.3 = (f32[256]{0:T(256)S(1)}, f32[256]{0:T(256)}, u32[]{:S(2)}) copy-start(f32[256]{0:T(256)} %param.16) | copy-start | bytes 3076
  2.4 16.5 %collective-permute-start.2 = (bf16[512,128]{1,0:T(8,128)(2,1)S(1)}, bf16[512,128]{1,0:T(8,128)(2,1)S(1)}, u32[]{:S(2)}, u32[]{:S(2)}) collective-permute-start(bf16[512,128]{1,0:T(8,128)(2,1)S(1)} %multiply_convert_fusion.1), channel_id=1, source_target_pairs={{0,28},{4,0},{8,4},{12,8},{16,12},{20,16},{24,20},{28,24},{1,29},{... | collective-permute-start | bytes 393224 | tf_op jit(solution)/shard_map/ppermute | solution.py:11
  8.5 10.5 %collective-permute-start.3 = (bf16[512,128]{1,0:T(8,128)(2,1)S(1)}, bf16[512,128]{1,0:T(8,128)(2,1)S(1)}, u32[]{:S(2)}, u32[]{:S(2)}) collective-permute-start(bf16[512,128]{1,0:T(8,128)(2,1)S(1)} %multiply_convert_fusion.1), channel_id=1, source_target_pairs={{0,24},{4,28},{8,0},{12,4},{16,8},{20,12},{24,16},{28,20},{1,25},{... | collective-permute-start | bytes 393224 | tf_op jit(solution)/shard_map/ppermute | solution.py:11
  8.9 8.9 %collective-permute-start.1 = (bf16[512,128]{1,0:T(8,128)(2,1)S(1)}, bf16[512,128]{1,0:T(8,128)(2,1)S(1)}, u32[]{:S(2)}, u32[]{:S(2)}) collective-permute-start(bf16[512,128]{1,0:T(8,128)(2,1)S(1)} %multiply_convert_fusion.1), channel_id=1, source_target_pairs={{0,4},{4,8},{8,12},{12,16},{16,20},{20,24},{24,28},{28,0},{1,5},{5... | collective-permute-start | bytes 393224 | tf_op jit(solution)/shard_map/ppermute | solution.py:11
  9.6 8.2 %collective-permute-start = (bf16[512,128]{1,0:T(8,128)(2,1)S(1)}, bf16[512,128]{1,0:T(8,128)(2,1)S(1)}, u32[]{:S(2)}, u32[]{:S(2)}) collective-permute-start(bf16[512,128]{1,0:T(8,128)(2,1)S(1)} %multiply_convert_fusion.1), channel_id=1, source_target_pairs={{0,8},{4,12},{8,16},{12,20},{16,24},{20,28},{24,0},{28,4},{1,9},{5... | collective-permute-start | bytes 393224 | tf_op jit(solution)/shard_map/ppermute | solution.py:11
  19.0 0.9 copy-start.1
  32.7 4.1 %collective-permute-start.6 = (bf16[512,128]{1,0:T(8,128)(2,1)S(1)}, bf16[512,128]{1,0:T(8,128)(2,1)S(1)}, u32[]{:S(2)}, u32[]{:S(2)}) collective-permute-start(bf16[512,128]{1,0:T(8,128)(2,1)S(1)} %bitcast.54), channel_id=1, source_target_pairs={{0,3},{1,0},{2,1},{3,2},{4,7},{5,4},{6,5},{7,6},{8,11},{9,8},{10,9... | collective-permute-start | bytes 393224 | tf_op jit(solution)/shard_map/ppermute | solution.py:11
  33.9 5.8 %collective-permute-start.4 = (bf16[512,128]{1,0:T(8,128)(2,1)S(1)}, bf16[512,128]{1,0:T(8,128)(2,1)S(1)}, u32[]{:S(2)}, u32[]{:S(2)}) collective-permute-start(bf16[512,128]{1,0:T(8,128)(2,1)S(1)} %bitcast.53), channel_id=1, source_target_pairs={{0,1},{1,2},{2,3},{3,0},{4,5},{5,6},{6,7},{7,4},{8,9},{9,10},{10,1... | collective-permute-start | bytes 393224 | tf_op jit(solution)/shard_map/ppermute | solution.py:11
  33.9 8.6 %collective-permute-start.5 = (bf16[512,128]{1,0:T(8,128)(2,1)S(1)}, bf16[512,128]{1,0:T(8,128)(2,1)S(1)}, u32[]{:S(2)}, u32[]{:S(2)}) collective-permute-start(bf16[512,128]{1,0:T(8,128)(2,1)S(1)} %bitcast.52), channel_id=1, source_target_pairs={{0,2},{1,3},{2,0},{3,1},{4,6},{5,7},{6,4},{7,5},{8,10},{9,11},{10,... | collective-permute-start | bytes 393224 | tf_op jit(solution)/shard_map/ppermute | solution.py:11
  45.0 5.8 %collective-permute-start.14 = (bf16[136,256]{1,0:T(8,128)(2,1)S(1)}, bf16[136,256]{1,0:T(8,128)(2,1)S(1)}, u32[]{:S(2)}, u32[]{:S(2)}) collective-permute-start(bf16[136,256]{1,0:T(8,128)(2,1)S(1)} %maximum_maximum_fusion), channel_id=1, source_target_pairs={{0,16},{1,17},{2,18},{3,19},{4,20},{5,21},{6,22},{7,23},{8,24},{9,... | collective-permute-start | bytes 208904 | tf_op jit(solution)/shard_map/ppermute | solution.py:122
  47.6 5.2 %collective-permute-start.9 = (bf16[512,128]{1,0:T(8,128)(2,1)S(1)}, bf16[512,128]{1,0:T(8,128)(2,1)S(1)}, u32[]{:S(2)}, u32[]{:S(2)}) collective-permute-start(bf16[512,128]{1,0:T(8,128)(2,1)S(1)} %fusion), channel_id=1, source_target_pairs={{0,1},{1,2},{2,3},{3,0},{4,5},{5,6},{6,7},{7,4},{8,9},{9,10},{10,1... | collective-permute-start | bytes 393224 | tf_op jit(solution)/shard_map/ppermute | solution.py:11
  47.6 6.4 %collective-permute-start.8 = (bf16[512,128]{1,0:T(8,128)(2,1)S(1)}, bf16[512,128]{1,0:T(8,128)(2,1)S(1)}, u32[]{:S(2)}, u32[]{:S(2)}) collective-permute-start(bf16[512,128]{1,0:T(8,128)(2,1)S(1)} %fusion), channel_id=1, source_target_pairs={{0,2},{1,3},{2,0},{3,1},{4,6},{5,7},{6,4},{7,5},{8,10},{9,11},{10,... | collective-permute-start | bytes 393224 | tf_op jit(solution)/shard_map/ppermute | solution.py:11
  48.6 6.0 %collective-permute-start.7 = (bf16[512,128]{1,0:T(8,128)(2,1)S(1)}, bf16[512,128]{1,0:T(8,128)(2,1)S(1)}, u32[]{:S(2)}, u32[]{:S(2)}) collective-permute-start(bf16[512,128]{1,0:T(8,128)(2,1)S(1)} %fusion), channel_id=1, source_target_pairs={{0,3},{1,0},{2,1},{3,2},{4,7},{5,4},{6,5},{7,6},{8,11},{9,8},{10,9... | collective-permute-start | bytes 393224 | tf_op jit(solution)/shard_map/ppermute | solution.py:11
  51.0 4.8 %collective-permute-start.15 = (bf16[136,256]{1,0:T(8,128)(2,1)S(1)}, bf16[136,256]{1,0:T(8,128)(2,1)S(1)}, u32[]{:S(2)}, u32[]{:S(2)}) collective-permute-start(bf16[136,256]{1,0:T(8,128)(2,1)S(1)} %add_convert_fusion.3), channel_id=1, source_target_pairs={{0,8},{1,9},{2,10},{3,11},{4,12},{5,13},{6,14},{7,15},{8,0},{9,1},... | collective-permute-start | bytes 208904 | tf_op jit(solution)/shard_map/ppermute | solution.py:122
  55.8 14.0 %collective-permute-start.16 = (bf16[136,256]{1,0:T(8,128)(2,1)S(1)}, bf16[136,256]{1,0:T(8,128)(2,1)S(1)}, u32[]{:S(2)}, u32[]{:S(2)}) collective-permute-start(bf16[136,256]{1,0:T(8,128)(2,1)S(1)} %add_convert_fusion.2), channel_id=1, source_target_pairs={{0,4},{1,5},{2,6},{3,7},{4,0},{5,1},{6,2},{7,3},{8,12},{9,13},{10,... | collective-permute-start | bytes 208904 | tf_op jit(solution)/shard_map/ppermute | solution.py:122
  69.7 11.1 %collective-permute-start.17 = (bf16[136,256]{1,0:T(8,128)(2,1)S(1)}, bf16[136,256]{1,0:T(8,128)(2,1)S(1)}, u32[]{:S(2)}, u32[]{:S(2)}) collective-permute-start(bf16[136,256]{1,0:T(8,128)(2,1)S(1)} %add_convert_fusion.1), channel_id=1, source_target_pairs={{0,2},{1,3},{2,0},{3,1},{4,6},{5,7},{6,4},{7,5},{8,10},{9,11},{10,... | collective-permute-start | bytes 208904 | tf_op jit(solution)/shard_map/ppermute | solution.py:122
  72.2 8.7 %collective-permute-start.13 = (bf16[512,128]{1,0:T(8,128)(2,1)S(1)}, bf16[512,128]{1,0:T(8,128)(2,1)S(1)}, u32[]{:S(2)}, u32[]{:S(2)}) collective-permute-start(bf16[512,128]{1,0:T(8,128)(2,1)S(1)} %bitcast.58), channel_id=1, source_target_pairs={{0,8},{4,12},{8,16},{12,20},{16,24},{20,28},{24,0},{28,4},{1,9},{5... | collective-permute-start | bytes 393224 | tf_op jit(solution)/shard_map/ppermute | solution.py:11
  72.3 9.2 %collective-permute-start.10 = (bf16[512,128]{1,0:T(8,128)(2,1)S(1)}, bf16[512,128]{1,0:T(8,128)(2,1)S(1)}, u32[]{:S(2)}, u32[]{:S(2)}) collective-permute-start(bf16[512,128]{1,0:T(8,128)(2,1)S(1)} %bitcast.57), channel_id=1, source_target_pairs={{0,24},{4,28},{8,0},{12,4},{16,8},{20,12},{24,16},{28,20},{1,25},{... | collective-permute-start | bytes 393224 | tf_op jit(solution)/shard_map/ppermute | solution.py:11
  76.1 9.0 %collective-permute-start.12 = (bf16[512,128]{1,0:T(8,128)(2,1)S(1)}, bf16[512,128]{1,0:T(8,128)(2,1)S(1)}, u32[]{:S(2)}, u32[]{:S(2)}) collective-permute-start(bf16[512,128]{1,0:T(8,128)(2,1)S(1)} %bitcast.56), channel_id=1, source_target_pairs={{0,4},{4,8},{8,12},{12,16},{16,20},{20,24},{24,28},{28,0},{1,5},{5... | collective-permute-start | bytes 393224 | tf_op jit(solution)/shard_map/ppermute | solution.py:11
  77.1 8.0 %collective-permute-start.11 = (bf16[512,128]{1,0:T(8,128)(2,1)S(1)}, bf16[512,128]{1,0:T(8,128)(2,1)S(1)}, u32[]{:S(2)}, u32[]{:S(2)}) collective-permute-start(bf16[512,128]{1,0:T(8,128)(2,1)S(1)} %bitcast.55), channel_id=1, source_target_pairs={{0,28},{4,0},{8,4},{12,8},{16,12},{20,16},{24,20},{28,24},{1,29},{... | collective-permute-start | bytes 393224 | tf_op jit(solution)/shard_map/ppermute | solution.py:11
  80.9 6.0 %collective-permute-start.18 = (bf16[136,256]{1,0:T(8,128)(2,1)S(1)}, bf16[136,256]{1,0:T(8,128)(2,1)S(1)}, u32[]{:S(2)}, u32[]{:S(2)}) collective-permute-start(bf16[136,256]{1,0:T(8,128)(2,1)S(1)} %add_convert_fusion), channel_id=1, source_target_pairs={{0,1},{1,0},{2,3},{3,2},{4,5},{5,4},{6,7},{7,6},{8,9},{9,8},{10,11... | collective-permute-start | bytes 208904 | tf_op jit(solution)/shard_map/ppermute | solution.py:122

commit v13 on v10

--- a/solution.py
+++ b/solution.py
@@ -26,10 +26,17 @@
 
     group = slot_chunk(chunk, 24)
 
-    kept = list(range(keep * own_tiles, (keep + 1) * own_tiles))
+    if keep is None:
+        kept = list(range(out_tiles))
+    else:
+        kept = list(range(keep * own_tiles, (keep + 1) * own_tiles))
     sent = [t for t in range(out_tiles) if t not in kept]
 
-    def kernel(rows_ref, cols_ref, counts_ref, adj_ref, opnd_ref, kept_ref, sent_ref, out_ref, prod_ref):
+    def kernel(rows_ref, cols_ref, counts_ref, adj_ref, opnd_ref, kept_ref, *rest):
+        if sent:
+            sent_ref, out_ref, prod_ref = rest
+        else:
+            out_ref, prod_ref = rest
         k = pl.program_id(0)
         j = pl.program_id(1)
 
@@ -67,7 +74,7 @@
         @pl.when((k == offset_count - 1) & (j == chunks - 1))
         def _():
             for place, t in enumerate(kept):
-                kept_ref[place] = out_ref[t] if forward else out_ref[t].T
+                kept_ref[place] = out_ref[t] if forward or keep is None else out_ref[t].T
             for place, t in enumerate(sent):
                 value = out_ref[t] if forward else out_ref[t].T
                 sent_ref[place] = value.astype(sent_ref.dtype)
@@ -93,7 +100,7 @@
             out_specs=[
                 pl.BlockSpec((len(kept), tile, out_width), whole_map),
                 pl.BlockSpec((len(sent), tile, out_width), whole_map),
-            ],
+            ][: 1 + bool(sent)],
             scratch_shapes=[
                 pltpu.VMEM((out_tiles, tile, out_width), jnp.float32),
                 pltpu.VMEM((chunk, tile, out_width), jnp.float32),
@@ -102,7 +109,7 @@
         out_shape=[
             jax.ShapeDtypeStruct((len(kept), tile, out_width), jnp.float32),
             jax.ShapeDtypeStruct((len(sent), tile, out_width), jnp.bfloat16),
-        ],
+        ][: 1 + bool(sent)],
         compiler_params=pltpu.CompilerParams(dimension_semantics=("arbitrary", "arbitrary")),
         cost_estimate=pl.CostEstimate(
             flops=flops, transcendentals=0, bytes_accessed=bytes_accessed
@@ -173,18 +180,16 @@
     grad_hidden = (row_scale[:, None] * grad_rows).astype(jnp.bfloat16)
     block_grad = lax.all_gather(grad_hidden, "col", axis=0, tiled=True)
     grad_tiles_t = jnp.swapaxes(block_grad.reshape(block_tiles, tile_size, features), 1, 2)
-    own_back, sent_back = tile_products(
+    (outgoing_t,) = tile_products(
         tile_rows, tile_cols, counts, adjacency, grad_tiles_t, offset_count * own_tiles,
-        own_tiles, False, reach_steps,
-    )
-    total_back = own_back.reshape(own_rows, features)
-    sent_back = sent_back.reshape(offset_count - 1, own_rows, features)
-    place = 0
+        own_tiles, False, None,
+    )
+    outgoing = jnp.swapaxes(outgoing_t, 1, 2).reshape(offset_count, own_rows, features)
+    total_back = outgoing[reach_steps]
     for k in range(offset_count):
         if k != reach_steps:
-            received = from_behind(sent_back[place], "blk", k - reach_steps)
-            total_back = total_back + received.astype(jnp.float32)
-            place += 1
+            sent = outgoing[k].astype(jnp.bfloat16)
+            total_back = total_back + from_behind(sent, "blk", k - reach_steps).astype(jnp.float32)
     grad_features = (row_scale[:, None] * total_back).astype(jnp.bfloat16)
     return (activations, grad_features, weight_sum * norm_factor, bias_sum * norm_factor)
 

time: 92.2 us -> 90.3 us (0.979)
  starting transfers between devices: 24.8 us -> 21.6 us
  waiting for transfers between devices: 22.5 us -> 20.7 us
  Pallas kernels: 22.7 us -> 23.7 us
  blocking collectives: 6.56 us -> 7.53 us
    ppermute x5, waiting for transfers between devices: 7.5 us -> 4.27 us  [all_sum(): lax.ppermute(value, axes, [(i, i ^ bit) for i in range(size)])]
    ppermute x5, starting transfers between devices: 6.23 us -> 4.46 us  [all_sum(): lax.ppermute(value, axes, [(i, i ^ bit) for i in range(size)])]
    ppermute x11, starting transfers between devices: 18.6 us -> 17.1 us  [from_behind(): lax.ppermute(value, axis, [(i, (i + by) % length) for i in range(length)])]
    another operation x0 -> x1, other arithmetic: none -> 1.42 us
    ppermute x11, waiting for transfers between devices: 15 us -> 16.4 us  [from_behind(): lax.ppermute(value, axis, [(i, (i + by) % length) for i in range(length)])]
    pallas_call x2, Pallas kernels: 22.7 us -> 23.7 us  [tile_products(): pl.pallas_call(kernel, grid_spec=pltpu.PrefetchScalarGridSpec(num_scalar_...]
    all_gather x1, blocking collectives: 6.56 us -> 7.53 us  [local(): block_grad = lax.all_gather(grad_hidden, 'col', axis=0, tiled=True)]
    convert_element_type x1, other arithmetic: 1.75 us -> 0.79 us  [local(): grad_features = (row_scale[:, None] * total_back).astype(jnp.bfloat16)]
  transfers between devices with their start and end apart: 16 -> 16, of which waited for: 8 -> 6; matrix products, arithmetic and copies ran while one was open for 7% -> 8% of each run, Pallas kernels for 13% -> 13%
where the time goes in v13:
time: 90.3 us; the launch traced here: 89.6 us
  Pallas kernels  23.7 us (26%)
  starting transfers between devices  21.6 us (24%)
  waiting for transfers between devices  20.7 us (23%)
  other arithmetic  8.87 us (10%)
  blocking collectives  7.53 us (8%)
  local copies, waits for them, and re-layouts  4.79 us (5%)
  matrix products  1.56 us (2%)
    pallas_call x2, Pallas kernels, tile_products(): pl.pallas_call(kernel, grid_spec=pltpu.PrefetchScalarGridSpec(num_scalar_...  23.7 us
    ppermute x11, starting transfers between devices, from_behind(): lax.ppermute(value, axis, [(i, (i + by) % length) for i in range(length)])  17.1 us
    ppermute x11, waiting for transfers between devices, from_behind(): lax.ppermute(value, axis, [(i, (i + by) % length) for i in range(length)])  16.4 us
    all_gather x1, blocking collectives, local(): block_grad = lax.all_gather(grad_hidden, 'col', axis=0, tiled=True)  7.53 us
    ppermute x5, starting transfers between devices, all_sum(): lax.ppermute(value, axes, [(i, i ^ bit) for i in range(size)])  4.46 us
    ppermute x5, waiting for transfers between devices, all_sum(): lax.ppermute(value, axes, [(i, i ^ bit) for i in range(size)])  4.27 us
  transfers between devices with their start and end apart: 16, of which 6 were waited for; matrix products, arithmetic and copies ran while one was open for 8% of the time, Pallas kernels for 13%

profile of v13, /device:TPU:0, one launch (start us, length us, event | category | flops | bytes accessed | tf_op | source)
XLA Modules:
  0.0 89.6 jit_solution(3324157746329240570)
XLA Ops:
  0.6 0.0 copy-start
  0.6 0.7 convert_rsqrt_fusion
  1.4 1.0 %multiply_convert_fusion.1 = bf16[512,128]{1,0:T(8,128)(2,1)S(1)} fusion(bf16[512,128]{1,0:T(8,128)(2,1)} %param.9, f32[512]{0:T(512)S(1)} %convert_rsqrt_fusion), kind=kLoop, calls=%fused_computation.17 | loop fusion | flops 196608 | bytes 264192 | tf_op jit(solution)/shard_map/convert_element_type | solution.py:145
  2.4 6.1 %collective-permute-start.2 = (bf16[512,128]{1,0:T(8,128)(2,1)S(1)}, bf16[512,128]{1,0:T(8,128)(2,1)S(1)}, u32[]{:S(2)}, u32[]{:S(2)}) collective-permute-start(bf16[512,128]{1,0:T(8,128)(2,1)S(1)} %multiply_convert_fusion.1), channel_id=1, source_target_pairs={{0,28},{4,0},{8,4},{12,8},{16,12},{20,16},{24,20},{28,24},{1,29},{... | collective-permute-start | bytes 393224 | tf_op jit(solution)/shard_map/ppermute | solution.py:11
  8.5 0.4 collective-permute-start.3
  8.9 0.6 collective-permute-start.1
  9.6 0.9 %collective-permute-start = (bf16[512,128]{1,0:T(8,128)(2,1)S(1)}, bf16[512,128]{1,0:T(8,128)(2,1)S(1)}, u32[]{:S(2)}, u32[]{:S(2)}) collective-permute-start(bf16[512,128]{1,0:T(8,128)(2,1)S(1)} %multiply_convert_fusion.1), channel_id=1, source_target_pairs={{0,8},{4,12},{8,16},{12,20},{16,24},{20,28},{24,0},{28,4},{1,9},{5... | collective-permute-start | bytes 393224 | tf_op jit(solution)/shard_map/ppermute | solution.py:11
  10.5 1.3 %add_select_fusion.rows_ref = s32[360]{0:T(512)} fusion(s32[360]{0:T(512)} %rows_ref.1, s32[]{:T(128)S(6)} %mul.57), kind=kLoop, calls=%fused_computation.28 | loop fusion | flops 4320 | bytes 2884 | tf_op jit(solution)/shard_map/jit(remainder)/select_n | solution.py:152
  11.8 6.0 %collective-permute-done = bf16[512,128]{1,0:T(8,128)(2,1)S(1)} collective-permute-done((bf16[512,128]{1,0:T(8,128)(2,1)S(1)}, bf16[512,128]{1,0:T(8,128)(2,1)S(1)}, u32[]{:S(2)}, u32[]{:S(2)}) %collective-permute-start) | collective-permute-done | bytes 131104 | tf_op jit(solution)/shard_map/ppermute | solution.py:11
  17.8 0.0 collective-permute-done.1
  17.8 1.1 %bitcast_dynamic-update-slice_fusion.2 = bf16[5,512,128]{2,1,0:T(8,128)(2,1)S(1)} fusion(bf16[5,512,128]{2,1,0:T(8,128)(2,1)S(1)} %bitcast_dynamic-update-slice_fusion.3, bf16[512,128]{1,0:T(8,128)(2,1)} %param.9, f32[512]{0:T(512)S(1)} %convert_rsqrt_fusion), kind=kLoop, calls=%fused_computation.22 | loop fusion | flops 196608 | bytes 264192
  18.9 0.0 collective-permute-done.2
  19.0 0.0 collective-permute-done.3
  19.0 0.0 copy-start.1
  19.0 0.8 copy-done.1
  19.9 11.7 %shard_map.120 = (f32[4,128,128]{2,1,0:T(8,128)}, bf16[12,128,128]{2,1,0:T(8,128)(2,1)}) custom-call(s32[360]{0:T(512)} %add_select_fusion.rows_ref, s32[360]{0:T(512)} %cols_ref.3, s32[5]{0:T(128)} %counts_ref.3, bf16[360,128,128]{2,1,0:T(8,128)(2,1)} %adj_ref.3, bf16[20,128,128]{2,1,0:T(8,128)(2,1)} %bitcast.55), custom_call_target="tpu_custom_call" | custom-call | flops 1509949440 | bytes 13500416 | tf_op jit(solution)/shard_map/pallas_call | solution.py:91
  31.6 1.1 %fusion.17 = (bf16[4,128,128]{2,1,0:T(8,128)(2,1)S(1)}, bf16[4,128,128]{2,1,0:T(8,128)(2,1)S(1)}, bf16[4,128,128]{2,1,0:T(8,128)(2,1)S(1)}) fusion(bf16[12,128,128]{2,1,0:T(8,128)(2,1)} %get-tuple-element.7), kind=kLoop, calls=%fused_computation.38 | loop fusion | bytes 786432 | tf_op jit(solution)/shard_map/slice | solution.py:159
  32.7 1.2 %collective-permute-start.6 = (bf16[512,128]{1,0:T(8,128)(2,1)S(1)}, bf16[512,128]{1,0:T(8,128)(2,1)S(1)}, u32[]{:S(2)}, u32[]{:S(2)}) collective-permute-start(bf16[512,128]{1,0:T(8,128)(2,1)S(1)} %bitcast.62), channel_id=1, source_target_pairs={{0,3},{1,0},{2,1},{3,2},{4,7},{5,4},{6,5},{7,6},{8,11},{9,8},{10,9... | collective-permute-start | bytes 393224 | tf_op jit(solution)/shard_map/ppermute | solution.py:11
  33.9 0.0 collective-permute-start.4
  33.9 1.7 %collective-permute-start.5 = (bf16[512,128]{1,0:T(8,128)(2,1)S(1)}, bf16[512,128]{1,0:T(8,128)(2,1)S(1)}, u32[]{:S(2)}, u32[]{:S(2)}) collective-permute-start(bf16[512,128]{1,0:T(8,128)(2,1)S(1)} %bitcast.60), channel_id=1, source_target_pairs={{0,2},{1,3},{2,0},{3,1},{4,6},{5,7},{6,4},{7,5},{8,10},{9,11},{10,... | collective-permute-start | bytes 393224 | tf_op jit(solution)/shard_map/ppermute | solution.py:11
  35.6 0.1 pad.2.clone
  35.6 1.5 %collective-permute-done.6 = bf16[512,128]{1,0:T(8,128)(2,1)S(1)} collective-permute-done((bf16[512,128]{1,0:T(8,128)(2,1)S(1)}, bf16[512,128]{1,0:T(8,128)(2,1)S(1)}, u32[]{:S(2)}, u32[]{:S(2)}) %collective-permute-start.6) | collective-permute-done | bytes 131104 | tf_op jit(solution)/shard_map/ppermute | solution.py:11
  37.1 2.6 %collective-permute-done.4 = bf16[512,128]{1,0:T(8,128)(2,1)S(1)} collective-permute-done((bf16[512,128]{1,0:T(8,128)(2,1)S(1)}, bf16[512,128]{1,0:T(8,128)(2,1)S(1)}, u32[]{:S(2)}, u32[]{:S(2)}) %collective-permute-start.4) | collective-permute-done | bytes 131104 | tf_op jit(solution)/shard_map/ppermute | solution.py:11
  39.7 2.3 %collective-permute-done.5 = bf16[512,128]{1,0:T(8,128)(2,1)S(1)} collective-permute-done((bf16[512,128]{1,0:T(8,128)(2,1)S(1)}, bf16[512,128]{1,0:T(8,128)(2,1)S(1)}, u32[]{:S(2)}, u32[]{:S(2)}) %collective-permute-start.5) | collective-permute-done | bytes 131104 | tf_op jit(solution)/shard_map/ppermute | solution.py:11
  41.9 1.1 %fusion.9 = bf16[512,128]{1,0:T(8,128)(2,1)S(1)} fusion(f32[4,128,128]{2,1,0:T(8,128)} %get-tuple-element.6, bf16[512,128]{1,0:T(8,128)(2,1)S(1)} %collective-permute-done.6, bf16[512,128]{1,0:T(8,128)(2,1)S(1)} %collective-permute-done.5, bf16[512,128]{1,0:T(8,128)(2,1)S(1)} %collective-permute-done.4, f32[512]{0:T(512)S(1)} %convert_rsqrt_fusion), kind=kLoop, calls=%fused_computation.16 | loop fusion | flops 524288 | bytes 788480 | tf_op jit(solution)/shard_map/convert_element_type | solution.py:160
  43.0 0.0 copy-done
  43.0 0.0 copy-done.2
  43.0 0.0 copy-done.3
  43.0 1.1 %fusion.15 = (f32[256]{0:T(256)S(1)}, bf16[512,256]{1,0:T(8,128)(2,1)S(1)}, bf16[512,256]{1,0:T(8,128)(2,1)}) fusion(bf16[512,256]{1,0:T(8,128)(2,1)S(1)} %copy-done.2, f32[256]{0:T(256)S(1)} %copy-done.3, bf16[512,128]{1,0:T(8,128)(2,1)S(1)} %fusion.9, bf16[128,256]{1,0:T(8,128)(2,1)S(1)} %copy-done), kind=kOutput, calls=%fused_computation.36 | convolution fusion | flops 35389184 | bytes 985088 | tf_op jit(solution)/shard_map/dot_general | solution.py:161
  44.2 0.2 fusion.10
  44.4 0.2 fusion
  44.6 0.1 maximum_maximum_fusion
  44.7 2.1 %collective-permute-start.11 = (f32[136,256]{1,0:T(8,128)S(1)}, f32[136,256]{1,0:T(8,128)S(1)}, u32[]{:S(2)}, u32[]{:S(2)}) collective-permute-start(f32[136,256]{1,0:T(8,128)S(1)} %maximum_maximum_fusion), channel_id=1, source_target_pairs={{0,16},{1,17},{2,18},{3,19},{4,20},{5,21},{6,22},{7,23},{8,24},{9,... | collective-permute-start | bytes 417800 | tf_op jit(solution)/shard_map/ppermute | solution.py:128
  46.8 7.5 %all_gather.3 = bf16[2048,128]{1,0:T(8,128)(2,1)S(1)} all-gather(bf16[512,128]{1,0:T(8,128)(2,1)S(1)} %fusion), channel_id=1, replica_groups=mesh['blk'=8,'col'=4] {'col'}, dimensions={0}, use_global_device_ids=true | all-gather | bytes 655360 | tf_op jit(solution)/shard_map/all_gather | solution.py:181
  54.4 1.0 %copy.13 = bf16[16,128,128]{1,2,0:T(8,128)(2,1)} copy(bf16[16,128,128]{2,1,0:T(8,128)(2,1)S(1)} %bitcast.54) | data formatting | bytes 1048576 | tf_op jit(solution)/shard_map/reshape | solution.py:182
  55.4 0.0 collective-permute-done.11
  55.4 0.1 fusion.14
  55.5 0.1 collective-permute-start.12
  55.6 12.0 %shard_map.121 = f32[20,128,128]{2,1,0:T(8,128)} custom-call(s32[360]{0:T(512)} %rows_ref.1, s32[360]{0:T(512)} %cols_ref.3, s32[5]{0:T(128)} %counts_ref.3, bf16[360,128,128]{2,1,0:T(8,128)(2,1)} %adj_ref.3, bf16[16,128,128]{2,1,0:T(8,128)(2,1)} %bitcast.53), custom_call_target="tpu_custom_call" | custom-call | flops 1509949440 | bytes 13631488 | tf_op jit(solution)/shard_map/pallas_call | solution.py:91
  67.6 0.0 collective-permute-done.12
  67.6 0.4 collective-permute-start.13
  68.0 1.4 %bitcast_convert_fusion = bf16[20,128,128]{1,2,0:T(8,128)(2,1)S(1)} fusion(f32[20,128,128]{2,1,0:T(8,128)} %shard_map.121), kind=kLoop, calls=%fused_computation.34 | loop fusion | flops 327680 | bytes 1966080 | tf_op jit(solution)/shard_map/convert.3
  69.4 4.3 %collective-permute-done.13 = f32[136,256]{1,0:T(8,128)S(1)} collective-permute-done((f32[136,256]{1,0:T(8,128)S(1)}, f32[136,256]{1,0:T(8,128)S(1)}, u32[]{:S(2)}, u32[]{:S(2)}) %collective-permute-start.13) | collective-permute-done | bytes 139296 | tf_op jit(solution)/shard_map/ppermute | solution.py:128
  73.7 1.8 %collective-permute-start.14 = (f32[136,256]{1,0:T(8,128)S(1)}, f32[136,256]{1,0:T(8,128)S(1)}, u32[]{:S(2)}, u32[]{:S(2)}) collective-permute-start(f32[136,256]{1,0:T(8,128)S(1)} %add.70), channel_id=1, source_target_pairs={{0,2},{1,3},{2,0},{3,1},{4,6},{5,7},{6,4},{7,5},{8,10},{9,11},{10,... | collective-permute-start | bytes 417800 | tf_op jit(solution)/shard_map/ppermute | solution.py:128
  75.5 0.1 copy.15
  75.7 0.1 copy.18
  75.8 0.1 copy.17
  75.9 0.1 copy.16
  76.1 2.3 %collective-permute-start.8 = (bf16[512,128]{1,0:T(8,128)(2,1)S(1)}, bf16[512,128]{1,0:T(8,128)(2,1)S(1)}, u32[]{:S(2)}, u32[]{:S(2)}) collective-permute-start(bf16[512,128]{1,0:T(8,128)(2,1)S(1)} %bitcast.59), channel_id=1, source_target_pairs={{0,28},{4,0},{8,4},{12,8},{16,12},{20,16},{24,20},{28,24},{1,29},{... | collective-permute-start | bytes 393224 | tf_op jit(solution)/shard_map/ppermute | solution.py:11
  78.4 0.0 collective-permute-start.9
  78.4 1.2 %collective-permute-start.10 = (bf16[512,128]{1,0:T(8,128)(2,1)S(1)}, bf16[512,128]{1,0:T(8,128)(2,1)S(1)}, u32[]{:S(2)}, u32[]{:S(2)}) collective-permute-start(bf16[512,128]{1,0:T(8,128)(2,1)S(1)} %bitcast.57), channel_id=1, source_target_pairs={{0,8},{4,12},{8,16},{12,20},{16,24},{20,28},{24,0},{28,4},{1,9},{5... | collective-permute-start | bytes 393224 | tf_op jit(solution)/shard_map/ppermute | solution.py:11
  79.7 2.6 %collective-permute-start.7 = (bf16[512,128]{1,0:T(8,128)(2,1)S(1)}, bf16[512,128]{1,0:T(8,128)(2,1)S(1)}, u32[]{:S(2)}, u32[]{:S(2)}) collective-permute-start(bf16[512,128]{1,0:T(8,128)(2,1)S(1)} %bitcast.56), channel_id=1, source_target_pairs={{0,24},{4,28},{8,0},{12,4},{16,8},{20,12},{24,16},{28,20},{1,25},{... | collective-permute-start | bytes 393224 | tf_op jit(solution)/shard_map/ppermute | solution.py:11
  82.2 1.0 %slice.52 = f32[4,128,128]{1,2,0:T(8,128)S(1)} slice(f32[20,128,128]{1,2,0:T(8,128)} %bitcast.52), slice={[8:12], [0:128], [0:128]} | slice | bytes 524288 | tf_op jit(solution)/shard_map/slice | solution.py:188
  83.2 0.1 copy.14
  83.3 0.0 collective-permute-done.14
  83.4 0.1 collective-permute-start.15
  83.5 0.0 collective-permute-done.8
  83.5 4.1 %collective-permute-done.9 = bf16[512,128]{1,0:T(8,128)(2,1)S(1)} collective-permute-done((bf16[512,128]{1,0:T(8,128)(2,1)S(1)}, bf16[512,128]{1,0:T(8,128)(2,1)S(1)}, u32[]{:S(2)}, u32[]{:S(2)}) %collective-permute-start.9) | collective-permute-done | bytes 131104 | tf_op jit(solution)/shard_map/ppermute | solution.py:11
  87.6 0.0 collective-permute-done.10
  87.6 0.0 collective-permute-done.7
  87.6 0.8 fusion.5
  88.4 0.0 collective-permute-done.15
  88.4 0.6 slice_multiply_fusion.1
  89.0 0.7 slice_multiply_fusion
  (12 shorter events, 0.2 us)
Async XLA Ops:
  0.6 42.4 %copy-start = (bf16[128,256]{1,0:T(8,128)(2,1)S(1)}, bf16[128,256]{1,0:T(8,128)(2,1)}, u32[]{:S(2)}) copy-start(bf16[128,256]{1,0:T(8,128)(2,1)} %param.15) | copy-start | bytes 196612
  2.4 16.5 %collective-permute-start.2 = (bf16[512,128]{1,0:T(8,128)(2,1)S(1)}, bf16[512,128]{1,0:T(8,128)(2,1)S(1)}, u32[]{:S(2)}, u32[]{:S(2)}) collective-permute-start(bf16[512,128]{1,0:T(8,128)(2,1)S(1)} %multiply_convert_fusion.1), channel_id=1, source_target_pairs={{0,28},{4,0},{8,4},{12,8},{16,12},{20,16},{24,20},{28,24},{1,29},{... | collective-permute-start | bytes 393224 | tf_op jit(solution)/shard_map/ppermute | solution.py:11
  8.5 10.5 %collective-permute-start.3 = (bf16[512,128]{1,0:T(8,128)(2,1)S(1)}, bf16[512,128]{1,0:T(8,128)(2,1)S(1)}, u32[]{:S(2)}, u32[]{:S(2)}) collective-permute-start(bf16[512,128]{1,0:T(8,128)(2,1)S(1)} %multiply_convert_fusion.1), channel_id=1, source_target_pairs={{0,24},{4,28},{8,0},{12,4},{16,8},{20,12},{24,16},{28,20},{1,25},{... | collective-permute-start | bytes 393224 | tf_op jit(solution)/shard_map/ppermute | solution.py:11
  8.9 8.9 %collective-permute-start.1 = (bf16[512,128]{1,0:T(8,128)(2,1)S(1)}, bf16[512,128]{1,0:T(8,128)(2,1)S(1)}, u32[]{:S(2)}, u32[]{:S(2)}) collective-permute-start(bf16[512,128]{1,0:T(8,128)(2,1)S(1)} %multiply_convert_fusion.1), channel_id=1, source_target_pairs={{0,4},{4,8},{8,12},{12,16},{16,20},{20,24},{24,28},{28,0},{1,5},{5... | collective-permute-start | bytes 393224 | tf_op jit(solution)/shard_map/ppermute | solution.py:11
  9.6 8.2 %collective-permute-start = (bf16[512,128]{1,0:T(8,128)(2,1)S(1)}, bf16[512,128]{1,0:T(8,128)(2,1)S(1)}, u32[]{:S(2)}, u32[]{:S(2)}) collective-permute-start(bf16[512,128]{1,0:T(8,128)(2,1)S(1)} %multiply_convert_fusion.1), channel_id=1, source_target_pairs={{0,8},{4,12},{8,16},{12,20},{16,24},{20,28},{24,0},{28,4},{1,9},{5... | collective-permute-start | bytes 393224 | tf_op jit(solution)/shard_map/ppermute | solution.py:11
  19.0 0.9 copy-start.1
  31.6 11.5 %copy-start.2 = (bf16[512,256]{1,0:T(8,128)(2,1)S(1)}, bf16[512,256]{1,0:T(8,128)(2,1)}, u32[]{:S(2)}) copy-start(bf16[512,256]{1,0:T(8,128)(2,1)} %param.17) | copy-start | bytes 786436
  31.6 11.5 %copy-start.3 = (f32[256]{0:T(256)S(1)}, f32[256]{0:T(256)}, u32[]{:S(2)}) copy-start(f32[256]{0:T(256)} %param.16) | copy-start | bytes 3076
  32.7 4.4 %collective-permute-start.6 = (bf16[512,128]{1,0:T(8,128)(2,1)S(1)}, bf16[512,128]{1,0:T(8,128)(2,1)S(1)}, u32[]{:S(2)}, u32[]{:S(2)}) collective-permute-start(bf16[512,128]{1,0:T(8,128)(2,1)S(1)} %bitcast.62), channel_id=1, source_target_pairs={{0,3},{1,0},{2,1},{3,2},{4,7},{5,4},{6,5},{7,6},{8,11},{9,8},{10,9... | collective-permute-start | bytes 393224 | tf_op jit(solution)/shard_map/ppermute | solution.py:11
  33.9 5.8 %collective-permute-start.4 = (bf16[512,128]{1,0:T(8,128)(2,1)S(1)}, bf16[512,128]{1,0:T(8,128)(2,1)S(1)}, u32[]{:S(2)}, u32[]{:S(2)}) collective-permute-start(bf16[512,128]{1,0:T(8,128)(2,1)S(1)} %bitcast.61), channel_id=1, source_target_pairs={{0,1},{1,2},{2,3},{3,0},{4,5},{5,6},{6,7},{7,4},{8,9},{9,10},{10,1... | collective-permute-start | bytes 393224 | tf_op jit(solution)/shard_map/ppermute | solution.py:11
  33.9 8.1 %collective-permute-start.5 = (bf16[512,128]{1,0:T(8,128)(2,1)S(1)}, bf16[512,128]{1,0:T(8,128)(2,1)S(1)}, u32[]{:S(2)}, u32[]{:S(2)}) collective-permute-start(bf16[512,128]{1,0:T(8,128)(2,1)S(1)} %bitcast.60), channel_id=1, source_target_pairs={{0,2},{1,3},{2,0},{3,1},{4,6},{5,7},{6,4},{7,5},{8,10},{9,11},{10,... | collective-permute-start | bytes 393224 | tf_op jit(solution)/shard_map/ppermute | solution.py:11
  44.7 10.7 %collective-permute-start.11 = (f32[136,256]{1,0:T(8,128)S(1)}, f32[136,256]{1,0:T(8,128)S(1)}, u32[]{:S(2)}, u32[]{:S(2)}) collective-permute-start(f32[136,256]{1,0:T(8,128)S(1)} %maximum_maximum_fusion), channel_id=1, source_target_pairs={{0,16},{1,17},{2,18},{3,19},{4,20},{5,21},{6,22},{7,23},{8,24},{9,... | collective-permute-start | bytes 417800 | tf_op jit(solution)/shard_map/ppermute | solution.py:128
  55.5 12.1 %collective-permute-start.12 = (f32[136,256]{1,0:T(8,128)S(1)}, f32[136,256]{1,0:T(8,128)S(1)}, u32[]{:S(2)}, u32[]{:S(2)}) collective-permute-start(f32[136,256]{1,0:T(8,128)S(1)} %fusion.14), channel_id=1, source_target_pairs={{0,8},{1,9},{2,10},{3,11},{4,12},{5,13},{6,14},{7,15},{8,0},{9,1},... | collective-permute-start | bytes 417800 | tf_op jit(solution)/shard_map/ppermute | solution.py:128
  67.6 6.1 %collective-permute-start.13 = (f32[136,256]{1,0:T(8,128)S(1)}, f32[136,256]{1,0:T(8,128)S(1)}, u32[]{:S(2)}, u32[]{:S(2)}) collective-permute-start(f32[136,256]{1,0:T(8,128)S(1)} %add.69), channel_id=1, source_target_pairs={{0,4},{1,5},{2,6},{3,7},{4,0},{5,1},{6,2},{7,3},{8,12},{9,13},{10,... | collective-permute-start | bytes 417800 | tf_op jit(solution)/shard_map/ppermute | solution.py:128
  73.7 9.7 %collective-permute-start.14 = (f32[136,256]{1,0:T(8,128)S(1)}, f32[136,256]{1,0:T(8,128)S(1)}, u32[]{:S(2)}, u32[]{:S(2)}) collective-permute-start(f32[136,256]{1,0:T(8,128)S(1)} %add.70), channel_id=1, source_target_pairs={{0,2},{1,3},{2,0},{3,1},{4,6},{5,7},{6,4},{7,5},{8,10},{9,11},{10,... | collective-permute-start | bytes 417800 | tf_op jit(solution)/shard_map/ppermute | solution.py:128
  76.1 7.4 %collective-permute-start.8 = (bf16[512,128]{1,0:T(8,128)(2,1)S(1)}, bf16[512,128]{1,0:T(8,128)(2,1)S(1)}, u32[]{:S(2)}, u32[]{:S(2)}) collective-permute-start(bf16[512,128]{1,0:T(8,128)(2,1)S(1)} %bitcast.59), channel_id=1, source_target_pairs={{0,28},{4,0},{8,4},{12,8},{16,12},{20,16},{24,20},{28,24},{1,29},{... | collective-permute-start | bytes 393224 | tf_op jit(solution)/shard_map/ppermute | solution.py:11
  78.4 9.2 %collective-permute-start.9 = (bf16[512,128]{1,0:T(8,128)(2,1)S(1)}, bf16[512,128]{1,0:T(8,128)(2,1)S(1)}, u32[]{:S(2)}, u32[]{:S(2)}) collective-permute-start(bf16[512,128]{1,0:T(8,128)(2,1)S(1)} %bitcast.58), channel_id=1, source_target_pairs={{0,4},{4,8},{8,12},{12,16},{16,20},{20,24},{24,28},{28,0},{1,5},{5... | collective-permute-start | bytes 393224 | tf_op jit(solution)/shard_map/ppermute | solution.py:11
  78.4 9.2 %collective-permute-start.10 = (bf16[512,128]{1,0:T(8,128)(2,1)S(1)}, bf16[512,128]{1,0:T(8,128)(2,1)S(1)}, u32[]{:S(2)}, u32[]{:S(2)}) collective-permute-start(bf16[512,128]{1,0:T(8,128)(2,1)S(1)} %bitcast.57), channel_id=1, source_target_pairs={{0,8},{4,12},{8,16},{12,20},{16,24},{20,28},{24,0},{28,4},{1,9},{5... | collective-permute-start | bytes 393224 | tf_op jit(solution)/shard_map/ppermute | solution.py:11
  79.7 7.9 %collective-permute-start.7 = (bf16[512,128]{1,0:T(8,128)(2,1)S(1)}, bf16[512,128]{1,0:T(8,128)(2,1)S(1)}, u32[]{:S(2)}, u32[]{:S(2)}) collective-permute-start(bf16[512,128]{1,0:T(8,128)(2,1)S(1)} %bitcast.56), channel_id=1, source_target_pairs={{0,24},{4,28},{8,0},{12,4},{16,8},{20,12},{24,16},{28,20},{1,25},{... | collective-permute-start | bytes 393224 | tf_op jit(solution)/shard_map/ppermute | solution.py:11
  83.4 5.0 %collective-permute-start.15 = (f32[136,256]{1,0:T(8,128)S(1)}, f32[136,256]{1,0:T(8,128)S(1)}, u32[]{:S(2)}, u32[]{:S(2)}) collective-permute-start(f32[136,256]{1,0:T(8,128)S(1)} %add.71), channel_id=1, source_target_pairs={{0,1},{1,0},{2,3},{3,2},{4,5},{5,4},{6,7},{7,6},{8,9},{9,8},{10,11... | collective-permute-start | bytes 417800 | tf_op jit(solution)/shard_map/ppermute | solution.py:128

commit v14 on v9

--- a/solution.py
+++ b/solution.py
@@ -15,7 +15,7 @@
     return max(c for c in range(1, limit + 1) if slot_count % c == 0)
 
 
-def tile_products(rows, cols, counts, adjacency, operand, out_tiles, own_tiles, forward):
+def tile_products(rows, cols, counts, adjacency, operand, out_tiles, own_tiles, forward, ks=None, acc=None):
     offset_count = counts.shape[0]
     slot_count = adjacency.shape[0] // offset_count
     tile = adjacency.shape[1]
@@ -25,14 +25,30 @@
     out_width = width if forward else tile
 
     group = slot_chunk(chunk, 24)
-
-    def kernel(rows_ref, cols_ref, counts_ref, adj_ref, opnd_ref, out_ref, prod_ref):
-        k = pl.program_id(0)
+    if ks is None:
+        ks = list(range(offset_count))
+
+    def offset_of(p):
+        k = ks[0]
+        for place in range(1, len(ks)):
+            k = jnp.where(p == place, ks[place], k)
+        return k
+
+    def kernel(rows_ref, cols_ref, counts_ref, adj_ref, opnd_ref, *rest):
+        if acc is None:
+            out_ref, prod_ref = rest
+        else:
+            acc_ref, out_ref, prod_ref = rest
+        p = pl.program_id(0)
+        k = offset_of(p)
         j = pl.program_id(1)
 
-        @pl.when((k == 0) & (j == 0))
+        @pl.when((p == 0) & (j == 0))
         def _():
-            out_ref[...] = jnp.zeros_like(out_ref)
+            if acc is None:
+                out_ref[...] = jnp.zeros_like(out_ref)
+            else:
+                out_ref[...] = acc_ref[...]
 
         live = counts_ref[k] - j * chunk
         first = k * slot_count + j * chunk
@@ -44,7 +60,7 @@
                 for i in range(start, start + group):
                     g = first + i
                     if forward:
-                        c = k * own_tiles + cols_ref[g]
+                        c = p * own_tiles + cols_ref[g]
                         prod_ref[i] = jnp.dot(
                             adj_ref[i], opnd_ref[c], preferred_element_type=jnp.float32
                         )
@@ -61,7 +77,8 @@
                 target = rows_ref[g] if forward else k * own_tiles + cols_ref[g]
                 out_ref[target] += prod_ref[i]
 
-    def adj_map(k, j, rows_ref, cols_ref, counts_ref):
+    def adj_map(p, j, rows_ref, cols_ref, counts_ref):
+        k = offset_of(p)
         last = jnp.maximum(counts_ref[k] - 1, 0) // chunk
         return (k * chunks + jnp.minimum(j, last), 0, 0)
 
@@ -74,20 +91,21 @@
         kernel,
         grid_spec=pltpu.PrefetchScalarGridSpec(
             num_scalar_prefetch=3,
-            grid=(offset_count, chunks),
+            grid=(len(ks), chunks),
             in_specs=[
                 pl.BlockSpec((chunk, tile, tile), adj_map),
                 pl.BlockSpec(operand.shape, whole_map),
-            ],
+            ] + ([] if acc is None else [pl.BlockSpec(acc.shape, whole_map)]),
             out_specs=pl.BlockSpec((out_tiles, tile, out_width), whole_map),
             scratch_shapes=[pltpu.VMEM((chunk, tile, out_width), jnp.float32)],
         ),
         out_shape=jax.ShapeDtypeStruct((out_tiles, tile, out_width), jnp.float32),
+        input_output_aliases={} if acc is None else {5: 0},
         compiler_params=pltpu.CompilerParams(dimension_semantics=("arbitrary", "arbitrary")),
         cost_estimate=pl.CostEstimate(
             flops=flops, transcendentals=0, bytes_accessed=bytes_accessed
         ),
-    )(rows, cols, counts, adjacency, operand)
+    )(*([rows, cols, counts, adjacency, operand] + ([] if acc is None else [acc])))
 
 
 def all_sum(value, axes):
@@ -116,16 +134,21 @@
     block_tiles = col_count * own_tiles
     row_scale = lax.rsqrt(degree.astype(jnp.float32))
     source = (row_scale[:, None] * node_features.astype(jnp.float32)).astype(jnp.bfloat16)
-    fetched = [
-        source if k == reach_steps else from_behind(source, "blk", reach_steps - k)
-        for k in range(offset_count)
-    ]
-    source_tiles = jnp.stack(fetched).reshape(offset_count * own_tiles, tile_size, features)
     col_index = lax.axis_index("col")
     rows_here = (tile_rows - col_index * own_tiles) % block_tiles
+    source_tiles = source.reshape(own_tiles, tile_size, features)
     block_sums = tile_products(
-        rows_here, tile_cols, counts, adjacency, source_tiles, block_tiles, own_tiles, True
-    )
+        rows_here, tile_cols, counts, adjacency, source_tiles, block_tiles, own_tiles, True,
+        [reach_steps],
+    )
+    far = [k for k in range(offset_count) if k != reach_steps]
+    fetched = jnp.stack([from_behind(source, "blk", reach_steps - k) for k in far])
+    fetched = fetched.reshape(len(far) * own_tiles, tile_size, features)
+    block_sums = tile_products(
+        rows_here, tile_cols, counts, adjacency, fetched, block_tiles, own_tiles, True,
+        far, block_sums,
+    )
+    block_sums = block_sums.reshape(block_tiles * tile_size, features)
     pieces = block_sums.reshape(col_count, own_rows, features)
     sums = pieces[0]
     for shift in range(1, col_count):

time: 89.2 us -> 87.4 us (0.980)
  Pallas kernels: 22.7 us -> 28.4 us
  waiting for transfers between devices: 18.7 us -> 13.3 us
  starting transfers between devices: 24.6 us -> 22.7 us
    pallas_call x2 -> x3, Pallas kernels: 22.7 us -> 28.4 us  [tile_products(): pl.pallas_call(kernel, grid_spec=pltpu.PrefetchScalarGridSpec(num_scalar_...]
    ppermute x11, waiting for transfers between devices: 15.8 us -> 10.3 us  [from_behind(): lax.ppermute(value, axis, [(i, (i + by) % length) for i in range(length)])]
    ppermute x11, starting transfers between devices: 19.2 us -> 16.6 us  [from_behind(): lax.ppermute(value, axis, [(i, (i + by) % length) for i in range(length)])]
    unnamed x1 -> x0, other arithmetic: 1.07 us -> none
    slice x2 -> x1, local copies, waits for them, and re-layouts: 0.01 us -> 0.97 us  [local(): sums = pieces[0]]
    unnamed x11 -> x8, local copies, waits for them, and re-layouts: 0.94 us -> 0.03 us
    another operation x2 -> x3, other arithmetic: 2.8 us -> 3.61 us
  transfers between devices with their start and end apart: 16 -> 16, of which waited for: 7 -> 6; matrix products, arithmetic and copies ran while one was open for 8% -> 8% of each run, Pallas kernels for 13% -> 20%
where the time goes in v14:
time: 87.4 us; the launch traced here: 86.1 us
  Pallas kernels  28.4 us (32%)
  starting transfers between devices  22.7 us (26%)
  waiting for transfers between devices  13.3 us (15%)
  other arithmetic  9.04 us (10%)
  blocking collectives  6.49 us (7%)
  local copies, waits for them, and re-layouts  3.77 us (4%)
  matrix products  1.58 us (2%)
    pallas_call x3, Pallas kernels, tile_products(): pl.pallas_call(kernel, grid_spec=pltpu.PrefetchScalarGridSpec(num_scalar_...  28.4 us
    ppermute x11, starting transfers between devices, from_behind(): lax.ppermute(value, axis, [(i, (i + by) % length) for i in range(length)])  16.6 us
    ppermute x11, waiting for transfers between devices, from_behind(): lax.ppermute(value, axis, [(i, (i + by) % length) for i in range(length)])  10.3 us
    all_gather x1, blocking collectives, local(): block_grad = lax.all_gather(grad_hidden, 'col', axis=0, tiled=True)  6.49 us
    ppermute x5, starting transfers between devices, all_sum(): lax.ppermute(value, axes, [(i, i ^ bit) for i in range(size)])  6.13 us
    ppermute x5, waiting for transfers between devices, all_sum(): lax.ppermute(value, axes, [(i, i ^ bit) for i in range(size)])  2.93 us
    another operation x2, other arithmetic  2.73 us
  transfers between devices with their start and end apart: 16, of which 6 were waited for; matrix products, arithmetic and copies ran while one was open for 8% of the time, Pallas kernels for 20%

profile of v14, /device:TPU:0, one launch (start us, length us, event | category | flops | bytes accessed | tf_op | source)
XLA Modules:
  0.0 86.1 jit_solution(16998464568656564883)
XLA Ops:
  0.6 0.0 copy-start
  0.6 0.7 convert_rsqrt_fusion
  1.4 1.0 %multiply_convert_fusion.1 = bf16[512,128]{1,0:T(8,128)(2,1)S(1)} fusion(bf16[512,128]{1,0:T(8,128)(2,1)} %param.9, f32[512]{0:T(512)S(1)} %convert_rsqrt_fusion), kind=kLoop, calls=%fused_computation.18 | loop fusion | flops 196608 | bytes 264192 | tf_op jit(solution)/shard_map/convert_element_type | solution.py:136
  2.4 0.0 copy-start.1
  2.4 5.1 %collective-permute-start.3 = (bf16[512,128]{1,0:T(8,128)(2,1)S(1)}, bf16[512,128]{1,0:T(8,128)(2,1)S(1)}, u32[]{:S(2)}, u32[]{:S(2)}) collective-permute-start(bf16[512,128]{1,0:T(8,128)(2,1)S(1)} %multiply_convert_fusion.1), channel_id=1, source_target_pairs={{0,24},{4,28},{8,0},{12,4},{16,8},{20,12},{24,16},{28,20},{1,25},{... | collective-permute-start | bytes 393224 | tf_op jit(solution)/shard_map/ppermute | solution.py:11
  7.5 1.4 %collective-permute-start.2 = (bf16[512,128]{1,0:T(8,128)(2,1)S(1)}, bf16[512,128]{1,0:T(8,128)(2,1)S(1)}, u32[]{:S(2)}, u32[]{:S(2)}) collective-permute-start(bf16[512,128]{1,0:T(8,128)(2,1)S(1)} %multiply_convert_fusion.1), channel_id=1, source_target_pairs={{0,28},{4,0},{8,4},{12,8},{16,12},{20,16},{24,20},{28,24},{1,29},{... | collective-permute-start | bytes 393224 | tf_op jit(solution)/shard_map/ppermute | solution.py:11
  8.9 0.6 collective-permute-start.1
  9.6 0.9 %collective-permute-start = (bf16[512,128]{1,0:T(8,128)(2,1)S(1)}, bf16[512,128]{1,0:T(8,128)(2,1)S(1)}, u32[]{:S(2)}, u32[]{:S(2)}) collective-permute-start(bf16[512,128]{1,0:T(8,128)(2,1)S(1)} %multiply_convert_fusion.1), channel_id=1, source_target_pairs={{0,8},{4,12},{8,16},{12,20},{16,24},{20,28},{24,0},{28,4},{1,9},{5... | collective-permute-start | bytes 393224 | tf_op jit(solution)/shard_map/ppermute | solution.py:11
  10.5 1.3 %add_select_fusion.rows_ref = s32[360]{0:T(512)} fusion(s32[360]{0:T(512)} %rows_ref.1, s32[]{:T(128)S(6)} %mul.57), kind=kLoop, calls=%fused_computation.24 | loop fusion | flops 4320 | bytes 2884 | tf_op jit(solution)/shard_map/jit(remainder)/select_n | solution.py:138
  11.8 4.8 %shard_map.120.rest_0_ = f32[16,128,128]{2,1,0:T(8,128)} custom-call(s32[360]{0:T(512)} %add_select_fusion.rows_ref, s32[360]{0:T(512)} %cols_ref.5, s32[5]{0:T(128)} %counts_ref.5, bf16[360,128,128]{2,1,0:T(8,128)(2,1)} %adj_ref.5, bf16[4,128,128]{2,1,0:T(8,128)(2,1)} %bitcast.51), custom_call_target="tpu_custom_call" | custom-call | flops 1509949440 | bytes 12976128 | tf_op jit(solution)/shard_map/pallas_call | solution.py:90
  16.5 0.0 collective-permute-done.3
  16.5 0.0 collective-permute-done.2
  16.5 1.2 %collective-permute-done.1 = bf16[512,128]{1,0:T(8,128)(2,1)S(1)} collective-permute-done((bf16[512,128]{1,0:T(8,128)(2,1)S(1)}, bf16[512,128]{1,0:T(8,128)(2,1)S(1)}, u32[]{:S(2)}, u32[]{:S(2)}) %collective-permute-start.1) | collective-permute-done | bytes 131104 | tf_op jit(solution)/shard_map/ppermute | solution.py:11
  17.7 0.0 collective-permute-done
  17.7 0.9 %pad_maximum_fusion = bf16[4,512,128]{2,1,0:T(8,128)(2,1)} fusion(bf16[1,512,128]{2,1,0:T(8,128)(2,1)S(1)} %bitcast.59, bf16[1,512,128]{2,1,0:T(8,128)(2,1)S(1)} %bitcast.60, bf16[1,512,128]{2,1,0:T(8,128)(2,1)S(1)} %bitcast.61, bf16[1,512,128]{2,1,0:T(8,128)(2,1)S(1)} %bitcast.62), kind=kLoop, calls=%fused_computation.3 | loop fusion | flops 786432 | bytes 1048576 | tf_op jit(solution)/shard_map/stack | solution.py:145
  18.6 11.1 %shard_map.121 = f32[16,128,128]{2,1,0:T(8,128)} custom-call(s32[360]{0:T(512)} %add_select_fusion.rows_ref, s32[360]{0:T(512)} %cols_ref.5, s32[5]{0:T(128)} %counts_ref.5, bf16[360,128,128]{2,1,0:T(8,128)(2,1)} %adj_ref.5, bf16[16,128,128]{2,1,0:T(8,128)(2,1)} %bitcast.49, f32[16,128,128]{2,1,0:T(8,128)} %shard_map.120.rest_0_), custom_call_target="tpu_custom_call", output_to_operand_aliasing={{}: (5, {})} | custom-call | flops 1509949440 | bytes 13369344 | tf_op jit(solution)/shard_map/pallas_call | solution.py:90
  29.7 1.3 %convert.11 = bf16[16,128,128]{2,1,0:T(8,128)(2,1)S(1)} convert(f32[16,128,128]{2,1,0:T(8,128)} %shard_map.121) | non-fusion elementwise | flops 262144 | bytes 1572864 | tf_op jit(solution)/shard_map/convert.6
  31.0 0.0 copy-start.2
  31.0 0.0 copy-start.3
  31.0 0.1 collective-permute-start.6
  31.1 0.5 collective-permute-start.4
  31.6 0.2 collective-permute-start.5
  31.8 0.1 pad.2.clone
  31.9 1.0 %slice.60 = f32[4,128,128]{2,1,0:T(8,128)S(1)} slice(f32[16,128,128]{2,1,0:T(8,128)} %shard_map.121), slice={[0:4], [0:128], [0:128]} | slice | bytes 524288 | tf_op jit(solution)/shard_map/slice | solution.py:153
  32.9 2.1 %collective-permute-done.6 = bf16[512,128]{1,0:T(8,128)(2,1)S(1)} collective-permute-done((bf16[512,128]{1,0:T(8,128)(2,1)S(1)}, bf16[512,128]{1,0:T(8,128)(2,1)S(1)}, u32[]{:S(2)}, u32[]{:S(2)}) %collective-permute-start.6) | collective-permute-done | bytes 131104 | tf_op jit(solution)/shard_map/ppermute | solution.py:11
  35.0 1.1 %collective-permute-done.4 = bf16[512,128]{1,0:T(8,128)(2,1)S(1)} collective-permute-done((bf16[512,128]{1,0:T(8,128)(2,1)S(1)}, bf16[512,128]{1,0:T(8,128)(2,1)S(1)}, u32[]{:S(2)}, u32[]{:S(2)}) %collective-permute-start.4) | collective-permute-done | bytes 131104 | tf_op jit(solution)/shard_map/ppermute | solution.py:11
  36.1 1.8 %collective-permute-done.5 = bf16[512,128]{1,0:T(8,128)(2,1)S(1)} collective-permute-done((bf16[512,128]{1,0:T(8,128)(2,1)S(1)}, bf16[512,128]{1,0:T(8,128)(2,1)S(1)}, u32[]{:S(2)}, u32[]{:S(2)}) %collective-permute-start.5) | collective-permute-done | bytes 131104 | tf_op jit(solution)/shard_map/ppermute | solution.py:11
  38.0 0.1 fusion.9
  38.1 1.1 %fusion.15 = (f32[256]{0:T(256)S(1)}, bf16[512,256]{1,0:T(8,128)(2,1)S(1)}, bf16[512,256]{1,0:T(8,128)(2,1)}) fusion(bf16[512,256]{1,0:T(8,128)(2,1)S(1)} %copy-done.2, f32[256]{0:T(256)S(1)} %copy-done.3, bf16[512,128]{1,0:T(8,128)(2,1)S(1)} %fusion.9, bf16[128,256]{1,0:T(8,128)(2,1)S(1)} %copy-done), kind=kOutput, calls=%fused_computation.32 | convolution fusion | flops 35389184 | bytes 985088 | tf_op jit(solution)/shard_map/dot_general | solution.py:158
  39.3 0.2 fusion.10
  39.5 0.2 fusion
  39.7 0.1 maximum_maximum_fusion
  39.8 3.3 %collective-permute-start.11 = (f32[136,256]{1,0:T(8,128)S(1)}, f32[136,256]{1,0:T(8,128)S(1)}, u32[]{:S(2)}, u32[]{:S(2)}) collective-permute-start(f32[136,256]{1,0:T(8,128)S(1)} %maximum_maximum_fusion), channel_id=1, source_target_pairs={{0,16},{1,17},{2,18},{3,19},{4,20},{5,21},{6,22},{7,23},{8,24},{9,... | collective-permute-start | bytes 417800 | tf_op jit(solution)/shard_map/ppermute | solution.py:119
  43.1 6.5 %all_gather.3 = bf16[2048,128]{1,0:T(8,128)(2,1)S(1)} all-gather(bf16[512,128]{1,0:T(8,128)(2,1)S(1)} %fusion), channel_id=1, replica_groups=mesh['blk'=8,'col'=4] {'col'}, dimensions={0}, use_global_device_ids=true | all-gather | bytes 655360 | tf_op jit(solution)/shard_map/all_gather | solution.py:178
  49.6 1.0 %copy.14 = bf16[16,128,128]{1,2,0:T(8,128)(2,1)} copy(bf16[16,128,128]{2,1,0:T(8,128)(2,1)S(1)} %bitcast.50) | data formatting | bytes 1048576 | tf_op jit(solution)/shard_map/reshape | solution.py:179
  50.6 0.0 collective-permute-done.11
  50.6 0.1 fusion.14
  50.7 1.6 %collective-permute-start.12 = (f32[136,256]{1,0:T(8,128)S(1)}, f32[136,256]{1,0:T(8,128)S(1)}, u32[]{:S(2)}, u32[]{:S(2)}) collective-permute-start(f32[136,256]{1,0:T(8,128)S(1)} %fusion.14), channel_id=1, source_target_pairs={{0,8},{1,9},{2,10},{3,11},{4,12},{5,13},{6,14},{7,15},{8,0},{9,1},... | collective-permute-start | bytes 417800 | tf_op jit(solution)/shard_map/ppermute | solution.py:119
  52.3 12.5 %shard_map.122 = f32[20,128,128]{2,1,0:T(8,128)} custom-call(s32[360]{0:T(512)} %rows_ref.1, s32[360]{0:T(512)} %cols_ref.5, s32[5]{0:T(128)} %counts_ref.5, bf16[360,128,128]{2,1,0:T(8,128)(2,1)} %adj_ref.5, bf16[16,128,128]{2,1,0:T(8,128)(2,1)} %bitcast.48), custom_call_target="tpu_custom_call" | custom-call | flops 1509949440 | bytes 13631488 | tf_op jit(solution)/shard_map/pallas_call | solution.py:90
  64.8 0.0 collective-permute-done.12
  64.8 0.8 collective-permute-start.13
  65.6 1.4 %bitcast_convert_fusion = bf16[20,128,128]{1,2,0:T(8,128)(2,1)S(1)} fusion(f32[20,128,128]{2,1,0:T(8,128)} %shard_map.122), kind=kLoop, calls=%fused_computation.30 | loop fusion | flops 327680 | bytes 1966080 | tf_op jit(solution)/shard_map/convert.3
  67.0 2.9 %collective-permute-done.13 = f32[136,256]{1,0:T(8,128)S(1)} collective-permute-done((f32[136,256]{1,0:T(8,128)S(1)}, f32[136,256]{1,0:T(8,128)S(1)}, u32[]{:S(2)}, u32[]{:S(2)}) %collective-permute-start.13) | collective-permute-done | bytes 139296 | tf_op jit(solution)/shard_map/ppermute | solution.py:119
  70.0 0.4 collective-permute-start.14
  70.5 0.1 copy.16
  70.6 0.1 copy.19
  70.7 0.1 copy.18
  70.9 0.1 copy.17
  71.0 3.9 %collective-permute-start.8 = (bf16[512,128]{1,0:T(8,128)(2,1)S(1)}, bf16[512,128]{1,0:T(8,128)(2,1)S(1)}, u32[]{:S(2)}, u32[]{:S(2)}) collective-permute-start(bf16[512,128]{1,0:T(8,128)(2,1)S(1)} %bitcast.55), channel_id=1, source_target_pairs={{0,28},{4,0},{8,4},{12,8},{16,12},{20,16},{24,20},{28,24},{1,29},{... | collective-permute-start | bytes 393224 | tf_op jit(solution)/shard_map/ppermute | solution.py:11
  74.9 0.0 collective-permute-start.9
  74.9 0.0 collective-permute-start.10
  74.9 3.8 %collective-permute-start.7 = (bf16[512,128]{1,0:T(8,128)(2,1)S(1)}, bf16[512,128]{1,0:T(8,128)(2,1)S(1)}, u32[]{:S(2)}, u32[]{:S(2)}) collective-permute-start(bf16[512,128]{1,0:T(8,128)(2,1)S(1)} %bitcast.52), channel_id=1, source_target_pairs={{0,24},{4,28},{8,0},{12,4},{16,8},{20,12},{24,16},{28,20},{1,25},{... | collective-permute-start | bytes 393224 | tf_op jit(solution)/shard_map/ppermute | solution.py:11
  78.7 1.0 %slice.64 = f32[4,128,128]{1,2,0:T(8,128)S(1)} slice(f32[20,128,128]{1,2,0:T(8,128)} %bitcast.47), slice={[8:12], [0:128], [0:128]} | slice | bytes 524288 | tf_op jit(solution)/shard_map/slice | solution.py:185
  79.7 0.1 copy.15
  79.9 0.0 collective-permute-done.14
  79.9 0.1 collective-permute-start.15
  80.0 0.0 collective-permute-done.8
  80.0 4.1 %collective-permute-done.9 = bf16[512,128]{1,0:T(8,128)(2,1)S(1)} collective-permute-done((bf16[512,128]{1,0:T(8,128)(2,1)S(1)}, bf16[512,128]{1,0:T(8,128)(2,1)S(1)}, u32[]{:S(2)}, u32[]{:S(2)}) %collective-permute-start.9) | collective-permute-done | bytes 131104 | tf_op jit(solution)/shard_map/ppermute | solution.py:11
  84.0 0.0 collective-permute-done.10
  84.0 0.0 collective-permute-done.7
  84.0 0.8 fusion.5
  84.8 0.0 collective-permute-done.15
  84.9 0.6 slice_multiply_fusion.1
  85.4 0.7 slice_multiply_fusion
  (11 shorter events, 0.2 us)
Async XLA Ops:
  0.6 37.5 %copy-start = (bf16[128,256]{1,0:T(8,128)(2,1)S(1)}, bf16[128,256]{1,0:T(8,128)(2,1)}, u32[]{:S(2)}) copy-start(bf16[128,256]{1,0:T(8,128)(2,1)} %param.15) | copy-start | bytes 196612
  2.4 9.4 %copy-start.1 = (bf16[512,128]{1,0:T(8,128)(2,1)}, bf16[512,128]{1,0:T(8,128)(2,1)S(1)}, u32[]{:S(2)}) copy-start(bf16[512,128]{1,0:T(8,128)(2,1)S(1)} %multiply_convert_fusion.1) | copy-start | bytes 393220
  2.4 14.1 %collective-permute-start.3 = (bf16[512,128]{1,0:T(8,128)(2,1)S(1)}, bf16[512,128]{1,0:T(8,128)(2,1)S(1)}, u32[]{:S(2)}, u32[]{:S(2)}) collective-permute-start(bf16[512,128]{1,0:T(8,128)(2,1)S(1)} %multiply_convert_fusion.1), channel_id=1, source_target_pairs={{0,24},{4,28},{8,0},{12,4},{16,8},{20,12},{24,16},{28,20},{1,25},{... | collective-permute-start | bytes 393224 | tf_op jit(solution)/shard_map/ppermute | solution.py:11
  7.5 9.0 %collective-permute-start.2 = (bf16[512,128]{1,0:T(8,128)(2,1)S(1)}, bf16[512,128]{1,0:T(8,128)(2,1)S(1)}, u32[]{:S(2)}, u32[]{:S(2)}) collective-permute-start(bf16[512,128]{1,0:T(8,128)(2,1)S(1)} %multiply_convert_fusion.1), channel_id=1, source_target_pairs={{0,28},{4,0},{8,4},{12,8},{16,12},{20,16},{24,20},{28,24},{1,29},{... | collective-permute-start | bytes 393224 | tf_op jit(solution)/shard_map/ppermute | solution.py:11
  8.9 8.8 %collective-permute-start.1 = (bf16[512,128]{1,0:T(8,128)(2,1)S(1)}, bf16[512,128]{1,0:T(8,128)(2,1)S(1)}, u32[]{:S(2)}, u32[]{:S(2)}) collective-permute-start(bf16[512,128]{1,0:T(8,128)(2,1)S(1)} %multiply_convert_fusion.1), channel_id=1, source_target_pairs={{0,4},{4,8},{8,12},{12,16},{16,20},{20,24},{24,28},{28,0},{1,5},{5... | collective-permute-start | bytes 393224 | tf_op jit(solution)/shard_map/ppermute | solution.py:11
  9.6 8.1 %collective-permute-start = (bf16[512,128]{1,0:T(8,128)(2,1)S(1)}, bf16[512,128]{1,0:T(8,128)(2,1)S(1)}, u32[]{:S(2)}, u32[]{:S(2)}) collective-permute-start(bf16[512,128]{1,0:T(8,128)(2,1)S(1)} %multiply_convert_fusion.1), channel_id=1, source_target_pairs={{0,8},{4,12},{8,16},{12,20},{16,24},{20,28},{24,0},{28,4},{1,9},{5... | collective-permute-start | bytes 393224 | tf_op jit(solution)/shard_map/ppermute | solution.py:11
  31.0 7.1 %copy-start.2 = (bf16[512,256]{1,0:T(8,128)(2,1)S(1)}, bf16[512,256]{1,0:T(8,128)(2,1)}, u32[]{:S(2)}) copy-start(bf16[512,256]{1,0:T(8,128)(2,1)} %param.17) | copy-start | bytes 786436
  31.0 7.1 %copy-start.3 = (f32[256]{0:T(256)S(1)}, f32[256]{0:T(256)}, u32[]{:S(2)}) copy-start(f32[256]{0:T(256)} %param.16) | copy-start | bytes 3076
  31.0 3.9 %collective-permute-start.6 = (bf16[512,128]{1,0:T(8,128)(2,1)S(1)}, bf16[512,128]{1,0:T(8,128)(2,1)S(1)}, u32[]{:S(2)}, u32[]{:S(2)}) collective-permute-start(bf16[512,128]{1,0:T(8,128)(2,1)S(1)} %bitcast.58), channel_id=1, source_target_pairs={{0,3},{1,0},{2,1},{3,2},{4,7},{5,4},{6,5},{7,6},{8,11},{9,8},{10,9... | collective-permute-start | bytes 393224 | tf_op jit(solution)/shard_map/ppermute | solution.py:11
  31.1 5.0 %collective-permute-start.4 = (bf16[512,128]{1,0:T(8,128)(2,1)S(1)}, bf16[512,128]{1,0:T(8,128)(2,1)S(1)}, u32[]{:S(2)}, u32[]{:S(2)}) collective-permute-start(bf16[512,128]{1,0:T(8,128)(2,1)S(1)} %bitcast.57), channel_id=1, source_target_pairs={{0,1},{1,2},{2,3},{3,0},{4,5},{5,6},{6,7},{7,4},{8,9},{9,10},{10,1... | collective-permute-start | bytes 393224 | tf_op jit(solution)/shard_map/ppermute | solution.py:11
  31.6 6.4 %collective-permute-start.5 = (bf16[512,128]{1,0:T(8,128)(2,1)S(1)}, bf16[512,128]{1,0:T(8,128)(2,1)S(1)}, u32[]{:S(2)}, u32[]{:S(2)}) collective-permute-start(bf16[512,128]{1,0:T(8,128)(2,1)S(1)} %bitcast.56), channel_id=1, source_target_pairs={{0,2},{1,3},{2,0},{3,1},{4,6},{5,7},{6,4},{7,5},{8,10},{9,11},{10,... | collective-permute-start | bytes 393224 | tf_op jit(solution)/shard_map/ppermute | solution.py:11
  39.8 10.8 %collective-permute-start.11 = (f32[136,256]{1,0:T(8,128)S(1)}, f32[136,256]{1,0:T(8,128)S(1)}, u32[]{:S(2)}, u32[]{:S(2)}) collective-permute-start(f32[136,256]{1,0:T(8,128)S(1)} %maximum_maximum_fusion), channel_id=1, source_target_pairs={{0,16},{1,17},{2,18},{3,19},{4,20},{5,21},{6,22},{7,23},{8,24},{9,... | collective-permute-start | bytes 417800 | tf_op jit(solution)/shard_map/ppermute | solution.py:119
  50.7 14.1 %collective-permute-start.12 = (f32[136,256]{1,0:T(8,128)S(1)}, f32[136,256]{1,0:T(8,128)S(1)}, u32[]{:S(2)}, u32[]{:S(2)}) collective-permute-start(f32[136,256]{1,0:T(8,128)S(1)} %fusion.14), channel_id=1, source_target_pairs={{0,8},{1,9},{2,10},{3,11},{4,12},{5,13},{6,14},{7,15},{8,0},{9,1},... | collective-permute-start | bytes 417800 | tf_op jit(solution)/shard_map/ppermute | solution.py:119
  64.8 5.1 %collective-permute-start.13 = (f32[136,256]{1,0:T(8,128)S(1)}, f32[136,256]{1,0:T(8,128)S(1)}, u32[]{:S(2)}, u32[]{:S(2)}) collective-permute-start(f32[136,256]{1,0:T(8,128)S(1)} %add.69), channel_id=1, source_target_pairs={{0,4},{1,5},{2,6},{3,7},{4,0},{5,1},{6,2},{7,3},{8,12},{9,13},{10,... | collective-permute-start | bytes 417800 | tf_op jit(solution)/shard_map/ppermute | solution.py:119
  70.0 9.9 %collective-permute-start.14 = (f32[136,256]{1,0:T(8,128)S(1)}, f32[136,256]{1,0:T(8,128)S(1)}, u32[]{:S(2)}, u32[]{:S(2)}) collective-permute-start(f32[136,256]{1,0:T(8,128)S(1)} %add.70), channel_id=1, source_target_pairs={{0,2},{1,3},{2,0},{3,1},{4,6},{5,7},{6,4},{7,5},{8,10},{9,11},{10,... | collective-permute-start | bytes 417800 | tf_op jit(solution)/shard_map/ppermute | solution.py:119
  71.0 9.0 %collective-permute-start.8 = (bf16[512,128]{1,0:T(8,128)(2,1)S(1)}, bf16[512,128]{1,0:T(8,128)(2,1)S(1)}, u32[]{:S(2)}, u32[]{:S(2)}) collective-permute-start(bf16[512,128]{1,0:T(8,128)(2,1)S(1)} %bitcast.55), channel_id=1, source_target_pairs={{0,28},{4,0},{8,4},{12,8},{16,12},{20,16},{24,20},{28,24},{1,29},{... | collective-permute-start | bytes 393224 | tf_op jit(solution)/shard_map/ppermute | solution.py:11
  74.9 9.1 %collective-permute-start.9 = (bf16[512,128]{1,0:T(8,128)(2,1)S(1)}, bf16[512,128]{1,0:T(8,128)(2,1)S(1)}, u32[]{:S(2)}, u32[]{:S(2)}) collective-permute-start(bf16[512,128]{1,0:T(8,128)(2,1)S(1)} %bitcast.54), channel_id=1, source_target_pairs={{0,4},{4,8},{8,12},{12,16},{16,20},{20,24},{24,28},{28,0},{1,5},{5... | collective-permute-start | bytes 393224 | tf_op jit(solution)/shard_map/ppermute | solution.py:11
  74.9 9.1 %collective-permute-start.10 = (bf16[512,128]{1,0:T(8,128)(2,1)S(1)}, bf16[512,128]{1,0:T(8,128)(2,1)S(1)}, u32[]{:S(2)}, u32[]{:S(2)}) collective-permute-start(bf16[512,128]{1,0:T(8,128)(2,1)S(1)} %bitcast.53), channel_id=1, source_target_pairs={{0,8},{4,12},{8,16},{12,20},{16,24},{20,28},{24,0},{28,4},{1,9},{5... | collective-permute-start | bytes 393224 | tf_op jit(solution)/shard_map/ppermute | solution.py:11
  74.9 9.1 %collective-permute-start.7 = (bf16[512,128]{1,0:T(8,128)(2,1)S(1)}, bf16[512,128]{1,0:T(8,128)(2,1)S(1)}, u32[]{:S(2)}, u32[]{:S(2)}) collective-permute-start(bf16[512,128]{1,0:T(8,128)(2,1)S(1)} %bitcast.52), channel_id=1, source_target_pairs={{0,24},{4,28},{8,0},{12,4},{16,8},{20,12},{24,16},{28,20},{1,25},{... | collective-permute-start | bytes 393224 | tf_op jit(solution)/shard_map/ppermute | solution.py:11
  79.9 4.9 %collective-permute-start.15 = (f32[136,256]{1,0:T(8,128)S(1)}, f32[136,256]{1,0:T(8,128)S(1)}, u32[]{:S(2)}, u32[]{:S(2)}) collective-permute-start(f32[136,256]{1,0:T(8,128)S(1)} %add.71), channel_id=1, source_target_pairs={{0,1},{1,0},{2,3},{3,2},{4,5},{5,4},{6,7},{7,6},{8,9},{9,8},{10,11... | collective-permute-start | bytes 417800 | tf_op jit(solution)/shard_map/ppermute | solution.py:119

commit v15 on v14

--- a/solution.py
+++ b/solution.py
@@ -74,7 +74,7 @@
             @pl.when(i < live)
             def _():
                 g = first + i
-                target = rows_ref[g] if forward else k * own_tiles + cols_ref[g]
+                target = rows_ref[g] if forward else p * own_tiles + cols_ref[g]
                 out_ref[target] += prod_ref[i]
 
     def adj_map(p, j, rows_ref, cols_ref, counts_ref):
@@ -177,16 +177,22 @@
     grad_hidden = (row_scale[:, None] * grad_rows).astype(jnp.bfloat16)
     block_grad = lax.all_gather(grad_hidden, "col", axis=0, tiled=True)
     grad_tiles_t = jnp.swapaxes(block_grad.reshape(block_tiles, tile_size, features), 1, 2)
-    outgoing_t = tile_products(
-        tile_rows, tile_cols, counts, adjacency, grad_tiles_t, offset_count * own_tiles,
-        own_tiles, False,
-    )
-    outgoing = jnp.swapaxes(outgoing_t, 1, 2).reshape(offset_count, own_rows, features)
-    total_back = outgoing[reach_steps]
-    for k in range(offset_count):
-        if k != reach_steps:
-            sent = outgoing[k].astype(jnp.bfloat16)
-            total_back = total_back + from_behind(sent, "blk", k - reach_steps).astype(jnp.float32)
+    far_t = tile_products(
+        tile_rows, tile_cols, counts, adjacency, grad_tiles_t, len(far) * own_tiles,
+        own_tiles, False, far,
+    )
+    far_back = jnp.swapaxes(far_t, 1, 2).reshape(len(far), own_rows, features)
+    received = [
+        from_behind(far_back[place].astype(jnp.bfloat16), "blk", k - reach_steps)
+        for place, k in enumerate(far)
+    ]
+    own_t = tile_products(
+        tile_rows, tile_cols, counts, adjacency, grad_tiles_t, own_tiles,
+        own_tiles, False, [reach_steps],
+    )
+    total_back = jnp.swapaxes(own_t, 1, 2).reshape(own_rows, features)
+    for part in received:
+        total_back = total_back + part.astype(jnp.float32)
     grad_features = (row_scale[:, None] * total_back).astype(jnp.bfloat16)
     return (activations, grad_features, weight_sum * norm_factor, bias_sum * norm_factor)
 

time: 87.4 us -> 84.2 us (0.963)
  waiting for transfers between devices: 13.3 us -> 8.08 us
  Pallas kernels: 28.4 us -> 31.4 us
  starting transfers between devices: 22.7 us -> 21.5 us
    ppermute x11, waiting for transfers between devices: 10.3 us -> 3.63 us  [from_behind(): lax.ppermute(value, axis, [(i, (i + by) % length) for i in range(length)])]
    pallas_call x3 -> x4, Pallas kernels: 28.4 us -> 31.4 us  [tile_products(): pl.pallas_call(kernel, grid_spec=pltpu.PrefetchScalarGridSpec(num_scalar_...]
    ppermute x5, starting transfers between devices: 6.13 us -> 4.05 us  [all_sum(): lax.ppermute(value, axes, [(i, i ^ bit) for i in range(size)])]
    ppermute x5, waiting for transfers between devices: 2.93 us -> 4.45 us  [all_sum(): lax.ppermute(value, axes, [(i, i ^ bit) for i in range(size)])]
    slice x7 -> x5, local copies, waits for them, and re-layouts: 1.67 us -> 0.56 us  [local(): far_back[place].astype(jnp.bfloat16)]
    transpose x0 -> x1, local copies, waits for them, and re-layouts: none -> 1.08 us  [local(): total_back = jnp.swapaxes(own_t, 1, 2).reshape(own_rows, features)]
    ppermute x11, starting transfers between devices: 16.6 us -> 17.5 us  [from_behind(): lax.ppermute(value, axis, [(i, (i + by) % length) for i in range(length)])]
  transfers between devices with their start and end apart: 16 -> 16, of which waited for: 6 -> 5; matrix products, arithmetic and copies ran while one was open for 8% -> 9% of each run, Pallas kernels for 20% -> 25%
where the time goes in v15:
time: 84.2 us; the launch traced here: 83.3 us
  Pallas kernels  31.4 us (37%)
  starting transfers between devices  21.5 us (26%)
  other arithmetic  8.94 us (11%)
  waiting for transfers between devices  8.08 us (10%)
  blocking collectives  7.21 us (9%)
  local copies, waits for them, and re-layouts  3.76 us (4%)
  matrix products  1.57 us (2%)
  between operations  0.87 us (1%)
    pallas_call x4, Pallas kernels, tile_products(): pl.pallas_call(kernel, grid_spec=pltpu.PrefetchScalarGridSpec(num_scalar_...  31.4 us
    ppermute x11, starting transfers between devices, from_behind(): lax.ppermute(value, axis, [(i, (i + by) % length) for i in range(length)])  17.5 us
    all_gather x1, blocking collectives, local(): block_grad = lax.all_gather(grad_hidden, 'col', axis=0, tiled=True)  7.21 us
    ppermute x5, waiting for transfers between devices, all_sum(): lax.ppermute(value, axes, [(i, i ^ bit) for i in range(size)])  4.45 us
    ppermute x5, starting transfers between devices, all_sum(): lax.ppermute(value, axes, [(i, i ^ bit) for i in range(size)])  4.05 us
    ppermute x11, waiting for transfers between devices, from_behind(): lax.ppermute(value, axis, [(i, (i + by) % length) for i in range(length)])  3.63 us
    another operation x2, other arithmetic  2.62 us
  transfers between devices with their start and end apart: 16, of which 5 were waited for; matrix products, arithmetic and copies ran while one was open for 9% of the time, Pallas kernels for 25%

profile of v15, /device:TPU:0, one launch (start us, length us, event | category | flops | bytes accessed | tf_op | source)
XLA Modules:
  0.0 83.3 jit_solution(4141257759939265209)
XLA Ops:
  0.6 0.0 copy-start
  0.6 0.7 convert_rsqrt_fusion
  1.4 1.0 %multiply_convert_fusion.1 = bf16[512,128]{1,0:T(8,128)(2,1)S(1)} fusion(bf16[512,128]{1,0:T(8,128)(2,1)} %param.9, f32[512]{0:T(512)S(1)} %convert_rsqrt_fusion), kind=kLoop, calls=%fused_computation.19 | loop fusion | flops 196608 | bytes 264192 | tf_op jit(solution)/shard_map/convert_element_type | solution.py:136
  2.4 0.0 copy-start.1
  2.4 3.1 %collective-permute-start = (bf16[512,128]{1,0:T(8,128)(2,1)S(1)}, bf16[512,128]{1,0:T(8,128)(2,1)S(1)}, u32[]{:S(2)}, u32[]{:S(2)}) collective-permute-start(bf16[512,128]{1,0:T(8,128)(2,1)S(1)} %multiply_convert_fusion.1), channel_id=1, source_target_pairs={{0,8},{4,12},{8,16},{12,20},{16,24},{20,28},{24,0},{28,4},{1,9},{5... | collective-permute-start | bytes 393224 | tf_op jit(solution)/shard_map/ppermute | solution.py:11
  5.5 1.5 %collective-permute-start.1 = (bf16[512,128]{1,0:T(8,128)(2,1)S(1)}, bf16[512,128]{1,0:T(8,128)(2,1)S(1)}, u32[]{:S(2)}, u32[]{:S(2)}) collective-permute-start(bf16[512,128]{1,0:T(8,128)(2,1)S(1)} %multiply_convert_fusion.1), channel_id=1, source_target_pairs={{0,4},{4,8},{8,12},{12,16},{16,20},{20,24},{24,28},{28,0},{1,5},{5... | collective-permute-start | bytes 393224 | tf_op jit(solution)/shard_map/ppermute | solution.py:11
  7.0 3.2 %collective-permute-start.2 = (bf16[512,128]{1,0:T(8,128)(2,1)S(1)}, bf16[512,128]{1,0:T(8,128)(2,1)S(1)}, u32[]{:S(2)}, u32[]{:S(2)}) collective-permute-start(bf16[512,128]{1,0:T(8,128)(2,1)S(1)} %multiply_convert_fusion.1), channel_id=1, source_target_pairs={{0,28},{4,0},{8,4},{12,8},{16,12},{20,16},{24,20},{28,24},{1,29},{... | collective-permute-start | bytes 393224 | tf_op jit(solution)/shard_map/ppermute | solution.py:11
  10.2 0.3 collective-permute-start.3
  10.5 1.3 %add_select_fusion.rows_ref = s32[360]{0:T(512)} fusion(s32[360]{0:T(512)} %rows_ref.3, s32[]{:T(128)S(6)} %mul.57), kind=kLoop, calls=%fused_computation.25 | loop fusion | flops 4320 | bytes 2884 | tf_op jit(solution)/shard_map/jit(remainder)/select_n | solution.py:138
  11.8 5.3 %shard_map.120.rest_0_ = f32[16,128,128]{2,1,0:T(8,128)} custom-call(s32[360]{0:T(512)} %add_select_fusion.rows_ref, s32[360]{0:T(512)} %cols_ref.7, s32[5]{0:T(128)} %counts_ref.7, bf16[360,128,128]{2,1,0:T(8,128)(2,1)} %adj_ref.7, bf16[4,128,128]{2,1,0:T(8,128)(2,1)} %bitcast.53), custom_call_target="tpu_custom_call" | custom-call | flops 1509949440 | bytes 12976128 | tf_op jit(solution)/shard_map/pallas_call | solution.py:90
  17.1 0.0 collective-permute-done
  17.2 0.0 collective-permute-done.1
  17.2 0.0 collective-permute-done.2
  17.2 0.0 collective-permute-done.3
  17.2 0.9 %pad_maximum_fusion = bf16[4,512,128]{2,1,0:T(8,128)(2,1)} fusion(bf16[1,512,128]{2,1,0:T(8,128)(2,1)S(1)} %bitcast.64, bf16[1,512,128]{2,1,0:T(8,128)(2,1)S(1)} %bitcast.63, bf16[1,512,128]{2,1,0:T(8,128)(2,1)S(1)} %bitcast.62, bf16[1,512,128]{2,1,0:T(8,128)(2,1)S(1)} %bitcast.61), kind=kLoop, calls=%fused_computation.3 | loop fusion | flops 786432 | bytes 1048576 | tf_op jit(solution)/shard_map/stack | solution.py:145
  18.1 10.6 %shard_map.121 = f32[16,128,128]{2,1,0:T(8,128)} custom-call(s32[360]{0:T(512)} %add_select_fusion.rows_ref, s32[360]{0:T(512)} %cols_ref.7, s32[5]{0:T(128)} %counts_ref.7, bf16[360,128,128]{2,1,0:T(8,128)(2,1)} %adj_ref.7, bf16[16,128,128]{2,1,0:T(8,128)(2,1)} %bitcast.50, f32[16,128,128]{2,1,0:T(8,128)} %shard_map.120.rest_0_), custom_call_target="tpu_custom_call", output_to_operand_aliasing={{}: (5, {})} | custom-call | flops 1509949440 | bytes 13369344 | tf_op jit(solution)/shard_map/pallas_call | solution.py:90
  28.7 1.3 %convert.11 = bf16[16,128,128]{2,1,0:T(8,128)(2,1)S(1)} convert(f32[16,128,128]{2,1,0:T(8,128)} %shard_map.121) | non-fusion elementwise | flops 262144 | bytes 1572864 | tf_op jit(solution)/shard_map/convert.6
  30.0 0.1 collective-permute-start.4
  30.1 1.9 %collective-permute-start.5 = (bf16[512,128]{1,0:T(8,128)(2,1)S(1)}, bf16[512,128]{1,0:T(8,128)(2,1)S(1)}, u32[]{:S(2)}, u32[]{:S(2)}) collective-permute-start(bf16[512,128]{1,0:T(8,128)(2,1)S(1)} %bitcast.59), channel_id=1, source_target_pairs={{0,2},{1,3},{2,0},{3,1},{4,6},{5,7},{6,4},{7,5},{8,10},{9,11},{10,... | collective-permute-start | bytes 393224 | tf_op jit(solution)/shard_map/ppermute | solution.py:11
  32.0 1.4 %collective-permute-start.6 = (bf16[512,128]{1,0:T(8,128)(2,1)S(1)}, bf16[512,128]{1,0:T(8,128)(2,1)S(1)}, u32[]{:S(2)}, u32[]{:S(2)}) collective-permute-start(bf16[512,128]{1,0:T(8,128)(2,1)S(1)} %bitcast.58), channel_id=1, source_target_pairs={{0,3},{1,0},{2,1},{3,2},{4,7},{5,4},{6,5},{7,6},{8,11},{9,8},{10,9... | collective-permute-start | bytes 393224 | tf_op jit(solution)/shard_map/ppermute | solution.py:11
  33.4 0.1 pad.2.clone
  33.4 1.0 %slice.55 = f32[4,128,128]{2,1,0:T(8,128)S(1)} slice(f32[16,128,128]{2,1,0:T(8,128)} %shard_map.121), slice={[0:4], [0:128], [0:128]} | slice | bytes 524288 | tf_op jit(solution)/shard_map/slice | solution.py:153
  34.4 0.8 collective-permute-done.4
  35.2 1.3 %collective-permute-done.5 = bf16[512,128]{1,0:T(8,128)(2,1)S(1)} collective-permute-done((bf16[512,128]{1,0:T(8,128)(2,1)S(1)}, bf16[512,128]{1,0:T(8,128)(2,1)S(1)}, u32[]{:S(2)}, u32[]{:S(2)}) %collective-permute-start.5) | collective-permute-done | bytes 131104 | tf_op jit(solution)/shard_map/ppermute | solution.py:11
  36.5 1.5 %collective-permute-done.6 = bf16[512,128]{1,0:T(8,128)(2,1)S(1)} collective-permute-done((bf16[512,128]{1,0:T(8,128)(2,1)S(1)}, bf16[512,128]{1,0:T(8,128)(2,1)S(1)}, u32[]{:S(2)}, u32[]{:S(2)}) %collective-permute-start.6) | collective-permute-done | bytes 131104 | tf_op jit(solution)/shard_map/ppermute | solution.py:11
  38.0 0.1 fusion.9
  38.1 0.0 copy-done
  38.2 0.0 copy-done.2
  38.2 1.1 %fusion.15 = (f32[256]{0:T(256)S(1)}, bf16[512,256]{1,0:T(8,128)(2,1)S(1)}, bf16[512,256]{1,0:T(8,128)(2,1)}) fusion(bf16[512,256]{1,0:T(8,128)(2,1)S(1)} %copy-done.2, f32[256]{0:T(256)S(1)} %copy-done.3, bf16[512,128]{1,0:T(8,128)(2,1)S(1)} %fusion.9, bf16[128,256]{1,0:T(8,128)(2,1)S(1)} %copy-done), kind=kOutput, calls=%fused_computation.32 | convolution fusion | flops 35389184 | bytes 985088 | tf_op jit(solution)/shard_map/dot_general | solution.py:158
  39.3 0.2 fusion.10
  39.5 0.2 fusion
  39.8 0.1 maximum_maximum_fusion
  39.8 0.8 collective-permute-start.11
  40.6 7.2 %all_gather.3 = bf16[2048,128]{1,0:T(8,128)(2,1)S(1)} all-gather(bf16[512,128]{1,0:T(8,128)(2,1)S(1)} %fusion), channel_id=1, replica_groups=mesh['blk'=8,'col'=4] {'col'}, dimensions={0}, use_global_device_ids=true | all-gather | bytes 655360 | tf_op jit(solution)/shard_map/all_gather | solution.py:178
  47.9 1.0 %copy.14 = bf16[16,128,128]{1,2,0:T(8,128)(2,1)} copy(bf16[16,128,128]{2,1,0:T(8,128)(2,1)S(1)} %bitcast.51) | data formatting | bytes 1048576 | tf_op jit(solution)/shard_map/reshape | solution.py:179
  48.9 10.3 %shard_map.123 = f32[16,128,128]{2,1,0:T(8,128)} custom-call(s32[360]{0:T(512)} %rows_ref.3, s32[360]{0:T(512)} %cols_ref.7, s32[5]{0:T(128)} %counts_ref.7, bf16[360,128,128]{2,1,0:T(8,128)(2,1)} %adj_ref.7, bf16[16,128,128]{2,1,0:T(8,128)(2,1)} %bitcast.48), custom_call_target="tpu_custom_call" | custom-call | flops 1509949440 | bytes 13369344 | tf_op jit(solution)/shard_map/pallas_call | solution.py:90
  59.2 0.0 collective-permute-done.11
  59.2 0.1 fusion.14
  59.3 0.9 %collective-permute-start.12 = (f32[136,256]{1,0:T(8,128)S(1)}, f32[136,256]{1,0:T(8,128)S(1)}, u32[]{:S(2)}, u32[]{:S(2)}) collective-permute-start(f32[136,256]{1,0:T(8,128)S(1)} %fusion.14), channel_id=1, source_target_pairs={{0,8},{1,9},{2,10},{3,11},{4,12},{5,13},{6,14},{7,15},{8,0},{9,1},... | collective-permute-start | bytes 417800 | tf_op jit(solution)/shard_map/ppermute | solution.py:119
  60.2 1.3 %convert_bitcast_fusion = bf16[16,128,128]{1,2,0:T(8,128)(2,1)S(1)} fusion(f32[16,128,128]{2,1,0:T(8,128)} %shard_map.123), kind=kLoop, calls=%fused_computation.4 | loop fusion | flops 262144 | bytes 1572864 | tf_op jit(solution)/shard_map/convert.3
  61.5 3.9 %collective-permute-done.12 = f32[136,256]{1,0:T(8,128)S(1)} collective-permute-done((f32[136,256]{1,0:T(8,128)S(1)}, f32[136,256]{1,0:T(8,128)S(1)}, u32[]{:S(2)}, u32[]{:S(2)}) %collective-permute-start.12) | collective-permute-done | bytes 139296 | tf_op jit(solution)/shard_map/ppermute | solution.py:119
  65.4 1.9 %collective-permute-start.13 = (f32[136,256]{1,0:T(8,128)S(1)}, f32[136,256]{1,0:T(8,128)S(1)}, u32[]{:S(2)}, u32[]{:S(2)}) collective-permute-start(f32[136,256]{1,0:T(8,128)S(1)} %add.69), channel_id=1, source_target_pairs={{0,4},{1,5},{2,6},{3,7},{4,0},{5,1},{6,2},{7,3},{8,12},{9,13},{10,... | collective-permute-start | bytes 417800 | tf_op jit(solution)/shard_map/ppermute | solution.py:119
  67.4 0.1 copy.19
  67.5 1.8 %collective-permute-start.10 = (bf16[512,128]{1,0:T(8,128)(2,1)S(1)}, bf16[512,128]{1,0:T(8,128)(2,1)S(1)}, u32[]{:S(2)}, u32[]{:S(2)}) collective-permute-start(bf16[512,128]{1,0:T(8,128)(2,1)S(1)} %bitcast.54), channel_id=1, source_target_pairs={{0,8},{4,12},{8,16},{12,20},{16,24},{20,28},{24,0},{28,4},{1,9},{5... | collective-permute-start | bytes 393224 | tf_op jit(solution)/shard_map/ppermute | solution.py:11
  69.3 0.1 copy.16
  69.4 2.1 %collective-permute-start.7 = (bf16[512,128]{1,0:T(8,128)(2,1)S(1)}, bf16[512,128]{1,0:T(8,128)(2,1)S(1)}, u32[]{:S(2)}, u32[]{:S(2)}) collective-permute-start(bf16[512,128]{1,0:T(8,128)(2,1)S(1)} %bitcast.55), channel_id=1, source_target_pairs={{0,24},{4,28},{8,0},{12,4},{16,8},{20,12},{24,16},{28,20},{1,25},{... | collective-permute-start | bytes 393224 | tf_op jit(solution)/shard_map/ppermute | solution.py:11
  71.6 0.1 copy.17
  71.7 0.1 collective-permute-start.8
  71.8 0.1 copy.18
  71.9 2.1 %collective-permute-start.9 = (bf16[512,128]{1,0:T(8,128)(2,1)S(1)}, bf16[512,128]{1,0:T(8,128)(2,1)S(1)}, u32[]{:S(2)}, u32[]{:S(2)}) collective-permute-start(bf16[512,128]{1,0:T(8,128)(2,1)S(1)} %bitcast.57), channel_id=1, source_target_pairs={{0,4},{4,8},{8,12},{12,16},{16,20},{20,24},{24,28},{28,0},{1,5},{5... | collective-permute-start | bytes 393224 | tf_op jit(solution)/shard_map/ppermute | solution.py:11
  74.0 0.0 collective-permute-done.13
  74.0 0.4 collective-permute-start.14
  74.4 5.1 %shard_map.122 = f32[4,128,128]{2,1,0:T(8,128)} custom-call(s32[360]{0:T(512)} %rows_ref.3, s32[360]{0:T(512)} %cols_ref.7, s32[5]{0:T(128)} %counts_ref.7, bf16[360,128,128]{2,1,0:T(8,128)(2,1)} %adj_ref.7, bf16[16,128,128]{2,1,0:T(8,128)(2,1)} %bitcast.49), custom_call_target="tpu_custom_call" | custom-call | flops 1509949440 | bytes 12582912 | tf_op jit(solution)/shard_map/pallas_call | solution.py:90
  79.5 1.1 %copy.15 = f32[4,128,128]{2,1,0:T(8,128)S(1)} copy(f32[4,128,128]{1,2,0:T(8,128)} %bitcast.52) | data formatting | bytes 524288 | tf_op jit(solution)/shard_map/transpose | solution.py:193
  80.6 0.0 collective-permute-done.14
  80.7 0.1 collective-permute-start.15
  80.7 0.0 collective-permute-done.10
  80.8 0.0 collective-permute-done.7
  80.8 0.0 collective-permute-done.8
  80.8 0.0 collective-permute-done.9
  80.8 0.8 fusion.5
  81.6 0.5 collective-permute-done.15
  82.1 0.7 slice_multiply_fusion
  82.8 0.6 slice_multiply_fusion.1
  (11 shorter events, 0.2 us)
Async XLA Ops:
  0.6 37.5 %copy-start = (bf16[128,256]{1,0:T(8,128)(2,1)S(1)}, bf16[128,256]{1,0:T(8,128)(2,1)}, u32[]{:S(2)}) copy-start(bf16[128,256]{1,0:T(8,128)(2,1)} %param.15) | copy-start | bytes 196612
  2.4 9.4 %copy-start.1 = (bf16[512,128]{1,0:T(8,128)(2,1)}, bf16[512,128]{1,0:T(8,128)(2,1)S(1)}, u32[]{:S(2)}) copy-start(bf16[512,128]{1,0:T(8,128)(2,1)S(1)} %multiply_convert_fusion.1) | copy-start | bytes 393220
  2.4 14.7 %collective-permute-start = (bf16[512,128]{1,0:T(8,128)(2,1)S(1)}, bf16[512,128]{1,0:T(8,128)(2,1)S(1)}, u32[]{:S(2)}, u32[]{:S(2)}) collective-permute-start(bf16[512,128]{1,0:T(8,128)(2,1)S(1)} %multiply_convert_fusion.1), channel_id=1, source_target_pairs={{0,8},{4,12},{8,16},{12,20},{16,24},{20,28},{24,0},{28,4},{1,9},{5... | collective-permute-start | bytes 393224 | tf_op jit(solution)/shard_map/ppermute | solution.py:11
  5.5 11.6 %collective-permute-start.1 = (bf16[512,128]{1,0:T(8,128)(2,1)S(1)}, bf16[512,128]{1,0:T(8,128)(2,1)S(1)}, u32[]{:S(2)}, u32[]{:S(2)}) collective-permute-start(bf16[512,128]{1,0:T(8,128)(2,1)S(1)} %multiply_convert_fusion.1), channel_id=1, source_target_pairs={{0,4},{4,8},{8,12},{12,16},{16,20},{20,24},{24,28},{28,0},{1,5},{5... | collective-permute-start | bytes 393224 | tf_op jit(solution)/shard_map/ppermute | solution.py:11
  7.0 10.2 %collective-permute-start.2 = (bf16[512,128]{1,0:T(8,128)(2,1)S(1)}, bf16[512,128]{1,0:T(8,128)(2,1)S(1)}, u32[]{:S(2)}, u32[]{:S(2)}) collective-permute-start(bf16[512,128]{1,0:T(8,128)(2,1)S(1)} %multiply_convert_fusion.1), channel_id=1, source_target_pairs={{0,28},{4,0},{8,4},{12,8},{16,12},{20,16},{24,20},{28,24},{1,29},{... | collective-permute-start | bytes 393224 | tf_op jit(solution)/shard_map/ppermute | solution.py:11
  10.2 6.9 %collective-permute-start.3 = (bf16[512,128]{1,0:T(8,128)(2,1)S(1)}, bf16[512,128]{1,0:T(8,128)(2,1)S(1)}, u32[]{:S(2)}, u32[]{:S(2)}) collective-permute-start(bf16[512,128]{1,0:T(8,128)(2,1)S(1)} %multiply_convert_fusion.1), channel_id=1, source_target_pairs={{0,24},{4,28},{8,0},{12,4},{16,8},{20,12},{24,16},{28,20},{1,25},{... | collective-permute-start | bytes 393224 | tf_op jit(solution)/shard_map/ppermute | solution.py:11
  17.1 21.0 %copy-start.2 = (bf16[512,256]{1,0:T(8,128)(2,1)S(1)}, bf16[512,256]{1,0:T(8,128)(2,1)}, u32[]{:S(2)}) copy-start(bf16[512,256]{1,0:T(8,128)(2,1)} %param.17) | copy-start | bytes 786436
  17.1 21.0 %copy-start.3 = (f32[256]{0:T(256)S(1)}, f32[256]{0:T(256)}, u32[]{:S(2)}) copy-start(f32[256]{0:T(256)} %param.16) | copy-start | bytes 3076
  30.0 5.2 %collective-permute-start.4 = (bf16[512,128]{1,0:T(8,128)(2,1)S(1)}, bf16[512,128]{1,0:T(8,128)(2,1)S(1)}, u32[]{:S(2)}, u32[]{:S(2)}) collective-permute-start(bf16[512,128]{1,0:T(8,128)(2,1)S(1)} %bitcast.60), channel_id=1, source_target_pairs={{0,1},{1,2},{2,3},{3,0},{4,5},{5,6},{6,7},{7,4},{8,9},{9,10},{10,1... | collective-permute-start | bytes 393224 | tf_op jit(solution)/shard_map/ppermute | solution.py:11
  30.1 6.4 %collective-permute-start.5 = (bf16[512,128]{1,0:T(8,128)(2,1)S(1)}, bf16[512,128]{1,0:T(8,128)(2,1)S(1)}, u32[]{:S(2)}, u32[]{:S(2)}) collective-permute-start(bf16[512,128]{1,0:T(8,128)(2,1)S(1)} %bitcast.59), channel_id=1, source_target_pairs={{0,2},{1,3},{2,0},{3,1},{4,6},{5,7},{6,4},{7,5},{8,10},{9,11},{10,... | collective-permute-start | bytes 393224 | tf_op jit(solution)/shard_map/ppermute | solution.py:11
  32.0 6.0 %collective-permute-start.6 = (bf16[512,128]{1,0:T(8,128)(2,1)S(1)}, bf16[512,128]{1,0:T(8,128)(2,1)S(1)}, u32[]{:S(2)}, u32[]{:S(2)}) collective-permute-start(bf16[512,128]{1,0:T(8,128)(2,1)S(1)} %bitcast.58), channel_id=1, source_target_pairs={{0,3},{1,0},{2,1},{3,2},{4,7},{5,4},{6,5},{7,6},{8,11},{9,8},{10,9... | collective-permute-start | bytes 393224 | tf_op jit(solution)/shard_map/ppermute | solution.py:11
  39.8 19.4 %collective-permute-start.11 = (f32[136,256]{1,0:T(8,128)S(1)}, f32[136,256]{1,0:T(8,128)S(1)}, u32[]{:S(2)}, u32[]{:S(2)}) collective-permute-start(f32[136,256]{1,0:T(8,128)S(1)} %maximum_maximum_fusion), channel_id=1, source_target_pairs={{0,16},{1,17},{2,18},{3,19},{4,20},{5,21},{6,22},{7,23},{8,24},{9,... | collective-permute-start | bytes 417800 | tf_op jit(solution)/shard_map/ppermute | solution.py:119
  59.3 6.1 %collective-permute-start.12 = (f32[136,256]{1,0:T(8,128)S(1)}, f32[136,256]{1,0:T(8,128)S(1)}, u32[]{:S(2)}, u32[]{:S(2)}) collective-permute-start(f32[136,256]{1,0:T(8,128)S(1)} %fusion.14), channel_id=1, source_target_pairs={{0,8},{1,9},{2,10},{3,11},{4,12},{5,13},{6,14},{7,15},{8,0},{9,1},... | collective-permute-start | bytes 417800 | tf_op jit(solution)/shard_map/ppermute | solution.py:119
  65.4 8.5 %collective-permute-start.13 = (f32[136,256]{1,0:T(8,128)S(1)}, f32[136,256]{1,0:T(8,128)S(1)}, u32[]{:S(2)}, u32[]{:S(2)}) collective-permute-start(f32[136,256]{1,0:T(8,128)S(1)} %add.69), channel_id=1, source_target_pairs={{0,4},{1,5},{2,6},{3,7},{4,0},{5,1},{6,2},{7,3},{8,12},{9,13},{10,... | collective-permute-start | bytes 417800 | tf_op jit(solution)/shard_map/ppermute | solution.py:119
  67.5 13.2 %collective-permute-start.10 = (bf16[512,128]{1,0:T(8,128)(2,1)S(1)}, bf16[512,128]{1,0:T(8,128)(2,1)S(1)}, u32[]{:S(2)}, u32[]{:S(2)}) collective-permute-start(bf16[512,128]{1,0:T(8,128)(2,1)S(1)} %bitcast.54), channel_id=1, source_target_pairs={{0,8},{4,12},{8,16},{12,20},{16,24},{20,28},{24,0},{28,4},{1,9},{5... | collective-permute-start | bytes 393224 | tf_op jit(solution)/shard_map/ppermute | solution.py:11
  69.4 11.3 %collective-permute-start.7 = (bf16[512,128]{1,0:T(8,128)(2,1)S(1)}, bf16[512,128]{1,0:T(8,128)(2,1)S(1)}, u32[]{:S(2)}, u32[]{:S(2)}) collective-permute-start(bf16[512,128]{1,0:T(8,128)(2,1)S(1)} %bitcast.55), channel_id=1, source_target_pairs={{0,24},{4,28},{8,0},{12,4},{16,8},{20,12},{24,16},{28,20},{1,25},{... | collective-permute-start | bytes 393224 | tf_op jit(solution)/shard_map/ppermute | solution.py:11
  71.7 9.1 %collective-permute-start.8 = (bf16[512,128]{1,0:T(8,128)(2,1)S(1)}, bf16[512,128]{1,0:T(8,128)(2,1)S(1)}, u32[]{:S(2)}, u32[]{:S(2)}) collective-permute-start(bf16[512,128]{1,0:T(8,128)(2,1)S(1)} %bitcast.56), channel_id=1, source_target_pairs={{0,28},{4,0},{8,4},{12,8},{16,12},{20,16},{24,20},{28,24},{1,29},{... | collective-permute-start | bytes 393224 | tf_op jit(solution)/shard_map/ppermute | solution.py:11
  71.9 8.9 %collective-permute-start.9 = (bf16[512,128]{1,0:T(8,128)(2,1)S(1)}, bf16[512,128]{1,0:T(8,128)(2,1)S(1)}, u32[]{:S(2)}, u32[]{:S(2)}) collective-permute-start(bf16[512,128]{1,0:T(8,128)(2,1)S(1)} %bitcast.57), channel_id=1, source_target_pairs={{0,4},{4,8},{8,12},{12,16},{16,20},{20,24},{24,28},{28,0},{1,5},{5... | collective-permute-start | bytes 393224 | tf_op jit(solution)/shard_map/ppermute | solution.py:11
  74.0 6.6 %collective-permute-start.14 = (f32[136,256]{1,0:T(8,128)S(1)}, f32[136,256]{1,0:T(8,128)S(1)}, u32[]{:S(2)}, u32[]{:S(2)}) collective-permute-start(f32[136,256]{1,0:T(8,128)S(1)} %add.70), channel_id=1, source_target_pairs={{0,2},{1,3},{2,0},{3,1},{4,6},{5,7},{6,4},{7,5},{8,10},{9,11},{10,... | collective-permute-start | bytes 417800 | tf_op jit(solution)/shard_map/ppermute | solution.py:119
  80.7 1.4 %collective-permute-start.15 = (f32[136,256]{1,0:T(8,128)S(1)}, f32[136,256]{1,0:T(8,128)S(1)}, u32[]{:S(2)}, u32[]{:S(2)}) collective-permute-start(f32[136,256]{1,0:T(8,128)S(1)} %add.71), channel_id=1, source_target_pairs={{0,1},{1,0},{2,3},{3,2},{4,5},{5,4},{6,7},{7,6},{8,9},{9,8},{10,11... | collective-permute-start | bytes 417800 | tf_op jit(solution)/shard_map/ppermute | solution.py:119

commit v16 on v15

--- a/solution.py
+++ b/solution.py
@@ -177,22 +177,24 @@
     grad_hidden = (row_scale[:, None] * grad_rows).astype(jnp.bfloat16)
     block_grad = lax.all_gather(grad_hidden, "col", axis=0, tiled=True)
     grad_tiles_t = jnp.swapaxes(block_grad.reshape(block_tiles, tile_size, features), 1, 2)
-    far_t = tile_products(
-        tile_rows, tile_cols, counts, adjacency, grad_tiles_t, len(far) * own_tiles,
-        own_tiles, False, far,
-    )
-    far_back = jnp.swapaxes(far_t, 1, 2).reshape(len(far), own_rows, features)
-    received = [
-        from_behind(far_back[place].astype(jnp.bfloat16), "blk", k - reach_steps)
-        for place, k in enumerate(far)
-    ]
+    received = {}
+    for distance in range(reach_steps, 0, -1):
+        pair = [reach_steps - distance, reach_steps + distance]
+        pair_t = tile_products(
+            tile_rows, tile_cols, counts, adjacency, grad_tiles_t, len(pair) * own_tiles,
+            own_tiles, False, pair,
+        )
+        pair_back = jnp.swapaxes(pair_t, 1, 2).reshape(len(pair), own_rows, features)
+        for place, k in enumerate(pair):
+            sent = pair_back[place].astype(jnp.bfloat16)
+            received[k] = from_behind(sent, "blk", k - reach_steps)
     own_t = tile_products(
         tile_rows, tile_cols, counts, adjacency, grad_tiles_t, own_tiles,
         own_tiles, False, [reach_steps],
     )
     total_back = jnp.swapaxes(own_t, 1, 2).reshape(own_rows, features)
-    for part in received:
-        total_back = total_back + part.astype(jnp.float32)
+    for k in sorted(received):
+        total_back = total_back + received[k].astype(jnp.float32)
     grad_features = (row_scale[:, None] * total_back).astype(jnp.bfloat16)
     return (activations, grad_features, weight_sum * norm_factor, bias_sum * norm_factor)
 

time: 84.2 us -> 90.9 us (1.080); the launches traced: 83.3 us -> 91.5 us
  waiting for transfers between devices: 8.08 us -> 13.5 us
  Pallas kernels: 31.4 us -> 33.6 us
    ppermute x5, waiting for transfers between devices: 4.45 us -> 9.86 us  [all_sum(): lax.ppermute(value, axes, [(i, i ^ bit) for i in range(size)])]
    pallas_call x4 -> x5, Pallas kernels: 31.4 us -> 33.6 us  [tile_products(): pl.pallas_call(kernel, grid_spec=pltpu.PrefetchScalarGridSpec(num_scalar_...]
    another operation x2 -> x3, other arithmetic: 2.62 us -> 3.46 us
  transfers between devices with their start and end apart: 16 -> 16, of which waited for: 5 -> 6; matrix products, arithmetic and copies ran while one was open for 9% -> 9% of each run, Pallas kernels for 25% -> 25%
where the time goes in v16:
time: 90.9 us; the launch traced here: 91.5 us
  Pallas kernels  33.6 us (37%)
  starting transfers between devices  21.1 us (23%)
  waiting for transfers between devices  13.5 us (15%)
  other arithmetic  9.77 us (11%)
  blocking collectives  7.28 us (8%)
  local copies, waits for them, and re-layouts  3.75 us (4%)
  matrix products  1.57 us (2%)
    pallas_call x5, Pallas kernels, tile_products(): pl.pallas_call(kernel, grid_spec=pltpu.PrefetchScalarGridSpec(num_scalar_...  33.6 us
    ppermute x11, starting transfers between devices, from_behind(): lax.ppermute(value, axis, [(i, (i + by) % length) for i in range(length)])  17.2 us
    ppermute x5, waiting for transfers between devices, all_sum(): lax.ppermute(value, axes, [(i, i ^ bit) for i in range(size)])  9.86 us
    all_gather x1, blocking collectives, local(): block_grad = lax.all_gather(grad_hidden, 'col', axis=0, tiled=True)  7.28 us
    ppermute x5, starting transfers between devices, all_sum(): lax.ppermute(value, axes, [(i, i ^ bit) for i in range(size)])  3.89 us
    ppermute x11, waiting for transfers between devices, from_behind(): lax.ppermute(value, axis, [(i, (i + by) % length) for i in range(length)])  3.63 us
    another operation x3, other arithmetic  3.46 us
  transfers between devices with their start and end apart: 16, of which 6 were waited for; matrix products, arithmetic and copies ran while one was open for 9% of the time, Pallas kernels for 25%

profile of v16, /device:TPU:0, one launch (start us, length us, event | category | flops | bytes accessed | tf_op | source)
XLA Modules:
  0.0 91.5 jit_solution(14663824350021320864)
XLA Ops:
  0.6 0.0 copy-start
  0.6 0.7 convert_rsqrt_fusion
  1.4 1.0 %multiply_convert_fusion.1 = bf16[512,128]{1,0:T(8,128)(2,1)S(1)} fusion(bf16[512,128]{1,0:T(8,128)(2,1)} %param.9, f32[512]{0:T(512)S(1)} %convert_rsqrt_fusion), kind=kLoop, calls=%fused_computation.20 | loop fusion | flops 196608 | bytes 264192 | tf_op jit(solution)/shard_map/convert_element_type | solution.py:136
  2.4 0.0 copy-start.1
  2.4 3.1 %collective-permute-start = (bf16[512,128]{1,0:T(8,128)(2,1)S(1)}, bf16[512,128]{1,0:T(8,128)(2,1)S(1)}, u32[]{:S(2)}, u32[]{:S(2)}) collective-permute-start(bf16[512,128]{1,0:T(8,128)(2,1)S(1)} %multiply_convert_fusion.1), channel_id=1, source_target_pairs={{0,8},{4,12},{8,16},{12,20},{16,24},{20,28},{24,0},{28,4},{1,9},{5... | collective-permute-start | bytes 393224 | tf_op jit(solution)/shard_map/ppermute | solution.py:11
  5.5 1.5 %collective-permute-start.1 = (bf16[512,128]{1,0:T(8,128)(2,1)S(1)}, bf16[512,128]{1,0:T(8,128)(2,1)S(1)}, u32[]{:S(2)}, u32[]{:S(2)}) collective-permute-start(bf16[512,128]{1,0:T(8,128)(2,1)S(1)} %multiply_convert_fusion.1), channel_id=1, source_target_pairs={{0,4},{4,8},{8,12},{12,16},{16,20},{20,24},{24,28},{28,0},{1,5},{5... | collective-permute-start | bytes 393224 | tf_op jit(solution)/shard_map/ppermute | solution.py:11
  7.0 3.2 %collective-permute-start.2 = (bf16[512,128]{1,0:T(8,128)(2,1)S(1)}, bf16[512,128]{1,0:T(8,128)(2,1)S(1)}, u32[]{:S(2)}, u32[]{:S(2)}) collective-permute-start(bf16[512,128]{1,0:T(8,128)(2,1)S(1)} %multiply_convert_fusion.1), channel_id=1, source_target_pairs={{0,28},{4,0},{8,4},{12,8},{16,12},{20,16},{24,20},{28,24},{1,29},{... | collective-permute-start | bytes 393224 | tf_op jit(solution)/shard_map/ppermute | solution.py:11
  10.2 0.3 collective-permute-start.3
  10.5 1.3 %add_select_fusion.rows_ref = s32[360]{0:T(512)} fusion(s32[360]{0:T(512)} %rows_ref.5, s32[]{:T(128)S(6)} %mul.57), kind=kLoop, calls=%fused_computation.26 | loop fusion | flops 4320 | bytes 2884 | tf_op jit(solution)/shard_map/jit(remainder)/select_n | solution.py:138
  11.8 5.3 %shard_map.120.rest_0_ = f32[16,128,128]{2,1,0:T(8,128)} custom-call(s32[360]{0:T(512)} %add_select_fusion.rows_ref, s32[360]{0:T(512)} %cols_ref.9, s32[5]{0:T(128)} %counts_ref.9, bf16[360,128,128]{2,1,0:T(8,128)(2,1)} %adj_ref.9, bf16[4,128,128]{2,1,0:T(8,128)(2,1)} %bitcast.56), custom_call_target="tpu_custom_call" | custom-call | flops 1509949440 | bytes 12976128 | tf_op jit(solution)/shard_map/pallas_call | solution.py:90
  17.2 0.0 collective-permute-done
  17.2 0.0 collective-permute-done.1
  17.2 0.0 collective-permute-done.2
  17.2 0.0 collective-permute-done.3
  17.2 0.9 pad_maximum_fusion
  18.1 10.4 %shard_map.121 = f32[16,128,128]{2,1,0:T(8,128)} custom-call(s32[360]{0:T(512)} %add_select_fusion.rows_ref, s32[360]{0:T(512)} %cols_ref.9, s32[5]{0:T(128)} %counts_ref.9, bf16[360,128,128]{2,1,0:T(8,128)(2,1)} %adj_ref.9, bf16[16,128,128]{2,1,0:T(8,128)(2,1)} %bitcast.53, f32[16,128,128]{2,1,0:T(8,128)} %shard_map.120.rest_0_), custom_call_target="tpu_custom_call", output_to_operand_aliasing={{}: (5, {})} | custom-call | flops 1509949440 | bytes 13369344 | tf_op jit(solution)/shard_map/pallas_call | solution.py:90
  28.4 1.3 %convert.13 = bf16[16,128,128]{2,1,0:T(8,128)(2,1)S(1)} convert(f32[16,128,128]{2,1,0:T(8,128)} %shard_map.121) | non-fusion elementwise | flops 262144 | bytes 1572864 | tf_op jit(solution)/shard_map/convert.6
  29.8 0.1 collective-permute-start.4
  29.8 1.6 %collective-permute-start.5 = (bf16[512,128]{1,0:T(8,128)(2,1)S(1)}, bf16[512,128]{1,0:T(8,128)(2,1)S(1)}, u32[]{:S(2)}, u32[]{:S(2)}) collective-permute-start(bf16[512,128]{1,0:T(8,128)(2,1)S(1)} %bitcast.62), channel_id=1, source_target_pairs={{0,2},{1,3},{2,0},{3,1},{4,6},{5,7},{6,4},{7,5},{8,10},{9,11},{10,... | collective-permute-start | bytes 393224 | tf_op jit(solution)/shard_map/ppermute | solution.py:11
  31.4 1.4 %collective-permute-start.6 = (bf16[512,128]{1,0:T(8,128)(2,1)S(1)}, bf16[512,128]{1,0:T(8,128)(2,1)S(1)}, u32[]{:S(2)}, u32[]{:S(2)}) collective-permute-start(bf16[512,128]{1,0:T(8,128)(2,1)S(1)} %bitcast.61), channel_id=1, source_target_pairs={{0,3},{1,0},{2,1},{3,2},{4,7},{5,4},{6,5},{7,6},{8,11},{9,8},{10,9... | collective-permute-start | bytes 393224 | tf_op jit(solution)/shard_map/ppermute | solution.py:11
  32.8 0.1 pad.2.clone
  32.9 1.0 %slice.55 = f32[4,128,128]{2,1,0:T(8,128)S(1)} slice(f32[16,128,128]{2,1,0:T(8,128)} %shard_map.121), slice={[0:4], [0:128], [0:128]} | slice | bytes 524288 | tf_op jit(solution)/shard_map/slice | solution.py:153
  33.9 1.1 %collective-permute-done.4 = bf16[512,128]{1,0:T(8,128)(2,1)S(1)} collective-permute-done((bf16[512,128]{1,0:T(8,128)(2,1)S(1)}, bf16[512,128]{1,0:T(8,128)(2,1)S(1)}, u32[]{:S(2)}, u32[]{:S(2)}) %collective-permute-start.4) | collective-permute-done | bytes 131104 | tf_op jit(solution)/shard_map/ppermute | solution.py:11
  35.0 1.3 %collective-permute-done.5 = bf16[512,128]{1,0:T(8,128)(2,1)S(1)} collective-permute-done((bf16[512,128]{1,0:T(8,128)(2,1)S(1)}, bf16[512,128]{1,0:T(8,128)(2,1)S(1)}, u32[]{:S(2)}, u32[]{:S(2)}) %collective-permute-start.5) | collective-permute-done | bytes 131104 | tf_op jit(solution)/shard_map/ppermute | solution.py:11
  36.3 1.2 %collective-permute-done.6 = bf16[512,128]{1,0:T(8,128)(2,1)S(1)} collective-permute-done((bf16[512,128]{1,0:T(8,128)(2,1)S(1)}, bf16[512,128]{1,0:T(8,128)(2,1)S(1)}, u32[]{:S(2)}, u32[]{:S(2)}) %collective-permute-start.6) | collective-permute-done | bytes 131104 | tf_op jit(solution)/shard_map/ppermute | solution.py:11
  37.5 0.1 fusion.9
  37.6 1.1 %fusion.15 = (f32[256]{0:T(256)S(1)}, bf16[512,256]{1,0:T(8,128)(2,1)S(1)}, bf16[512,256]{1,0:T(8,128)(2,1)}) fusion(bf16[512,256]{1,0:T(8,128)(2,1)S(1)} %copy-done.2, f32[256]{0:T(256)S(1)} %copy-done.3, bf16[512,128]{1,0:T(8,128)(2,1)S(1)} %fusion.9, bf16[128,256]{1,0:T(8,128)(2,1)S(1)} %copy-done), kind=kOutput, calls=%fused_computation.33 | convolution fusion | flops 35389184 | bytes 985088 | tf_op jit(solution)/shard_map/dot_general | solution.py:158
  38.7 0.2 fusion.10
  39.0 0.2 fusion
  39.2 0.1 maximum_maximum_fusion
  39.3 1.6 %collective-permute-start.11 = (f32[136,256]{1,0:T(8,128)S(1)}, f32[136,256]{1,0:T(8,128)S(1)}, u32[]{:S(2)}, u32[]{:S(2)}) collective-permute-start(f32[136,256]{1,0:T(8,128)S(1)} %maximum_maximum_fusion), channel_id=1, source_target_pairs={{0,16},{1,17},{2,18},{3,19},{4,20},{5,21},{6,22},{7,23},{8,24},{9,... | collective-permute-start | bytes 417800 | tf_op jit(solution)/shard_map/ppermute | solution.py:119
  40.9 7.3 %all_gather.3 = bf16[2048,128]{1,0:T(8,128)(2,1)S(1)} all-gather(bf16[512,128]{1,0:T(8,128)(2,1)S(1)} %fusion), channel_id=1, replica_groups=mesh['blk'=8,'col'=4] {'col'}, dimensions={0}, use_global_device_ids=true | all-gather | bytes 655360 | tf_op jit(solution)/shard_map/all_gather | solution.py:178
  48.2 1.0 %copy.14 = bf16[16,128,128]{1,2,0:T(8,128)(2,1)} copy(bf16[16,128,128]{2,1,0:T(8,128)(2,1)S(1)} %bitcast.54) | data formatting | bytes 1048576 | tf_op jit(solution)/shard_map/reshape | solution.py:179
  49.2 6.7 %shard_map.123 = f32[8,128,128]{2,1,0:T(8,128)} custom-call(s32[360]{0:T(512)} %rows_ref.5, s32[360]{0:T(512)} %cols_ref.9, s32[5]{0:T(128)} %counts_ref.9, bf16[360,128,128]{2,1,0:T(8,128)(2,1)} %adj_ref.9, bf16[16,128,128]{2,1,0:T(8,128)(2,1)} %bitcast.50), custom_call_target="tpu_custom_call" | custom-call | flops 1509949440 | bytes 12845056 | tf_op jit(solution)/shard_map/pallas_call | solution.py:90
  55.9 1.1 %convert_bitcast_fusion.1 = bf16[8,128,128]{1,2,0:T(8,128)(2,1)S(1)} fusion(f32[8,128,128]{2,1,0:T(8,128)} %shard_map.123), kind=kLoop, calls=%fused_computation.19 | loop fusion | flops 131072 | bytes 786432 | tf_op jit(solution)/shard_map/convert.3
  57.0 0.1 copy.19
  57.1 0.7 collective-permute-start.10
  57.8 0.1 copy.16
  58.0 3.2 %collective-permute-start.7 = (bf16[512,128]{1,0:T(8,128)(2,1)S(1)}, bf16[512,128]{1,0:T(8,128)(2,1)S(1)}, u32[]{:S(2)}, u32[]{:S(2)}) collective-permute-start(bf16[512,128]{1,0:T(8,128)(2,1)S(1)} %bitcast.58), channel_id=1, source_target_pairs={{0,24},{4,28},{8,0},{12,4},{16,8},{20,12},{24,16},{28,20},{1,25},{... | collective-permute-start | bytes 393224 | tf_op jit(solution)/shard_map/ppermute | solution.py:11
  61.2 6.1 %shard_map.124 = f32[8,128,128]{2,1,0:T(8,128)} custom-call(s32[360]{0:T(512)} %rows_ref.5, s32[360]{0:T(512)} %cols_ref.9, s32[5]{0:T(128)} %counts_ref.9, bf16[360,128,128]{2,1,0:T(8,128)(2,1)} %adj_ref.9, bf16[16,128,128]{2,1,0:T(8,128)(2,1)} %bitcast.51), custom_call_target="tpu_custom_call" | custom-call | flops 1509949440 | bytes 12845056 | tf_op jit(solution)/shard_map/pallas_call | solution.py:90
  67.3 0.0 collective-permute-done.11
  67.3 0.1 fusion.14
  67.4 0.1 collective-permute-start.12
  67.5 1.1 %convert_bitcast_fusion = bf16[8,128,128]{1,2,0:T(8,128)(2,1)S(1)} fusion(f32[8,128,128]{2,1,0:T(8,128)} %shard_map.124), kind=kLoop, calls=%fused_computation.18 | loop fusion | flops 131072 | bytes 786432 | tf_op jit(solution)/shard_map/convert.2
  68.6 4.7 %collective-permute-done.12 = f32[136,256]{1,0:T(8,128)S(1)} collective-permute-done((f32[136,256]{1,0:T(8,128)S(1)}, f32[136,256]{1,0:T(8,128)S(1)}, u32[]{:S(2)}, u32[]{:S(2)}) %collective-permute-start.12) | collective-permute-done | bytes 139296 | tf_op jit(solution)/shard_map/ppermute | solution.py:119
  73.3 0.7 collective-permute-start.13
  74.0 0.1 copy.17
  74.2 1.4 %collective-permute-start.8 = (bf16[512,128]{1,0:T(8,128)(2,1)S(1)}, bf16[512,128]{1,0:T(8,128)(2,1)S(1)}, u32[]{:S(2)}, u32[]{:S(2)}) collective-permute-start(bf16[512,128]{1,0:T(8,128)(2,1)S(1)} %bitcast.59), channel_id=1, source_target_pairs={{0,28},{4,0},{8,4},{12,8},{16,12},{20,16},{24,20},{28,24},{1,29},{... | collective-permute-start | bytes 393224 | tf_op jit(solution)/shard_map/ppermute | solution.py:11
  75.6 0.1 copy.18
  75.7 0.7 collective-permute-start.9
  76.4 4.7 %collective-permute-done.13 = f32[136,256]{1,0:T(8,128)S(1)} collective-permute-done((f32[136,256]{1,0:T(8,128)S(1)}, f32[136,256]{1,0:T(8,128)S(1)}, u32[]{:S(2)}, u32[]{:S(2)}) %collective-permute-start.13) | collective-permute-done | bytes 139296 | tf_op jit(solution)/shard_map/ppermute | solution.py:119
  81.1 1.4 %collective-permute-start.14 = (f32[136,256]{1,0:T(8,128)S(1)}, f32[136,256]{1,0:T(8,128)S(1)}, u32[]{:S(2)}, u32[]{:S(2)}) collective-permute-start(f32[136,256]{1,0:T(8,128)S(1)} %add.70), channel_id=1, source_target_pairs={{0,2},{1,3},{2,0},{3,1},{4,6},{5,7},{6,4},{7,5},{8,10},{9,11},{10,... | collective-permute-start | bytes 417800 | tf_op jit(solution)/shard_map/ppermute | solution.py:119
  82.5 5.1 %shard_map.122 = f32[4,128,128]{2,1,0:T(8,128)} custom-call(s32[360]{0:T(512)} %rows_ref.5, s32[360]{0:T(512)} %cols_ref.9, s32[5]{0:T(128)} %counts_ref.9, bf16[360,128,128]{2,1,0:T(8,128)(2,1)} %adj_ref.9, bf16[16,128,128]{2,1,0:T(8,128)(2,1)} %bitcast.52), custom_call_target="tpu_custom_call" | custom-call | flops 1509949440 | bytes 12582912 | tf_op jit(solution)/shard_map/pallas_call | solution.py:90
  87.7 1.1 %copy.15 = f32[4,128,128]{2,1,0:T(8,128)S(1)} copy(f32[4,128,128]{1,2,0:T(8,128)} %bitcast.55) | data formatting | bytes 524288 | tf_op jit(solution)/shard_map/transpose | solution.py:195
  88.7 0.0 collective-permute-done.14
  88.8 0.1 collective-permute-start.15
  88.9 0.0 collective-permute-done.10
  88.9 0.0 collective-permute-done.7
  88.9 0.0 collective-permute-done.8
  88.9 0.0 collective-permute-done.9
  88.9 0.8 fusion.5
  89.7 0.5 collective-permute-done.15
  90.2 0.7 slice_multiply_fusion
  90.9 0.6 slice_multiply_fusion.1
  (14 shorter events, 0.2 us)
Async XLA Ops:
  0.6 37.0 %copy-start = (bf16[128,256]{1,0:T(8,128)(2,1)S(1)}, bf16[128,256]{1,0:T(8,128)(2,1)}, u32[]{:S(2)}) copy-start(bf16[128,256]{1,0:T(8,128)(2,1)} %param.15) | copy-start | bytes 196612
  2.4 9.4 %copy-start.1 = (bf16[512,128]{1,0:T(8,128)(2,1)}, bf16[512,128]{1,0:T(8,128)(2,1)S(1)}, u32[]{:S(2)}) copy-start(bf16[512,128]{1,0:T(8,128)(2,1)S(1)} %multiply_convert_fusion.1) | copy-start | bytes 393220
  2.4 14.7 %collective-permute-start = (bf16[512,128]{1,0:T(8,128)(2,1)S(1)}, bf16[512,128]{1,0:T(8,128)(2,1)S(1)}, u32[]{:S(2)}, u32[]{:S(2)}) collective-permute-start(bf16[512,128]{1,0:T(8,128)(2,1)S(1)} %multiply_convert_fusion.1), channel_id=1, source_target_pairs={{0,8},{4,12},{8,16},{12,20},{16,24},{20,28},{24,0},{28,4},{1,9},{5... | collective-permute-start | bytes 393224 | tf_op jit(solution)/shard_map/ppermute | solution.py:11
  5.5 11.6 %collective-permute-start.1 = (bf16[512,128]{1,0:T(8,128)(2,1)S(1)}, bf16[512,128]{1,0:T(8,128)(2,1)S(1)}, u32[]{:S(2)}, u32[]{:S(2)}) collective-permute-start(bf16[512,128]{1,0:T(8,128)(2,1)S(1)} %multiply_convert_fusion.1), channel_id=1, source_target_pairs={{0,4},{4,8},{8,12},{12,16},{16,20},{20,24},{24,28},{28,0},{1,5},{5... | collective-permute-start | bytes 393224 | tf_op jit(solution)/shard_map/ppermute | solution.py:11
  7.0 10.2 %collective-permute-start.2 = (bf16[512,128]{1,0:T(8,128)(2,1)S(1)}, bf16[512,128]{1,0:T(8,128)(2,1)S(1)}, u32[]{:S(2)}, u32[]{:S(2)}) collective-permute-start(bf16[512,128]{1,0:T(8,128)(2,1)S(1)} %multiply_convert_fusion.1), channel_id=1, source_target_pairs={{0,28},{4,0},{8,4},{12,8},{16,12},{20,16},{24,20},{28,24},{1,29},{... | collective-permute-start | bytes 393224 | tf_op jit(solution)/shard_map/ppermute | solution.py:11
  10.2 6.9 %collective-permute-start.3 = (bf16[512,128]{1,0:T(8,128)(2,1)S(1)}, bf16[512,128]{1,0:T(8,128)(2,1)S(1)}, u32[]{:S(2)}, u32[]{:S(2)}) collective-permute-start(bf16[512,128]{1,0:T(8,128)(2,1)S(1)} %multiply_convert_fusion.1), channel_id=1, source_target_pairs={{0,24},{4,28},{8,0},{12,4},{16,8},{20,12},{24,16},{28,20},{1,25},{... | collective-permute-start | bytes 393224 | tf_op jit(solution)/shard_map/ppermute | solution.py:11
  17.1 20.5 %copy-start.2 = (bf16[512,256]{1,0:T(8,128)(2,1)S(1)}, bf16[512,256]{1,0:T(8,128)(2,1)}, u32[]{:S(2)}) copy-start(bf16[512,256]{1,0:T(8,128)(2,1)} %param.17) | copy-start | bytes 786436
  17.1 20.5 %copy-start.3 = (f32[256]{0:T(256)S(1)}, f32[256]{0:T(256)}, u32[]{:S(2)}) copy-start(f32[256]{0:T(256)} %param.16) | copy-start | bytes 3076
  29.8 5.2 %collective-permute-start.4 = (bf16[512,128]{1,0:T(8,128)(2,1)S(1)}, bf16[512,128]{1,0:T(8,128)(2,1)S(1)}, u32[]{:S(2)}, u32[]{:S(2)}) collective-permute-start(bf16[512,128]{1,0:T(8,128)(2,1)S(1)} %bitcast.63), channel_id=1, source_target_pairs={{0,1},{1,2},{2,3},{3,0},{4,5},{5,6},{6,7},{7,4},{8,9},{9,10},{10,1... | collective-permute-start | bytes 393224 | tf_op jit(solution)/shard_map/ppermute | solution.py:11
  29.8 6.4 %collective-permute-start.5 = (bf16[512,128]{1,0:T(8,128)(2,1)S(1)}, bf16[512,128]{1,0:T(8,128)(2,1)S(1)}, u32[]{:S(2)}, u32[]{:S(2)}) collective-permute-start(bf16[512,128]{1,0:T(8,128)(2,1)S(1)} %bitcast.62), channel_id=1, source_target_pairs={{0,2},{1,3},{2,0},{3,1},{4,6},{5,7},{6,4},{7,5},{8,10},{9,11},{10,... | collective-permute-start | bytes 393224 | tf_op jit(solution)/shard_map/ppermute | solution.py:11
  31.4 6.0 %collective-permute-start.6 = (bf16[512,128]{1,0:T(8,128)(2,1)S(1)}, bf16[512,128]{1,0:T(8,128)(2,1)S(1)}, u32[]{:S(2)}, u32[]{:S(2)}) collective-permute-start(bf16[512,128]{1,0:T(8,128)(2,1)S(1)} %bitcast.61), channel_id=1, source_target_pairs={{0,3},{1,0},{2,1},{3,2},{4,7},{5,4},{6,5},{7,6},{8,11},{9,8},{10,9... | collective-permute-start | bytes 393224 | tf_op jit(solution)/shard_map/ppermute | solution.py:11
  39.3 28.0 %collective-permute-start.11 = (f32[136,256]{1,0:T(8,128)S(1)}, f32[136,256]{1,0:T(8,128)S(1)}, u32[]{:S(2)}, u32[]{:S(2)}) collective-permute-start(f32[136,256]{1,0:T(8,128)S(1)} %maximum_maximum_fusion), channel_id=1, source_target_pairs={{0,16},{1,17},{2,18},{3,19},{4,20},{5,21},{6,22},{7,23},{8,24},{9,... | collective-permute-start | bytes 417800 | tf_op jit(solution)/shard_map/ppermute | solution.py:119
  57.1 31.7 %collective-permute-start.10 = (bf16[512,128]{1,0:T(8,128)(2,1)S(1)}, bf16[512,128]{1,0:T(8,128)(2,1)S(1)}, u32[]{:S(2)}, u32[]{:S(2)}) collective-permute-start(bf16[512,128]{1,0:T(8,128)(2,1)S(1)} %bitcast.57), channel_id=1, source_target_pairs={{0,8},{4,12},{8,16},{12,20},{16,24},{20,28},{24,0},{28,4},{1,9},{5... | collective-permute-start | bytes 393224 | tf_op jit(solution)/shard_map/ppermute | solution.py:11
  58.0 30.9 %collective-permute-start.7 = (bf16[512,128]{1,0:T(8,128)(2,1)S(1)}, bf16[512,128]{1,0:T(8,128)(2,1)S(1)}, u32[]{:S(2)}, u32[]{:S(2)}) collective-permute-start(bf16[512,128]{1,0:T(8,128)(2,1)S(1)} %bitcast.58), channel_id=1, source_target_pairs={{0,24},{4,28},{8,0},{12,4},{16,8},{20,12},{24,16},{28,20},{1,25},{... | collective-permute-start | bytes 393224 | tf_op jit(solution)/shard_map/ppermute | solution.py:11
  67.4 5.9 %collective-permute-start.12 = (f32[136,256]{1,0:T(8,128)S(1)}, f32[136,256]{1,0:T(8,128)S(1)}, u32[]{:S(2)}, u32[]{:S(2)}) collective-permute-start(f32[136,256]{1,0:T(8,128)S(1)} %fusion.14), channel_id=1, source_target_pairs={{0,8},{1,9},{2,10},{3,11},{4,12},{5,13},{6,14},{7,15},{8,0},{9,1},... | collective-permute-start | bytes 417800 | tf_op jit(solution)/shard_map/ppermute | solution.py:119
  73.3 7.8 %collective-permute-start.13 = (f32[136,256]{1,0:T(8,128)S(1)}, f32[136,256]{1,0:T(8,128)S(1)}, u32[]{:S(2)}, u32[]{:S(2)}) collective-permute-start(f32[136,256]{1,0:T(8,128)S(1)} %add.69), channel_id=1, source_target_pairs={{0,4},{1,5},{2,6},{3,7},{4,0},{5,1},{6,2},{7,3},{8,12},{9,13},{10,... | collective-permute-start | bytes 417800 | tf_op jit(solution)/shard_map/ppermute | solution.py:119
  74.2 14.7 %collective-permute-start.8 = (bf16[512,128]{1,0:T(8,128)(2,1)S(1)}, bf16[512,128]{1,0:T(8,128)(2,1)S(1)}, u32[]{:S(2)}, u32[]{:S(2)}) collective-permute-start(bf16[512,128]{1,0:T(8,128)(2,1)S(1)} %bitcast.59), channel_id=1, source_target_pairs={{0,28},{4,0},{8,4},{12,8},{16,12},{20,16},{24,20},{28,24},{1,29},{... | collective-permute-start | bytes 393224 | tf_op jit(solution)/shard_map/ppermute | solution.py:11
  75.7 13.2 %collective-permute-start.9 = (bf16[512,128]{1,0:T(8,128)(2,1)S(1)}, bf16[512,128]{1,0:T(8,128)(2,1)S(1)}, u32[]{:S(2)}, u32[]{:S(2)}) collective-permute-start(bf16[512,128]{1,0:T(8,128)(2,1)S(1)} %bitcast.60), channel_id=1, source_target_pairs={{0,4},{4,8},{8,12},{12,16},{16,20},{20,24},{24,28},{28,0},{1,5},{5... | collective-permute-start | bytes 393224 | tf_op jit(solution)/shard_map/ppermute | solution.py:11
  81.1 7.6 %collective-permute-start.14 = (f32[136,256]{1,0:T(8,128)S(1)}, f32[136,256]{1,0:T(8,128)S(1)}, u32[]{:S(2)}, u32[]{:S(2)}) collective-permute-start(f32[136,256]{1,0:T(8,128)S(1)} %add.70), channel_id=1, source_target_pairs={{0,2},{1,3},{2,0},{3,1},{4,6},{5,7},{6,4},{7,5},{8,10},{9,11},{10,... | collective-permute-start | bytes 417800 | tf_op jit(solution)/shard_map/ppermute | solution.py:119
  88.8 1.4 %collective-permute-start.15 = (f32[136,256]{1,0:T(8,128)S(1)}, f32[136,256]{1,0:T(8,128)S(1)}, u32[]{:S(2)}, u32[]{:S(2)}) collective-permute-start(f32[136,256]{1,0:T(8,128)S(1)} %add.71), channel_id=1, source_target_pairs={{0,1},{1,0},{2,3},{3,2},{4,5},{5,4},{6,7},{7,6},{8,9},{9,8},{10,11... | collective-permute-start | bytes 417800 | tf_op jit(solution)/shard_map/ppermute | solution.py:119
